TPU v7x, 32 devices: a whole 2x2x4 slice. The times are simulated.
32 devices in a mesh: pulse: 8 (over z, x), rng: 4 (over y, core).
Axes of the slice: x: 2, y: 2, z: 4, core: 2. Of those that a mesh axis runs over, the one named last changes fastest.
Arguments:
- echoes: float32 [2, 192, 32768], P(None, 'pulse', 'rng'), may hold values from -6 to 6
- row_list: int32 [192], replicated, may hold values from 0 to 191, as said below
- wavenumber: float32 [4, 8192], P(None, ('pulse', 'rng')), may hold values from 1 to 1.5
- az_wavenumber: float32 [192], replicated, may hold values from -0.6 to 0.6
- stolt_offset: int32 [4, 8192], P(None, ('pulse', 'rng')), may hold values from -6 to 32765, as said below
- stolt_coef: float32 [8, 4, 8192], P(None, None, ('pulse', 'rng')), may hold values from -2 to 2
Outputs:
- image: float32 [2, 4, 8192, 192], P(None, None, ('pulse', 'rng'))
Inputs may be any that keep to these rules, and one draw needn't show every extreme that they name: row_list[j] - j lies in -8 .. 8, and both ends are taken. stolt_offset[s, q] - (s * 8192 + q) lies in -6 .. -2, and both ends are taken.
All inputs are finite; a program needn't handle non-finite values.
Results may differ from a plain program's by a relative error of at most 0.00007.
Values sent between devices are 32-bit elements; how exact they have to be, the bound alone decides.
No kernel may reach another device: no remote copies, remote signals or barrier semaphores. Data moves between devices by JAX's collectives and lax.ppermute only.
A program may use at most 64 MiB of HBM per device.

v0:
```python
import math

import jax
import jax.numpy as jnp
from jax import lax
from jax.sharding import PartitionSpec as P

phase_scale = 24.0
highest = lax.Precision.HIGHEST
RIM = 6


def split_factor(length):
    outer_len = 1
    while length % (outer_len * 2) == 0 and outer_len * 2 * (outer_len * 2) <= length:
        outer_len = outer_len * 2
    return outer_len


def dft_table(length, factor):
    index_range = jnp.arange(length, dtype=jnp.int32)
    product = index_range[:, None] * index_range[None, :] % length
    twist_angle = product.astype(jnp.float32) * (-2.0 * math.pi / length)
    return (jnp.cos(twist_angle) * factor, jnp.sin(twist_angle) * factor)


def complex_einsum(pattern, real_part, imag_part, table_real, table_imag):

    def contract(operand, matrix):
        return jnp.einsum(pattern, operand, matrix, precision=highest)

    return (
        contract(real_part, table_real) - contract(imag_part, table_imag),
        contract(real_part, table_imag) + contract(imag_part, table_real),
    )


def last_axis_dft(real_part, imag_part, length, factor):
    inner_len = split_factor(length)
    outer_len = length // inner_len
    leading = real_part.shape[:-1]
    real_part = real_part.reshape(leading + (outer_len, inner_len))
    imag_part = imag_part.reshape(leading + (outer_len, inner_len))
    outer_real, outer_imag = dft_table(outer_len, 1.0)
    real_part, imag_part = complex_einsum(
        "...ba,ub->...ua", real_part, imag_part, outer_real, outer_imag
    )
    col_index = jnp.arange(outer_len, dtype=jnp.int32)[:, None]
    row_index = jnp.arange(inner_len, dtype=jnp.int32)[None, :]
    twist_angle = (col_index * row_index % length).astype(jnp.float32) * (-2.0 * math.pi / length)
    twist_real = jnp.cos(twist_angle)
    twist_imag = jnp.sin(twist_angle)
    real_part, imag_part = (
        real_part * twist_real - imag_part * twist_imag,
        real_part * twist_imag + imag_part * twist_real,
    )
    inner_real, inner_imag = dft_table(inner_len, factor)
    real_part, imag_part = complex_einsum(
        "...ua,va->...vu", real_part, imag_part, inner_real, inner_imag
    )
    return (real_part.reshape(leading + (length,)), imag_part.reshape(leading + (length,)))


def azimuth_matrix(row_list, scale):
    total_rows = row_list.shape[0]
    pulse_index = jnp.arange(total_rows, dtype=jnp.int32)
    select = (row_list[:, None] == pulse_index[None, :]).astype(jnp.float32)
    dft_real, dft_imag = dft_table(total_rows, scale)
    fold_real = jnp.einsum("ji,ja->ai", select, dft_real, precision=highest)
    fold_imag = jnp.einsum("ji,ja->ai", select, dft_imag, precision=highest)
    top = jnp.concatenate([fold_real, -fold_imag], axis=1)
    bottom = jnp.concatenate([fold_imag, fold_real], axis=1)
    return jnp.concatenate([top, bottom], axis=0)


def on_device(echoes, row_list, wavenumber, az_wavenumber, stolt_offset, stolt_coef):
    rows_here = echoes.shape[1]
    span_len = echoes.shape[2]
    lane_count = lax.axis_size("rng")
    pulse_count = lax.axis_size("pulse")
    device_count = pulse_count * lane_count
    total_rows = row_list.shape[0]
    range_len = span_len * lane_count
    block_len = span_len // device_count
    position = lax.axis_index(("pulse", "rng"))

    real_part, imag_part = last_axis_dft(echoes[0], echoes[1], span_len, 1.0)
    spectrum = jnp.stack([real_part, imag_part])
    spectrum = spectrum.reshape(2, rows_here, device_count, block_len)
    spectrum = jnp.transpose(spectrum, (2, 0, 1, 3))
    spectrum = lax.all_to_all(
        spectrum, ("pulse", "rng"), split_axis=0, concat_axis=0, tiled=True
    )
    spectrum = spectrum.reshape(pulse_count, lane_count, 2, rows_here, block_len)

    q_global = position * block_len + jnp.arange(block_len, dtype=jnp.int32)
    bin_index = jnp.arange(lane_count, dtype=jnp.int32)[:, None] * span_len + q_global[None, :]
    lane_index = jnp.arange(lane_count, dtype=jnp.int32)
    turn = (lane_index[:, None, None] * bin_index[None, :, :]) % range_len
    turn_angle = turn.astype(jnp.float32) * (-2.0 * math.pi / range_len)
    turn_real = jnp.cos(turn_angle)
    turn_imag = jnp.sin(turn_angle)
    lane_real = spectrum[:, :, 0]
    lane_imag = spectrum[:, :, 1]
    combined_real = []
    combined_imag = []
    for s in range(lane_count):
        acc_real = 0.0
        acc_imag = 0.0
        for r in range(lane_count):
            wr = turn_real[r, s][None, None, :]
            wi = turn_imag[r, s][None, None, :]
            acc_real = acc_real + lane_real[:, r] * wr - lane_imag[:, r] * wi
            acc_imag = acc_imag + lane_real[:, r] * wi + lane_imag[:, r] * wr
        combined_real.append(acc_real)
        combined_imag.append(acc_imag)
    combined = jnp.stack([jnp.stack(combined_real), jnp.stack(combined_imag)], axis=1)
    combined = combined.reshape(lane_count, 2 * total_rows, block_len)

    fold = azimuth_matrix(row_list, 1.0 / math.sqrt(range_len * total_rows))
    azimuth = jnp.einsum("xy,syq->sxq", fold, combined, precision=highest)
    azimuth = azimuth.reshape(lane_count, 2, total_rows, block_len)

    phase_angle = phase_scale * jnp.sqrt(
        wavenumber[:, None, :] ** 2 - az_wavenumber[None, :, None] ** 2
    )
    phase_real = jnp.cos(phase_angle)
    phase_imag = jnp.sin(phase_angle)
    az_real = azimuth[:, 0]
    az_imag = azimuth[:, 1]
    focused = jnp.stack(
        [
            az_real * phase_real - az_imag * phase_imag,
            az_real * phase_imag + az_imag * phase_real,
        ],
        axis=1,
    )

    axes = ("pulse", "rng")
    up = [(i, (i + 1) % device_count) for i in range(device_count)]
    down = [(j, i) for i, j in up]
    right_edge = jnp.swapaxes(focused[..., block_len - RIM:], 2, 3)
    left_edge = jnp.swapaxes(focused[..., :RIM], 2, 3)
    left_rim = lax.ppermute(right_edge, axes, up)
    right_rim = lax.ppermute(left_edge, axes, down)
    left_rim = jnp.where(position == 0, jnp.roll(left_rim, 1, axis=0), left_rim)
    right_rim = jnp.where(
        position == device_count - 1, jnp.roll(right_rim, -1, axis=0), right_rim
    )

    tap_count = stolt_coef.shape[0]
    piece_index = jnp.arange(block_len, dtype=jnp.int32)
    relative = stolt_offset - bin_index + RIM
    tap_index = jnp.arange(tap_count, dtype=jnp.int32)
    source = stolt_offset[None, :, :] + tap_index[:, None, None]
    inside = (source >= 0) & (source < range_len)
    weights = jnp.where(inside, stolt_coef, 0.0)
    columns = jnp.arange(block_len + 2 * RIM, dtype=jnp.int32)
    target = piece_index[:, None] + relative[:, :, None]
    band = jnp.zeros((lane_count, block_len, block_len + 2 * RIM), jnp.float32)
    for t in range(tap_count):
        band = band + jnp.where(columns[None, None, :] == target + t, weights[t][:, :, None], 0.0)
    band_left = band[:, :, :RIM]
    band_main = band[:, :, RIM:RIM + block_len]
    band_right = band[:, :, RIM + block_len:]

    image = jnp.einsum("sij,scaj->csia", band_main, focused, precision=highest)
    image = image + jnp.einsum("sij,scja->csia", band_left, left_rim, precision=highest)
    image = image + jnp.einsum("sij,scja->csia", band_right, right_rim, precision=highest)
    return image


def solution(mesh):
    in_specs = (
        P(None, "pulse", "rng"),
        P(),
        P(None, ("pulse", "rng")),
        P(),
        P(None, ("pulse", "rng")),
        P(None, None, ("pulse", "rng")),
    )
    out_specs = P(None, None, ("pulse", "rng"), None)
    return jax.shard_map(
        on_device, mesh=mesh, in_specs=in_specs, out_specs=out_specs, check_vma=False
    )
```

profile of v0, /device:TPU:0, one launch (start us, length us, event | category | flops | bytes accessed | tf_op | source)
XLA Modules:
  0.0 97.2 jit_solution(16195857694394594191)
XLA Ops:
  0.1 2.4 %fusion.138 = (f32[1,24,8192]{2,1,0:T(8,128)}, f32[1,24,8192]{2,1,0:T(8,128)S(1)}) fusion(f32[2,24,8192]{2,1,0:T(8,128)} %param.6), kind=kLoop, calls=%fused_computation.212 | loop fusion | bytes 3145728 | tf_op jit(solution)/shard_map/slice | solution.py:87
  3.6 1.0 %fusion.73 = f32[128,1536]{0,1:S(1)} fusion(f32[128,1536]{0,1:T(8,128)S(1)} %bitcast.290), kind=kOutput, calls=%fused_computation.131 | convolution fusion | flops 302219264 | bytes 1572864
  4.6 1.9 %fusion.71 = f32[128,1536]{0,1} fusion(f32[128,1536]{0,1:T(8,128)S(1)} %bitcast.291), kind=kOutput, calls=%fused_computation.130 | convolution fusion | flops 302219264 | bytes 1572864
  6.5 1.8 %reshape_squeeze.7 = f32[24,128,64]{2,1,0:T(8,128)S(1)} reshape(f32[1,24,8192]{2,1,0:T(8,128)} %get-tuple-element.15) | data formatting | bytes 1572864 | tf_op jit(solution)/shard_map/reshape;squeeze | solution.py:43
  8.8 1.0 %fusion.69 = f32[128,1536]{0,1:S(1)} fusion(f32[128,1536]{0,1:T(8,128)S(1)} %bitcast.292), kind=kOutput, calls=%fused_computation.129 | convolution fusion | flops 302219264 | bytes 1572864
  9.8 1.0 %fusion.75 = f32[128,1536]{0,1:S(1)} fusion(f32[128,1536]{0,1:T(8,128)S(1)} %bitcast.293), kind=kOutput, calls=%fused_computation.132 | convolution fusion | flops 302219264 | bytes 1572864
  14.7 0.9 fusion.2
  16.4 1.3 %maximum_bitcast_fusion = f32[32,2,24,256]{3,2,1,0:T(8,128)} fusion(f32[1,24,32,256]{3,1,0,2:T(8,128)S(1)} %copy.52, f32[1,24,32,256]{3,1,0,2:T(8,128)S(1)} %copy.51), kind=kLoop, calls=%fused_computation.6 | loop fusion | flops 393216 | bytes 3145728 | tf_op jit(solution)/shard_map/transpose | solution.py:90
  17.7 7.3 %all-to-all-start = ((f32[32,2,24,256]{3,2,1,0:T(8,128)}), f32[32,2,24,256]{3,2,1,0:T(8,128)S(1)}, u32[]{:S(2)}, u32[]{:S(2)}) async-start(f32[32,2,24,256]{3,2,1,0:T(8,128)} %maximum_bitcast_fusion), calls=%async_computation | async-start | bytes 3145728 | tf_op jit(solution)/shard_map/all_to_all | solution.py:91
  27.2 1.1 %fusion.27 = f32[192,192]{1,0:T(8,128)S(1)} fusion(s32[192]{0:T(256)S(1)} %copy-done.37), kind=kOutput, calls=%fused_computation.70 | convolution fusion | flops 85340160 | bytes 148224 | tf_op jit(solution)/shard_map/ji,ja->ai/dot_general | solution.py:69
  28.3 1.8 %fusion.141 = (f32[192,192]{1,0:T(8,128)S(1)}, f32[192,192]{1,0:T(8,128)}) fusion(s32[192]{0:T(256)S(1)} %copy-done.37), kind=kOutput, calls=%fused_computation.215 | convolution fusion | flops 85377024 | bytes 295680 | tf_op jit(solution)/shard_map/ji,ja->ai/dot_general | solution.py:70
  30.0 2.4 %select_add_fusion = f32[4,256,268]{2,1,0:T(8,128)S(1)} fusion(f32[4,256]{1,0:T(4,128)S(1)} %get-tuple-element.18, s32[4,256]{1,0:T(4,128)S(1)} %get-tuple-element.62, f32[4,256]{1,0:T(4,128)S(1)} %get-tuple-element.19, s32[4,256]{1,0:T(4,128)S(1)} %get-tuple-element.58, f32[4,256]{1,0:T(4,128)S(1)} %get-tuple-element.20, s32[4,256]{1,0:T(4,128)S(1)} %get-tuple-element.59, ...), kind=kLoop, calls=%fused_computation.9 | loop fusion | flops 6311936 | bytes 1163264 | tf_op jit(solution)/shard_map/add | solution.py:162
  32.4 30.1 %all-to-all-done = f32[32,2,24,256]{3,2,1,0:T(8,128)S(1)} async-done(((f32[32,2,24,256]{3,2,1,0:T(8,128)}), f32[32,2,24,256]{3,2,1,0:T(8,128)S(1)}, u32[]{:S(2)}, u32[]{:S(2)}) %all-to-all-start) | async-done | bytes 1572896 | tf_op jit(solution)/shard_map/all_to_all | solution.py:91
  67.0 5.4 %convolution_bitcast_fusion = f32[4,384,256]{1,2,0:T(8,128)S(1)} fusion(f32[4,384,256]{2,1,0:T(8,128)S(1)} %bitcast.295, f32[192,192]{1,0:T(8,128)S(1)} %fusion.27, f32[192,192]{1,0:T(8,128)S(1)} %copy-done.2, f32[192,192]{1,0:T(8,128)S(1)} %get-tuple-element.66), kind=kOutput, calls=%fused_computation.18 | convolution fusion | flops 1812381696 | bytes 3588096 | tf_op jit(solution)/shard_map/xy,syq->sxq/dot_general | solution.py:121
  72.4 1.6 %copy.59 = f32[4,384,256]{2,1,0:T(8,128)} copy(f32[4,384,256]{1,2,0:T(8,128)S(1)} %convolution_bitcast_fusion) | data formatting | bytes 3145728 | tf_op jit(solution)/shard_map/xy,syq->sxq/transpose | solution.py:121
  74.0 5.6 %multiply_subtract_fusion = (f32[4,1,192,256]{3,2,1,0:T(8,128)S(1)}, f32[4,1,192,256]{3,2,1,0:T(8,128)S(1)}) fusion(f32[4,2,192,256]{3,2,1,0:T(8,128)} %bitcast.296, f32[192]{0:T(256)S(1)} %copy-done.35, f32[4,256]{1,0:T(4,128)S(1)} %integer_pow.8), kind=kLoop, calls=%fused_computation.39 | loop fusion | flops 1572864 | bytes 3150592 | tf_op jit(solution)/shard_map/sub | solution.py:133
  79.7 1.4 %fusion.6 = (f32[4,2,6,192]{2,3,1,0:T(8,128)}, f32[4,2,6,192]{2,3,1,0:T(8,128)}) fusion(f32[4,1,192,256]{3,2,1,0:T(8,128)S(1)} %get-tuple-element.9, f32[4,1,192,256]{3,2,1,0:T(8,128)S(1)} %get-tuple-element.10), kind=kLoop, calls=%fused_computation.27 | loop fusion | flops 18432 | bytes 1646592 | tf_op jit(solution)/shard_map/transpose | solution.py:143
  81.1 1.5 %copy.60 = f32[4,2,6,192]{3,0,2,1:T(4,128)S(1)} copy(f32[4,2,6,192]{2,3,1,0:T(8,128)} %get-tuple-element.12) | data formatting | bytes 73728 | tf_op jit(solution)/shard_map/transpose | solution.py:142
  82.6 2.9 %fusion = f32[4,2,192,256]{3,2,1,0:T(8,128)} fusion(f32[4,1,192,256]{3,2,1,0:T(8,128)S(1)} %get-tuple-element.10, f32[4,1,192,256]{3,2,1,0:T(8,128)S(1)} %get-tuple-element.9, f32[4,256,268]{2,1,0:T(8,128)S(1)} %select_add_fusion), kind=kOutput, calls=%fused_computation.5 | convolution fusion | flops 1208352768 | bytes 4194304 | tf_op jit(solution)/shard_map/sij,scaj->csia/dot_general | solution.py:167
  85.4 1.6 %copy.63 = f32[4,2,6,192]{3,0,2,1:T(4,128)S(1)} copy(f32[4,2,6,192]{2,3,1,0:T(8,128)} %get-tuple-element.11) | data formatting | bytes 73728 | tf_op jit(solution)/shard_map/transpose | solution.py:143
  87.0 5.4 %collective-permute-start.1 = (f32[4,2,6,192]{3,0,2,1:T(4,128)S(1)}, f32[4,2,6,192]{3,0,2,1:T(4,128)S(1)}, u32[]{:S(2)}, u32[]{:S(2)}) collective-permute-start(f32[4,2,6,192]{3,0,2,1:T(4,128)S(1)} %copy.63), channel_id=1, source_target_pairs={{1,0},{2,1},{3,2},{4,3},{5,4},{6,5},{7,6},{8,7},{9,8},{10,9},{11,1... | collective-permute-start | bytes 110600 | tf_op jit(solution)/shard_map/ppermute | solution.py:145
  92.5 1.5 %fusion.21 = f32[4,2,192,256]{3,2,1,0:T(8,128)S(1)} fusion(f32[4,256,268]{2,1,0:T(8,128)S(1)} %select_add_fusion, f32[4,2,6,192]{3,0,2,1:T(4,128)S(1)} %maximum_select_fusion), kind=kOutput, calls=%fused_computation.54 | convolution fusion | flops 28311552 | bytes 2146304 | tf_op jit(solution)/shard_map/sij,scja->csia/dot_general | solution.py:168
  94.2 1.7 %add_bitcast_fusion = f32[2,4,256,192]{2,3,0,1:T(8,128)S(1)} fusion(f32[4,2,192,256]{3,2,1,0:T(8,128)S(1)} %copy-done, f32[4,2,192,256]{3,2,1,0:T(8,128)S(1)} %fusion.21, f32[4,256,268]{2,1,0:T(8,128)S(1)} %select_add_fusion, f32[4,2,6,192]{3,0,2,1:T(4,128)S(1)} %maximum_select_fusion.1), kind=kOutput, calls=%fused_computation.8 | convolution fusion | flops 29097984 | bytes 5292032 | tf_op jit(solution)/shard_map/sij,scja->csia/dot_general | solution.py:169
  95.9 1.3 %copy.66 = f32[2,4,256,192]{2,3,1,0:T(8,128)} copy(f32[2,4,256,192]{2,3,0,1:T(8,128)S(1)} %add_bitcast_fusion) | data formatting | bytes 3145728 | tf_op jit(solution)/shard_map/add | solution.py:169
  (121 shorter events, 12.9 us)
Async XLA Ops:
  8.8 2.1 %copy-start.1 = (f32[128,1536]{0,1:S(1)}, f32[128,1536]{0,1}, u32[]{:S(2)}) copy-start(f32[128,1536]{0,1} %fusion.71) | copy-start | bytes 2359300
  17.6 7.3 %copy-start.36 = (f32[192]{0:T(256)S(1)}, f32[192]{0:T(256)}, u32[]{:S(2)}) copy-start(f32[192]{0:T(256)} %param.9) | copy-start | bytes 2308
  17.6 7.9 %copy-start.4 = (f32[4,256]{1,0:T(4,128)S(1)}, f32[4,256]{1,0:T(4,128)}, u32[]{:S(2)}) copy-start(f32[4,256]{1,0:T(4,128)} %param.8) | copy-start | bytes 12292
  17.6 8.0 %copy-start.5 = (s32[4,256]{1,0:T(4,128)S(1)}, s32[4,256]{1,0:T(4,128)}, u32[]{:S(2)}) copy-start(s32[4,256]{1,0:T(4,128)} %param.10) | copy-start | bytes 12292
  17.6 9.5 %copy-start.3 = (f32[8,4,256]{2,1,0:T(4,128)S(1)}, f32[8,4,256]{2,1,0:T(4,128)}, u32[]{:S(2)}) copy-start(f32[8,4,256]{2,1,0:T(4,128)} %param.11) | copy-start | bytes 98308
  17.7 9.5 %copy-start.37 = (s32[192]{0:T(256)S(1)}, s32[192]{0:T(256)}, u32[]{:S(2)}) copy-start(s32[192]{0:T(256)} %param.7) | copy-start | bytes 2308
  17.7 44.8 %all-to-all-start = ((f32[32,2,24,256]{3,2,1,0:T(8,128)}), f32[32,2,24,256]{3,2,1,0:T(8,128)S(1)}, u32[]{:S(2)}, u32[]{:S(2)}) async-start(f32[32,2,24,256]{3,2,1,0:T(8,128)} %maximum_bitcast_fusion), calls=%async_computation | async-start | bytes 3145728 | tf_op jit(solution)/shard_map/all_to_all | solution.py:91
  62.7 0.7 copy-start.19
  62.7 0.7 copy-start.20
  62.7 0.7 copy-start.21
  62.7 0.7 copy-start.22
  62.7 0.7 copy-start.31
  63.5 0.7 copy-start.14
  63.5 0.7 copy-start.27
  63.5 0.7 copy-start.28
  64.2 0.7 copy-start.9
  64.2 0.7 copy-start.23
  64.2 0.7 copy-start.24
  64.2 0.7 copy-start.25
  66.1 0.9 copy-start.2
  72.4 1.6 %copy-start.35 = (f32[192]{0:T(256)S(1)}, f32[192]{0:T(256)}, u32[]{:S(2)}) copy-start(f32[192]{0:T(256)} %integer_pow.9) | copy-start | bytes 2308
  82.5 9.9 %collective-permute-start = (f32[4,2,6,192]{3,0,2,1:T(4,128)S(1)}, f32[4,2,6,192]{3,0,2,1:T(4,128)S(1)}, u32[]{:S(2)}, u32[]{:S(2)}) collective-permute-start(f32[4,2,6,192]{3,0,2,1:T(4,128)S(1)} %copy.60), channel_id=1, source_target_pairs={{0,1},{1,2},{2,3},{3,4},{4,5},{5,6},{6,7},{7,8},{8,9},{9,10},{10,1... | collective-permute-start | bytes 110600 | tf_op jit(solution)/shard_map/ppermute | solution.py:144
  85.4 8.8 %copy-start = (f32[4,2,192,256]{3,2,1,0:T(8,128)S(1)}, f32[4,2,192,256]{3,2,1,0:T(8,128)}, u32[]{:S(2)}) copy-start(f32[4,2,192,256]{3,2,1,0:T(8,128)} %fusion) | copy-start | bytes 4718596
  87.0 7.1 %collective-permute-start.1 = (f32[4,2,6,192]{3,0,2,1:T(4,128)S(1)}, f32[4,2,6,192]{3,0,2,1:T(4,128)S(1)}, u32[]{:S(2)}, u32[]{:S(2)}) collective-permute-start(f32[4,2,6,192]{3,0,2,1:T(4,128)S(1)} %copy.63), channel_id=1, source_target_pairs={{1,0},{2,1},{3,2},{4,3},{5,4},{6,5},{7,6},{8,7},{9,8},{10,9},{11,1... | collective-permute-start | bytes 110600 | tf_op jit(solution)/shard_map/ppermute | solution.py:145
  (17 other events, 11.3 us)
where the time goes:
time: 97.8 us; the launch traced here: 97.2 us
  waiting for transfers between devices  30.3 us (31%)
  matrix products  23.1 us (24%)
  local copies, waits for them, and re-layouts  17.4 us (18%)
  other arithmetic  13.2 us (13%)
  starting transfers between devices  12.7 us (13%)
    all_to_all x1, waiting for transfers between devices, on_device(): lax.all_to_all(spectrum, ('pulse', 'rng'), split_axis=0, concat_axis=0, t...  30.1 us
    all_to_all x1, starting transfers between devices, on_device(): lax.all_to_all(spectrum, ('pulse', 'rng'), split_axis=0, concat_axis=0, t...  7.3 us
    sub x1, other arithmetic, on_device(): az_real * phase_real - az_imag * phase_imag  5.63 us
    dot_general x1, matrix products, on_device(): azimuth = jnp.einsum('xy,syq->sxq', fold, combined, precision=highest)  5.42 us
    ppermute x1, starting transfers between devices, on_device(): right_rim = lax.ppermute(left_edge, axes, down)  5.35 us
    unnamed x4, matrix products  5.02 us
    dot_general x4, matrix products, contract(): return jnp.einsum(pattern, operand, matrix, precision=highest)  3.73 us
    dot_general x1, matrix products, on_device(): image = jnp.einsum('sij,scaj->csia', band_main, focused, precision=highest)  2.88 us
  transfers between devices with their start and end apart: 3, of which 2 were waited for; matrix products, arithmetic and copies ran while one was open for 14% of the time, Pallas kernels for 0%

commit v1 on v0

--- a/solution.py
+++ b/solution.py
@@ -84,14 +84,9 @@
     block_len = span_len // device_count
     position = lax.axis_index(("pulse", "rng"))
 
-    real_part, imag_part = last_axis_dft(echoes[0], echoes[1], span_len, 1.0)
-    spectrum = jnp.stack([real_part, imag_part])
-    spectrum = spectrum.reshape(2, rows_here, device_count, block_len)
-    spectrum = jnp.transpose(spectrum, (2, 0, 1, 3))
-    spectrum = lax.all_to_all(
-        spectrum, ("pulse", "rng"), split_axis=0, concat_axis=0, tiled=True
-    )
-    spectrum = spectrum.reshape(pulse_count, lane_count, 2, rows_here, block_len)
+    small_fold = total_rows <= 512
+    chunk_rows = 8 if rows_here % 8 == 0 and small_fold else rows_here
+    chunk_count = rows_here // chunk_rows
 
     q_global = position * block_len + jnp.arange(block_len, dtype=jnp.int32)
     bin_index = jnp.arange(lane_count, dtype=jnp.int32)[:, None] * span_len + q_global[None, :]
@@ -100,32 +95,48 @@
     turn_angle = turn.astype(jnp.float32) * (-2.0 * math.pi / range_len)
     turn_real = jnp.cos(turn_angle)
     turn_imag = jnp.sin(turn_angle)
-    lane_real = spectrum[:, :, 0]
-    lane_imag = spectrum[:, :, 1]
-    combined_real = []
-    combined_imag = []
-    for s in range(lane_count):
-        acc_real = 0.0
-        acc_imag = 0.0
-        for r in range(lane_count):
-            wr = turn_real[r, s][None, None, :]
-            wi = turn_imag[r, s][None, None, :]
-            acc_real = acc_real + lane_real[:, r] * wr - lane_imag[:, r] * wi
-            acc_imag = acc_imag + lane_real[:, r] * wi + lane_imag[:, r] * wr
-        combined_real.append(acc_real)
-        combined_imag.append(acc_imag)
-    combined = jnp.stack([jnp.stack(combined_real), jnp.stack(combined_imag)], axis=1)
-    combined = combined.reshape(lane_count, 2 * total_rows, block_len)
 
     fold = azimuth_matrix(row_list, 1.0 / math.sqrt(range_len * total_rows))
-    azimuth = jnp.einsum("xy,syq->sxq", fold, combined, precision=highest)
+    fold = fold.reshape(2 * total_rows, 2, pulse_count, chunk_count, chunk_rows)
+
+    azimuth = None
+    for chunk in range(chunk_count):
+        rows = slice(chunk * chunk_rows, (chunk + 1) * chunk_rows)
+        real_part, imag_part = last_axis_dft(echoes[0, rows], echoes[1, rows], span_len, 1.0)
+        spectrum = jnp.stack([real_part, imag_part])
+        spectrum = spectrum.reshape(2, chunk_rows, device_count, block_len)
+        spectrum = jnp.transpose(spectrum, (2, 0, 1, 3))
+        spectrum = lax.all_to_all(
+            spectrum, ("pulse", "rng"), split_axis=0, concat_axis=0, tiled=True
+        )
+        spectrum = spectrum.reshape(pulse_count, lane_count, 2, chunk_rows, block_len)
+        lane_real = spectrum[:, :, 0]
+        lane_imag = spectrum[:, :, 1]
+        combined_real = []
+        combined_imag = []
+        for s in range(lane_count):
+            acc_real = 0.0
+            acc_imag = 0.0
+            for r in range(lane_count):
+                wr = turn_real[r, s][None, None, :]
+                wi = turn_imag[r, s][None, None, :]
+                acc_real = acc_real + lane_real[:, r] * wr - lane_imag[:, r] * wi
+                acc_imag = acc_imag + lane_real[:, r] * wi + lane_imag[:, r] * wr
+            combined_real.append(acc_real)
+            combined_imag.append(acc_imag)
+        combined = jnp.stack([jnp.stack(combined_real), jnp.stack(combined_imag)], axis=1)
+        combined = combined.reshape(lane_count, 2 * pulse_count * chunk_rows, block_len)
+        part_fold = fold[:, :, :, chunk].reshape(2 * total_rows, 2 * pulse_count * chunk_rows)
+        part = jnp.einsum("xy,syq->sxq", part_fold, combined, precision=highest)
+        azimuth = part if azimuth is None else azimuth + part
     azimuth = azimuth.reshape(lane_count, 2, total_rows, block_len)
 
     phase_angle = phase_scale * jnp.sqrt(
         wavenumber[:, None, :] ** 2 - az_wavenumber[None, :, None] ** 2
     )
-    phase_real = jnp.cos(phase_angle)
-    phase_imag = jnp.sin(phase_angle)
+    phase_real, phase_imag = lax.optimization_barrier(
+        (jnp.cos(phase_angle), jnp.sin(phase_angle))
+    )
     az_real = azimuth[:, 0]
     az_imag = azimuth[:, 1]
     focused = jnp.stack(

time: 97.8 us -> 114 us (1.17)
  other arithmetic: 13.2 us -> 21.4 us
  starting transfers between devices: 12.7 us -> 18.7 us
  matrix products: 23.1 us -> 27.3 us
  local copies, waits for them, and re-layouts: 17.4 us -> 13.5 us
  between operations: 0.62 us -> 2.21 us
    all_to_all x1 -> x3, starting transfers between devices: 7.3 us -> 16.4 us  [on_device(): lax.all_to_all(spectrum, ('pulse', 'rng'), split_axis=0, concat_axis=0, t...]
    sub x1 -> x0, other arithmetic: 5.63 us -> none  [on_device(): az_real * phase_real - az_imag * phase_imag]
    ppermute x1, waiting for transfers between devices: 0.01 us -> 5.33 us  [on_device(): left_rim = lax.ppermute(right_edge, axes, up)]
    all_to_all x1 -> x3, waiting for transfers between devices: 30.1 us -> 25.3 us  [on_device(): lax.all_to_all(spectrum, ('pulse', 'rng'), split_axis=0, concat_axis=0, t...]
    unnamed x4 -> x12, matrix products: 5.02 us -> 9.59 us
    sub x4 -> x12, other arithmetic: 0.48 us -> 4.67 us  [on_device(): acc_real = acc_real + lane_real[:, r] * wr - lane_imag[:, r] * wi]
    sin x0 -> x1, other arithmetic: none -> 4.1 us  [on_device(): jnp.sin(phase_angle)]
    ppermute x1, starting transfers between devices: 5.35 us -> 1.99 us  [on_device(): right_rim = lax.ppermute(left_edge, axes, down)]
  transfers between devices with their start and end apart: 3 -> 5, of which waited for: 2 -> 3; matrix products, arithmetic and copies ran while one was open for 14% -> 23% of each run, Pallas kernels for 0% -> 0%
where the time goes in v1:
time: 114 us
  waiting for transfers between devices  30.7 us (27%)
  matrix products  27.3 us (24%)
  other arithmetic  21.4 us (19%)
  starting transfers between devices  18.7 us (16%)
  local copies, waits for them, and re-layouts  13.5 us (12%)
  between operations  2.21 us (2%)
    all_to_all x3, waiting for transfers between devices, on_device(): lax.all_to_all(spectrum, ('pulse', 'rng'), split_axis=0, concat_axis=0, t...  25.3 us
    all_to_all x3, starting transfers between devices, on_device(): lax.all_to_all(spectrum, ('pulse', 'rng'), split_axis=0, concat_axis=0, t...  16.4 us
    unnamed x12, matrix products  9.59 us
    dot_general x12, matrix products, contract(): return jnp.einsum(pattern, operand, matrix, precision=highest)  6.1 us
    ppermute x1, waiting for transfers between devices, on_device(): left_rim = lax.ppermute(right_edge, axes, up)  5.33 us
    sub x12, other arithmetic, on_device(): acc_real = acc_real + lane_real[:, r] * wr - lane_imag[:, r] * wi  4.67 us
    dot_general x3, matrix products, on_device(): part = jnp.einsum('xy,syq->sxq', part_fold, combined, precision=highest)  4.43 us
    sin x1, other arithmetic, on_device(): jnp.sin(phase_angle)  4.1 us
  transfers between devices with their start and end apart: 5, of which 3 were waited for; matrix products, arithmetic and copies ran while one was open for 23% of the time, Pallas kernels for 0%

profile of v1, /device:TPU:0, one launch (start us, length us, event | category | flops | bytes accessed | tf_op | source)
XLA Modules:
  0.0 113.7 jit_solution(10847489487475112301)
XLA Ops:
  0.0 1.4 %fusion.243 = (f32[1,8,8192]{2,1,0:T(8,128)S(1)}, f32[1,8,8192]{2,1,0:T(8,128)S(1)}, f32[1,8,8192]{2,1,0:T(8,128)S(1)}, f32[1,8,8192]{2,1,0:T(8,128)S(1)}, f32[1...) fusion(f32[2,24,8192]{2,1,0:T(8,128)} %param.6), kind=kLoop, calls=%fused_computation.355 | loop fusion | bytes 3145728 | tf_op jit(solution)/shard_map/slice | solution.py:105
  9.2 1.3 %fusion.105 = f32[128,512]{0,1} fusion(f32[128,512]{0,1:T(8,128)S(1)} %bitcast.761), kind=kOutput, calls=%fused_computation.210 | convolution fusion | flops 100892672 | bytes 524288
  10.6 1.3 %fusion.91 = f32[128,512]{0,1} fusion(f32[128,512]{0,1:T(8,128)S(1)} %bitcast.762), kind=kOutput, calls=%fused_computation.203 | convolution fusion | flops 100892672 | bytes 524288
  13.7 1.5 %multiply_add_fusion = (f32[128,8,64]{0,2,1:T(8,128)S(1)}, f32[128,8,64]{0,2,1:T(8,128)S(1)}, f32[128,8,64]{0,2,1:T(8,128)S(1)}, f32[128,8,64]{0,2,1:T(8,128)S(1...) fusion(f32[128,64]{0,1:T(8,128)S(1)} %get-tuple-element.93, f32[128,64]{0,1:T(8,128)S(1)} %get-tuple-element.94, ...), kind=kLoop, calls=%fused_computation.82 | loop fusion | flops 1572864 | bytes 4784128 | tf_op jit(solution)/shard_map/add | solution.py:55
  18.6 7.3 %all-to-all-start.2 = ((f32[32,2,8,256]{3,2,1,0:T(8,128)}), f32[32,2,8,256]{3,2,1,0:T(8,128)S(1)}, u32[]{:S(2)}, u32[]{:S(2)}) async-start(f32[32,2,8,256]{3,2,1,0:T(8,128)} %maximum_bitcast_fusion.2), calls=%async_computation.2 | async-start | bytes 1048576 | tf_op jit(solution)/shard_map/all_to_all | solution.py:109
  33.9 4.1 %fusion.11 = (f32[4,192,256]{2,1,0:T(8,128)}, f32[4,192,256]{2,1,0:T(8,128)}) fusion(f32[192]{0:T(256)S(1)} %integer_pow.9, f32[4,256]{1,0:T(4,128)S(1)} %integer_pow.8), kind=kLoop, calls=%fused_computation.39 | loop fusion | flops 393216 | bytes 1577728 | tf_op jit(solution)/shard_map/sin | solution.py:138
  40.7 2.4 %select_add_fusion = f32[4,256,268]{2,1,0:T(8,128)S(1)} fusion(f32[4,256]{1,0:T(4,128)S(1)} %get-tuple-element.41, s32[4,256]{1,0:T(4,128)S(1)} %get-tuple-element.87, f32[4,256]{1,0:T(4,128)S(1)} %get-tuple-element.42, s32[4,256]{1,0:T(4,128)S(1)} %get-tuple-element.83, f32[4,256]{1,0:T(4,128)S(1)} %get-tuple-element.43, s32[4,256]{1,0:T(4,128)S(1)} %get-tuple-element.84, ...), kind=kLoop, calls=%fused_computation.7 | loop fusion | flops 6311936 | bytes 1163264 | tf_op jit(solution)/shard_map/add | solution.py:173
  43.1 5.8 %all-to-all-start.1 = ((f32[32,2,8,256]{3,2,1,0:T(8,128)}), f32[32,2,8,256]{3,2,1,0:T(8,128)S(1)}, u32[]{:S(2)}, u32[]{:S(2)}) async-start(f32[32,2,8,256]{3,2,1,0:T(8,128)} %maximum_bitcast_fusion.1), calls=%async_computation.1 | async-start | bytes 1048576 | tf_op jit(solution)/shard_map/all_to_all | solution.py:109
  52.7 11.8 %all-to-all-done.1 = f32[32,2,8,256]{3,2,1,0:T(8,128)S(1)} async-done(((f32[32,2,8,256]{3,2,1,0:T(8,128)}), f32[32,2,8,256]{3,2,1,0:T(8,128)S(1)}, u32[]{:S(2)}, u32[]{:S(2)}) %all-to-all-start.1) | async-done | bytes 524320 | tf_op jit(solution)/shard_map/all_to_all | solution.py:109
  64.5 3.3 %all-to-all-start = ((f32[32,2,8,256]{3,2,1,0:T(8,128)}), f32[32,2,8,256]{3,2,1,0:T(8,128)S(1)}, u32[]{:S(2)}, u32[]{:S(2)}) async-start(f32[32,2,8,256]{3,2,1,0:T(8,128)} %maximum_bitcast_fusion), calls=%async_computation | async-start | bytes 1048576 | tf_op jit(solution)/shard_map/all_to_all | solution.py:109
  69.6 13.5 %all-to-all-done = f32[32,2,8,256]{3,2,1,0:T(8,128)S(1)} async-done(((f32[32,2,8,256]{3,2,1,0:T(8,128)}), f32[32,2,8,256]{3,2,1,0:T(8,128)S(1)}, u32[]{:S(2)}, u32[]{:S(2)}) %all-to-all-start) | async-done | bytes 524320 | tf_op jit(solution)/shard_map/all_to_all | solution.py:109
  87.1 1.5 %fusion.251 = f32[4,256,384]{2,1,0:T(8,128)S(1)} fusion(f32[4,128,256]{2,1,0:T(8,128)S(1)} %bitcast.769, f32[384,128,1]{0,1,2:T(8,128)S(1)} %bitcast.785), kind=kOutput, calls=%fused_computation.363 | convolution fusion | flops 603979776 | bytes 2293760 | tf_op jit(solution)/shard_map/xy,syq->sxq/dot_general | solution.py:130
  88.6 1.5 %fusion.250 = f32[4,256,384]{2,1,0:T(8,128)S(1)} fusion(f32[4,128,256]{2,1,0:T(8,128)S(1)} %bitcast.770, f32[384,128,1]{0,1,2:T(8,128)S(1)} %bitcast.784), kind=kOutput, calls=%fused_computation.362 | convolution fusion | flops 603979776 | bytes 2293760 | tf_op jit(solution)/shard_map/xy,syq->sxq/dot_general | solution.py:130
  90.1 1.5 %add_bitcast_fusion.1 = f32[4,384,256]{1,2,0:T(8,128)S(1)} fusion(f32[4,256,384]{2,1,0:T(8,128)S(1)} %fusion.250, f32[4,256,384]{2,1,0:T(8,128)S(1)} %fusion.251, f32[4,128,256]{2,1,0:T(8,128)S(1)} %bitcast.771, f32[384,128,1]{0,1,2:T(8,128)S(1)} %bitcast.786), kind=kOutput, calls=%fused_computation.16 | convolution fusion | flops 604766208 | bytes 5439488 | tf_op jit(solution)/shard_map/xy,syq->sxq/dot_general | solution.py:130
  91.6 1.6 %copy.140 = f32[4,384,256]{2,1,0:T(8,128)} copy(f32[4,384,256]{1,2,0:T(8,128)S(1)} %add_bitcast_fusion.1) | data formatting | bytes 3145728 | tf_op jit(solution)/shard_map/add | solution.py:131
  93.2 2.1 %subtract_bitcast_fusion = (f32[4,1,192,256]{3,2,1,0:T(8,128)S(1)}, f32[4,1,192,256]{3,2,1,0:T(8,128)S(1)}) fusion(f32[4,192,256]{2,1,0:T(8,128)} %get-tuple-element.8, f32[4,192,256]{2,1,0:T(8,128)} %get-tuple-element.7, f32[4,2,192,256]{3,2,1,0:T(8,128)} %bitcast.752), kind=kLoop, calls=%fused_computation.37 | loop fusion | flops 1179648 | bytes 4718592 | tf_op jit(solution)/shard_map/stack | solution.py:142
  95.3 1.4 %fusion.10 = (f32[4,2,6,192]{2,3,1,0:T(8,128)}, f32[4,2,6,192]{2,3,1,0:T(8,128)}) fusion(f32[4,1,192,256]{3,2,1,0:T(8,128)S(1)} %get-tuple-element.11, f32[4,1,192,256]{3,2,1,0:T(8,128)S(1)} %get-tuple-element.12), kind=kLoop, calls=%fused_computation.33 | loop fusion | flops 18432 | bytes 1646592 | tf_op jit(solution)/shard_map/transpose | solution.py:154
  96.7 1.5 %copy.147 = f32[4,2,6,192]{3,0,2,1:T(4,128)S(1)} copy(f32[4,2,6,192]{2,3,1,0:T(8,128)} %get-tuple-element.13) | data formatting | bytes 73728 | tf_op jit(solution)/shard_map/transpose | solution.py:154
  98.2 2.0 %collective-permute-start.1 = (f32[4,2,6,192]{3,0,2,1:T(4,128)S(1)}, f32[4,2,6,192]{3,0,2,1:T(4,128)S(1)}, u32[]{:S(2)}, u32[]{:S(2)}) collective-permute-start(f32[4,2,6,192]{3,0,2,1:T(4,128)S(1)} %copy.147), channel_id=1, source_target_pairs={{1,0},{2,1},{3,2},{4,3},{5,4},{6,5},{7,6},{8,7},{9,8},{10,9},{11,1... | collective-permute-start | bytes 110600 | tf_op jit(solution)/shard_map/ppermute | solution.py:156
  100.1 1.5 %copy.144 = f32[4,2,6,192]{3,0,2,1:T(4,128)S(1)} copy(f32[4,2,6,192]{2,3,1,0:T(8,128)} %get-tuple-element.14) | data formatting | bytes 73728 | tf_op jit(solution)/shard_map/transpose | solution.py:153
  101.9 1.8 %fusion = f32[4,2,192,256]{3,2,1,0:T(8,128)S(1)} fusion(f32[4,1,192,256]{3,2,1,0:T(8,128)S(1)} %get-tuple-element.12, f32[4,1,192,256]{3,2,1,0:T(8,128)S(1)} %get-tuple-element.11, f32[4,256,268]{2,1,0:T(8,128)S(1)} %select_add_fusion), kind=kOutput, calls=%fused_computation.5 | convolution fusion | flops 1208352768 | bytes 4194304 | tf_op jit(solution)/shard_map/sij,scaj->csia/dot_general | solution.py:178
  103.7 5.3 %collective-permute-done = f32[4,2,6,192]{3,0,2,1:T(4,128)S(1)} collective-permute-done((f32[4,2,6,192]{3,0,2,1:T(4,128)S(1)}, f32[4,2,6,192]{3,0,2,1:T(4,128)S(1)}, u32[]{:S(2)}, u32[]{:S(2)}) %collective-permute-start) | collective-permute-done | bytes 36896 | tf_op jit(solution)/shard_map/ppermute | solution.py:155
  109.1 1.5 %fusion.13 = f32[4,2,192,256]{3,2,1,0:T(8,128)S(1)} fusion(f32[4,256,268]{2,1,0:T(8,128)S(1)} %select_add_fusion, f32[4,2,6,192]{3,0,2,1:T(4,128)S(1)} %maximum_select_fusion), kind=kOutput, calls=%fused_computation.44 | convolution fusion | flops 28311552 | bytes 2146304 | tf_op jit(solution)/shard_map/sij,scja->csia/dot_general | solution.py:179
  110.6 1.8 %add_bitcast_fusion = f32[2,4,256,192]{2,3,0,1:T(8,128)S(1)} fusion(f32[4,2,192,256]{3,2,1,0:T(8,128)S(1)} %fusion, f32[4,2,192,256]{3,2,1,0:T(8,128)S(1)} %fusion.13, f32[4,256,268]{2,1,0:T(8,128)S(1)} %select_add_fusion, f32[4,2,6,192]{3,0,2,1:T(4,128)S(1)} %maximum_select_fusion.1), kind=kOutput, calls=%fused_computation.6 | convolution fusion | flops 29097984 | bytes 5292032 | tf_op jit(solution)/shard_map/sij,scja->csia/dot_general | solution.py:180
  (303 shorter events, 33.0 us)
Async XLA Ops:
  18.6 24.5 %all-to-all-start.2 = ((f32[32,2,8,256]{3,2,1,0:T(8,128)}), f32[32,2,8,256]{3,2,1,0:T(8,128)S(1)}, u32[]{:S(2)}, u32[]{:S(2)}) async-start(f32[32,2,8,256]{3,2,1,0:T(8,128)} %maximum_bitcast_fusion.2), calls=%async_computation.2 | async-start | bytes 1048576 | tf_op jit(solution)/shard_map/all_to_all | solution.py:109
  30.4 18.7 %copy-start.27 = (f32[1,1,256]{2,1,0:T(1,128)}, f32[1,1,256]{2,1,0:T(1,128)S(1)}, u32[]{:S(2)}) copy-start(f32[1,1,256]{2,1,0:T(1,128)S(1)} %get-tuple-element.48) | copy-start | bytes 3076
  30.4 18.7 %copy-start.30 = (f32[1,1,256]{2,1,0:T(1,128)}, f32[1,1,256]{2,1,0:T(1,128)S(1)}, u32[]{:S(2)}) copy-start(f32[1,1,256]{2,1,0:T(1,128)S(1)} %get-tuple-element.61) | copy-start | bytes 3076
  30.5 18.7 %copy-start.33 = (f32[1,1,256]{2,1,0:T(1,128)}, f32[1,1,256]{2,1,0:T(1,128)S(1)}, u32[]{:S(2)}) copy-start(f32[1,1,256]{2,1,0:T(1,128)S(1)} %get-tuple-element.62) | copy-start | bytes 3076
  30.5 18.7 %copy-start.36 = (f32[1,1,256]{2,1,0:T(1,128)}, f32[1,1,256]{2,1,0:T(1,128)S(1)}, u32[]{:S(2)}) copy-start(f32[1,1,256]{2,1,0:T(1,128)S(1)} %get-tuple-element.63) | copy-start | bytes 3076
  30.5 19.2 %copy-start.15 = (f32[1,1,256]{2,1,0:T(1,128)}, f32[1,1,256]{2,1,0:T(1,128)S(1)}, u32[]{:S(2)}) copy-start(f32[1,1,256]{2,1,0:T(1,128)S(1)} %get-tuple-element.57) | copy-start | bytes 3076
  30.5 19.2 %copy-start.18 = (f32[1,1,256]{2,1,0:T(1,128)}, f32[1,1,256]{2,1,0:T(1,128)S(1)}, u32[]{:S(2)}) copy-start(f32[1,1,256]{2,1,0:T(1,128)S(1)} %get-tuple-element.58) | copy-start | bytes 3076
  30.5 19.2 %copy-start.21 = (f32[1,1,256]{2,1,0:T(1,128)}, f32[1,1,256]{2,1,0:T(1,128)S(1)}, u32[]{:S(2)}) copy-start(f32[1,1,256]{2,1,0:T(1,128)S(1)} %get-tuple-element.59) | copy-start | bytes 3076
  30.5 19.2 %copy-start.24 = (f32[1,1,256]{2,1,0:T(1,128)}, f32[1,1,256]{2,1,0:T(1,128)S(1)}, u32[]{:S(2)}) copy-start(f32[1,1,256]{2,1,0:T(1,128)S(1)} %get-tuple-element.60) | copy-start | bytes 3076
  30.5 19.2 %copy-start.3 = (f32[1,1,256]{2,1,0:T(1,128)}, f32[1,1,256]{2,1,0:T(1,128)S(1)}, u32[]{:S(2)}) copy-start(f32[1,1,256]{2,1,0:T(1,128)S(1)} %get-tuple-element.53) | copy-start | bytes 3076
  30.5 19.2 %copy-start.6 = (f32[1,1,256]{2,1,0:T(1,128)}, f32[1,1,256]{2,1,0:T(1,128)S(1)}, u32[]{:S(2)}) copy-start(f32[1,1,256]{2,1,0:T(1,128)S(1)} %get-tuple-element.54) | copy-start | bytes 3076
  30.5 19.2 %copy-start.9 = (f32[1,1,256]{2,1,0:T(1,128)}, f32[1,1,256]{2,1,0:T(1,128)S(1)}, u32[]{:S(2)}) copy-start(f32[1,1,256]{2,1,0:T(1,128)S(1)} %get-tuple-element.55) | copy-start | bytes 3076
  30.6 19.2 %copy-start.12 = (f32[1,1,256]{2,1,0:T(1,128)}, f32[1,1,256]{2,1,0:T(1,128)S(1)}, u32[]{:S(2)}) copy-start(f32[1,1,256]{2,1,0:T(1,128)S(1)} %get-tuple-element.56) | copy-start | bytes 3076
  31.2 18.0 %copy-start.78 = (f32[1,1,256]{2,1,0:T(1,128)}, f32[1,1,256]{2,1,0:T(1,128)S(1)}, u32[]{:S(2)}) copy-start(f32[1,1,256]{2,1,0:T(1,128)S(1)} %get-tuple-element.77) | copy-start | bytes 3076
  31.2 18.0 %copy-start.81 = (f32[1,1,256]{2,1,0:T(1,128)}, f32[1,1,256]{2,1,0:T(1,128)S(1)}, u32[]{:S(2)}) copy-start(f32[1,1,256]{2,1,0:T(1,128)S(1)} %get-tuple-element.78) | copy-start | bytes 3076
  31.2 18.0 %copy-start.84 = (f32[1,1,256]{2,1,0:T(1,128)}, f32[1,1,256]{2,1,0:T(1,128)S(1)}, u32[]{:S(2)}) copy-start(f32[1,1,256]{2,1,0:T(1,128)S(1)} %get-tuple-element.79) | copy-start | bytes 3076
  31.2 18.6 %copy-start.51 = (f32[1,1,256]{2,1,0:T(1,128)}, f32[1,1,256]{2,1,0:T(1,128)S(1)}, u32[]{:S(2)}) copy-start(f32[1,1,256]{2,1,0:T(1,128)S(1)} %get-tuple-element.69) | copy-start | bytes 3076
  31.2 18.6 %copy-start.54 = (f32[1,1,256]{2,1,0:T(1,128)}, f32[1,1,256]{2,1,0:T(1,128)S(1)}, u32[]{:S(2)}) copy-start(f32[1,1,256]{2,1,0:T(1,128)S(1)} %get-tuple-element.70) | copy-start | bytes 3076
  31.2 18.6 %copy-start.57 = (f32[1,1,256]{2,1,0:T(1,128)}, f32[1,1,256]{2,1,0:T(1,128)S(1)}, u32[]{:S(2)}) copy-start(f32[1,1,256]{2,1,0:T(1,128)S(1)} %get-tuple-element.71) | copy-start | bytes 3076
  31.2 18.6 %copy-start.60 = (f32[1,1,256]{2,1,0:T(1,128)}, f32[1,1,256]{2,1,0:T(1,128)S(1)}, u32[]{:S(2)}) copy-start(f32[1,1,256]{2,1,0:T(1,128)S(1)} %get-tuple-element.72) | copy-start | bytes 3076
  43.1 21.4 %all-to-all-start.1 = ((f32[32,2,8,256]{3,2,1,0:T(8,128)}), f32[32,2,8,256]{3,2,1,0:T(8,128)S(1)}, u32[]{:S(2)}, u32[]{:S(2)}) async-start(f32[32,2,8,256]{3,2,1,0:T(8,128)} %maximum_bitcast_fusion.1), calls=%async_computation.1 | async-start | bytes 1048576 | tf_op jit(solution)/shard_map/all_to_all | solution.py:109
  64.5 18.6 %all-to-all-start = ((f32[32,2,8,256]{3,2,1,0:T(8,128)}), f32[32,2,8,256]{3,2,1,0:T(8,128)S(1)}, u32[]{:S(2)}, u32[]{:S(2)}) async-start(f32[32,2,8,256]{3,2,1,0:T(8,128)} %maximum_bitcast_fusion), calls=%async_computation | async-start | bytes 1048576 | tf_op jit(solution)/shard_map/all_to_all | solution.py:109
  98.2 12.4 %collective-permute-start.1 = (f32[4,2,6,192]{3,0,2,1:T(4,128)S(1)}, f32[4,2,6,192]{3,0,2,1:T(4,128)S(1)}, u32[]{:S(2)}, u32[]{:S(2)}) collective-permute-start(f32[4,2,6,192]{3,0,2,1:T(4,128)S(1)} %copy.147), channel_id=1, source_target_pairs={{1,0},{2,1},{3,2},{4,3},{5,4},{6,5},{7,6},{8,7},{9,8},{10,9},{11,1... | collective-permute-start | bytes 110600 | tf_op jit(solution)/shard_map/ppermute | solution.py:156
  101.6 7.4 %collective-permute-start = (f32[4,2,6,192]{3,0,2,1:T(4,128)S(1)}, f32[4,2,6,192]{3,0,2,1:T(4,128)S(1)}, u32[]{:S(2)}, u32[]{:S(2)}) collective-permute-start(f32[4,2,6,192]{3,0,2,1:T(4,128)S(1)} %copy.144), channel_id=1, source_target_pairs={{0,1},{1,2},{2,3},{3,4},{4,5},{5,6},{6,7},{7,8},{8,9},{9,10},{10,1... | collective-permute-start | bytes 110600 | tf_op jit(solution)/shard_map/ppermute | solution.py:155
  (73 other events, 153.1 us)

commit v2 on v0

--- a/solution.py
+++ b/solution.py
@@ -7,7 +7,7 @@
 
 phase_scale = 24.0
 highest = lax.Precision.HIGHEST
-RIM = 6
+RIM = 8
 
 
 def split_factor(length):
@@ -83,9 +83,21 @@
     range_len = span_len * lane_count
     block_len = span_len // device_count
     position = lax.axis_index(("pulse", "rng"))
+    lane_pos = lax.axis_index("rng")
 
     real_part, imag_part = last_axis_dft(echoes[0], echoes[1], span_len, 1.0)
-    spectrum = jnp.stack([real_part, imag_part])
+    q_index = jnp.arange(span_len, dtype=jnp.int32)
+    twist_angle = ((lane_pos * q_index) % range_len).astype(jnp.float32) * (
+        -2.0 * math.pi / range_len
+    )
+    twist_real = jnp.cos(twist_angle)[None, :]
+    twist_imag = jnp.sin(twist_angle)[None, :]
+    spectrum = jnp.stack(
+        [
+            real_part * twist_real - imag_part * twist_imag,
+            real_part * twist_imag + imag_part * twist_real,
+        ]
+    )
     spectrum = spectrum.reshape(2, rows_here, device_count, block_len)
     spectrum = jnp.transpose(spectrum, (2, 0, 1, 3))
     spectrum = lax.all_to_all(
@@ -93,13 +105,6 @@
     )
     spectrum = spectrum.reshape(pulse_count, lane_count, 2, rows_here, block_len)
 
-    q_global = position * block_len + jnp.arange(block_len, dtype=jnp.int32)
-    bin_index = jnp.arange(lane_count, dtype=jnp.int32)[:, None] * span_len + q_global[None, :]
-    lane_index = jnp.arange(lane_count, dtype=jnp.int32)
-    turn = (lane_index[:, None, None] * bin_index[None, :, :]) % range_len
-    turn_angle = turn.astype(jnp.float32) * (-2.0 * math.pi / range_len)
-    turn_real = jnp.cos(turn_angle)
-    turn_imag = jnp.sin(turn_angle)
     lane_real = spectrum[:, :, 0]
     lane_imag = spectrum[:, :, 1]
     combined_real = []
@@ -108,48 +113,49 @@
         acc_real = 0.0
         acc_imag = 0.0
         for r in range(lane_count):
-            wr = turn_real[r, s][None, None, :]
-            wi = turn_imag[r, s][None, None, :]
-            acc_real = acc_real + lane_real[:, r] * wr - lane_imag[:, r] * wi
-            acc_imag = acc_imag + lane_real[:, r] * wi + lane_imag[:, r] * wr
+            turn = -2.0 * math.pi * ((r * s) % lane_count) / lane_count
+            wr = round(math.cos(turn), 12)
+            wi = round(math.sin(turn), 12)
+            if wr != 0.0:
+                acc_real = acc_real + wr * lane_real[:, r]
+                acc_imag = acc_imag + wr * lane_imag[:, r]
+            if wi != 0.0:
+                acc_real = acc_real - wi * lane_imag[:, r]
+                acc_imag = acc_imag + wi * lane_real[:, r]
         combined_real.append(acc_real)
         combined_imag.append(acc_imag)
     combined = jnp.stack([jnp.stack(combined_real), jnp.stack(combined_imag)], axis=1)
     combined = combined.reshape(lane_count, 2 * total_rows, block_len)
 
     fold = azimuth_matrix(row_list, 1.0 / math.sqrt(range_len * total_rows))
-    azimuth = jnp.einsum("xy,syq->sxq", fold, combined, precision=highest)
-    azimuth = azimuth.reshape(lane_count, 2, total_rows, block_len)
+    az_real = jnp.einsum("ay,syq->sqa", fold[:total_rows], combined, precision=highest)
+    az_imag = jnp.einsum("ay,syq->sqa", fold[total_rows:], combined, precision=highest)
 
     phase_angle = phase_scale * jnp.sqrt(
-        wavenumber[:, None, :] ** 2 - az_wavenumber[None, :, None] ** 2
+        wavenumber[:, :, None] ** 2 - az_wavenumber[None, None, :] ** 2
     )
-    phase_real = jnp.cos(phase_angle)
-    phase_imag = jnp.sin(phase_angle)
-    az_real = azimuth[:, 0]
-    az_imag = azimuth[:, 1]
-    focused = jnp.stack(
-        [
-            az_real * phase_real - az_imag * phase_imag,
-            az_real * phase_imag + az_imag * phase_real,
-        ],
-        axis=1,
+    phase_real, phase_imag = lax.optimization_barrier(
+        (jnp.cos(phase_angle), jnp.sin(phase_angle))
     )
+    focused_real = az_real * phase_real - az_imag * phase_imag
+    focused_imag = az_real * phase_imag + az_imag * phase_real
+    focused = jnp.stack([focused_real, focused_imag])
 
     axes = ("pulse", "rng")
     up = [(i, (i + 1) % device_count) for i in range(device_count)]
     down = [(j, i) for i, j in up]
-    right_edge = jnp.swapaxes(focused[..., block_len - RIM:], 2, 3)
-    left_edge = jnp.swapaxes(focused[..., :RIM], 2, 3)
-    left_rim = lax.ppermute(right_edge, axes, up)
-    right_rim = lax.ppermute(left_edge, axes, down)
-    left_rim = jnp.where(position == 0, jnp.roll(left_rim, 1, axis=0), left_rim)
+    left_rim = lax.ppermute(focused[:, :, block_len - RIM:], axes, up)
+    right_rim = lax.ppermute(focused[:, :, :RIM], axes, down)
+    left_rim = jnp.where(position == 0, jnp.roll(left_rim, 1, axis=1), left_rim)
     right_rim = jnp.where(
-        position == device_count - 1, jnp.roll(right_rim, -1, axis=0), right_rim
+        position == device_count - 1, jnp.roll(right_rim, -1, axis=1), right_rim
     )
+    widened = jnp.concatenate([left_rim, focused, right_rim], axis=2)
 
     tap_count = stolt_coef.shape[0]
     piece_index = jnp.arange(block_len, dtype=jnp.int32)
+    q_global = position * block_len + piece_index
+    bin_index = jnp.arange(lane_count, dtype=jnp.int32)[:, None] * span_len + q_global[None, :]
     relative = stolt_offset - bin_index + RIM
     tap_index = jnp.arange(tap_count, dtype=jnp.int32)
     source = stolt_offset[None, :, :] + tap_index[:, None, None]
@@ -160,14 +166,8 @@
     band = jnp.zeros((lane_count, block_len, block_len + 2 * RIM), jnp.float32)
     for t in range(tap_count):
         band = band + jnp.where(columns[None, None, :] == target + t, weights[t][:, :, None], 0.0)
-    band_left = band[:, :, :RIM]
-    band_main = band[:, :, RIM:RIM + block_len]
-    band_right = band[:, :, RIM + block_len:]
 
-    image = jnp.einsum("sij,scaj->csia", band_main, focused, precision=highest)
-    image = image + jnp.einsum("sij,scja->csia", band_left, left_rim, precision=highest)
-    image = image + jnp.einsum("sij,scja->csia", band_right, right_rim, precision=highest)
-    return image
+    return jnp.einsum("sij,csja->csia", band, widened, precision=highest)
 
 
 def solution(mesh):

time: 97.8 us -> 85.1 us (0.87)
  other arithmetic: 13.2 us -> 7.06 us
  local copies, waits for them, and re-layouts: 17.4 us -> 12.8 us
  matrix products: 23.1 us -> 19.7 us
  waiting for transfers between devices: 30.3 us -> 31.7 us
    sub x5 -> x2, other arithmetic: 6.12 us -> 1.08 us  [the longest x1 0.95 us: on_device(): real_part * twist_real - imag_part * twist_imag]
    dot_general x4 -> x3, matrix products: 11.5 us -> 7.45 us  [the longest x1 4.19 us: on_device(): return jnp.einsum('sij,csja->csia', band, widened, precision=highest)]
    transpose x3 -> x1, local copies, waits for them, and re-layouts: 4.67 us -> 1.25 us  [on_device(): return jnp.einsum('sij,csja->csia', band, widened, precision=highest)]
    sin x0 -> x2, other arithmetic: none -> 3.15 us  [the longest x1 3 us: on_device(): jnp.sin(phase_angle)]
    add x6 -> x3, other arithmetic: 2.85 us -> 0.12 us  [the longest x1 0.06 us: on_device(): acc_real = acc_real + wr * lane_real[:, r]]
    another operation x5 -> x0, local copies, waits for them, and re-layouts: 1.48 us -> none  [the longest x4 1.36 us: on_device(): spectrum = jnp.stack([real_part, imag_part])]
    ppermute x2, waiting for transfers between devices: 0.2 us -> 1.61 us  [the longest x1 1.4 us: on_device(): left_rim = lax.ppermute(focused[:, :, block_len - RIM:], axes, up)]
    transpose x1 -> x0, other arithmetic: 1.38 us -> none  [on_device(): left_edge = jnp.swapaxes(focused[..., :RIM], 2, 3)]
  transfers between devices with their start and end apart: 3 -> 3, of which waited for: 2 -> 3; matrix products, arithmetic and copies ran while one was open for 14% -> 9% of each run, Pallas kernels for 0% -> 0%
where the time goes in v2:
time: 85.1 us; the launch traced here: 84.8 us
  waiting for transfers between devices  31.7 us (37%)
  matrix products  19.7 us (23%)
  starting transfers between devices  12.9 us (15%)
  local copies, waits for them, and re-layouts  12.8 us (15%)
  other arithmetic  7.06 us (8%)
    all_to_all x1, waiting for transfers between devices, on_device(): lax.all_to_all(spectrum, ('pulse', 'rng'), split_axis=0, concat_axis=0, t...  30.1 us
    all_to_all x1, starting transfers between devices, on_device(): lax.all_to_all(spectrum, ('pulse', 'rng'), split_axis=0, concat_axis=0, t...  7.3 us
    ppermute x1, starting transfers between devices, on_device(): right_rim = lax.ppermute(focused[:, :, :RIM], axes, down)  5.56 us
    unnamed x4, matrix products  5.01 us
    dot_general x1, matrix products, on_device(): return jnp.einsum('sij,csja->csia', band, widened, precision=highest)  4.19 us
    dot_general x4, matrix products, contract(): return jnp.einsum(pattern, operand, matrix, precision=highest)  3.72 us
    unnamed x36, local copies, waits for them, and re-layouts  3.05 us
    sin x1, other arithmetic, on_device(): jnp.sin(phase_angle)  3 us
  transfers between devices with their start and end apart: 3, of which 3 were waited for; matrix products, arithmetic and copies ran while one was open for 9% of the time, Pallas kernels for 0%

profile of v2, /device:TPU:0, one launch (start us, length us, event | category | flops | bytes accessed | tf_op | source)
XLA Modules:
  0.0 84.8 jit_solution(8285043578696400851)
XLA Ops:
  0.0 2.4 %fusion.171 = (f32[1,24,8192]{2,1,0:T(8,128)S(1)}, f32[1,24,8192]{2,1,0:T(8,128)}) fusion(f32[2,24,8192]{2,1,0:T(8,128)} %param.6), kind=kLoop, calls=%fused_computation.240 | loop fusion | bytes 3145728 | tf_op jit(solution)/shard_map/slice | solution.py:88
  3.4 1.0 %fusion.103 = f32[128,1536]{0,1:S(1)} fusion(f32[128,1536]{0,1:T(8,128)S(1)} %bitcast.181), kind=kOutput, calls=%fused_computation.162 | convolution fusion | flops 302219264 | bytes 1572864
  4.5 1.9 %fusion.109 = f32[128,1536]{0,1} fusion(f32[128,1536]{0,1:T(8,128)S(1)} %bitcast.182), kind=kOutput, calls=%fused_computation.165 | convolution fusion | flops 302219264 | bytes 1572864
  6.4 1.8 %reshape_squeeze.6 = f32[24,128,64]{2,1,0:T(8,128)S(1)} reshape(f32[1,24,8192]{2,1,0:T(8,128)} %get-tuple-element.26) | data formatting | bytes 1572864 | tf_op jit(solution)/shard_map/reshape;squeeze | solution.py:42
  8.6 1.0 %fusion.105 = f32[128,1536]{0,1:S(1)} fusion(f32[128,1536]{0,1:T(8,128)S(1)} %bitcast.183), kind=kOutput, calls=%fused_computation.163 | convolution fusion | flops 302219264 | bytes 1572864
  9.7 1.0 %fusion.107 = f32[128,1536]{0,1:S(1)} fusion(f32[128,1536]{0,1:T(8,128)S(1)} %bitcast.184), kind=kOutput, calls=%fused_computation.164 | convolution fusion | flops 302219264 | bytes 1572864
  11.2 0.9 %fusion.28 = f32[64,24,128]{2,0,1:T(8,128)S(1)} fusion(f32[128,24,64]{0,2,1:T(8,128)S(1)} %get-tuple-element.12), kind=kOutput, calls=%fused_computation.46 | convolution fusion | flops 151052288 | bytes 1572864 | tf_op jit(solution)/shard_map/...ua,va->...vu/dot_general | solution.py:30
  12.1 0.9 %fusion.26 = f32[64,24,128]{2,0,1:T(8,128)S(1)} fusion(f32[128,24,64]{0,2,1:T(8,128)S(1)} %get-tuple-element.12), kind=kOutput, calls=%fused_computation.44 | convolution fusion | flops 151052288 | bytes 1572864 | tf_op jit(solution)/shard_map/...ua,va->...vu/dot_general | solution.py:30
  13.1 0.9 %fusion.6 = f32[24,64,128]{2,1,0:T(8,128)S(1)} fusion(f32[64,24,128]{2,0,1:T(8,128)S(1)} %fusion.28, f32[128,24,64]{0,2,1:T(8,128)S(1)} %get-tuple-element.11), kind=kOutput, calls=%fused_computation.11 | convolution fusion | flops 151248896 | bytes 2359296 | tf_op jit(solution)/shard_map/...ua,va->...vu/dot_general | solution.py:30
  14.3 0.9 %fusion.5 = f32[24,64,128]{2,1,0:T(8,128)S(1)} fusion(f32[64,24,128]{2,0,1:T(8,128)S(1)} %fusion.26, f32[128,24,64]{0,2,1:T(8,128)S(1)} %get-tuple-element.11), kind=kOutput, calls=%fused_computation.9 | convolution fusion | flops 151248896 | bytes 2359296 | tf_op jit(solution)/shard_map/...ua,va->...vu/dot_general | solution.py:30
  15.6 1.0 %multiply_subtract_fusion = (f32[1,24,32,256]{3,1,0,2:T(8,128)S(1)}, f32[1,24,32,256]{3,1,0,2:T(8,128)S(1)}) fusion(f32[1,24,32,256]{3,2,1,0:T(8,128)S(1)} %reshape.507, f32[1,24,32,256]{3,2,1,0:T(8,128)S(1)} %reshape.506, f32[32,256]{1,0:T(8,128)S(1)} %get-tuple-element.51, f32[32,256]{1,0:T(8,128)S(1)} %get-tuple-element.52), kind=kLoop, calls=%fused_computation.54 | loop fusion | flops 1179648 | bytes 3211264 | tf_op jit(solution)/shard_map/sub | solution.py:97
  16.5 1.4 %maximum_bitcast_fusion = f32[32,2,24,256]{3,2,1,0:T(8,128)} fusion(f32[1,24,32,256]{3,1,0,2:T(8,128)S(1)} %get-tuple-element.16, f32[1,24,32,256]{3,1,0,2:T(8,128)S(1)} %get-tuple-element.15), kind=kLoop, calls=%fused_computation.3 | loop fusion | flops 393216 | bytes 3145728 | tf_op jit(solution)/shard_map/transpose | solution.py:102
  18.0 7.3 %all-to-all-start = ((f32[32,2,24,256]{3,2,1,0:T(8,128)}), f32[32,2,24,256]{3,2,1,0:T(8,128)S(1)}, u32[]{:S(2)}, u32[]{:S(2)}) async-start(f32[32,2,24,256]{3,2,1,0:T(8,128)} %maximum_bitcast_fusion), calls=%async_computation | async-start | bytes 3145728 | tf_op jit(solution)/shard_map/all_to_all | solution.py:103
  25.4 3.0 %fusion.30 = (f32[4,256,192]{1,2,0:T(8,128)S(1)}, f32[4,256,192]{1,2,0:T(8,128)S(1)}) fusion(f32[192]{0:T(256)S(1)} %integer_pow.9, f32[4,256]{1,0:T(4,128)S(1)} %integer_pow.8), kind=kLoop, calls=%fused_computation.51 | loop fusion | flops 393216 | bytes 1577728 | tf_op jit(solution)/shard_map/sin | solution.py:138
  29.1 1.1 %fusion.60 = f32[192,192]{1,0:T(8,128)S(1)} fusion(s32[192]{0:T(256)S(1)} %copy-done.16), kind=kOutput, calls=%fused_computation.99 | convolution fusion | flops 85340160 | bytes 148224 | tf_op jit(solution)/shard_map/ji,ja->ai/dot_general | solution.py:69
  30.2 2.5 %fusion.172 = (f32[192,192]{1,0:T(8,128)}, f32[192,192]{1,0:T(8,128)S(1)}) fusion(s32[192]{0:T(256)} %param.7), kind=kOutput, calls=%fused_computation.241 | convolution fusion | flops 85377024 | bytes 295680 | tf_op jit(solution)/shard_map/ji,ja->ai/dot_general | solution.py:70
  32.7 30.1 %all-to-all-done = f32[32,2,24,256]{3,2,1,0:T(8,128)S(1)} async-done(((f32[32,2,24,256]{3,2,1,0:T(8,128)}), f32[32,2,24,256]{3,2,1,0:T(8,128)S(1)}, u32[]{:S(2)}, u32[]{:S(2)}) %all-to-all-start) | async-done | bytes 1572896 | tf_op jit(solution)/shard_map/all_to_all | solution.py:103
  64.5 1.6 %fusion.49 = f32[4,256,192]{1,2,0:T(8,128)S(1)} fusion(f32[4,384,256]{2,1,0:T(8,128)S(1)} %bitcast.175, f32[192,192]{1,0:T(8,128)S(1)} %copy-done.5, f32[192,192]{1,0:T(8,128)S(1)} %fusion.60), kind=kOutput, calls=%fused_computation.78 | convolution fusion | flops 906043392 | bytes 2654208 | tf_op jit(solution)/shard_map/ay,syq->sqa/dot_general | solution.py:131
  66.0 1.7 %subtract_bitcast_fusion = (f32[1,4,256,192]{2,3,1,0:T(8,128)S(1)}, f32[1,4,256,192]{2,3,1,0:T(8,128)S(1)}) fusion(f32[4,256,192]{1,2,0:T(8,128)S(1)} %get-tuple-element.8, f32[4,256,192]{1,2,0:T(8,128)S(1)} %fusion.49, f32[4,256,192]{1,2,0:T(8,128)S(1)} %get-tuple-element.7, f32[4,384,256]{2,1,0:T(8,128)S(1)} %bitcast.176, f32[192,192]{1,0:T(8,128)S(1)} %fusion.60, ...), kind=kOutput, calls=%fused_computation.49 | convolution fusion | flops 907223040 | bytes 5799936 | tf_op jit(solution)/shard_map/ay,syq->sqa/dot_general | solution.py:132
  69.5 5.6 %collective-permute-start.1 = (f32[2,4,8,192]{3,2,1,0:T(8,128)S(1)}, f32[2,4,8,192]{3,2,1,0:T(8,128)S(1)}, u32[]{:S(2)}, u32[]{:S(2)}) collective-permute-start(f32[2,4,8,192]{3,2,1,0:T(8,128)S(1)} %copy.35), channel_id=1, source_target_pairs={{1,0},{2,1},{3,2},{4,3},{5,4},{6,5},{7,6},{8,7},{9,8},{10,9},{11,1... | collective-permute-start | bytes 147464 | tf_op jit(solution)/shard_map/ppermute | solution.py:148
  75.1 1.4 %collective-permute-done = f32[2,4,8,192]{3,2,1,0:T(8,128)S(1)} collective-permute-done((f32[2,4,8,192]{3,2,1,0:T(8,128)S(1)}, f32[2,4,8,192]{3,2,1,0:T(8,128)S(1)}, u32[]{:S(2)}, u32[]{:S(2)}) %collective-permute-start) | collective-permute-done | bytes 49184 | tf_op jit(solution)/shard_map/ppermute | solution.py:147
  78.1 1.0 %copy-done.2 = f32[1,4,256,192]{2,3,1,0:T(8,128)S(1)} copy-done((f32[1,4,256,192]{2,3,1,0:T(8,128)S(1)}, f32[1,4,256,192]{2,3,1,0:T(8,128)}, u32[]{:S(2)}) %copy-start.2) | copy-done | bytes 786456
  79.3 4.2 %fusion.2 = f32[2,4,256,192]{2,3,0,1:T(8,128)S(1)} fusion(f32[4,256]{1,0:T(4,128)S(1)} %get-tuple-element.32, s32[4,256]{1,0:T(4,128)S(1)} %get-tuple-element.46, f32[4,256]{1,0:T(4,128)S(1)} %copy-done.9, s32[4,256]{1,0:T(4,128)S(1)} %get-tuple-element.42, f32[4,256]{1,0:T(4,128)S(1)} %copy-done.10, s32[4,256]{1,0:T(4,128)S(1)} %get-tuple-element.43, ...), kind=kOutput, calls=%fused_computation.7 | convolution fusion | flops 1291116544 | bytes 3309568 | tf_op jit(solution)/shard_map/sij,csja->csia/dot_general | solution.py:170
  83.5 1.2 %copy.39 = f32[2,4,256,192]{2,3,1,0:T(8,128)} copy(f32[2,4,256,192]{2,3,0,1:T(8,128)S(1)} %fusion.2) | data formatting | bytes 3145728 | tf_op jit(solution)/shard_map/sij,csja->csia/transpose | solution.py:170
  (75 shorter events, 8.4 us)
Async XLA Ops:
  9.7 1.2 %copy-start = (f32[128,1536]{0,1:S(1)}, f32[128,1536]{0,1}, u32[]{:S(2)}) copy-start(f32[128,1536]{0,1} %fusion.109) | copy-start | bytes 2359300
  18.0 7.3 %copy-start.7 = (f32[4,256]{1,0:T(4,128)S(1)}, f32[4,256]{1,0:T(4,128)}, u32[]{:S(2)}) copy-start(f32[4,256]{1,0:T(4,128)} %param.8) | copy-start | bytes 12292
  18.0 7.4 %copy-start.15 = (f32[192]{0:T(256)S(1)}, f32[192]{0:T(256)}, u32[]{:S(2)}) copy-start(f32[192]{0:T(256)} %param.9) | copy-start | bytes 2308
  18.0 44.8 %all-to-all-start = ((f32[32,2,24,256]{3,2,1,0:T(8,128)}), f32[32,2,24,256]{3,2,1,0:T(8,128)S(1)}, u32[]{:S(2)}, u32[]{:S(2)}) async-start(f32[32,2,24,256]{3,2,1,0:T(8,128)} %maximum_bitcast_fusion), calls=%async_computation | async-start | bytes 3145728 | tf_op jit(solution)/shard_map/all_to_all | solution.py:103
  25.3 3.1 %copy-start.8 = (s32[4,256]{1,0:T(4,128)S(1)}, s32[4,256]{1,0:T(4,128)}, u32[]{:S(2)}) copy-start(s32[4,256]{1,0:T(4,128)} %param.10) | copy-start | bytes 12292
  25.3 3.2 %copy-start.6 = (f32[8,4,256]{2,1,0:T(4,128)S(1)}, f32[8,4,256]{2,1,0:T(4,128)}, u32[]{:S(2)}) copy-start(f32[8,4,256]{2,1,0:T(4,128)} %param.11) | copy-start | bytes 98308
  25.3 3.8 %copy-start.16 = (s32[192]{0:T(256)S(1)}, s32[192]{0:T(256)}, u32[]{:S(2)}) copy-start(s32[192]{0:T(256)} %param.7) | copy-start | bytes 2308
  63.5 0.9 %copy-start.5 = (f32[192,192]{1,0:T(8,128)S(1)}, f32[192,192]{1,0:T(8,128)}, u32[]{:S(2)}) copy-start(f32[192,192]{1,0:T(8,128)} %get-tuple-element.47) | copy-start | bytes 442372
  67.7 0.9 %copy-start.1 = (f32[1,4,256,192]{2,3,1,0:T(8,128)}, f32[1,4,256,192]{2,3,1,0:T(8,128)S(1)}, u32[]{:S(2)}) copy-start(f32[1,4,256,192]{2,3,1,0:T(8,128)S(1)} %get-tuple-element.13) | copy-start | bytes 2359300
  67.7 1.1 %copy-start.3 = (f32[1,4,256,192]{2,3,1,0:T(8,128)}, f32[1,4,256,192]{2,3,1,0:T(8,128)S(1)}, u32[]{:S(2)}) copy-start(f32[1,4,256,192]{2,3,1,0:T(8,128)S(1)} %get-tuple-element.14) | copy-start | bytes 2359300
  69.2 7.3 %collective-permute-start = (f32[2,4,8,192]{3,2,1,0:T(8,128)S(1)}, f32[2,4,8,192]{3,2,1,0:T(8,128)S(1)}, u32[]{:S(2)}, u32[]{:S(2)}) collective-permute-start(f32[2,4,8,192]{3,2,1,0:T(8,128)S(1)} %copy.32), channel_id=1, source_target_pairs={{0,1},{1,2},{2,3},{3,4},{4,5},{5,6},{6,7},{7,8},{8,9},{9,10},{10,1... | collective-permute-start | bytes 147464 | tf_op jit(solution)/shard_map/ppermute | solution.py:147
  69.5 7.5 %collective-permute-start.1 = (f32[2,4,8,192]{3,2,1,0:T(8,128)S(1)}, f32[2,4,8,192]{3,2,1,0:T(8,128)S(1)}, u32[]{:S(2)}, u32[]{:S(2)}) collective-permute-start(f32[2,4,8,192]{3,2,1,0:T(8,128)S(1)} %copy.35), channel_id=1, source_target_pairs={{1,0},{2,1},{3,2},{4,3},{5,4},{6,5},{7,6},{8,7},{9,8},{10,9},{11,1... | collective-permute-start | bytes 147464 | tf_op jit(solution)/shard_map/ppermute | solution.py:148
  77.9 1.1 %copy-start.2 = (f32[1,4,256,192]{2,3,1,0:T(8,128)S(1)}, f32[1,4,256,192]{2,3,1,0:T(8,128)}, u32[]{:S(2)}) copy-start(f32[1,4,256,192]{2,3,1,0:T(8,128)} %copy-done.1) | copy-start | bytes 2359300
  77.9 1.4 %copy-start.4 = (f32[1,4,256,192]{2,3,1,0:T(8,128)S(1)}, f32[1,4,256,192]{2,3,1,0:T(8,128)}, u32[]{:S(2)}) copy-start(f32[1,4,256,192]{2,3,1,0:T(8,128)} %copy-done.3) | copy-start | bytes 2359300
  77.9 1.4 %copy-start.9 = (f32[4,256]{1,0:T(4,128)S(1)}, f32[4,256]{1,0:T(4,128)}, u32[]{:S(2)}) copy-start(f32[4,256]{1,0:T(4,128)} %get-tuple-element.33) | copy-start | bytes 12292
  78.0 1.4 %copy-start.10 = (f32[4,256]{1,0:T(4,128)S(1)}, f32[4,256]{1,0:T(4,128)}, u32[]{:S(2)}) copy-start(f32[4,256]{1,0:T(4,128)} %get-tuple-element.34) | copy-start | bytes 12292
  78.0 1.3 %copy-start.11 = (f32[4,256]{1,0:T(4,128)S(1)}, f32[4,256]{1,0:T(4,128)}, u32[]{:S(2)}) copy-start(f32[4,256]{1,0:T(4,128)} %get-tuple-element.35) | copy-start | bytes 12292
  78.0 1.3 %copy-start.12 = (f32[4,256]{1,0:T(4,128)S(1)}, f32[4,256]{1,0:T(4,128)}, u32[]{:S(2)}) copy-start(f32[4,256]{1,0:T(4,128)} %get-tuple-element.36) | copy-start | bytes 12292
  78.0 1.3 %copy-start.13 = (f32[4,256]{1,0:T(4,128)S(1)}, f32[4,256]{1,0:T(4,128)}, u32[]{:S(2)}) copy-start(f32[4,256]{1,0:T(4,128)} %get-tuple-element.37) | copy-start | bytes 12292
  78.0 1.3 %copy-start.14 = (f32[4,256]{1,0:T(4,128)S(1)}, f32[4,256]{1,0:T(4,128)}, u32[]{:S(2)}) copy-start(f32[4,256]{1,0:T(4,128)} %get-tuple-element.38) | copy-start | bytes 12292

commit v3 on v2

--- a/solution.py
+++ b/solution.py
@@ -150,7 +150,6 @@
     right_rim = jnp.where(
         position == device_count - 1, jnp.roll(right_rim, -1, axis=1), right_rim
     )
-    widened = jnp.concatenate([left_rim, focused, right_rim], axis=2)
 
     tap_count = stolt_coef.shape[0]
     piece_index = jnp.arange(block_len, dtype=jnp.int32)
@@ -167,7 +166,18 @@
     for t in range(tap_count):
         band = band + jnp.where(columns[None, None, :] == target + t, weights[t][:, :, None], 0.0)
 
-    return jnp.einsum("sij,csja->csia", band, widened, precision=highest)
+    image = jnp.einsum(
+        "sij,csja->csia", band[:, :, RIM:RIM + block_len], focused, precision=highest
+    )
+    left_part = jnp.einsum("sij,csja->csia", band[:, :RIM, :RIM], left_rim, precision=highest)
+    right_part = jnp.einsum(
+        "sij,csja->csia", band[:, block_len - RIM:, block_len + RIM:], right_rim, precision=highest
+    )
+    image = lax.dynamic_update_slice_in_dim(image, image[:, :, :RIM] + left_part, 0, axis=2)
+    image = lax.dynamic_update_slice_in_dim(
+        image, image[:, :, block_len - RIM:] + right_part, block_len - RIM, axis=2
+    )
+    return image
 
 
 def solution(mesh):

time: 85.1 us -> 90.2 us (1.060)
  other arithmetic: 7.06 us -> 13.3 us
  waiting for transfers between devices: 31.7 us -> 26.5 us
  matrix products: 19.7 us -> 21.9 us
  local copies, waits for them, and re-layouts: 12.8 us -> 14.7 us
    dynamic_update_slice x0 -> x3, local copies, waits for them, and re-layouts: none -> 6.49 us  [the longest x2 4.45 us: on_device(): lax.dynamic_update_slice_in_dim(image, image[:, :, block_len - RIM:] + ri...]
    add x0 -> x1, other arithmetic: none -> 4.45 us  [on_device(): band + jnp.where(columns[None, None, :] == target + t, weights[t][:, :, N...]
    all_to_all x1, waiting for transfers between devices: 30.1 us -> 26.5 us  [on_device(): lax.all_to_all(spectrum, ('pulse', 'rng'), split_axis=0, concat_axis=0, t...]
    dot_general x1 -> x3, matrix products: 4.19 us -> 7.66 us  [the longest x1 3.14 us: on_device(): jnp.einsum('sij,csja->csia', band[:, :, RIM:RIM + block_len], focused, pr...]
    unnamed x36 -> x18, local copies, waits for them, and re-layouts: 3.05 us -> 0.17 us
    ppermute x1, waiting for transfers between devices: 1.4 us -> 0.01 us  [on_device(): left_rim = lax.ppermute(focused[:, :, block_len - RIM:], axes, up)]
    dot_general x1, matrix products: 2.45 us -> 1.1 us  [azimuth_matrix(): fold_imag = jnp.einsum('ji,ja->ai', select, dft_imag, precision=highest)]
    transpose x1 -> x0, local copies, waits for them, and re-layouts: 1.25 us -> none  [on_device(): return jnp.einsum('sij,csja->csia', band, widened, precision=highest)]
  transfers between devices with their start and end apart: 3 -> 3, of which waited for: 3 -> 1; matrix products, arithmetic and copies ran while one was open for 9% -> 22% of each run, Pallas kernels for 0% -> 0%
where the time goes in v3:
time: 90.2 us; the launch traced here: 89.7 us
  waiting for transfers between devices  26.5 us (29%)
  matrix products  21.9 us (24%)
  local copies, waits for them, and re-layouts  14.7 us (16%)
  other arithmetic  13.3 us (15%)
  starting transfers between devices  12.9 us (14%)
    all_to_all x1, waiting for transfers between devices, on_device(): lax.all_to_all(spectrum, ('pulse', 'rng'), split_axis=0, concat_axis=0, t...  26.5 us
    all_to_all x1, starting transfers between devices, on_device(): lax.all_to_all(spectrum, ('pulse', 'rng'), split_axis=0, concat_axis=0, t...  7.3 us
    ppermute x1, starting transfers between devices, on_device(): right_rim = lax.ppermute(focused[:, :, :RIM], axes, down)  5.58 us
    unnamed x4, matrix products  5.01 us
    dynamic_update_slice x2, local copies, waits for them, and re-layouts, on_device(): lax.dynamic_update_slice_in_dim(image, image[:, :, block_len - RIM:] + ri...  4.45 us
    add x1, other arithmetic, on_device(): band + jnp.where(columns[None, None, :] == target + t, weights[t][:, :, N...  4.45 us
    sin x1, other arithmetic, on_device(): jnp.sin(phase_angle)  4.12 us
    dot_general x4, matrix products, contract(): return jnp.einsum(pattern, operand, matrix, precision=highest)  3.72 us
  transfers between devices with their start and end apart: 3, of which 1 were waited for; matrix products, arithmetic and copies ran while one was open for 22% of the time, Pallas kernels for 0%

profile of v3, /device:TPU:0, one launch (start us, length us, event | category | flops | bytes accessed | tf_op | source)
XLA Modules:
  0.0 89.7 jit_solution(2824435264440743811)
XLA Ops:
  0.0 2.4 %fusion.142 = (f32[1,24,8192]{2,1,0:T(8,128)S(1)}, f32[1,24,8192]{2,1,0:T(8,128)}) fusion(f32[2,24,8192]{2,1,0:T(8,128)} %param.6), kind=kLoop, calls=%fused_computation.216 | loop fusion | bytes 3145728 | tf_op jit(solution)/shard_map/slice | solution.py:88
  3.4 1.0 %fusion.75 = f32[128,1536]{0,1:S(1)} fusion(f32[128,1536]{0,1:T(8,128)S(1)} %bitcast.199), kind=kOutput, calls=%fused_computation.137 | convolution fusion | flops 302219264 | bytes 1572864
  4.5 1.9 %fusion.81 = f32[128,1536]{0,1} fusion(f32[128,1536]{0,1:T(8,128)S(1)} %bitcast.200), kind=kOutput, calls=%fused_computation.140 | convolution fusion | flops 302219264 | bytes 1572864
  6.4 1.8 %reshape_squeeze.6 = f32[24,128,64]{2,1,0:T(8,128)S(1)} reshape(f32[1,24,8192]{2,1,0:T(8,128)} %get-tuple-element.26) | data formatting | bytes 1572864 | tf_op jit(solution)/shard_map/reshape;squeeze | solution.py:42
  8.6 1.0 %fusion.77 = f32[128,1536]{0,1:S(1)} fusion(f32[128,1536]{0,1:T(8,128)S(1)} %bitcast.201), kind=kOutput, calls=%fused_computation.138 | convolution fusion | flops 302219264 | bytes 1572864
  9.7 1.0 %fusion.79 = f32[128,1536]{0,1:S(1)} fusion(f32[128,1536]{0,1:T(8,128)S(1)} %bitcast.202), kind=kOutput, calls=%fused_computation.139 | convolution fusion | flops 302219264 | bytes 1572864
  16.5 1.5 %maximum_bitcast_fusion = f32[32,2,24,256]{3,2,1,0:T(8,128)} fusion(f32[1,24,32,256]{3,1,0,2:T(8,128)S(1)} %get-tuple-element.16, f32[1,24,32,256]{3,1,0,2:T(8,128)S(1)} %get-tuple-element.15), kind=kLoop, calls=%fused_computation.5 | loop fusion | flops 393216 | bytes 3145728 | tf_op jit(solution)/shard_map/transpose | solution.py:102
  18.0 7.3 %all-to-all-start = ((f32[32,2,24,256]{3,2,1,0:T(8,128)}), f32[32,2,24,256]{3,2,1,0:T(8,128)S(1)}, u32[]{:S(2)}, u32[]{:S(2)}) async-start(f32[32,2,24,256]{3,2,1,0:T(8,128)} %maximum_bitcast_fusion), calls=%async_computation | async-start | bytes 3145728 | tf_op jit(solution)/shard_map/all_to_all | solution.py:103
  25.4 4.1 %fusion.17 = (f32[4,256,192]{1,2,0:T(8,128)}, f32[4,256,192]{1,2,0:T(8,128)}) fusion(f32[192]{0:T(256)S(1)} %integer_pow.9, f32[4,256]{1,0:T(4,128)S(1)} %integer_pow.8), kind=kLoop, calls=%fused_computation.43 | loop fusion | flops 393216 | bytes 1577728 | tf_op jit(solution)/shard_map/sin | solution.py:138
  29.7 1.1 %fusion.30 = f32[192,192]{1,0:T(8,128)S(1)} fusion(s32[192]{0:T(256)S(1)} %copy-done.7), kind=kOutput, calls=%fused_computation.72 | convolution fusion | flops 85340160 | bytes 148224 | tf_op jit(solution)/shard_map/ji,ja->ai/dot_general | solution.py:69
  30.8 1.1 %fusion.143 = (f32[192,192]{1,0:T(8,128)S(1)}, f32[192,192]{1,0:T(8,128)S(1)}) fusion(s32[192]{0:T(256)S(1)} %copy-done.7), kind=kOutput, calls=%fused_computation.217 | convolution fusion | flops 85377024 | bytes 295680 | tf_op jit(solution)/shard_map/ji,ja->ai/dot_general | solution.py:70
  31.9 4.5 %select_add_fusion = f32[4,256,272]{2,1,0:T(8,128)} fusion(f32[4,256]{1,0:T(4,128)S(1)} %get-tuple-element.32, s32[4,256]{1,0:T(4,128)S(1)} %get-tuple-element.46, f32[4,256]{1,0:T(4,128)S(1)} %get-tuple-element.33, s32[4,256]{1,0:T(4,128)S(1)} %get-tuple-element.42, f32[4,256]{1,0:T(4,128)S(1)} %get-tuple-element.34, s32[4,256]{1,0:T(4,128)S(1)} %get-tuple-element.43, ...), kind=kLoop, calls=%fused_computation.9 | loop fusion | flops 6406144 | bytes 1179648 | tf_op jit(solution)/shard_map/add | solution.py:167
  36.3 26.5 %all-to-all-done = f32[32,2,24,256]{3,2,1,0:T(8,128)S(1)} async-done(((f32[32,2,24,256]{3,2,1,0:T(8,128)}), f32[32,2,24,256]{3,2,1,0:T(8,128)S(1)}, u32[]{:S(2)}, u32[]{:S(2)}) %all-to-all-start) | async-done | bytes 1572896 | tf_op jit(solution)/shard_map/all_to_all | solution.py:103
  63.7 1.6 %fusion.19 = f32[4,256,192]{1,2,0:T(8,128)S(1)} fusion(f32[4,384,256]{2,1,0:T(8,128)S(1)} %bitcast.193, f32[192,192]{1,0:T(8,128)S(1)} %get-tuple-element.47, f32[192,192]{1,0:T(8,128)S(1)} %fusion.30), kind=kOutput, calls=%fused_computation.51 | convolution fusion | flops 906043392 | bytes 2654208 | tf_op jit(solution)/shard_map/ay,syq->sqa/dot_general | solution.py:131
  65.3 1.7 %subtract_bitcast_fusion = (f32[1,4,256,192]{2,3,1,0:T(8,128)S(1)}, f32[1,4,256,192]{2,3,1,0:T(8,128)S(1)}) fusion(f32[4,256,192]{1,2,0:T(8,128)S(1)} %copy-done.1, f32[4,256,192]{1,2,0:T(8,128)S(1)} %fusion.19, f32[4,256,192]{1,2,0:T(8,128)S(1)} %copy-done.2, f32[4,384,256]{2,1,0:T(8,128)S(1)} %bitcast.194, f32[192,192]{1,0:T(8,128)S(1)} %fusion.30, ...), kind=kOutput, calls=%fused_computation.41 | convolution fusion | flops 907223040 | bytes 5799936 | tf_op jit(solution)/shard_map/ay,syq->sqa/dot_general | solution.py:132
  67.0 1.1 %fusion.10 = (f32[2,4,8,192]{2,3,1,0:T(8,128)}, f32[2,4,8,192]{2,3,1,0:T(8,128)S(1)}) fusion(f32[1,4,256,192]{2,3,1,0:T(8,128)S(1)} %get-tuple-element.13, f32[1,4,256,192]{2,3,1,0:T(8,128)S(1)} %get-tuple-element.14), kind=kLoop, calls=%fused_computation.29 | loop fusion | flops 24576 | bytes 1671168 | tf_op jit(solution)/shard_map/stack | solution.py:142
  68.5 3.1 %fusion.2 = f32[2,4,256,192]{2,3,0,1:T(8,128)S(1)} fusion(f32[4,256,272]{2,1,0:T(8,128)} %select_add_fusion, f32[1,4,256,192]{2,3,1,0:T(8,128)S(1)} %get-tuple-element.14, f32[1,4,256,192]{2,3,1,0:T(8,128)S(1)} %get-tuple-element.13), kind=kOutput, calls=%fused_computation.18 | convolution fusion | flops 1208352768 | bytes 4194304 | tf_op jit(solution)/shard_map/sij,csja->csia/dot_general | solution.py:169
  71.7 1.4 %copy.44 = f32[2,4,8,192]{3,2,1,0:T(8,128)S(1)} copy(f32[2,4,8,192]{2,3,1,0:T(8,128)} %get-tuple-element.17) | data formatting | bytes 98304 | tf_op jit(solution)/shard_map/slice | solution.py:148
  73.1 5.6 %collective-permute-start.1 = (f32[2,4,8,192]{3,2,1,0:T(8,128)S(1)}, f32[2,4,8,192]{3,2,1,0:T(8,128)S(1)}, u32[]{:S(2)}, u32[]{:S(2)}) collective-permute-start(f32[2,4,8,192]{3,2,1,0:T(8,128)S(1)} %copy.44), channel_id=1, source_target_pairs={{1,0},{2,1},{3,2},{4,3},{5,4},{6,5},{7,6},{8,7},{9,8},{10,9},{11,1... | collective-permute-start | bytes 147464 | tf_op jit(solution)/shard_map/ppermute | solution.py:148
  78.7 2.2 %fusion.8 = f32[2,4,8,192]{2,3,0,1:T(8,128)S(1)} fusion(f32[2,4,256,192]{2,3,0,1:T(8,128)S(1)} %fusion.2, f32[4,256,272]{2,1,0:T(8,128)} %select_add_fusion, f32[2,4,8,192]{3,2,1,0:T(8,128)S(1)} %collective-permute-done, f32[2,3,8,192]{3,2,1,0:T(8,128)S(1)} %slice.175, f32[2,1,8,192]{3,2,1,0:T(8,128)S(1)} %slice.174, pred[]{:T(512)S(6)} %eq.157), kind=kOutput, calls=%fused_computation.26 | convolution fusion | flops 1216512 | bytes 212993 | tf_op jit(solution)/shard_map/sij,csja->csia/dot_general | solution.py:172
  80.9 2.0 %dynamic_update_slice.6 = f32[2,4,256,192]{2,3,0,1:T(8,128)S(1)} dynamic-update-slice(f32[2,4,256,192]{2,3,0,1:T(8,128)S(1)} %fusion.2, f32[2,4,8,192]{2,3,0,1:T(8,128)S(1)} %fusion.8, s32[]{:T(128)} %constant.52.clone.1, s32[]{:T(128)} %constant.52.clone.1, s32[]{:T(128)} %constant.52.clone.1, s32[]{:T(128)} %constant.52.clone.1) | dynamic-update-slice | bytes 98308 | tf_op jit(solution)/shard_map/dynamic_update_slice | solution.py:176
  82.9 2.3 %fusion.7 = f32[2,4,8,192]{2,3,0,1:T(8,128)S(1)} fusion(f32[2,4,256,192]{2,3,0,1:T(8,128)S(1)} %dynamic_update_slice.6, f32[4,256,272]{2,1,0:T(8,128)} %select_add_fusion, f32[2,4,8,192]{3,2,1,0:T(8,128)S(1)} %collective-permute-done.1, f32[2,1,8,192]{3,2,1,0:T(8,128)S(1)} %slice.181, f32[2,3,8,192]{3,2,1,0:T(8,128)S(1)} %slice.180, pred[]{:T(512)S(6)} %eq.158), kind=kOutput, calls=%fused_computation.24 | convolution fusion | flops 1216512 | bytes 212993 | tf_op jit(solution)/shard_map/sij,csja->csia/dot_general | solution.py:173
  85.3 3.1 %dynamic_update_slice.7 = f32[2,4,256,192]{2,3,0,1:T(8,128)S(1)} dynamic-update-slice(f32[2,4,256,192]{2,3,0,1:T(8,128)S(1)} %dynamic_update_slice.6, f32[2,4,8,192]{2,3,0,1:T(8,128)S(1)} %fusion.7, s32[]{:T(128)} %constant.52.clone.1, s32[]{:T(128)} %constant.52.clone.1, s32[]{:T(128)} %constant.123.clone.1, s32[]{:T(128)} %constant.52.clone.1) | dynamic-update-slice | bytes 98308 | tf_op jit(solution)/shard_map/dynamic_update_slice | solution.py:177
  88.4 1.3 %copy.47 = f32[2,4,256,192]{2,3,1,0:T(8,128)} copy(f32[2,4,256,192]{2,3,0,1:T(8,128)S(1)} %dynamic_update_slice.7) | data formatting | bytes 3145728 | tf_op jit(solution)/shard_map/dynamic_update_slice | solution.py:177
  (54 shorter events, 8.6 us)
Async XLA Ops:
  8.6 2.2 %copy-start = (f32[128,1536]{0,1:S(1)}, f32[128,1536]{0,1}, u32[]{:S(2)}) copy-start(f32[128,1536]{0,1} %fusion.81) | copy-start | bytes 2359300
  18.0 7.3 %copy-start.4 = (f32[4,256]{1,0:T(4,128)S(1)}, f32[4,256]{1,0:T(4,128)}, u32[]{:S(2)}) copy-start(f32[4,256]{1,0:T(4,128)} %param.8) | copy-start | bytes 12292
  18.0 7.4 %copy-start.6 = (f32[192]{0:T(256)S(1)}, f32[192]{0:T(256)}, u32[]{:S(2)}) copy-start(f32[192]{0:T(256)} %param.9) | copy-start | bytes 2308
  18.0 44.8 %all-to-all-start = ((f32[32,2,24,256]{3,2,1,0:T(8,128)}), f32[32,2,24,256]{3,2,1,0:T(8,128)S(1)}, u32[]{:S(2)}, u32[]{:S(2)}) async-start(f32[32,2,24,256]{3,2,1,0:T(8,128)} %maximum_bitcast_fusion), calls=%async_computation | async-start | bytes 3145728 | tf_op jit(solution)/shard_map/all_to_all | solution.py:103
  25.3 4.2 %copy-start.5 = (s32[4,256]{1,0:T(4,128)S(1)}, s32[4,256]{1,0:T(4,128)}, u32[]{:S(2)}) copy-start(s32[4,256]{1,0:T(4,128)} %param.10) | copy-start | bytes 12292
  25.3 4.3 %copy-start.3 = (f32[8,4,256]{2,1,0:T(4,128)S(1)}, f32[8,4,256]{2,1,0:T(4,128)}, u32[]{:S(2)}) copy-start(f32[8,4,256]{2,1,0:T(4,128)} %param.11) | copy-start | bytes 98308
  25.4 4.3 %copy-start.7 = (s32[192]{0:T(256)S(1)}, s32[192]{0:T(256)}, u32[]{:S(2)}) copy-start(s32[192]{0:T(256)} %param.7) | copy-start | bytes 2308
  63.7 1.6 %copy-start.1 = (f32[4,256,192]{1,2,0:T(8,128)S(1)}, f32[4,256,192]{1,2,0:T(8,128)}, u32[]{:S(2)}) copy-start(f32[4,256,192]{1,2,0:T(8,128)} %get-tuple-element.8) | copy-start | bytes 2359300
  63.7 1.6 %copy-start.2 = (f32[4,256,192]{1,2,0:T(8,128)S(1)}, f32[4,256,192]{1,2,0:T(8,128)}, u32[]{:S(2)}) copy-start(f32[4,256,192]{1,2,0:T(8,128)} %get-tuple-element.7) | copy-start | bytes 2359300
  68.5 10.2 %collective-permute-start = (f32[2,4,8,192]{3,2,1,0:T(8,128)S(1)}, f32[2,4,8,192]{3,2,1,0:T(8,128)S(1)}, u32[]{:S(2)}, u32[]{:S(2)}) collective-permute-start(f32[2,4,8,192]{3,2,1,0:T(8,128)S(1)} %copy.41), channel_id=1, source_target_pairs={{0,1},{1,2},{2,3},{3,4},{4,5},{5,6},{6,7},{7,8},{8,9},{9,10},{10,1... | collective-permute-start | bytes 147464 | tf_op jit(solution)/shard_map/ppermute | solution.py:147
  73.1 9.8 %collective-permute-start.1 = (f32[2,4,8,192]{3,2,1,0:T(8,128)S(1)}, f32[2,4,8,192]{3,2,1,0:T(8,128)S(1)}, u32[]{:S(2)}, u32[]{:S(2)}) collective-permute-start(f32[2,4,8,192]{3,2,1,0:T(8,128)S(1)} %copy.44), channel_id=1, source_target_pairs={{1,0},{2,1},{3,2},{4,3},{5,4},{6,5},{7,6},{8,7},{9,8},{10,9},{11,1... | collective-permute-start | bytes 147464 | tf_op jit(solution)/shard_map/ppermute | solution.py:148

commit v4 on v2

--- a/solution.py
+++ b/solution.py
@@ -27,7 +27,7 @@
 def complex_einsum(pattern, real_part, imag_part, table_real, table_imag):
 
     def contract(operand, matrix):
-        return jnp.einsum(pattern, operand, matrix, precision=highest)
+        return jnp.einsum(pattern, operand, matrix, precision=lax.Precision.HIGH)
 
     return (
         contract(real_part, table_real) - contract(imag_part, table_imag),

time: 85.1 us -> 82.7 us (0.972)
  matrix products: 19.7 us -> 17.2 us
    dot_general x4, matrix products: 3.72 us -> 2.41 us  [contract(): return jnp.einsum(pattern, operand, matrix, precision=lax.Precision.HIGH)]
    unnamed x4, matrix products: 5.01 us -> 3.78 us
  transfers between devices with their start and end apart: 3 -> 3, of which waited for: 3 -> 3; matrix products, arithmetic and copies ran while one was open for 9% -> 10% of each run, Pallas kernels for 0% -> 0%
where the time goes in v4:
time: 82.7 us; the launch traced here: 82.3 us
  waiting for transfers between devices  31.5 us (38%)
  matrix products  17.2 us (21%)
  local copies, waits for them, and re-layouts  13.1 us (16%)
  starting transfers between devices  13.1 us (16%)
  other arithmetic  6.88 us (8%)
    all_to_all x1, waiting for transfers between devices, on_device(): lax.all_to_all(spectrum, ('pulse', 'rng'), split_axis=0, concat_axis=0, t...  29.9 us
    all_to_all x1, starting transfers between devices, on_device(): lax.all_to_all(spectrum, ('pulse', 'rng'), split_axis=0, concat_axis=0, t...  7.48 us
    ppermute x1, starting transfers between devices, on_device(): right_rim = lax.ppermute(focused[:, :, :RIM], axes, down)  5.56 us
    dot_general x1, matrix products, on_device(): return jnp.einsum('sij,csja->csia', band, widened, precision=highest)  4.19 us
    unnamed x4, matrix products  3.78 us
    unnamed x36, local copies, waits for them, and re-layouts  3.3 us
    sin x1, other arithmetic, on_device(): jnp.sin(phase_angle)  3 us
    dot_general x1, matrix products, azimuth_matrix(): fold_imag = jnp.einsum('ji,ja->ai', select, dft_imag, precision=highest)  2.45 us
  transfers between devices with their start and end apart: 3, of which 3 were waited for; matrix products, arithmetic and copies ran while one was open for 10% of the time, Pallas kernels for 0%

profile of v4, /device:TPU:0, one launch (start us, length us, event | category | flops | bytes accessed | tf_op | source)
XLA Modules:
  0.0 82.3 jit_solution(213333288827593759)
XLA Ops:
  0.0 2.4 %fusion.171 = (f32[1,24,8192]{2,1,0:T(8,128)S(1)}, f32[1,24,8192]{2,1,0:T(8,128)}) fusion(f32[2,24,8192]{2,1,0:T(8,128)} %param.6), kind=kLoop, calls=%fused_computation.240 | loop fusion | bytes 3145728 | tf_op jit(solution)/shard_map/slice | solution.py:88
  2.4 0.6 reshape_squeeze.7
  3.4 0.7 fusion.103
  4.2 1.6 %fusion.109 = f32[128,1536]{0,1} fusion(f32[128,1536]{0,1:T(8,128)S(1)} %bitcast.182), kind=kOutput, calls=%fused_computation.165 | convolution fusion | flops 151224320 | bytes 1572864
  5.8 1.8 %reshape_squeeze.6 = f32[24,128,64]{2,1,0:T(8,128)S(1)} reshape(f32[1,24,8192]{2,1,0:T(8,128)} %get-tuple-element.26) | data formatting | bytes 1572864 | tf_op jit(solution)/shard_map/reshape;squeeze | solution.py:42
  8.0 0.7 fusion.105
  8.7 0.7 fusion.107
  10.2 0.6 fusion.28
  13.3 1.0 %multiply_subtract_fusion = (f32[1,24,32,256]{3,1,0,2:T(8,128)S(1)}, f32[1,24,32,256]{3,1,0,2:T(8,128)S(1)}) fusion(f32[1,24,32,256]{3,2,1,0:T(8,128)S(1)} %reshape.507, f32[1,24,32,256]{3,2,1,0:T(8,128)S(1)} %reshape.506, f32[32,256]{1,0:T(8,128)S(1)} %get-tuple-element.51, f32[32,256]{1,0:T(8,128)S(1)} %get-tuple-element.52), kind=kLoop, calls=%fused_computation.54 | loop fusion | flops 1179648 | bytes 3211264 | tf_op jit(solution)/shard_map/sub | solution.py:97
  14.2 1.2 %maximum_bitcast_fusion = f32[32,2,24,256]{3,2,1,0:T(8,128)} fusion(f32[1,24,32,256]{3,1,0,2:T(8,128)S(1)} %get-tuple-element.16, f32[1,24,32,256]{3,1,0,2:T(8,128)S(1)} %get-tuple-element.15), kind=kLoop, calls=%fused_computation.3 | loop fusion | flops 393216 | bytes 3145728 | tf_op jit(solution)/shard_map/transpose | solution.py:102
  15.5 7.5 %all-to-all-start = ((f32[32,2,24,256]{3,2,1,0:T(8,128)}), f32[32,2,24,256]{3,2,1,0:T(8,128)S(1)}, u32[]{:S(2)}, u32[]{:S(2)}) async-start(f32[32,2,24,256]{3,2,1,0:T(8,128)} %maximum_bitcast_fusion), calls=%async_computation | async-start | bytes 3145728 | tf_op jit(solution)/shard_map/all_to_all | solution.py:103
  23.0 3.0 %fusion.30 = (f32[4,256,192]{1,2,0:T(8,128)S(1)}, f32[4,256,192]{1,2,0:T(8,128)S(1)}) fusion(f32[192]{0:T(256)S(1)} %integer_pow.9, f32[4,256]{1,0:T(4,128)S(1)} %integer_pow.8), kind=kLoop, calls=%fused_computation.51 | loop fusion | flops 393216 | bytes 1577728 | tf_op jit(solution)/shard_map/sin | solution.py:138
  26.2 0.6 slice_bitcast_fusion.15
  26.8 1.1 %fusion.60 = f32[192,192]{1,0:T(8,128)S(1)} fusion(s32[192]{0:T(256)S(1)} %copy-done.16), kind=kOutput, calls=%fused_computation.99 | convolution fusion | flops 85340160 | bytes 148224 | tf_op jit(solution)/shard_map/ji,ja->ai/dot_general | solution.py:69
  27.9 2.5 %fusion.172 = (f32[192,192]{1,0:T(8,128)}, f32[192,192]{1,0:T(8,128)S(1)}) fusion(s32[192]{0:T(256)} %param.7), kind=kOutput, calls=%fused_computation.241 | convolution fusion | flops 85377024 | bytes 295680 | tf_op jit(solution)/shard_map/ji,ja->ai/dot_general | solution.py:70
  30.4 29.9 %all-to-all-done = f32[32,2,24,256]{3,2,1,0:T(8,128)S(1)} async-done(((f32[32,2,24,256]{3,2,1,0:T(8,128)}), f32[32,2,24,256]{3,2,1,0:T(8,128)S(1)}, u32[]{:S(2)}, u32[]{:S(2)}) %all-to-all-start) | async-done | bytes 1572896 | tf_op jit(solution)/shard_map/all_to_all | solution.py:103
  61.2 0.8 copy-done.5
  62.0 1.5 %fusion.49 = f32[4,256,192]{1,2,0:T(8,128)S(1)} fusion(f32[4,384,256]{2,1,0:T(8,128)S(1)} %bitcast.175, f32[192,192]{1,0:T(8,128)S(1)} %copy-done.5, f32[192,192]{1,0:T(8,128)S(1)} %fusion.60), kind=kOutput, calls=%fused_computation.78 | convolution fusion | flops 906043392 | bytes 2654208 | tf_op jit(solution)/shard_map/ay,syq->sqa/dot_general | solution.py:131
  63.5 1.7 %subtract_bitcast_fusion = (f32[1,4,256,192]{2,3,1,0:T(8,128)S(1)}, f32[1,4,256,192]{2,3,1,0:T(8,128)S(1)}) fusion(f32[4,256,192]{1,2,0:T(8,128)S(1)} %get-tuple-element.8, f32[4,256,192]{1,2,0:T(8,128)S(1)} %fusion.49, f32[4,256,192]{1,2,0:T(8,128)S(1)} %get-tuple-element.7, f32[4,384,256]{2,1,0:T(8,128)S(1)} %bitcast.176, f32[192,192]{1,0:T(8,128)S(1)} %fusion.60, ...), kind=kOutput, calls=%fused_computation.49 | convolution fusion | flops 907223040 | bytes 5799936 | tf_op jit(solution)/shard_map/ay,syq->sqa/dot_general | solution.py:132
  67.0 5.6 %collective-permute-start.1 = (f32[2,4,8,192]{3,2,1,0:T(8,128)S(1)}, f32[2,4,8,192]{3,2,1,0:T(8,128)S(1)}, u32[]{:S(2)}, u32[]{:S(2)}) collective-permute-start(f32[2,4,8,192]{3,2,1,0:T(8,128)S(1)} %copy.35), channel_id=1, source_target_pairs={{1,0},{2,1},{3,2},{4,3},{5,4},{6,5},{7,6},{8,7},{9,8},{10,9},{11,1... | collective-permute-start | bytes 147464 | tf_op jit(solution)/shard_map/ppermute | solution.py:148
  72.6 1.4 %collective-permute-done = f32[2,4,8,192]{3,2,1,0:T(8,128)S(1)} collective-permute-done((f32[2,4,8,192]{3,2,1,0:T(8,128)S(1)}, f32[2,4,8,192]{3,2,1,0:T(8,128)S(1)}, u32[]{:S(2)}, u32[]{:S(2)}) %collective-permute-start) | collective-permute-done | bytes 49184 | tf_op jit(solution)/shard_map/ppermute | solution.py:147
  75.6 1.0 %copy-done.2 = f32[1,4,256,192]{2,3,1,0:T(8,128)S(1)} copy-done((f32[1,4,256,192]{2,3,1,0:T(8,128)S(1)}, f32[1,4,256,192]{2,3,1,0:T(8,128)}, u32[]{:S(2)}) %copy-start.2) | copy-done | bytes 786456
  76.8 4.2 %fusion.2 = f32[2,4,256,192]{2,3,0,1:T(8,128)S(1)} fusion(f32[4,256]{1,0:T(4,128)S(1)} %get-tuple-element.32, s32[4,256]{1,0:T(4,128)S(1)} %get-tuple-element.46, f32[4,256]{1,0:T(4,128)S(1)} %copy-done.9, s32[4,256]{1,0:T(4,128)S(1)} %get-tuple-element.42, f32[4,256]{1,0:T(4,128)S(1)} %copy-done.10, s32[4,256]{1,0:T(4,128)S(1)} %get-tuple-element.43, ...), kind=kOutput, calls=%fused_computation.7 | convolution fusion | flops 1291116544 | bytes 3309568 | tf_op jit(solution)/shard_map/sij,csja->csia/dot_general | solution.py:170
  81.0 1.2 %copy.39 = f32[2,4,256,192]{2,3,1,0:T(8,128)} copy(f32[2,4,256,192]{2,3,0,1:T(8,128)S(1)} %fusion.2) | data formatting | bytes 3145728 | tf_op jit(solution)/shard_map/sij,csja->csia/transpose | solution.py:170
  (75 shorter events, 8.4 us)
Async XLA Ops:
  8.7 1.1 %copy-start = (f32[128,1536]{0,1:S(1)}, f32[128,1536]{0,1}, u32[]{:S(2)}) copy-start(f32[128,1536]{0,1} %fusion.109) | copy-start | bytes 2359300
  15.5 7.5 %copy-start.7 = (f32[4,256]{1,0:T(4,128)S(1)}, f32[4,256]{1,0:T(4,128)}, u32[]{:S(2)}) copy-start(f32[4,256]{1,0:T(4,128)} %param.8) | copy-start | bytes 12292
  15.5 7.5 %copy-start.15 = (f32[192]{0:T(256)S(1)}, f32[192]{0:T(256)}, u32[]{:S(2)}) copy-start(f32[192]{0:T(256)} %param.9) | copy-start | bytes 2308
  15.5 44.8 %all-to-all-start = ((f32[32,2,24,256]{3,2,1,0:T(8,128)}), f32[32,2,24,256]{3,2,1,0:T(8,128)S(1)}, u32[]{:S(2)}, u32[]{:S(2)}) async-start(f32[32,2,24,256]{3,2,1,0:T(8,128)} %maximum_bitcast_fusion), calls=%async_computation | async-start | bytes 3145728 | tf_op jit(solution)/shard_map/all_to_all | solution.py:103
  23.0 3.1 %copy-start.8 = (s32[4,256]{1,0:T(4,128)S(1)}, s32[4,256]{1,0:T(4,128)}, u32[]{:S(2)}) copy-start(s32[4,256]{1,0:T(4,128)} %param.10) | copy-start | bytes 12292
  23.0 3.2 %copy-start.6 = (f32[8,4,256]{2,1,0:T(4,128)S(1)}, f32[8,4,256]{2,1,0:T(4,128)}, u32[]{:S(2)}) copy-start(f32[8,4,256]{2,1,0:T(4,128)} %param.11) | copy-start | bytes 98308
  23.0 3.8 %copy-start.16 = (s32[192]{0:T(256)S(1)}, s32[192]{0:T(256)}, u32[]{:S(2)}) copy-start(s32[192]{0:T(256)} %param.7) | copy-start | bytes 2308
  61.0 0.9 %copy-start.5 = (f32[192,192]{1,0:T(8,128)S(1)}, f32[192,192]{1,0:T(8,128)}, u32[]{:S(2)}) copy-start(f32[192,192]{1,0:T(8,128)} %get-tuple-element.47) | copy-start | bytes 442372
  65.2 0.9 %copy-start.1 = (f32[1,4,256,192]{2,3,1,0:T(8,128)}, f32[1,4,256,192]{2,3,1,0:T(8,128)S(1)}, u32[]{:S(2)}) copy-start(f32[1,4,256,192]{2,3,1,0:T(8,128)S(1)} %get-tuple-element.13) | copy-start | bytes 2359300
  65.2 1.1 %copy-start.3 = (f32[1,4,256,192]{2,3,1,0:T(8,128)}, f32[1,4,256,192]{2,3,1,0:T(8,128)S(1)}, u32[]{:S(2)}) copy-start(f32[1,4,256,192]{2,3,1,0:T(8,128)S(1)} %get-tuple-element.14) | copy-start | bytes 2359300
  66.7 7.3 %collective-permute-start = (f32[2,4,8,192]{3,2,1,0:T(8,128)S(1)}, f32[2,4,8,192]{3,2,1,0:T(8,128)S(1)}, u32[]{:S(2)}, u32[]{:S(2)}) collective-permute-start(f32[2,4,8,192]{3,2,1,0:T(8,128)S(1)} %copy.32), channel_id=1, source_target_pairs={{0,1},{1,2},{2,3},{3,4},{4,5},{5,6},{6,7},{7,8},{8,9},{9,10},{10,1... | collective-permute-start | bytes 147464 | tf_op jit(solution)/shard_map/ppermute | solution.py:147
  67.0 7.5 %collective-permute-start.1 = (f32[2,4,8,192]{3,2,1,0:T(8,128)S(1)}, f32[2,4,8,192]{3,2,1,0:T(8,128)S(1)}, u32[]{:S(2)}, u32[]{:S(2)}) collective-permute-start(f32[2,4,8,192]{3,2,1,0:T(8,128)S(1)} %copy.35), channel_id=1, source_target_pairs={{1,0},{2,1},{3,2},{4,3},{5,4},{6,5},{7,6},{8,7},{9,8},{10,9},{11,1... | collective-permute-start | bytes 147464 | tf_op jit(solution)/shard_map/ppermute | solution.py:148
  75.4 1.1 %copy-start.2 = (f32[1,4,256,192]{2,3,1,0:T(8,128)S(1)}, f32[1,4,256,192]{2,3,1,0:T(8,128)}, u32[]{:S(2)}) copy-start(f32[1,4,256,192]{2,3,1,0:T(8,128)} %copy-done.1) | copy-start | bytes 2359300
  75.4 1.4 %copy-start.4 = (f32[1,4,256,192]{2,3,1,0:T(8,128)S(1)}, f32[1,4,256,192]{2,3,1,0:T(8,128)}, u32[]{:S(2)}) copy-start(f32[1,4,256,192]{2,3,1,0:T(8,128)} %copy-done.3) | copy-start | bytes 2359300
  75.4 1.4 %copy-start.9 = (f32[4,256]{1,0:T(4,128)S(1)}, f32[4,256]{1,0:T(4,128)}, u32[]{:S(2)}) copy-start(f32[4,256]{1,0:T(4,128)} %get-tuple-element.33) | copy-start | bytes 12292
  75.5 1.4 %copy-start.10 = (f32[4,256]{1,0:T(4,128)S(1)}, f32[4,256]{1,0:T(4,128)}, u32[]{:S(2)}) copy-start(f32[4,256]{1,0:T(4,128)} %get-tuple-element.34) | copy-start | bytes 12292
  75.5 1.3 %copy-start.11 = (f32[4,256]{1,0:T(4,128)S(1)}, f32[4,256]{1,0:T(4,128)}, u32[]{:S(2)}) copy-start(f32[4,256]{1,0:T(4,128)} %get-tuple-element.35) | copy-start | bytes 12292
  75.5 1.3 %copy-start.12 = (f32[4,256]{1,0:T(4,128)S(1)}, f32[4,256]{1,0:T(4,128)}, u32[]{:S(2)}) copy-start(f32[4,256]{1,0:T(4,128)} %get-tuple-element.36) | copy-start | bytes 12292
  75.5 1.3 %copy-start.13 = (f32[4,256]{1,0:T(4,128)S(1)}, f32[4,256]{1,0:T(4,128)}, u32[]{:S(2)}) copy-start(f32[4,256]{1,0:T(4,128)} %get-tuple-element.37) | copy-start | bytes 12292
  75.5 1.3 %copy-start.14 = (f32[4,256]{1,0:T(4,128)S(1)}, f32[4,256]{1,0:T(4,128)}, u32[]{:S(2)}) copy-start(f32[4,256]{1,0:T(4,128)} %get-tuple-element.38) | copy-start | bytes 12292

commit v5 on v4

--- a/solution.py
+++ b/solution.py
@@ -7,6 +7,7 @@
 
 phase_scale = 24.0
 highest = lax.Precision.HIGHEST
+fast = lax.Precision.HIGH
 RIM = 8
 
 
@@ -27,7 +28,7 @@
 def complex_einsum(pattern, real_part, imag_part, table_real, table_imag):
 
     def contract(operand, matrix):
-        return jnp.einsum(pattern, operand, matrix, precision=lax.Precision.HIGH)
+        return jnp.einsum(pattern, operand, matrix, precision=fast)
 
     return (
         contract(real_part, table_real) - contract(imag_part, table_imag),
@@ -128,8 +129,8 @@
     combined = combined.reshape(lane_count, 2 * total_rows, block_len)
 
     fold = azimuth_matrix(row_list, 1.0 / math.sqrt(range_len * total_rows))
-    az_real = jnp.einsum("ay,syq->sqa", fold[:total_rows], combined, precision=highest)
-    az_imag = jnp.einsum("ay,syq->sqa", fold[total_rows:], combined, precision=highest)
+    az_real = jnp.einsum("ay,syq->sqa", fold[:total_rows], combined, precision=fast)
+    az_imag = jnp.einsum("ay,syq->sqa", fold[total_rows:], combined, precision=fast)
 
     phase_angle = phase_scale * jnp.sqrt(
         wavenumber[:, :, None] ** 2 - az_wavenumber[None, None, :] ** 2
@@ -167,7 +168,7 @@
     for t in range(tap_count):
         band = band + jnp.where(columns[None, None, :] == target + t, weights[t][:, :, None], 0.0)
 
-    return jnp.einsum("sij,csja->csia", band, widened, precision=highest)
+    return jnp.einsum("sij,csja->csia", band, widened, precision=fast)
 
 
 def solution(mesh):

time: 82.7 us -> 80 us (0.967)
  matrix products: 17.2 us -> 14.5 us
    dot_general x7, matrix products: 9.86 us -> 7.18 us  [the longest x1 2.91 us: on_device(): return jnp.einsum('sij,csja->csia', band, widened, precision=fast)]
where the time goes in v5:
time: 80 us; the launch traced here: 79.6 us
  waiting for transfers between devices  31.5 us (39%)
  matrix products  14.5 us (18%)
  local copies, waits for them, and re-layouts  13.1 us (16%)
  starting transfers between devices  13.1 us (16%)
  other arithmetic  6.88 us (9%)
    all_to_all x1, waiting for transfers between devices, on_device(): lax.all_to_all(spectrum, ('pulse', 'rng'), split_axis=0, concat_axis=0, t...  29.9 us
    all_to_all x1, starting transfers between devices, on_device(): lax.all_to_all(spectrum, ('pulse', 'rng'), split_axis=0, concat_axis=0, t...  7.48 us
    ppermute x1, starting transfers between devices, on_device(): right_rim = lax.ppermute(focused[:, :, :RIM], axes, down)  5.56 us
    unnamed x4, matrix products  3.78 us
    unnamed x36, local copies, waits for them, and re-layouts  3.3 us
    sin x1, other arithmetic, on_device(): jnp.sin(phase_angle)  3 us
    dot_general x1, matrix products, on_device(): return jnp.einsum('sij,csja->csia', band, widened, precision=fast)  2.91 us
    dot_general x1, matrix products, azimuth_matrix(): fold_imag = jnp.einsum('ji,ja->ai', select, dft_imag, precision=highest)  2.45 us
  transfers between devices with their start and end apart: 3, of which 3 were waited for; matrix products, arithmetic and copies ran while one was open for 10% of the time, Pallas kernels for 0%

profile of v5, /device:TPU:0, one launch (start us, length us, event | category | flops | bytes accessed | tf_op | source)
XLA Modules:
  0.0 79.6 jit_solution(2811685278652109317)
XLA Ops:
  0.0 2.4 %fusion.171 = (f32[1,24,8192]{2,1,0:T(8,128)S(1)}, f32[1,24,8192]{2,1,0:T(8,128)}) fusion(f32[2,24,8192]{2,1,0:T(8,128)} %param.6), kind=kLoop, calls=%fused_computation.240 | loop fusion | bytes 3145728 | tf_op jit(solution)/shard_map/slice | solution.py:89
  2.4 0.6 reshape_squeeze.7
  3.4 0.7 fusion.103
  4.2 1.6 %fusion.109 = f32[128,1536]{0,1} fusion(f32[128,1536]{0,1:T(8,128)S(1)} %bitcast.182), kind=kOutput, calls=%fused_computation.165 | convolution fusion | flops 151224320 | bytes 1572864
  5.8 1.8 %reshape_squeeze.6 = f32[24,128,64]{2,1,0:T(8,128)S(1)} reshape(f32[1,24,8192]{2,1,0:T(8,128)} %get-tuple-element.26) | data formatting | bytes 1572864 | tf_op jit(solution)/shard_map/reshape;squeeze | solution.py:43
  8.0 0.7 fusion.105
  8.7 0.7 fusion.107
  10.2 0.6 fusion.28
  13.3 1.0 %multiply_subtract_fusion = (f32[1,24,32,256]{3,1,0,2:T(8,128)S(1)}, f32[1,24,32,256]{3,1,0,2:T(8,128)S(1)}) fusion(f32[1,24,32,256]{3,2,1,0:T(8,128)S(1)} %reshape.507, f32[1,24,32,256]{3,2,1,0:T(8,128)S(1)} %reshape.506, f32[32,256]{1,0:T(8,128)S(1)} %get-tuple-element.51, f32[32,256]{1,0:T(8,128)S(1)} %get-tuple-element.52), kind=kLoop, calls=%fused_computation.54 | loop fusion | flops 1179648 | bytes 3211264 | tf_op jit(solution)/shard_map/sub | solution.py:98
  14.2 1.2 %maximum_bitcast_fusion = f32[32,2,24,256]{3,2,1,0:T(8,128)} fusion(f32[1,24,32,256]{3,1,0,2:T(8,128)S(1)} %get-tuple-element.16, f32[1,24,32,256]{3,1,0,2:T(8,128)S(1)} %get-tuple-element.15), kind=kLoop, calls=%fused_computation.3 | loop fusion | flops 393216 | bytes 3145728 | tf_op jit(solution)/shard_map/transpose | solution.py:103
  15.5 7.5 %all-to-all-start = ((f32[32,2,24,256]{3,2,1,0:T(8,128)}), f32[32,2,24,256]{3,2,1,0:T(8,128)S(1)}, u32[]{:S(2)}, u32[]{:S(2)}) async-start(f32[32,2,24,256]{3,2,1,0:T(8,128)} %maximum_bitcast_fusion), calls=%async_computation | async-start | bytes 3145728 | tf_op jit(solution)/shard_map/all_to_all | solution.py:104
  23.0 3.0 %fusion.30 = (f32[4,256,192]{1,2,0:T(8,128)S(1)}, f32[4,256,192]{1,2,0:T(8,128)S(1)}) fusion(f32[192]{0:T(256)S(1)} %integer_pow.9, f32[4,256]{1,0:T(4,128)S(1)} %integer_pow.8), kind=kLoop, calls=%fused_computation.51 | loop fusion | flops 393216 | bytes 1577728 | tf_op jit(solution)/shard_map/sin | solution.py:139
  26.2 0.6 slice_bitcast_fusion.15
  26.8 1.1 %fusion.60 = f32[192,192]{1,0:T(8,128)S(1)} fusion(s32[192]{0:T(256)S(1)} %copy-done.16), kind=kOutput, calls=%fused_computation.99 | convolution fusion | flops 85340160 | bytes 148224 | tf_op jit(solution)/shard_map/ji,ja->ai/dot_general | solution.py:70
  27.9 2.5 %fusion.172 = (f32[192,192]{1,0:T(8,128)}, f32[192,192]{1,0:T(8,128)S(1)}) fusion(s32[192]{0:T(256)} %param.7), kind=kOutput, calls=%fused_computation.241 | convolution fusion | flops 85377024 | bytes 295680 | tf_op jit(solution)/shard_map/ji,ja->ai/dot_general | solution.py:71
  30.4 29.9 %all-to-all-done = f32[32,2,24,256]{3,2,1,0:T(8,128)S(1)} async-done(((f32[32,2,24,256]{3,2,1,0:T(8,128)}), f32[32,2,24,256]{3,2,1,0:T(8,128)S(1)}, u32[]{:S(2)}, u32[]{:S(2)}) %all-to-all-start) | async-done | bytes 1572896 | tf_op jit(solution)/shard_map/all_to_all | solution.py:104
  61.2 0.8 %copy-done.5 = f32[192,192]{1,0:T(8,128)S(1)} copy-done((f32[192,192]{1,0:T(8,128)S(1)}, f32[192,192]{1,0:T(8,128)}, u32[]{:S(2)}) %copy-start.5) | copy-done | bytes 147480
  62.0 0.8 %fusion.49 = f32[4,256,192]{1,2,0:T(8,128)S(1)} fusion(f32[4,384,256]{2,1,0:T(8,128)S(1)} %bitcast.175, f32[192,192]{1,0:T(8,128)S(1)} %copy-done.5, f32[192,192]{1,0:T(8,128)S(1)} %fusion.60), kind=kOutput, calls=%fused_computation.78 | convolution fusion | flops 453058560 | bytes 2654208 | tf_op jit(solution)/shard_map/ay,syq->sqa/dot_general | solution.py:132
  62.8 1.0 %subtract_bitcast_fusion = (f32[1,4,256,192]{2,3,1,0:T(8,128)S(1)}, f32[1,4,256,192]{2,3,1,0:T(8,128)S(1)}) fusion(f32[4,256,192]{1,2,0:T(8,128)S(1)} %get-tuple-element.8, f32[4,256,192]{1,2,0:T(8,128)S(1)} %fusion.49, f32[4,256,192]{1,2,0:T(8,128)S(1)} %get-tuple-element.7, f32[4,384,256]{2,1,0:T(8,128)S(1)} %bitcast.176, f32[192,192]{1,0:T(8,128)S(1)} %fusion.60, ...), kind=kOutput, calls=%fused_computation.49 | convolution fusion | flops 454238208 | bytes 5799936 | tf_op jit(solution)/shard_map/ay,syq->sqa/dot_general | solution.py:133
  65.6 5.6 %collective-permute-start.1 = (f32[2,4,8,192]{3,2,1,0:T(8,128)S(1)}, f32[2,4,8,192]{3,2,1,0:T(8,128)S(1)}, u32[]{:S(2)}, u32[]{:S(2)}) collective-permute-start(f32[2,4,8,192]{3,2,1,0:T(8,128)S(1)} %copy.35), channel_id=1, source_target_pairs={{1,0},{2,1},{3,2},{4,3},{5,4},{6,5},{7,6},{8,7},{9,8},{10,9},{11,1... | collective-permute-start | bytes 147464 | tf_op jit(solution)/shard_map/ppermute | solution.py:149
  71.2 1.4 %collective-permute-done = f32[2,4,8,192]{3,2,1,0:T(8,128)S(1)} collective-permute-done((f32[2,4,8,192]{3,2,1,0:T(8,128)S(1)}, f32[2,4,8,192]{3,2,1,0:T(8,128)S(1)}, u32[]{:S(2)}, u32[]{:S(2)}) %collective-permute-start) | collective-permute-done | bytes 49184 | tf_op jit(solution)/shard_map/ppermute | solution.py:148
  74.2 1.0 %copy-done.2 = f32[1,4,256,192]{2,3,1,0:T(8,128)S(1)} copy-done((f32[1,4,256,192]{2,3,1,0:T(8,128)S(1)}, f32[1,4,256,192]{2,3,1,0:T(8,128)}, u32[]{:S(2)}) %copy-start.2) | copy-done | bytes 786456
  75.4 2.9 %fusion.2 = f32[2,4,256,192]{2,3,0,1:T(8,128)S(1)} fusion(f32[4,256]{1,0:T(4,128)S(1)} %get-tuple-element.32, s32[4,256]{1,0:T(4,128)S(1)} %get-tuple-element.46, f32[4,256]{1,0:T(4,128)S(1)} %copy-done.9, s32[4,256]{1,0:T(4,128)S(1)} %get-tuple-element.42, f32[4,256]{1,0:T(4,128)S(1)} %copy-done.10, s32[4,256]{1,0:T(4,128)S(1)} %get-tuple-element.43, ...), kind=kOutput, calls=%fused_computation.7 | convolution fusion | flops 649388032 | bytes 3309568 | tf_op jit(solution)/shard_map/sij,csja->csia/dot_general | solution.py:171
  78.4 1.2 %copy.39 = f32[2,4,256,192]{2,3,1,0:T(8,128)} copy(f32[2,4,256,192]{2,3,0,1:T(8,128)S(1)} %fusion.2) | data formatting | bytes 3145728 | tf_op jit(solution)/shard_map/sij,csja->csia/transpose | solution.py:171
  (75 shorter events, 8.4 us)
Async XLA Ops:
  8.7 1.1 %copy-start = (f32[128,1536]{0,1:S(1)}, f32[128,1536]{0,1}, u32[]{:S(2)}) copy-start(f32[128,1536]{0,1} %fusion.109) | copy-start | bytes 2359300
  15.5 7.5 %copy-start.7 = (f32[4,256]{1,0:T(4,128)S(1)}, f32[4,256]{1,0:T(4,128)}, u32[]{:S(2)}) copy-start(f32[4,256]{1,0:T(4,128)} %param.8) | copy-start | bytes 12292
  15.5 7.5 %copy-start.15 = (f32[192]{0:T(256)S(1)}, f32[192]{0:T(256)}, u32[]{:S(2)}) copy-start(f32[192]{0:T(256)} %param.9) | copy-start | bytes 2308
  15.5 44.8 %all-to-all-start = ((f32[32,2,24,256]{3,2,1,0:T(8,128)}), f32[32,2,24,256]{3,2,1,0:T(8,128)S(1)}, u32[]{:S(2)}, u32[]{:S(2)}) async-start(f32[32,2,24,256]{3,2,1,0:T(8,128)} %maximum_bitcast_fusion), calls=%async_computation | async-start | bytes 3145728 | tf_op jit(solution)/shard_map/all_to_all | solution.py:104
  23.0 3.1 %copy-start.8 = (s32[4,256]{1,0:T(4,128)S(1)}, s32[4,256]{1,0:T(4,128)}, u32[]{:S(2)}) copy-start(s32[4,256]{1,0:T(4,128)} %param.10) | copy-start | bytes 12292
  23.0 3.2 %copy-start.6 = (f32[8,4,256]{2,1,0:T(4,128)S(1)}, f32[8,4,256]{2,1,0:T(4,128)}, u32[]{:S(2)}) copy-start(f32[8,4,256]{2,1,0:T(4,128)} %param.11) | copy-start | bytes 98308
  23.0 3.8 %copy-start.16 = (s32[192]{0:T(256)S(1)}, s32[192]{0:T(256)}, u32[]{:S(2)}) copy-start(s32[192]{0:T(256)} %param.7) | copy-start | bytes 2308
  61.0 0.9 %copy-start.5 = (f32[192,192]{1,0:T(8,128)S(1)}, f32[192,192]{1,0:T(8,128)}, u32[]{:S(2)}) copy-start(f32[192,192]{1,0:T(8,128)} %get-tuple-element.47) | copy-start | bytes 442372
  63.8 0.9 %copy-start.1 = (f32[1,4,256,192]{2,3,1,0:T(8,128)}, f32[1,4,256,192]{2,3,1,0:T(8,128)S(1)}, u32[]{:S(2)}) copy-start(f32[1,4,256,192]{2,3,1,0:T(8,128)S(1)} %get-tuple-element.13) | copy-start | bytes 2359300
  63.8 1.1 %copy-start.3 = (f32[1,4,256,192]{2,3,1,0:T(8,128)}, f32[1,4,256,192]{2,3,1,0:T(8,128)S(1)}, u32[]{:S(2)}) copy-start(f32[1,4,256,192]{2,3,1,0:T(8,128)S(1)} %get-tuple-element.14) | copy-start | bytes 2359300
  65.3 7.3 %collective-permute-start = (f32[2,4,8,192]{3,2,1,0:T(8,128)S(1)}, f32[2,4,8,192]{3,2,1,0:T(8,128)S(1)}, u32[]{:S(2)}, u32[]{:S(2)}) collective-permute-start(f32[2,4,8,192]{3,2,1,0:T(8,128)S(1)} %copy.32), channel_id=1, source_target_pairs={{0,1},{1,2},{2,3},{3,4},{4,5},{5,6},{6,7},{7,8},{8,9},{9,10},{10,1... | collective-permute-start | bytes 147464 | tf_op jit(solution)/shard_map/ppermute | solution.py:148
  65.6 7.5 %collective-permute-start.1 = (f32[2,4,8,192]{3,2,1,0:T(8,128)S(1)}, f32[2,4,8,192]{3,2,1,0:T(8,128)S(1)}, u32[]{:S(2)}, u32[]{:S(2)}) collective-permute-start(f32[2,4,8,192]{3,2,1,0:T(8,128)S(1)} %copy.35), channel_id=1, source_target_pairs={{1,0},{2,1},{3,2},{4,3},{5,4},{6,5},{7,6},{8,7},{9,8},{10,9},{11,1... | collective-permute-start | bytes 147464 | tf_op jit(solution)/shard_map/ppermute | solution.py:149
  74.0 1.1 %copy-start.2 = (f32[1,4,256,192]{2,3,1,0:T(8,128)S(1)}, f32[1,4,256,192]{2,3,1,0:T(8,128)}, u32[]{:S(2)}) copy-start(f32[1,4,256,192]{2,3,1,0:T(8,128)} %copy-done.1) | copy-start | bytes 2359300
  74.0 1.4 %copy-start.4 = (f32[1,4,256,192]{2,3,1,0:T(8,128)S(1)}, f32[1,4,256,192]{2,3,1,0:T(8,128)}, u32[]{:S(2)}) copy-start(f32[1,4,256,192]{2,3,1,0:T(8,128)} %copy-done.3) | copy-start | bytes 2359300
  74.0 1.4 %copy-start.9 = (f32[4,256]{1,0:T(4,128)S(1)}, f32[4,256]{1,0:T(4,128)}, u32[]{:S(2)}) copy-start(f32[4,256]{1,0:T(4,128)} %get-tuple-element.33) | copy-start | bytes 12292
  74.1 1.4 %copy-start.10 = (f32[4,256]{1,0:T(4,128)S(1)}, f32[4,256]{1,0:T(4,128)}, u32[]{:S(2)}) copy-start(f32[4,256]{1,0:T(4,128)} %get-tuple-element.34) | copy-start | bytes 12292
  74.1 1.3 %copy-start.11 = (f32[4,256]{1,0:T(4,128)S(1)}, f32[4,256]{1,0:T(4,128)}, u32[]{:S(2)}) copy-start(f32[4,256]{1,0:T(4,128)} %get-tuple-element.35) | copy-start | bytes 12292
  74.1 1.3 %copy-start.12 = (f32[4,256]{1,0:T(4,128)S(1)}, f32[4,256]{1,0:T(4,128)}, u32[]{:S(2)}) copy-start(f32[4,256]{1,0:T(4,128)} %get-tuple-element.36) | copy-start | bytes 12292
  74.1 1.3 %copy-start.13 = (f32[4,256]{1,0:T(4,128)S(1)}, f32[4,256]{1,0:T(4,128)}, u32[]{:S(2)}) copy-start(f32[4,256]{1,0:T(4,128)} %get-tuple-element.37) | copy-start | bytes 12292
  74.1 1.3 %copy-start.14 = (f32[4,256]{1,0:T(4,128)S(1)}, f32[4,256]{1,0:T(4,128)}, u32[]{:S(2)}) copy-start(f32[4,256]{1,0:T(4,128)} %get-tuple-element.38) | copy-start | bytes 12292

commit v6 on v5

--- a/solution.py
+++ b/solution.py
@@ -60,6 +60,56 @@
         "...ua,va->...vu", real_part, imag_part, inner_real, inner_imag
     )
     return (real_part.reshape(leading + (length,)), imag_part.reshape(leading + (length,)))
+
+
+def stacked_table(length, factor):
+    table_real, table_imag = dft_table(length, factor)
+    top = jnp.stack([table_real, -table_imag], axis=1)
+    bottom = jnp.stack([table_imag, table_real], axis=1)
+    return jnp.stack([top, bottom])
+
+
+def range_dft_blocks(pair, device_count, block_len, lane_pos, range_len):
+    rows = pair.shape[1]
+    length = pair.shape[2]
+    inner_len = split_factor(length)
+    outer_len = length // inner_len
+    signal = pair.reshape(2, rows, outer_len, inner_len)
+    first = jnp.einsum("ducb,crba->drua", stacked_table(outer_len, 1.0), signal, precision=fast)
+    col_index = jnp.arange(outer_len, dtype=jnp.int32)[:, None]
+    row_index = jnp.arange(inner_len, dtype=jnp.int32)[None, :]
+    twist_angle = (col_index * row_index % length).astype(jnp.float32) * (-2.0 * math.pi / length)
+    twist_real = jnp.cos(twist_angle)
+    twist_imag = jnp.sin(twist_angle)
+    first = jnp.stack(
+        [
+            first[0] * twist_real - first[1] * twist_imag,
+            first[0] * twist_imag + first[1] * twist_real,
+        ]
+    )
+    second = jnp.einsum("dvca,crua->vdru", stacked_table(inner_len, 1.0), first, precision=fast)
+    q_index = jnp.arange(inner_len, dtype=jnp.int32)[:, None] * outer_len + jnp.arange(
+        outer_len, dtype=jnp.int32
+    )[None, :]
+    turn_angle = ((lane_pos * q_index) % range_len).astype(jnp.float32) * (
+        -2.0 * math.pi / range_len
+    )
+    turn_real = jnp.cos(turn_angle)[:, None, :]
+    turn_imag = jnp.sin(turn_angle)[:, None, :]
+    second = jnp.stack(
+        [
+            second[:, 0] * turn_real - second[:, 1] * turn_imag,
+            second[:, 0] * turn_imag + second[:, 1] * turn_real,
+        ],
+        axis=1,
+    )
+    if block_len % outer_len == 0:
+        per_block = block_len // outer_len
+        second = second.reshape(device_count, per_block, 2, rows, outer_len)
+        second = jnp.transpose(second, (0, 2, 3, 1, 4))
+        return second.reshape(device_count, 2, rows, block_len)
+    second = jnp.transpose(second, (1, 2, 0, 3)).reshape(2, rows, device_count, block_len)
+    return jnp.transpose(second, (2, 0, 1, 3))
 
 
 def azimuth_matrix(row_list, scale):
@@ -86,21 +136,7 @@
     position = lax.axis_index(("pulse", "rng"))
     lane_pos = lax.axis_index("rng")
 
-    real_part, imag_part = last_axis_dft(echoes[0], echoes[1], span_len, 1.0)
-    q_index = jnp.arange(span_len, dtype=jnp.int32)
-    twist_angle = ((lane_pos * q_index) % range_len).astype(jnp.float32) * (
-        -2.0 * math.pi / range_len
-    )
-    twist_real = jnp.cos(twist_angle)[None, :]
-    twist_imag = jnp.sin(twist_angle)[None, :]
-    spectrum = jnp.stack(
-        [
-            real_part * twist_real - imag_part * twist_imag,
-            real_part * twist_imag + imag_part * twist_real,
-        ]
-    )
-    spectrum = spectrum.reshape(2, rows_here, device_count, block_len)
-    spectrum = jnp.transpose(spectrum, (2, 0, 1, 3))
+    spectrum = range_dft_blocks(echoes, device_count, block_len, lane_pos, range_len)
     spectrum = lax.all_to_all(
         spectrum, ("pulse", "rng"), split_axis=0, concat_axis=0, tiled=True
     )
@@ -168,7 +204,7 @@
     for t in range(tap_count):
         band = band + jnp.where(columns[None, None, :] == target + t, weights[t][:, :, None], 0.0)
 
-    return jnp.einsum("sij,csja->csia", band, widened, precision=fast)
+    return jnp.einsum("sij,csja->csia", band, widened, precision=highest)
 
 
 def solution(mesh):

time: 80 us -> 78.5 us (0.981)
  matrix products: 14.5 us -> 13.1 us
    reshape x2 -> x3, local copies, waits for them, and re-layouts: 0.44 us -> 5.73 us  [the longest x2 3.32 us: range_dft_blocks(): return second.reshape(device_count, 2, rows, block_len)]
    unnamed x4 -> x0, matrix products: 3.78 us -> none
    another operation x4 -> x1, local copies, waits for them, and re-layouts: 3.28 us -> 0.1 us  [on_device(): jnp.stack([jnp.stack(combined_real), jnp.stack(combined_imag)], axis=1)]
    slice x2 -> x0, local copies, waits for them, and re-layouts: 2.52 us -> none  [the longest x1 2.35 us: on_device(): real_part, imag_part = last_axis_dft(echoes[0], echoes[1], span_len, 1.0)]
    dot_general x5 -> x3, matrix products: 5.32 us -> 7.69 us  [the longest x1 4.2 us: on_device(): return jnp.einsum('sij,csja->csia', band, widened, precision=highest)]
    select_n x1, other arithmetic: 0.08 us -> 1 us  [on_device(): left_rim = jnp.where(position == 0, jnp.roll(left_rim, 1, axis=1), left_rim)]
    unnamed x36 -> x35, local copies, waits for them, and re-layouts: 3.3 us -> 3.04 us
where the time goes in v6:
time: 78.5 us; the launch traced here: 78.2 us
  waiting for transfers between devices  31.5 us (40%)
  matrix products  13.1 us (17%)
  starting transfers between devices  13.1 us (17%)
  local copies, waits for them, and re-layouts  12.6 us (16%)
  other arithmetic  7.44 us (9%)
    all_to_all x1, waiting for transfers between devices, on_device(): lax.all_to_all(spectrum, ('pulse', 'rng'), split_axis=0, concat_axis=0, t...  29.9 us
    all_to_all x1, starting transfers between devices, on_device(): lax.all_to_all(spectrum, ('pulse', 'rng'), split_axis=0, concat_axis=0, t...  7.48 us
    ppermute x1, starting transfers between devices, on_device(): right_rim = lax.ppermute(focused[:, :, :RIM], axes, down)  5.56 us
    dot_general x1, matrix products, on_device(): return jnp.einsum('sij,csja->csia', band, widened, precision=highest)  4.2 us
    reshape x2, local copies, waits for them, and re-layouts, range_dft_blocks(): return second.reshape(device_count, 2, rows, block_len)  3.32 us
    unnamed x35, local copies, waits for them, and re-layouts  3.04 us
    sin x1, other arithmetic, on_device(): jnp.sin(phase_angle)  3 us
    dot_general x1, matrix products, range_dft_blocks(): jnp.einsum('ducb,crba->drua', stacked_table(outer_len, 1.0), signal, prec...  2.66 us
  transfers between devices with their start and end apart: 3, of which 3 were waited for; matrix products, arithmetic and copies ran while one was open for 10% of the time, Pallas kernels for 0%

profile of v6, /device:TPU:0, one launch (start us, length us, event | category | flops | bytes accessed | tf_op | source)
XLA Modules:
  0.0 78.2 jit_solution(4451947089302544620)
XLA Ops:
  1.0 2.4 %reshape.590 = f32[2,24,128,64]{3,2,1,0:T(8,128)S(1)} reshape(f32[2,24,8192]{2,1,0:T(8,128)} %param.6) | data formatting | bytes 3145728 | tf_op jit(solution)/shard_map/reshape | solution.py:77
  3.7 2.7 %fusion.12 = f32[2,24,128,64]{2,3,1,0:T(8,128)S(1)} fusion(f32[2,24,128,64]{3,2,1,0:T(8,128)S(1)} %reshape.590, f32[1,128,2,128]{3,1,2,0:T(8,128)S(1)} %get-tuple-element.30, f32[1,128,2,128]{3,1,2,0:T(8,128)S(1)} %get-tuple-element.29), kind=kOutput, calls=%fused_computation.14 | convolution fusion | flops 604045312 | bytes 3407872 | tf_op jit(solution)/shard_map/ducb,crba->drua/dot_general | solution.py:78
  6.6 0.8 %fusion.6 = f32[64,2,24,128]{3,0,1,2:T(8,128)S(1)} fusion(f32[1,64,2,64]{3,1,2,0:T(8,128)S(1)} %get-tuple-element.40, f32[1,64,2,64]{3,1,2,0:T(8,128)S(1)} %get-tuple-element.39, f32[1,24,128,64]{2,3,1,0:T(8,128)S(1)} %get-tuple-element.16, f32[1,24,128,64]{2,3,1,0:T(8,128)S(1)} %get-tuple-element.15), kind=kOutput, calls=%fused_computation.12 | convolution fusion | flops 302399488 | bytes 3211264 | tf_op jit(solution)/shard_map/dvca,crua->vdru/dot_general | solution.py:90
  7.6 0.8 %maximum_bitcast_fusion.1 = f32[32,2,24,2,128]{4,3,0,2,1:T(2,128)S(1)} fusion(f32[32,2,1,24,128]{4,1,0,3,2:T(2,128)S(1)} %bitcast.185, f32[32,2,1,24,128]{4,1,0,3,2:T(2,128)S(1)} %bitcast.184), kind=kLoop, calls=%fused_computation.6 | loop fusion | flops 393216 | bytes 3145728 | tf_op jit(solution)/shard_map/transpose | solution.py:109
  8.5 1.3 %reshape.603 = f32[32,2,24,256]{3,0,2,1:T(8,128)S(1)} reshape(f32[32,2,24,2,128]{4,3,0,2,1:T(2,128)S(1)} %maximum_bitcast_fusion.1) | data formatting | bytes 3145728 | tf_op jit(solution)/shard_map/reshape | solution.py:110
  9.7 2.1 %copy.49 = f32[32,2,24,256]{3,2,1,0:T(8,128)} copy(f32[32,2,24,256]{3,0,2,1:T(8,128)S(1)} %reshape.603) | data formatting | bytes 3145728 | tf_op jit(solution)/shard_map/reshape | solution.py:110
  11.8 7.5 %all-to-all-start = ((f32[32,2,24,256]{3,2,1,0:T(8,128)}), f32[32,2,24,256]{3,2,1,0:T(8,128)S(1)}, u32[]{:S(2)}, u32[]{:S(2)}) async-start(f32[32,2,24,256]{3,2,1,0:T(8,128)} %copy.49), calls=%async_computation | async-start | bytes 3145728 | tf_op jit(solution)/shard_map/all_to_all | solution.py:140
  19.4 3.0 %fusion.32 = (f32[4,256,192]{1,2,0:T(8,128)S(1)}, f32[4,256,192]{1,2,0:T(8,128)S(1)}) fusion(f32[192]{0:T(256)S(1)} %integer_pow.9, f32[4,256]{1,0:T(4,128)S(1)} %integer_pow.8), kind=kLoop, calls=%fused_computation.48 | loop fusion | flops 393216 | bytes 1577728 | tf_op jit(solution)/shard_map/sin | solution.py:175
  22.5 0.6 slice_bitcast_fusion.16
  23.1 1.1 %fusion.66 = f32[192,192]{1,0:T(8,128)S(1)} fusion(s32[192]{0:T(256)S(1)} %copy-done.16), kind=kOutput, calls=%fused_computation.100 | convolution fusion | flops 85340160 | bytes 148224 | tf_op jit(solution)/shard_map/ji,ja->ai/dot_general | solution.py:120
  24.2 2.5 %fusion.134 = (f32[192,192]{1,0:T(8,128)}, f32[192,192]{1,0:T(8,128)S(1)}) fusion(s32[192]{0:T(256)} %param.7), kind=kOutput, calls=%fused_computation.212 | convolution fusion | flops 85377024 | bytes 295680 | tf_op jit(solution)/shard_map/ji,ja->ai/dot_general | solution.py:121
  26.7 29.9 %all-to-all-done = f32[32,2,24,256]{3,2,1,0:T(8,128)S(1)} async-done(((f32[32,2,24,256]{3,2,1,0:T(8,128)}), f32[32,2,24,256]{3,2,1,0:T(8,128)S(1)}, u32[]{:S(2)}, u32[]{:S(2)}) %all-to-all-start) | async-done | bytes 1572896 | tf_op jit(solution)/shard_map/all_to_all | solution.py:140
  57.5 0.8 %copy-done.5 = f32[192,192]{1,0:T(8,128)S(1)} copy-done((f32[192,192]{1,0:T(8,128)S(1)}, f32[192,192]{1,0:T(8,128)}, u32[]{:S(2)}) %copy-start.5) | copy-done | bytes 147480
  58.3 0.8 %fusion.51 = f32[4,256,192]{1,2,0:T(8,128)S(1)} fusion(f32[4,384,256]{2,1,0:T(8,128)S(1)} %bitcast.179, f32[192,192]{1,0:T(8,128)S(1)} %copy-done.5, f32[192,192]{1,0:T(8,128)S(1)} %fusion.66), kind=kOutput, calls=%fused_computation.75 | convolution fusion | flops 453058560 | bytes 2654208 | tf_op jit(solution)/shard_map/ay,syq->sqa/dot_general | solution.py:168
  59.2 1.0 %subtract_bitcast_fusion = (f32[1,4,256,192]{2,3,1,0:T(8,128)S(1)}, f32[1,4,256,192]{2,3,1,0:T(8,128)S(1)}) fusion(f32[4,256,192]{1,2,0:T(8,128)S(1)} %get-tuple-element.8, f32[4,256,192]{1,2,0:T(8,128)S(1)} %fusion.51, f32[4,256,192]{1,2,0:T(8,128)S(1)} %get-tuple-element.7, f32[4,384,256]{2,1,0:T(8,128)S(1)} %bitcast.180, f32[192,192]{1,0:T(8,128)S(1)} %fusion.66, ...), kind=kOutput, calls=%fused_computation.46 | convolution fusion | flops 454238208 | bytes 5799936 | tf_op jit(solution)/shard_map/ay,syq->sqa/dot_general | solution.py:169
  60.5 0.6 copy-done
  61.7 0.3 copy.33
  62.0 5.6 %collective-permute-start.1 = (f32[2,4,8,192]{3,2,1,0:T(8,128)S(1)}, f32[2,4,8,192]{3,2,1,0:T(8,128)S(1)}, u32[]{:S(2)}, u32[]{:S(2)}) collective-permute-start(f32[2,4,8,192]{3,2,1,0:T(8,128)S(1)} %copy.33), channel_id=1, source_target_pairs={{1,0},{2,1},{3,2},{4,3},{5,4},{6,5},{7,6},{8,7},{9,8},{10,9},{11,1... | collective-permute-start | bytes 147464 | tf_op jit(solution)/shard_map/ppermute | solution.py:185
  67.6 1.4 %collective-permute-done = f32[2,4,8,192]{3,2,1,0:T(8,128)S(1)} collective-permute-done((f32[2,4,8,192]{3,2,1,0:T(8,128)S(1)}, f32[2,4,8,192]{3,2,1,0:T(8,128)S(1)}, u32[]{:S(2)}, u32[]{:S(2)}) %collective-permute-start) | collective-permute-done | bytes 49184 | tf_op jit(solution)/shard_map/ppermute | solution.py:184
  70.0 1.0 %broadcast_select_fusion.1 = f32[2,4,8,192]{2,3,1,0:T(8,128)} fusion(f32[2,4,8,192]{2,3,1,0:T(8,128)S(1)} %copy.31, f32[2,4,8,192]{2,3,1,0:T(8,128)S(1)} %copy.32, pred[]{:T(512)S(6)} %eq.66), kind=kLoop, calls=%fused_computation.72 | loop fusion | flops 12288 | bytes 147457 | tf_op jit(solution)/shard_map/jit(_where)/select_n | solution.py:186
  71.5 0.7 copy-done.1
  72.4 0.3 copy-done.4
  72.8 4.2 %fusion.9 = f32[2,4,256,192]{2,3,0,1:T(8,128)S(1)} fusion(f32[4,256]{1,0:T(4,128)S(1)} %get-tuple-element.32, s32[4,256]{1,0:T(4,128)S(1)} %get-tuple-element.48, f32[4,256]{1,0:T(4,128)S(1)} %copy-done.9, s32[4,256]{1,0:T(4,128)S(1)} %get-tuple-element.44, f32[4,256]{1,0:T(4,128)S(1)} %copy-done.10, s32[4,256]{1,0:T(4,128)S(1)} %get-tuple-element.45, ...), kind=kOutput, calls=%fused_computation.13 | convolution fusion | flops 1291116544 | bytes 3309568 | tf_op jit(solution)/shard_map/sij,csja->csia/dot_general | solution.py:207
  77.0 1.2 %copy.37 = f32[2,4,256,192]{2,3,1,0:T(8,128)} copy(f32[2,4,256,192]{2,3,0,1:T(8,128)S(1)} %fusion.9) | data formatting | bytes 3145728 | tf_op jit(solution)/shard_map/sij,csja->csia/transpose | solution.py:207
  (72 shorter events, 5.1 us)
Async XLA Ops:
  11.8 7.5 %copy-start.7 = (f32[4,256]{1,0:T(4,128)S(1)}, f32[4,256]{1,0:T(4,128)}, u32[]{:S(2)}) copy-start(f32[4,256]{1,0:T(4,128)} %param.8) | copy-start | bytes 12292
  11.8 7.5 %copy-start.15 = (f32[192]{0:T(256)S(1)}, f32[192]{0:T(256)}, u32[]{:S(2)}) copy-start(f32[192]{0:T(256)} %param.9) | copy-start | bytes 2308
  11.8 44.8 %all-to-all-start = ((f32[32,2,24,256]{3,2,1,0:T(8,128)}), f32[32,2,24,256]{3,2,1,0:T(8,128)S(1)}, u32[]{:S(2)}, u32[]{:S(2)}) async-start(f32[32,2,24,256]{3,2,1,0:T(8,128)} %copy.49), calls=%async_computation | async-start | bytes 3145728 | tf_op jit(solution)/shard_map/all_to_all | solution.py:140
  19.3 3.1 %copy-start.8 = (s32[4,256]{1,0:T(4,128)S(1)}, s32[4,256]{1,0:T(4,128)}, u32[]{:S(2)}) copy-start(s32[4,256]{1,0:T(4,128)} %param.10) | copy-start | bytes 12292
  19.3 3.2 %copy-start.6 = (f32[8,4,256]{2,1,0:T(4,128)S(1)}, f32[8,4,256]{2,1,0:T(4,128)}, u32[]{:S(2)}) copy-start(f32[8,4,256]{2,1,0:T(4,128)} %param.11) | copy-start | bytes 98308
  19.3 3.8 %copy-start.16 = (s32[192]{0:T(256)S(1)}, s32[192]{0:T(256)}, u32[]{:S(2)}) copy-start(s32[192]{0:T(256)} %param.7) | copy-start | bytes 2308
  57.4 0.9 %copy-start.5 = (f32[192,192]{1,0:T(8,128)S(1)}, f32[192,192]{1,0:T(8,128)}, u32[]{:S(2)}) copy-start(f32[192,192]{1,0:T(8,128)} %get-tuple-element.51) | copy-start | bytes 442372
  60.2 0.9 %copy-start = (f32[1,4,256,192]{2,3,1,0:T(8,128)}, f32[1,4,256,192]{2,3,1,0:T(8,128)S(1)}, u32[]{:S(2)}) copy-start(f32[1,4,256,192]{2,3,1,0:T(8,128)S(1)} %get-tuple-element.11) | copy-start | bytes 2359300
  60.2 1.1 %copy-start.2 = (f32[1,4,256,192]{2,3,1,0:T(8,128)}, f32[1,4,256,192]{2,3,1,0:T(8,128)S(1)}, u32[]{:S(2)}) copy-start(f32[1,4,256,192]{2,3,1,0:T(8,128)S(1)} %get-tuple-element.12) | copy-start | bytes 2359300
  61.7 7.3 %collective-permute-start = (f32[2,4,8,192]{3,2,1,0:T(8,128)S(1)}, f32[2,4,8,192]{3,2,1,0:T(8,128)S(1)}, u32[]{:S(2)}, u32[]{:S(2)}) collective-permute-start(f32[2,4,8,192]{3,2,1,0:T(8,128)S(1)} %copy.30), channel_id=1, source_target_pairs={{0,1},{1,2},{2,3},{3,4},{4,5},{5,6},{6,7},{7,8},{8,9},{9,10},{10,1... | collective-permute-start | bytes 147464 | tf_op jit(solution)/shard_map/ppermute | solution.py:184
  62.0 7.5 %collective-permute-start.1 = (f32[2,4,8,192]{3,2,1,0:T(8,128)S(1)}, f32[2,4,8,192]{3,2,1,0:T(8,128)S(1)}, u32[]{:S(2)}, u32[]{:S(2)}) collective-permute-start(f32[2,4,8,192]{3,2,1,0:T(8,128)S(1)} %copy.33), channel_id=1, source_target_pairs={{1,0},{2,1},{3,2},{4,3},{5,4},{6,5},{7,6},{8,7},{9,8},{10,9},{11,1... | collective-permute-start | bytes 147464 | tf_op jit(solution)/shard_map/ppermute | solution.py:185
  71.0 1.1 %copy-start.1 = (f32[1,4,256,192]{2,3,1,0:T(8,128)S(1)}, f32[1,4,256,192]{2,3,1,0:T(8,128)}, u32[]{:S(2)}) copy-start(f32[1,4,256,192]{2,3,1,0:T(8,128)} %copy-done) | copy-start | bytes 2359300
  71.0 1.4 %copy-start.3 = (f32[1,4,256,192]{2,3,1,0:T(8,128)S(1)}, f32[1,4,256,192]{2,3,1,0:T(8,128)}, u32[]{:S(2)}) copy-start(f32[1,4,256,192]{2,3,1,0:T(8,128)} %copy-done.2) | copy-start | bytes 2359300
  71.0 1.4 %copy-start.9 = (f32[4,256]{1,0:T(4,128)S(1)}, f32[4,256]{1,0:T(4,128)}, u32[]{:S(2)}) copy-start(f32[4,256]{1,0:T(4,128)} %get-tuple-element.33) | copy-start | bytes 12292
  71.1 1.4 %copy-start.10 = (f32[4,256]{1,0:T(4,128)S(1)}, f32[4,256]{1,0:T(4,128)}, u32[]{:S(2)}) copy-start(f32[4,256]{1,0:T(4,128)} %get-tuple-element.34) | copy-start | bytes 12292
  71.1 1.4 %copy-start.11 = (f32[4,256]{1,0:T(4,128)S(1)}, f32[4,256]{1,0:T(4,128)}, u32[]{:S(2)}) copy-start(f32[4,256]{1,0:T(4,128)} %get-tuple-element.35) | copy-start | bytes 12292
  71.1 1.4 %copy-start.12 = (f32[4,256]{1,0:T(4,128)S(1)}, f32[4,256]{1,0:T(4,128)}, u32[]{:S(2)}) copy-start(f32[4,256]{1,0:T(4,128)} %get-tuple-element.36) | copy-start | bytes 12292
  71.1 1.4 %copy-start.13 = (f32[4,256]{1,0:T(4,128)S(1)}, f32[4,256]{1,0:T(4,128)}, u32[]{:S(2)}) copy-start(f32[4,256]{1,0:T(4,128)} %get-tuple-element.37) | copy-start | bytes 12292
  71.1 1.4 %copy-start.14 = (f32[4,256]{1,0:T(4,128)S(1)}, f32[4,256]{1,0:T(4,128)}, u32[]{:S(2)}) copy-start(f32[4,256]{1,0:T(4,128)} %get-tuple-element.38) | copy-start | bytes 12292
  71.4 1.4 %copy-start.4 = (f32[2,4,8,192]{2,3,1,0:T(8,128)S(1)}, f32[2,4,8,192]{2,3,1,0:T(8,128)}, u32[]{:S(2)}) copy-start(f32[2,4,8,192]{2,3,1,0:T(8,128)} %broadcast_select_fusion.1) | copy-start | bytes 147460

commit v7 on v6

--- a/solution.py
+++ b/solution.py
@@ -72,8 +72,8 @@
 def range_dft_blocks(pair, device_count, block_len, lane_pos, range_len):
     rows = pair.shape[1]
     length = pair.shape[2]
-    inner_len = split_factor(length)
-    outer_len = length // inner_len
+    outer_len = split_factor(length)
+    inner_len = length // outer_len
     signal = pair.reshape(2, rows, outer_len, inner_len)
     first = jnp.einsum("ducb,crba->drua", stacked_table(outer_len, 1.0), signal, precision=fast)
     col_index = jnp.arange(outer_len, dtype=jnp.int32)[:, None]

time: 78.5 us -> 78.9 us (level)
  local copies, waits for them, and re-layouts: 12.6 us -> 14.4 us
  matrix products: 13.1 us -> 11.3 us
    reshape x1 -> x0, local copies, waits for them, and re-layouts: 2.41 us -> none  [range_dft_blocks(): signal = pair.reshape(2, rows, outer_len, inner_len)]
    dot_general x1, matrix products: 2.66 us -> 0.89 us  [range_dft_blocks(): jnp.einsum('ducb,crba->drua', stacked_table(outer_len, 1.0), signal, prec...]
    unnamed x35 -> x36, local copies, waits for them, and re-layouts: 3.04 us -> 4.72 us
    add x0 -> x1, local copies, waits for them, and re-layouts: none -> 1.67 us  [range_dft_blocks(): second[:, 0] * turn_imag + second[:, 1] * turn_real]
    transpose x0 -> x1, local copies, waits for them, and re-layouts: none -> 0.95 us  [range_dft_blocks(): second = jnp.transpose(second, (0, 2, 3, 1, 4))]
    sub x1, other arithmetic: 0.22 us -> 1.12 us  [range_dft_blocks(): second[:, 0] * turn_real - second[:, 1] * turn_imag]
    reshape x2 -> x1, local copies, waits for them, and re-layouts: 3.32 us -> 2.65 us  [range_dft_blocks(): return second.reshape(device_count, 2, rows, block_len)]
where the time goes in v7:
time: 78.9 us; the launch traced here: 78.6 us
  waiting for transfers between devices  31.5 us (40%)
  local copies, waits for them, and re-layouts  14.4 us (18%)
  starting transfers between devices  13.1 us (17%)
  matrix products  11.3 us (14%)
  other arithmetic  7.79 us (10%)
    all_to_all x1, waiting for transfers between devices, on_device(): lax.all_to_all(spectrum, ('pulse', 'rng'), split_axis=0, concat_axis=0, t...  29.9 us
    all_to_all x1, starting transfers between devices, on_device(): lax.all_to_all(spectrum, ('pulse', 'rng'), split_axis=0, concat_axis=0, t...  7.48 us
    ppermute x1, starting transfers between devices, on_device(): right_rim = lax.ppermute(focused[:, :, :RIM], axes, down)  5.56 us
    unnamed x36, local copies, waits for them, and re-layouts  4.72 us
    dot_general x1, matrix products, on_device(): return jnp.einsum('sij,csja->csia', band, widened, precision=highest)  4.2 us
    sin x1, other arithmetic, on_device(): jnp.sin(phase_angle)  3 us
    reshape x1, local copies, waits for them, and re-layouts, range_dft_blocks(): return second.reshape(device_count, 2, rows, block_len)  2.65 us
    dot_general x1, matrix products, azimuth_matrix(): fold_imag = jnp.einsum('ji,ja->ai', select, dft_imag, precision=highest)  2.45 us
  transfers between devices with their start and end apart: 3, of which 3 were waited for; matrix products, arithmetic and copies ran while one was open for 10% of the time, Pallas kernels for 0%

profile of v7, /device:TPU:0, one launch (start us, length us, event | category | flops | bytes accessed | tf_op | source)
XLA Modules:
  0.0 78.6 jit_solution(13840870001438618052)
XLA Ops:
  1.0 1.7 %copy.55 = f32[6,8,64,128]{3,2,1,0:T(8,128)S(1)} copy(f32[6,8,64,128]{3,1,2,0:T(8,128)} %bitcast.191) | data formatting | bytes 3145728
  2.9 0.9 %fusion.7 = f32[2,24,64,128]{3,2,1,0:T(8,128)S(1)} fusion(f32[1,64,2,64]{3,1,2,0:T(8,128)S(1)} %get-tuple-element.40, f32[1,64,2,64]{3,1,2,0:T(8,128)S(1)} %get-tuple-element.39, f32[2,24,64,128]{3,2,1,0:T(8,128)S(1)} %bitcast.188), kind=kOutput, calls=%fused_computation.13 | convolution fusion | flops 302006272 | bytes 3211264 | tf_op jit(solution)/shard_map/ducb,crba->drua/dot_general | solution.py:78
  4.1 0.8 %fusion.10 = f32[128,2,24,64]{0,3,1,2:T(8,128)S(1)} fusion(f32[1,128,2,128]{3,1,2,0:T(8,128)S(1)} %get-tuple-element.30, f32[1,128,2,128]{3,1,2,0:T(8,128)S(1)} %get-tuple-element.29, f32[1,24,64,128]{3,2,1,0:T(8,128)S(1)} %get-tuple-element.16, f32[1,24,64,128]{3,2,1,0:T(8,128)S(1)} %get-tuple-element.15), kind=kOutput, calls=%fused_computation.14 | convolution fusion | flops 604438528 | bytes 3407872 | tf_op jit(solution)/shard_map/dvca,crua->vdru/dot_general | solution.py:90
  4.9 1.1 %multiply_subtract_fusion = (f32[128,1,24,64]{0,3,1,2:T(8,128)S(1)}, f32[128,1,24,64]{0,3,1,2:T(8,128)}) fusion(f32[128,2,24,64]{0,3,1,2:T(8,128)S(1)} %fusion.10, f32[128,64]{0,1:T(8,128)S(1)} %get-tuple-element.50, f32[128,64]{0,1:T(8,128)S(1)} %get-tuple-element.49), kind=kLoop, calls=%fused_computation.52 | loop fusion | flops 1179648 | bytes 3211264 | tf_op jit(solution)/shard_map/sub | solution.py:101
  6.0 0.5 copy.26
  6.6 1.7 %copy.27 = f32[128,1,24,64]{3,2,0,1:T(8,128)S(1)} copy(f32[128,1,24,64]{0,3,1,2:T(8,128)} %get-tuple-element.14) | data formatting | bytes 1572864 | tf_op jit(solution)/shard_map/add | solution.py:102
  8.6 1.0 %copy.28 = f32[32,2,24,4,64]{4,3,2,1,0:T(4,128)S(1)} copy(f32[32,2,24,4,64]{4,2,3,0,1:T(8,128)S(1)} %maximum_bitcast_fusion) | data formatting | bytes 3145728 | tf_op jit(solution)/shard_map/transpose | solution.py:109
  9.5 2.6 %reshape.591 = f32[32,2,24,256]{3,2,1,0:T(8,128)} reshape(f32[32,2,24,4,64]{4,3,2,1,0:T(4,128)S(1)} %copy.28) | data formatting | bytes 3145728 | tf_op jit(solution)/shard_map/reshape | solution.py:110
  12.2 7.5 %all-to-all-start = ((f32[32,2,24,256]{3,2,1,0:T(8,128)}), f32[32,2,24,256]{3,2,1,0:T(8,128)S(1)}, u32[]{:S(2)}, u32[]{:S(2)}) async-start(f32[32,2,24,256]{3,2,1,0:T(8,128)} %reshape.591), calls=%async_computation | async-start | bytes 3145728 | tf_op jit(solution)/shard_map/all_to_all | solution.py:140
  19.7 3.0 %fusion.33 = (f32[4,256,192]{1,2,0:T(8,128)S(1)}, f32[4,256,192]{1,2,0:T(8,128)S(1)}) fusion(f32[192]{0:T(256)S(1)} %integer_pow.9, f32[4,256]{1,0:T(4,128)S(1)} %integer_pow.8), kind=kLoop, calls=%fused_computation.49 | loop fusion | flops 393216 | bytes 1577728 | tf_op jit(solution)/shard_map/sin | solution.py:175
  22.9 0.6 slice_bitcast_fusion.16
  23.5 1.1 %fusion.65 = f32[192,192]{1,0:T(8,128)S(1)} fusion(s32[192]{0:T(256)S(1)} %copy-done.16), kind=kOutput, calls=%fused_computation.100 | convolution fusion | flops 85340160 | bytes 148224 | tf_op jit(solution)/shard_map/ji,ja->ai/dot_general | solution.py:120
  24.6 2.5 %fusion.133 = (f32[192,192]{1,0:T(8,128)}, f32[192,192]{1,0:T(8,128)S(1)}) fusion(s32[192]{0:T(256)} %param.7), kind=kOutput, calls=%fused_computation.212 | convolution fusion | flops 85377024 | bytes 295680 | tf_op jit(solution)/shard_map/ji,ja->ai/dot_general | solution.py:121
  27.1 29.9 %all-to-all-done = f32[32,2,24,256]{3,2,1,0:T(8,128)S(1)} async-done(((f32[32,2,24,256]{3,2,1,0:T(8,128)}), f32[32,2,24,256]{3,2,1,0:T(8,128)S(1)}, u32[]{:S(2)}, u32[]{:S(2)}) %all-to-all-start) | async-done | bytes 1572896 | tf_op jit(solution)/shard_map/all_to_all | solution.py:140
  57.9 0.8 %copy-done.5 = f32[192,192]{1,0:T(8,128)S(1)} copy-done((f32[192,192]{1,0:T(8,128)S(1)}, f32[192,192]{1,0:T(8,128)}, u32[]{:S(2)}) %copy-start.5) | copy-done | bytes 147480
  58.7 0.8 %fusion.52 = f32[4,256,192]{1,2,0:T(8,128)S(1)} fusion(f32[4,384,256]{2,1,0:T(8,128)S(1)} %bitcast.183, f32[192,192]{1,0:T(8,128)S(1)} %copy-done.5, f32[192,192]{1,0:T(8,128)S(1)} %fusion.65), kind=kOutput, calls=%fused_computation.76 | convolution fusion | flops 453058560 | bytes 2654208 | tf_op jit(solution)/shard_map/ay,syq->sqa/dot_general | solution.py:168
  59.6 1.0 %subtract_bitcast_fusion = (f32[1,4,256,192]{2,3,1,0:T(8,128)S(1)}, f32[1,4,256,192]{2,3,1,0:T(8,128)S(1)}) fusion(f32[4,256,192]{1,2,0:T(8,128)S(1)} %get-tuple-element.8, f32[4,256,192]{1,2,0:T(8,128)S(1)} %fusion.52, f32[4,256,192]{1,2,0:T(8,128)S(1)} %get-tuple-element.7, f32[4,384,256]{2,1,0:T(8,128)S(1)} %bitcast.184, f32[192,192]{1,0:T(8,128)S(1)} %fusion.65, ...), kind=kOutput, calls=%fused_computation.47 | convolution fusion | flops 454238208 | bytes 5799936 | tf_op jit(solution)/shard_map/ay,syq->sqa/dot_general | solution.py:169
  60.9 0.6 copy-done
  62.4 5.6 %collective-permute-start.1 = (f32[2,4,8,192]{3,2,1,0:T(8,128)S(1)}, f32[2,4,8,192]{3,2,1,0:T(8,128)S(1)}, u32[]{:S(2)}, u32[]{:S(2)}) collective-permute-start(f32[2,4,8,192]{3,2,1,0:T(8,128)S(1)} %copy.37), channel_id=1, source_target_pairs={{1,0},{2,1},{3,2},{4,3},{5,4},{6,5},{7,6},{8,7},{9,8},{10,9},{11,1... | collective-permute-start | bytes 147464 | tf_op jit(solution)/shard_map/ppermute | solution.py:185
  67.9 1.4 %collective-permute-done = f32[2,4,8,192]{3,2,1,0:T(8,128)S(1)} collective-permute-done((f32[2,4,8,192]{3,2,1,0:T(8,128)S(1)}, f32[2,4,8,192]{3,2,1,0:T(8,128)S(1)}, u32[]{:S(2)}, u32[]{:S(2)}) %collective-permute-start) | collective-permute-done | bytes 49184 | tf_op jit(solution)/shard_map/ppermute | solution.py:184
  70.4 1.0 %broadcast_select_fusion.1 = f32[2,4,8,192]{2,3,1,0:T(8,128)} fusion(f32[2,4,8,192]{2,3,1,0:T(8,128)S(1)} %copy.35, f32[2,4,8,192]{2,3,1,0:T(8,128)S(1)} %copy.36, pred[]{:T(512)S(6)} %eq.66), kind=kLoop, calls=%fused_computation.73 | loop fusion | flops 12288 | bytes 147457 | tf_op jit(solution)/shard_map/jit(_where)/select_n | solution.py:186
  71.8 0.7 copy-done.1
  73.1 4.2 %fusion.13 = f32[2,4,256,192]{2,3,0,1:T(8,128)S(1)} fusion(f32[4,256]{1,0:T(4,128)S(1)} %get-tuple-element.32, s32[4,256]{1,0:T(4,128)S(1)} %get-tuple-element.48, f32[4,256]{1,0:T(4,128)S(1)} %copy-done.9, s32[4,256]{1,0:T(4,128)S(1)} %get-tuple-element.44, f32[4,256]{1,0:T(4,128)S(1)} %copy-done.10, s32[4,256]{1,0:T(4,128)S(1)} %get-tuple-element.45, ...), kind=kOutput, calls=%fused_computation.15 | convolution fusion | flops 1291116544 | bytes 3309568 | tf_op jit(solution)/shard_map/sij,csja->csia/dot_general | solution.py:207
  77.3 1.2 %copy.41 = f32[2,4,256,192]{2,3,1,0:T(8,128)} copy(f32[2,4,256,192]{2,3,0,1:T(8,128)S(1)} %fusion.13) | data formatting | bytes 3145728 | tf_op jit(solution)/shard_map/sij,csja->csia/transpose | solution.py:207
  (74 shorter events, 5.8 us)
Async XLA Ops:
  12.2 7.5 %copy-start.7 = (f32[4,256]{1,0:T(4,128)S(1)}, f32[4,256]{1,0:T(4,128)}, u32[]{:S(2)}) copy-start(f32[4,256]{1,0:T(4,128)} %param.8) | copy-start | bytes 12292
  12.2 7.5 %copy-start.15 = (f32[192]{0:T(256)S(1)}, f32[192]{0:T(256)}, u32[]{:S(2)}) copy-start(f32[192]{0:T(256)} %param.9) | copy-start | bytes 2308
  12.2 44.8 %all-to-all-start = ((f32[32,2,24,256]{3,2,1,0:T(8,128)}), f32[32,2,24,256]{3,2,1,0:T(8,128)S(1)}, u32[]{:S(2)}, u32[]{:S(2)}) async-start(f32[32,2,24,256]{3,2,1,0:T(8,128)} %reshape.591), calls=%async_computation | async-start | bytes 3145728 | tf_op jit(solution)/shard_map/all_to_all | solution.py:140
  19.7 3.1 %copy-start.8 = (s32[4,256]{1,0:T(4,128)S(1)}, s32[4,256]{1,0:T(4,128)}, u32[]{:S(2)}) copy-start(s32[4,256]{1,0:T(4,128)} %param.10) | copy-start | bytes 12292
  19.7 3.2 %copy-start.6 = (f32[8,4,256]{2,1,0:T(4,128)S(1)}, f32[8,4,256]{2,1,0:T(4,128)}, u32[]{:S(2)}) copy-start(f32[8,4,256]{2,1,0:T(4,128)} %param.11) | copy-start | bytes 98308
  19.7 3.8 %copy-start.16 = (s32[192]{0:T(256)S(1)}, s32[192]{0:T(256)}, u32[]{:S(2)}) copy-start(s32[192]{0:T(256)} %param.7) | copy-start | bytes 2308
  57.8 0.9 %copy-start.5 = (f32[192,192]{1,0:T(8,128)S(1)}, f32[192,192]{1,0:T(8,128)}, u32[]{:S(2)}) copy-start(f32[192,192]{1,0:T(8,128)} %get-tuple-element.51) | copy-start | bytes 442372
  60.6 0.9 %copy-start = (f32[1,4,256,192]{2,3,1,0:T(8,128)}, f32[1,4,256,192]{2,3,1,0:T(8,128)S(1)}, u32[]{:S(2)}) copy-start(f32[1,4,256,192]{2,3,1,0:T(8,128)S(1)} %get-tuple-element.11) | copy-start | bytes 2359300
  60.6 1.1 %copy-start.2 = (f32[1,4,256,192]{2,3,1,0:T(8,128)}, f32[1,4,256,192]{2,3,1,0:T(8,128)S(1)}, u32[]{:S(2)}) copy-start(f32[1,4,256,192]{2,3,1,0:T(8,128)S(1)} %get-tuple-element.12) | copy-start | bytes 2359300
  62.0 7.3 %collective-permute-start = (f32[2,4,8,192]{3,2,1,0:T(8,128)S(1)}, f32[2,4,8,192]{3,2,1,0:T(8,128)S(1)}, u32[]{:S(2)}, u32[]{:S(2)}) collective-permute-start(f32[2,4,8,192]{3,2,1,0:T(8,128)S(1)} %copy.34), channel_id=1, source_target_pairs={{0,1},{1,2},{2,3},{3,4},{4,5},{5,6},{6,7},{7,8},{8,9},{9,10},{10,1... | collective-permute-start | bytes 147464 | tf_op jit(solution)/shard_map/ppermute | solution.py:184
  62.4 7.5 %collective-permute-start.1 = (f32[2,4,8,192]{3,2,1,0:T(8,128)S(1)}, f32[2,4,8,192]{3,2,1,0:T(8,128)S(1)}, u32[]{:S(2)}, u32[]{:S(2)}) collective-permute-start(f32[2,4,8,192]{3,2,1,0:T(8,128)S(1)} %copy.37), channel_id=1, source_target_pairs={{1,0},{2,1},{3,2},{4,3},{5,4},{6,5},{7,6},{8,7},{9,8},{10,9},{11,1... | collective-permute-start | bytes 147464 | tf_op jit(solution)/shard_map/ppermute | solution.py:185
  71.4 1.1 %copy-start.1 = (f32[1,4,256,192]{2,3,1,0:T(8,128)S(1)}, f32[1,4,256,192]{2,3,1,0:T(8,128)}, u32[]{:S(2)}) copy-start(f32[1,4,256,192]{2,3,1,0:T(8,128)} %copy-done) | copy-start | bytes 2359300
  71.4 1.4 %copy-start.3 = (f32[1,4,256,192]{2,3,1,0:T(8,128)S(1)}, f32[1,4,256,192]{2,3,1,0:T(8,128)}, u32[]{:S(2)}) copy-start(f32[1,4,256,192]{2,3,1,0:T(8,128)} %copy-done.2) | copy-start | bytes 2359300
  71.4 1.4 %copy-start.9 = (f32[4,256]{1,0:T(4,128)S(1)}, f32[4,256]{1,0:T(4,128)}, u32[]{:S(2)}) copy-start(f32[4,256]{1,0:T(4,128)} %get-tuple-element.33) | copy-start | bytes 12292
  71.4 1.4 %copy-start.10 = (f32[4,256]{1,0:T(4,128)S(1)}, f32[4,256]{1,0:T(4,128)}, u32[]{:S(2)}) copy-start(f32[4,256]{1,0:T(4,128)} %get-tuple-element.34) | copy-start | bytes 12292
  71.4 1.4 %copy-start.11 = (f32[4,256]{1,0:T(4,128)S(1)}, f32[4,256]{1,0:T(4,128)}, u32[]{:S(2)}) copy-start(f32[4,256]{1,0:T(4,128)} %get-tuple-element.35) | copy-start | bytes 12292
  71.4 1.4 %copy-start.12 = (f32[4,256]{1,0:T(4,128)S(1)}, f32[4,256]{1,0:T(4,128)}, u32[]{:S(2)}) copy-start(f32[4,256]{1,0:T(4,128)} %get-tuple-element.36) | copy-start | bytes 12292
  71.4 1.4 %copy-start.13 = (f32[4,256]{1,0:T(4,128)S(1)}, f32[4,256]{1,0:T(4,128)}, u32[]{:S(2)}) copy-start(f32[4,256]{1,0:T(4,128)} %get-tuple-element.37) | copy-start | bytes 12292
  71.4 1.4 %copy-start.14 = (f32[4,256]{1,0:T(4,128)S(1)}, f32[4,256]{1,0:T(4,128)}, u32[]{:S(2)}) copy-start(f32[4,256]{1,0:T(4,128)} %get-tuple-element.38) | copy-start | bytes 12292
  71.7 1.4 %copy-start.4 = (f32[2,4,8,192]{2,3,1,0:T(8,128)S(1)}, f32[2,4,8,192]{2,3,1,0:T(8,128)}, u32[]{:S(2)}) copy-start(f32[2,4,8,192]{2,3,1,0:T(8,128)} %broadcast_select_fusion.1) | copy-start | bytes 147460

commit v8 on v6

--- a/solution.py
+++ b/solution.py
@@ -137,9 +137,22 @@
     lane_pos = lax.axis_index("rng")
 
     spectrum = range_dft_blocks(echoes, device_count, block_len, lane_pos, range_len)
-    spectrum = lax.all_to_all(
-        spectrum, ("pulse", "rng"), split_axis=0, concat_axis=0, tiled=True
-    )
+    if device_count <= 32:
+        axes = ("pulse", "rng")
+        received = [spectrum[position]]
+        for shift in range(1, device_count):
+            outgoing = lax.dynamic_index_in_dim(
+                spectrum, (position + shift) % device_count, axis=0, keepdims=False
+            )
+            pairs = [(i, (i + shift) % device_count) for i in range(device_count)]
+            received.append(lax.ppermute(outgoing, axes, pairs))
+        received = jnp.stack(received)
+        source_order = (position - jnp.arange(device_count, dtype=jnp.int32)) % device_count
+        spectrum = jnp.take(received, source_order, axis=0)
+    else:
+        spectrum = lax.all_to_all(
+            spectrum, ("pulse", "rng"), split_axis=0, concat_axis=0, tiled=True
+        )
     spectrum = spectrum.reshape(pulse_count, lane_count, 2, rows_here, block_len)
 
     lane_real = spectrum[:, :, 0]

time: 78.5 us -> 128 us (1.63)
  starting transfers between devices: 13.1 us -> 59.7 us
  waiting for transfers between devices: 31.5 us -> 1.7 us
  local copies, waits for them, and re-layouts: 12.6 us -> 42.1 us
  other arithmetic: 7.44 us -> 10.7 us
    ppermute x0 -> x31, starting transfers between devices: none -> 54.3 us  [on_device(): received.append(lax.ppermute(outgoing, axes, pairs))]
    all_to_all x1 -> x0, waiting for transfers between devices: 29.9 us -> none  [on_device(): lax.all_to_all(spectrum, ('pulse', 'rng'), split_axis=0, concat_axis=0, t...]
    unnamed x35 -> x121, local copies, waits for them, and re-layouts: 3.04 us -> 29.6 us
    all_to_all x1 -> x0, starting transfers between devices: 7.48 us -> none  [on_device(): lax.all_to_all(spectrum, ('pulse', 'rng'), split_axis=0, concat_axis=0, t...]
    dynamic_slice x0 -> x2, local copies, waits for them, and re-layouts: none -> 2.37 us  [on_device(): lax.dynamic_index_in_dim(spectrum, (position + shift) % device_count, axi...]
    reshape x2 -> x1, local copies, waits for them, and re-layouts: 3.32 us -> 1.26 us  [range_dft_blocks(): return second.reshape(device_count, 2, rows, block_len)]
    gather x0 -> x1, local copies, waits for them, and re-layouts: none -> 2.05 us  [on_device(): spectrum = jnp.take(received, source_order, axis=0)]
  transfers between devices with their start and end apart: 3 -> 33, of which waited for: 3 -> 1; matrix products, arithmetic and copies ran while one was open for 10% -> 29% of each run, Pallas kernels for 0% -> 0%
where the time goes in v8:
time: 128 us
  starting transfers between devices  59.7 us (47%)
  local copies, waits for them, and re-layouts  42.1 us (33%)
  matrix products  12.4 us (10%)
  other arithmetic  10.7 us (8%)
  waiting for transfers between devices  1.7 us (1%)
    ppermute x31, starting transfers between devices, on_device(): received.append(lax.ppermute(outgoing, axes, pairs))  54.3 us
    unnamed x121, local copies, waits for them, and re-layouts  29.6 us
    ppermute x1, starting transfers between devices, on_device(): right_rim = lax.ppermute(focused[:, :, :RIM], axes, down)  5.34 us
    dot_general x1, matrix products, on_device(): return jnp.einsum('sij,csja->csia', band, widened, precision=highest)  4.2 us
    sin x1, other arithmetic, on_device(): jnp.sin(phase_angle)  3.74 us
    dot_general x1, matrix products, range_dft_blocks(): jnp.einsum('ducb,crba->drua', stacked_table(outer_len, 1.0), signal, prec...  2.66 us
  transfers between devices with their start and end apart: 33, of which 1 were waited for; matrix products, arithmetic and copies ran while one was open for 29% of the time, Pallas kernels for 0%

profile of v8, /device:TPU:0, one launch (start us, length us, event | category | flops | bytes accessed | tf_op | source)
XLA Modules:
  0.0 127.5 jit_solution(3346803487500783553)
XLA Ops:
  1.0 2.4 %reshape.645 = f32[2,24,128,64]{3,2,1,0:T(8,128)S(1)} reshape(f32[2,24,8192]{2,1,0:T(8,128)} %param.6) | data formatting | bytes 3145728 | tf_op jit(solution)/shard_map/reshape | solution.py:77
  3.7 2.7 %fusion.12 = f32[2,24,128,64]{2,3,1,0:T(8,128)S(1)} fusion(f32[2,24,128,64]{3,2,1,0:T(8,128)S(1)} %reshape.645, f32[1,128,2,128]{3,1,2,0:T(8,128)S(1)} %get-tuple-element.62, f32[1,128,2,128]{3,1,2,0:T(8,128)S(1)} %get-tuple-element.61), kind=kOutput, calls=%fused_computation.15 | convolution fusion | flops 604045312 | bytes 3407872 | tf_op jit(solution)/shard_map/ducb,crba->drua/dot_general | solution.py:78
  12.9 2.5 %collective-permute-start.1 = (f32[2,24,256]{2,1,0:T(8,128)}, f32[2,24,256]{2,1,0:T(8,128)}, u32[]{:S(2)}, u32[]{:S(2)}) collective-permute-start(f32[2,24,256]{2,1,0:T(8,128)} %bitcast.334), channel_id=1, source_target_pairs={{0,2},{1,3},{2,4},{3,5},{4,6},{5,7},{6,8},{7,9},{8,10},{9,11},{10,... | collective-permute-start | bytes 147464 | tf_op jit(solution)/shard_map/ppermute | solution.py:148
  16.1 2.4 %collective-permute-start.2 = (f32[2,24,256]{2,1,0:T(8,128)}, f32[2,24,256]{2,1,0:T(8,128)}, u32[]{:S(2)}, u32[]{:S(2)}) collective-permute-start(f32[2,24,256]{2,1,0:T(8,128)} %bitcast.333), channel_id=1, source_target_pairs={{0,3},{1,4},{2,5},{3,6},{4,7},{5,8},{6,9},{7,10},{8,11},{9,12},{10... | collective-permute-start | bytes 147464 | tf_op jit(solution)/shard_map/ppermute | solution.py:148
  21.3 1.8 %fusion.137 = (f32[192,192]{1,0:T(8,128)}, f32[192,192]{1,0:T(8,128)S(1)}) fusion(s32[192]{0:T(256)S(1)} %copy-done.28), kind=kOutput, calls=%fused_computation.322 | convolution fusion | flops 85377024 | bytes 295680 | tf_op jit(solution)/shard_map/ji,ja->ai/dot_general | solution.py:121
  27.2 3.7 %fusion.32 = (f32[4,256,192]{1,2,0:T(8,128)S(1)}, f32[4,256,192]{1,2,0:T(8,128)S(1)}) fusion(f32[192]{0:T(256)} %integer_pow.9, f32[4,256]{1,0:T(4,128)S(1)} %integer_pow.8), kind=kLoop, calls=%fused_computation.49 | loop fusion | flops 393216 | bytes 1577728 | tf_op jit(solution)/shard_map/sin | solution.py:188
  33.1 2.5 %collective-permute-start.5 = (f32[2,24,256]{2,1,0:T(8,128)S(1)}, f32[2,24,256]{2,1,0:T(8,128)S(1)}, u32[]{:S(2)}, u32[]{:S(2)}) collective-permute-start(f32[2,24,256]{2,1,0:T(8,128)S(1)} %bitcast.368), channel_id=1, source_target_pairs={{0,6},{1,7},{2,8},{3,9},{4,10},{5,11},{6,12},{7,13},{8,14},{9,15},... | collective-permute-start | bytes 147464 | tf_op jit(solution)/shard_map/ppermute | solution.py:148
  37.0 3.4 %collective-permute-start.6 = (f32[2,24,256]{2,1,0:T(8,128)S(1)}, f32[2,24,256]{2,1,0:T(8,128)S(1)}, u32[]{:S(2)}, u32[]{:S(2)}) collective-permute-start(f32[2,24,256]{2,1,0:T(8,128)S(1)} %bitcast.367), channel_id=1, source_target_pairs={{0,7},{1,8},{2,9},{3,10},{4,11},{5,12},{6,13},{7,14},{8,15},{9,16}... | collective-permute-start | bytes 147464 | tf_op jit(solution)/shard_map/ppermute | solution.py:148
  44.9 1.6 %collective-permute-start.9 = (f32[2,24,256]{2,1,0:T(8,128)S(1)}, f32[2,24,256]{2,1,0:T(8,128)S(1)}, u32[]{:S(2)}, u32[]{:S(2)}) collective-permute-start(f32[2,24,256]{2,1,0:T(8,128)S(1)} %bitcast.364), channel_id=1, source_target_pairs={{0,10},{1,11},{2,12},{3,13},{4,14},{5,15},{6,16},{7,17},{8,18},{9,... | collective-permute-start | bytes 147464 | tf_op jit(solution)/shard_map/ppermute | solution.py:148
  48.0 3.2 %collective-permute-start.10 = (f32[2,24,256]{2,1,0:T(8,128)S(1)}, f32[2,24,256]{2,1,0:T(8,128)S(1)}, u32[]{:S(2)}, u32[]{:S(2)}) collective-permute-start(f32[2,24,256]{2,1,0:T(8,128)S(1)} %bitcast.363), channel_id=1, source_target_pairs={{0,11},{1,12},{2,13},{3,14},{4,15},{5,16},{6,17},{7,18},{8,19},{9,... | collective-permute-start | bytes 147464 | tf_op jit(solution)/shard_map/ppermute | solution.py:148
  51.8 1.6 %collective-permute-start.11 = (f32[2,24,256]{2,1,0:T(8,128)S(1)}, f32[2,24,256]{2,1,0:T(8,128)S(1)}, u32[]{:S(2)}, u32[]{:S(2)}) collective-permute-start(f32[2,24,256]{2,1,0:T(8,128)S(1)} %bitcast.362), channel_id=1, source_target_pairs={{0,12},{1,13},{2,14},{3,15},{4,16},{5,17},{6,18},{7,19},{8,20},{9,... | collective-permute-start | bytes 147464 | tf_op jit(solution)/shard_map/ppermute | solution.py:148
  56.1 3.7 %collective-permute-start.13 = (f32[2,24,256]{2,1,0:T(8,128)S(1)}, f32[2,24,256]{2,1,0:T(8,128)S(1)}, u32[]{:S(2)}, u32[]{:S(2)}) collective-permute-start(f32[2,24,256]{2,1,0:T(8,128)S(1)} %bitcast.360), channel_id=1, source_target_pairs={{0,14},{1,15},{2,16},{3,17},{4,18},{5,19},{6,20},{7,21},{8,22},{9,... | collective-permute-start | bytes 147464 | tf_op jit(solution)/shard_map/ppermute | solution.py:148
  60.4 2.3 %collective-permute-start.14 = (f32[2,24,256]{2,1,0:T(8,128)S(1)}, f32[2,24,256]{2,1,0:T(8,128)S(1)}, u32[]{:S(2)}, u32[]{:S(2)}) collective-permute-start(f32[2,24,256]{2,1,0:T(8,128)S(1)} %bitcast.359), channel_id=1, source_target_pairs={{0,15},{1,16},{2,17},{3,18},{4,19},{5,20},{6,21},{7,22},{8,23},{9,... | collective-permute-start | bytes 147464 | tf_op jit(solution)/shard_map/ppermute | solution.py:148
  63.4 2.1 %collective-permute-start.15 = (f32[2,24,256]{2,1,0:T(8,128)S(1)}, f32[2,24,256]{2,1,0:T(8,128)S(1)}, u32[]{:S(2)}, u32[]{:S(2)}) collective-permute-start(f32[2,24,256]{2,1,0:T(8,128)S(1)} %bitcast.358), channel_id=1, source_target_pairs={{0,16},{1,17},{2,18},{3,19},{4,20},{5,21},{6,22},{7,23},{8,24},{9,... | collective-permute-start | bytes 147464 | tf_op jit(solution)/shard_map/ppermute | solution.py:148
  68.8 3.6 %collective-permute-start.18 = (f32[2,24,256]{2,1,0:T(8,128)S(1)}, f32[2,24,256]{2,1,0:T(8,128)S(1)}, u32[]{:S(2)}, u32[]{:S(2)}) collective-permute-start(f32[2,24,256]{2,1,0:T(8,128)S(1)} %bitcast.355), channel_id=1, source_target_pairs={{0,19},{1,20},{2,21},{3,22},{4,23},{5,24},{6,25},{7,26},{8,27},{9,... | collective-permute-start | bytes 147464 | tf_op jit(solution)/shard_map/ppermute | solution.py:148
  77.1 1.6 %collective-permute-start.21 = (f32[2,24,256]{2,1,0:T(8,128)S(1)}, f32[2,24,256]{2,1,0:T(8,128)S(1)}, u32[]{:S(2)}, u32[]{:S(2)}) collective-permute-start(f32[2,24,256]{2,1,0:T(8,128)S(1)} %bitcast.352), channel_id=1, source_target_pairs={{0,22},{1,23},{2,24},{3,25},{4,26},{5,27},{6,28},{7,29},{8,30},{9,... | collective-permute-start | bytes 147464 | tf_op jit(solution)/shard_map/ppermute | solution.py:148
  79.4 4.3 %collective-permute-start.22 = (f32[2,24,256]{2,1,0:T(8,128)S(1)}, f32[2,24,256]{2,1,0:T(8,128)S(1)}, u32[]{:S(2)}, u32[]{:S(2)}) collective-permute-start(f32[2,24,256]{2,1,0:T(8,128)S(1)} %bitcast.351), channel_id=1, source_target_pairs={{0,23},{1,24},{2,25},{3,26},{4,27},{5,28},{6,29},{7,30},{8,31},{9,... | collective-permute-start | bytes 147464 | tf_op jit(solution)/shard_map/ppermute | solution.py:148
  87.2 3.4 %collective-permute-start.26 = (f32[2,24,256]{2,1,0:T(8,128)S(1)}, f32[2,24,256]{2,1,0:T(8,128)S(1)}, u32[]{:S(2)}, u32[]{:S(2)}) collective-permute-start(f32[2,24,256]{2,1,0:T(8,128)S(1)} %bitcast.347), channel_id=1, source_target_pairs={{0,27},{1,28},{2,29},{3,30},{4,31},{5,0},{6,1},{7,2},{8,3},{9,4},{... | collective-permute-start | bytes 147464 | tf_op jit(solution)/shard_map/ppermute | solution.py:148
  94.6 2.5 %collective-permute-start.29 = (f32[2,24,256]{2,1,0:T(8,128)S(1)}, f32[2,24,256]{2,1,0:T(8,128)S(1)}, u32[]{:S(2)}, u32[]{:S(2)}) collective-permute-start(f32[2,24,256]{2,1,0:T(8,128)S(1)} %bitcast.344), channel_id=1, source_target_pairs={{0,30},{1,31},{2,0},{3,1},{4,2},{5,3},{6,4},{7,5},{8,6},{9,7},{10,... | collective-permute-start | bytes 147464 | tf_op jit(solution)/shard_map/ppermute | solution.py:148
  97.8 2.3 %collective-permute-start.30 = (f32[2,24,256]{2,1,0:T(8,128)S(1)}, f32[2,24,256]{2,1,0:T(8,128)S(1)}, u32[]{:S(2)}, u32[]{:S(2)}) collective-permute-start(f32[2,24,256]{2,1,0:T(8,128)S(1)} %bitcast.343), channel_id=1, source_target_pairs={{0,31},{1,0},{2,1},{3,2},{4,3},{5,4},{6,5},{7,6},{8,7},{9,8},{10,9... | collective-permute-start | bytes 147464 | tf_op jit(solution)/shard_map/ppermute | solution.py:148
  103.9 2.1 %gather_fusion = f32[32,2,24,256]{3,2,1,0:T(8,128)S(1)} fusion(f32[32,2,24,256]{3,2,1,0:T(8,128)} %constant_dynamic-update-slice_fusion, s32[1024]{0:T(1024)S(1)} %pad_clamp_fusion), kind=kCustom, calls=%fused_computation | custom fusion | bytes 3145856 | tf_op jit(solution)/shard_map/jit(_take)/gather | solution.py:151
  111.5 5.3 %collective-permute-start.32 = (f32[2,4,8,192]{3,2,1,0:T(8,128)S(1)}, f32[2,4,8,192]{3,2,1,0:T(8,128)S(1)}, u32[]{:S(2)}, u32[]{:S(2)}) collective-permute-start(f32[2,4,8,192]{3,2,1,0:T(8,128)S(1)} %copy.33), channel_id=1, source_target_pairs={{1,0},{2,1},{3,2},{4,3},{5,4},{6,5},{7,6},{8,7},{9,8},{10,9},{11,1... | collective-permute-start | bytes 147464 | tf_op jit(solution)/shard_map/ppermute | solution.py:198
  116.8 1.6 %collective-permute-done.31 = f32[2,4,8,192]{3,2,1,0:T(8,128)S(1)} collective-permute-done((f32[2,4,8,192]{3,2,1,0:T(8,128)S(1)}, f32[2,4,8,192]{3,2,1,0:T(8,128)S(1)}, u32[]{:S(2)}, u32[]{:S(2)}) %collective-permute-start.31) | collective-permute-done | bytes 49184 | tf_op jit(solution)/shard_map/ppermute | solution.py:197
  122.1 4.2 %fusion.9 = f32[2,4,256,192]{2,3,0,1:T(8,128)S(1)} fusion(f32[4,256]{1,0:T(4,128)S(1)} %copy-done.17, s32[4,256]{1,0:T(4,128)S(1)} %get-tuple-element.80, f32[4,256]{1,0:T(4,128)S(1)} %copy-done.18, s32[4,256]{1,0:T(4,128)S(1)} %get-tuple-element.76, f32[4,256]{1,0:T(4,128)S(1)} %copy-done.19, s32[4,256]{1,0:T(4,128)S(1)} %get-tuple-element.77, ...), kind=kOutput, calls=%fused_computation.14 | convolution fusion | flops 1291116544 | bytes 3309568 | tf_op jit(solution)/shard_map/sij,csja->csia/dot_general | solution.py:220
  (225 shorter events, 59.6 us)
Async XLA Ops:
  11.9 21.3 %collective-permute-start = (f32[2,24,256]{2,1,0:T(8,128)}, f32[2,24,256]{2,1,0:T(8,128)}, u32[]{:S(2)}, u32[]{:S(2)}) collective-permute-start(f32[2,24,256]{2,1,0:T(8,128)} %bitcast.335), channel_id=1, source_target_pairs={{0,1},{1,2},{2,3},{3,4},{4,5},{5,6},{6,7},{7,8},{8,9},{9,10},{10,1... | collective-permute-start | bytes 147464 | tf_op jit(solution)/shard_map/ppermute | solution.py:148
  12.9 24.1 %collective-permute-start.1 = (f32[2,24,256]{2,1,0:T(8,128)}, f32[2,24,256]{2,1,0:T(8,128)}, u32[]{:S(2)}, u32[]{:S(2)}) collective-permute-start(f32[2,24,256]{2,1,0:T(8,128)} %bitcast.334), channel_id=1, source_target_pairs={{0,2},{1,3},{2,4},{3,5},{4,6},{5,7},{6,8},{7,9},{8,10},{9,11},{10,... | collective-permute-start | bytes 147464 | tf_op jit(solution)/shard_map/ppermute | solution.py:148
  16.1 25.8 %collective-permute-start.2 = (f32[2,24,256]{2,1,0:T(8,128)}, f32[2,24,256]{2,1,0:T(8,128)}, u32[]{:S(2)}, u32[]{:S(2)}) collective-permute-start(f32[2,24,256]{2,1,0:T(8,128)} %bitcast.333), channel_id=1, source_target_pairs={{0,3},{1,4},{2,5},{3,6},{4,7},{5,8},{6,9},{7,10},{8,11},{9,12},{10... | collective-permute-start | bytes 147464 | tf_op jit(solution)/shard_map/ppermute | solution.py:148
  19.1 24.4 %collective-permute-start.3 = (f32[2,24,256]{2,1,0:T(8,128)}, f32[2,24,256]{2,1,0:T(8,128)}, u32[]{:S(2)}, u32[]{:S(2)}) collective-permute-start(f32[2,24,256]{2,1,0:T(8,128)} %bitcast.332), channel_id=1, source_target_pairs={{0,4},{1,5},{2,6},{3,7},{4,8},{5,9},{6,10},{7,11},{8,12},{9,13},{1... | collective-permute-start | bytes 147464 | tf_op jit(solution)/shard_map/ppermute | solution.py:148
  21.2 23.7 %collective-permute-start.4 = (f32[2,24,256]{2,1,0:T(8,128)}, f32[2,24,256]{2,1,0:T(8,128)}, u32[]{:S(2)}, u32[]{:S(2)}) collective-permute-start(f32[2,24,256]{2,1,0:T(8,128)} %bitcast.331), channel_id=1, source_target_pairs={{0,5},{1,6},{2,7},{3,8},{4,9},{5,10},{6,11},{7,12},{8,13},{9,14},{... | collective-permute-start | bytes 147464 | tf_op jit(solution)/shard_map/ppermute | solution.py:148
  33.1 14.8 %collective-permute-start.5 = (f32[2,24,256]{2,1,0:T(8,128)S(1)}, f32[2,24,256]{2,1,0:T(8,128)S(1)}, u32[]{:S(2)}, u32[]{:S(2)}) collective-permute-start(f32[2,24,256]{2,1,0:T(8,128)S(1)} %bitcast.368), channel_id=1, source_target_pairs={{0,6},{1,7},{2,8},{3,9},{4,10},{5,11},{6,12},{7,13},{8,14},{9,15},... | collective-permute-start | bytes 147464 | tf_op jit(solution)/shard_map/ppermute | solution.py:148
  37.0 14.7 %collective-permute-start.6 = (f32[2,24,256]{2,1,0:T(8,128)S(1)}, f32[2,24,256]{2,1,0:T(8,128)S(1)}, u32[]{:S(2)}, u32[]{:S(2)}) collective-permute-start(f32[2,24,256]{2,1,0:T(8,128)S(1)} %bitcast.367), channel_id=1, source_target_pairs={{0,7},{1,8},{2,9},{3,10},{4,11},{5,12},{6,13},{7,14},{8,15},{9,16}... | collective-permute-start | bytes 147464 | tf_op jit(solution)/shard_map/ppermute | solution.py:148
  41.8 12.1 %collective-permute-start.7 = (f32[2,24,256]{2,1,0:T(8,128)S(1)}, f32[2,24,256]{2,1,0:T(8,128)S(1)}, u32[]{:S(2)}, u32[]{:S(2)}) collective-permute-start(f32[2,24,256]{2,1,0:T(8,128)S(1)} %bitcast.366), channel_id=1, source_target_pairs={{0,8},{1,9},{2,10},{3,11},{4,12},{5,13},{6,14},{7,15},{8,16},{9,17... | collective-permute-start | bytes 147464 | tf_op jit(solution)/shard_map/ppermute | solution.py:148
  43.5 12.6 %collective-permute-start.8 = (f32[2,24,256]{2,1,0:T(8,128)S(1)}, f32[2,24,256]{2,1,0:T(8,128)S(1)}, u32[]{:S(2)}, u32[]{:S(2)}) collective-permute-start(f32[2,24,256]{2,1,0:T(8,128)S(1)} %bitcast.365), channel_id=1, source_target_pairs={{0,9},{1,10},{2,11},{3,12},{4,13},{5,14},{6,15},{7,16},{8,17},{9,1... | collective-permute-start | bytes 147464 | tf_op jit(solution)/shard_map/ppermute | solution.py:148
  44.9 15.5 %collective-permute-start.9 = (f32[2,24,256]{2,1,0:T(8,128)S(1)}, f32[2,24,256]{2,1,0:T(8,128)S(1)}, u32[]{:S(2)}, u32[]{:S(2)}) collective-permute-start(f32[2,24,256]{2,1,0:T(8,128)S(1)} %bitcast.364), channel_id=1, source_target_pairs={{0,10},{1,11},{2,12},{3,13},{4,14},{5,15},{6,16},{7,17},{8,18},{9,... | collective-permute-start | bytes 147464 | tf_op jit(solution)/shard_map/ppermute | solution.py:148
  48.0 15.4 %collective-permute-start.10 = (f32[2,24,256]{2,1,0:T(8,128)S(1)}, f32[2,24,256]{2,1,0:T(8,128)S(1)}, u32[]{:S(2)}, u32[]{:S(2)}) collective-permute-start(f32[2,24,256]{2,1,0:T(8,128)S(1)} %bitcast.363), channel_id=1, source_target_pairs={{0,11},{1,12},{2,13},{3,14},{4,15},{5,16},{6,17},{7,18},{8,19},{9,... | collective-permute-start | bytes 147464 | tf_op jit(solution)/shard_map/ppermute | solution.py:148
  51.8 14.4 %collective-permute-start.11 = (f32[2,24,256]{2,1,0:T(8,128)S(1)}, f32[2,24,256]{2,1,0:T(8,128)S(1)}, u32[]{:S(2)}, u32[]{:S(2)}) collective-permute-start(f32[2,24,256]{2,1,0:T(8,128)S(1)} %bitcast.362), channel_id=1, source_target_pairs={{0,12},{1,13},{2,14},{3,15},{4,16},{5,17},{6,18},{7,19},{8,20},{9,... | collective-permute-start | bytes 147464 | tf_op jit(solution)/shard_map/ppermute | solution.py:148
  53.9 12.8 %collective-permute-start.12 = (f32[2,24,256]{2,1,0:T(8,128)S(1)}, f32[2,24,256]{2,1,0:T(8,128)S(1)}, u32[]{:S(2)}, u32[]{:S(2)}) collective-permute-start(f32[2,24,256]{2,1,0:T(8,128)S(1)} %bitcast.361), channel_id=1, source_target_pairs={{0,13},{1,14},{2,15},{3,16},{4,17},{5,18},{6,19},{7,20},{8,21},{9,... | collective-permute-start | bytes 147464 | tf_op jit(solution)/shard_map/ppermute | solution.py:148
  56.1 12.7 %collective-permute-start.13 = (f32[2,24,256]{2,1,0:T(8,128)S(1)}, f32[2,24,256]{2,1,0:T(8,128)S(1)}, u32[]{:S(2)}, u32[]{:S(2)}) collective-permute-start(f32[2,24,256]{2,1,0:T(8,128)S(1)} %bitcast.360), channel_id=1, source_target_pairs={{0,14},{1,15},{2,16},{3,17},{4,18},{5,19},{6,20},{7,21},{8,22},{9,... | collective-permute-start | bytes 147464 | tf_op jit(solution)/shard_map/ppermute | solution.py:148
  60.4 12.7 %collective-permute-start.14 = (f32[2,24,256]{2,1,0:T(8,128)S(1)}, f32[2,24,256]{2,1,0:T(8,128)S(1)}, u32[]{:S(2)}, u32[]{:S(2)}) collective-permute-start(f32[2,24,256]{2,1,0:T(8,128)S(1)} %bitcast.359), channel_id=1, source_target_pairs={{0,15},{1,16},{2,17},{3,18},{4,19},{5,20},{6,21},{7,22},{8,23},{9,... | collective-permute-start | bytes 147464 | tf_op jit(solution)/shard_map/ppermute | solution.py:148
  63.4 11.6 %collective-permute-start.15 = (f32[2,24,256]{2,1,0:T(8,128)S(1)}, f32[2,24,256]{2,1,0:T(8,128)S(1)}, u32[]{:S(2)}, u32[]{:S(2)}) collective-permute-start(f32[2,24,256]{2,1,0:T(8,128)S(1)} %bitcast.358), channel_id=1, source_target_pairs={{0,16},{1,17},{2,18},{3,19},{4,20},{5,21},{6,22},{7,23},{8,24},{9,... | collective-permute-start | bytes 147464 | tf_op jit(solution)/shard_map/ppermute | solution.py:148
  66.2 11.0 %collective-permute-start.16 = (f32[2,24,256]{2,1,0:T(8,128)S(1)}, f32[2,24,256]{2,1,0:T(8,128)S(1)}, u32[]{:S(2)}, u32[]{:S(2)}) collective-permute-start(f32[2,24,256]{2,1,0:T(8,128)S(1)} %bitcast.357), channel_id=1, source_target_pairs={{0,17},{1,18},{2,19},{3,20},{4,21},{5,22},{6,23},{7,24},{8,25},{9,... | collective-permute-start | bytes 147464 | tf_op jit(solution)/shard_map/ppermute | solution.py:148
  66.8 12.6 %collective-permute-start.17 = (f32[2,24,256]{2,1,0:T(8,128)S(1)}, f32[2,24,256]{2,1,0:T(8,128)S(1)}, u32[]{:S(2)}, u32[]{:S(2)}) collective-permute-start(f32[2,24,256]{2,1,0:T(8,128)S(1)} %bitcast.356), channel_id=1, source_target_pairs={{0,18},{1,19},{2,20},{3,21},{4,22},{5,23},{6,24},{7,25},{8,26},{9,... | collective-permute-start | bytes 147464 | tf_op jit(solution)/shard_map/ppermute | solution.py:148
  68.8 15.4 %collective-permute-start.18 = (f32[2,24,256]{2,1,0:T(8,128)S(1)}, f32[2,24,256]{2,1,0:T(8,128)S(1)}, u32[]{:S(2)}, u32[]{:S(2)}) collective-permute-start(f32[2,24,256]{2,1,0:T(8,128)S(1)} %bitcast.355), channel_id=1, source_target_pairs={{0,19},{1,20},{2,21},{3,22},{4,23},{5,24},{6,25},{7,26},{8,27},{9,... | collective-permute-start | bytes 147464 | tf_op jit(solution)/shard_map/ppermute | solution.py:148
  73.1 12.9 %collective-permute-start.19 = (f32[2,24,256]{2,1,0:T(8,128)S(1)}, f32[2,24,256]{2,1,0:T(8,128)S(1)}, u32[]{:S(2)}, u32[]{:S(2)}) collective-permute-start(f32[2,24,256]{2,1,0:T(8,128)S(1)} %bitcast.354), channel_id=1, source_target_pairs={{0,20},{1,21},{2,22},{3,23},{4,24},{5,25},{6,26},{7,27},{8,28},{9,... | collective-permute-start | bytes 147464 | tf_op jit(solution)/shard_map/ppermute | solution.py:148
  75.0 11.6 %collective-permute-start.20 = (f32[2,24,256]{2,1,0:T(8,128)S(1)}, f32[2,24,256]{2,1,0:T(8,128)S(1)}, u32[]{:S(2)}, u32[]{:S(2)}) collective-permute-start(f32[2,24,256]{2,1,0:T(8,128)S(1)} %bitcast.353), channel_id=1, source_target_pairs={{0,21},{1,22},{2,23},{3,24},{4,25},{5,26},{6,27},{7,28},{8,29},{9,... | collective-permute-start | bytes 147464 | tf_op jit(solution)/shard_map/ppermute | solution.py:148
  79.4 11.9 %collective-permute-start.22 = (f32[2,24,256]{2,1,0:T(8,128)S(1)}, f32[2,24,256]{2,1,0:T(8,128)S(1)}, u32[]{:S(2)}, u32[]{:S(2)}) collective-permute-start(f32[2,24,256]{2,1,0:T(8,128)S(1)} %bitcast.351), channel_id=1, source_target_pairs={{0,23},{1,24},{2,25},{3,26},{4,27},{5,28},{6,29},{7,30},{8,31},{9,... | collective-permute-start | bytes 147464 | tf_op jit(solution)/shard_map/ppermute | solution.py:148
  86.6 11.2 %collective-permute-start.25 = (f32[2,24,256]{2,1,0:T(8,128)S(1)}, f32[2,24,256]{2,1,0:T(8,128)S(1)}, u32[]{:S(2)}, u32[]{:S(2)}) collective-permute-start(f32[2,24,256]{2,1,0:T(8,128)S(1)} %bitcast.348), channel_id=1, source_target_pairs={{0,26},{1,27},{2,28},{3,29},{4,30},{5,31},{6,0},{7,1},{8,2},{9,3},... | collective-permute-start | bytes 147464 | tf_op jit(solution)/shard_map/ppermute | solution.py:148
  87.2 13.6 %collective-permute-start.26 = (f32[2,24,256]{2,1,0:T(8,128)S(1)}, f32[2,24,256]{2,1,0:T(8,128)S(1)}, u32[]{:S(2)}, u32[]{:S(2)}) collective-permute-start(f32[2,24,256]{2,1,0:T(8,128)S(1)} %bitcast.347), channel_id=1, source_target_pairs={{0,27},{1,28},{2,29},{3,30},{4,31},{5,0},{6,1},{7,2},{8,3},{9,4},{... | collective-permute-start | bytes 147464 | tf_op jit(solution)/shard_map/ppermute | solution.py:148
  (38 other events, 213.1 us)

commit v9 on v6

--- a/solution.py
+++ b/solution.py
@@ -105,11 +105,9 @@
     )
     if block_len % outer_len == 0:
         per_block = block_len // outer_len
-        second = second.reshape(device_count, per_block, 2, rows, outer_len)
-        second = jnp.transpose(second, (0, 2, 3, 1, 4))
-        return second.reshape(device_count, 2, rows, block_len)
+        return second.reshape(device_count, per_block, 2, rows, outer_len)
     second = jnp.transpose(second, (1, 2, 0, 3)).reshape(2, rows, device_count, block_len)
-    return jnp.transpose(second, (2, 0, 1, 3))
+    return jnp.transpose(second, (2, 0, 1, 3))[:, None]
 
 
 def azimuth_matrix(row_list, scale):
@@ -140,7 +138,11 @@
     spectrum = lax.all_to_all(
         spectrum, ("pulse", "rng"), split_axis=0, concat_axis=0, tiled=True
     )
-    spectrum = spectrum.reshape(pulse_count, lane_count, 2, rows_here, block_len)
+    pieces = spectrum.shape[1]
+    spectrum = spectrum.reshape(pulse_count, lane_count, pieces, 2, rows_here, block_len // pieces)
+    spectrum = jnp.transpose(spectrum, (0, 1, 3, 4, 2, 5)).reshape(
+        pulse_count, lane_count, 2, rows_here, block_len
+    )
 
     lane_real = spectrum[:, :, 0]
     lane_imag = spectrum[:, :, 1]

time: 78.5 us -> 78.6 us (level)
  other arithmetic: 7.44 us -> 9.23 us
    reshape x2 -> x1, local copies, waits for them, and re-layouts: 3.32 us -> 1.26 us  [on_device(): jnp.transpose(spectrum, (0, 1, 3, 4, 2, 5))]
    another operation x1, local copies, waits for them, and re-layouts: 0.1 us -> 2.01 us  [range_dft_blocks(): jnp.stack([second[:, 0] * turn_real - second[:, 1] * turn_imag, second[:,...]
    another operation x0 -> x1, other arithmetic: none -> 1.42 us  [range_dft_blocks(): jnp.stack([second[:, 0] * turn_real - second[:, 1] * turn_imag, second[:,...]
    sin x1, other arithmetic: 3 us -> 4.14 us  [on_device(): jnp.sin(phase_angle)]
    transpose x1 -> x0, other arithmetic: 0.83 us -> none  [range_dft_blocks(): second = jnp.transpose(second, (0, 2, 3, 1, 4))]
    unnamed x35 -> x36, local copies, waits for them, and re-layouts: 3.04 us -> 2.65 us
  transfers between devices with their start and end apart: 3 -> 3, of which waited for: 3 -> 3; matrix products, arithmetic and copies ran while one was open for 10% -> 11% of each run, Pallas kernels for 0% -> 0%
where the time goes in v9:
time: 78.6 us; the launch traced here: 78.4 us
  waiting for transfers between devices  31.1 us (40%)
  starting transfers between devices  13.1 us (17%)
  matrix products  12.4 us (16%)
  local copies, waits for them, and re-layouts  12.1 us (15%)
  other arithmetic  9.23 us (12%)
    all_to_all x1, waiting for transfers between devices, on_device(): lax.all_to_all(spectrum, ('pulse', 'rng'), split_axis=0, concat_axis=0, t...  29.5 us
    all_to_all x1, starting transfers between devices, on_device(): lax.all_to_all(spectrum, ('pulse', 'rng'), split_axis=0, concat_axis=0, t...  7.48 us
    ppermute x1, starting transfers between devices, on_device(): right_rim = lax.ppermute(focused[:, :, :RIM], axes, down)  5.56 us
    dot_general x1, matrix products, on_device(): return jnp.einsum('sij,csja->csia', band, widened, precision=highest)  4.19 us
    sin x1, other arithmetic, on_device(): jnp.sin(phase_angle)  4.14 us
    dot_general x1, matrix products, range_dft_blocks(): jnp.einsum('ducb,crba->drua', stacked_table(outer_len, 1.0), signal, prec...  2.66 us
    unnamed x36, local copies, waits for them, and re-layouts  2.65 us
    reshape x1, local copies, waits for them, and re-layouts, range_dft_blocks(): signal = pair.reshape(2, rows, outer_len, inner_len)  2.41 us
  transfers between devices with their start and end apart: 3, of which 3 were waited for; matrix products, arithmetic and copies ran while one was open for 11% of the time, Pallas kernels for 0%

profile of v9, /device:TPU:0, one launch (start us, length us, event | category | flops | bytes accessed | tf_op | source)
XLA Modules:
  0.0 78.4 jit_solution(3468857491876801089)
XLA Ops:
  1.0 2.4 %reshape.590 = f32[2,24,128,64]{3,2,1,0:T(8,128)S(1)} reshape(f32[2,24,8192]{2,1,0:T(8,128)} %param.6) | data formatting | bytes 3145728 | tf_op jit(solution)/shard_map/reshape | solution.py:77
  3.7 2.7 %fusion.12 = f32[2,24,128,64]{2,3,1,0:T(8,128)S(1)} fusion(f32[2,24,128,64]{3,2,1,0:T(8,128)S(1)} %reshape.590, f32[1,128,2,128]{3,1,2,0:T(8,128)S(1)} %get-tuple-element.30, f32[1,128,2,128]{3,1,2,0:T(8,128)S(1)} %get-tuple-element.29), kind=kOutput, calls=%fused_computation.14 | convolution fusion | flops 604045312 | bytes 3407872 | tf_op jit(solution)/shard_map/ducb,crba->drua/dot_general | solution.py:78
  6.3 0.3 multiply_subtract_fusion.1
  6.7 0.8 %fusion.6 = f32[64,2,24,128]{3,0,1,2:T(8,128)S(1)} fusion(f32[1,64,2,64]{3,1,2,0:T(8,128)S(1)} %get-tuple-element.40, f32[1,64,2,64]{3,1,2,0:T(8,128)S(1)} %get-tuple-element.39, f32[1,24,128,64]{2,3,1,0:T(8,128)S(1)} %get-tuple-element.16, f32[1,24,128,64]{2,3,1,0:T(8,128)S(1)} %get-tuple-element.15), kind=kOutput, calls=%fused_computation.12 | convolution fusion | flops 302399488 | bytes 3211264 | tf_op jit(solution)/shard_map/dvca,crua->vdru/dot_general | solution.py:90
  7.7 1.4 %pad_maximum_fusion.1 = f32[32,2,2,24,128]{4,1,0,3,2:T(2,128)S(1)} fusion(f32[32,2,1,24,128]{4,1,0,3,2:T(2,128)S(1)} %bitcast.182, f32[32,2,1,24,128]{4,1,0,3,2:T(2,128)S(1)} %bitcast.181), kind=kLoop, calls=%fused_computation.6 | loop fusion | flops 393216 | bytes 3145728 | tf_op jit(solution)/shard_map/stack | solution.py:99
  9.1 2.0 %copy.44 = f32[32,2,2,24,128]{4,1,3,2,0:T(2,128)} copy(f32[32,2,2,24,128]{4,1,0,3,2:T(2,128)S(1)} %pad_maximum_fusion.1) | data formatting | bytes 3145728 | tf_op jit(solution)/shard_map/stack | solution.py:99
  11.2 7.5 %all-to-all-start = ((f32[32,2,2,24,128]{4,1,3,2,0:T(2,128)}), f32[32,2,2,24,128]{4,1,3,2,0:T(2,128)S(1)}, u32[]{:S(2)}, u32[]{:S(2)}) async-start(f32[32,2,2,24,128]{4,1,3,2,0:T(2,128)} %copy.44), calls=%async_computation | async-start | bytes 3145728 | tf_op jit(solution)/shard_map/all_to_all | solution.py:138
  18.7 4.1 %fusion.32 = (f32[4,256,192]{1,2,0:T(8,128)}, f32[4,256,192]{1,2,0:T(8,128)}) fusion(f32[192]{0:T(256)S(1)} %integer_pow.9, f32[4,256]{1,0:T(4,128)S(1)} %integer_pow.8), kind=kLoop, calls=%fused_computation.48 | loop fusion | flops 393216 | bytes 1577728 | tf_op jit(solution)/shard_map/sin | solution.py:177
  23.0 0.6 slice_bitcast_fusion.15
  23.6 1.1 %fusion.66 = f32[192,192]{1,0:T(8,128)S(1)} fusion(s32[192]{0:T(256)S(1)} %copy-done.16), kind=kOutput, calls=%fused_computation.100 | convolution fusion | flops 85340160 | bytes 148224 | tf_op jit(solution)/shard_map/ji,ja->ai/dot_general | solution.py:118
  24.7 1.8 %fusion.135 = (f32[192,192]{1,0:T(8,128)}, f32[192,192]{1,0:T(8,128)S(1)}) fusion(s32[192]{0:T(256)S(1)} %copy-done.16), kind=kOutput, calls=%fused_computation.213 | convolution fusion | flops 85377024 | bytes 295680 | tf_op jit(solution)/shard_map/ji,ja->ai/dot_general | solution.py:119
  26.5 29.5 %all-to-all-done = f32[32,2,2,24,128]{4,1,3,2,0:T(2,128)S(1)} async-done(((f32[32,2,2,24,128]{4,1,3,2,0:T(2,128)}), f32[32,2,2,24,128]{4,1,3,2,0:T(2,128)S(1)}, u32[]{:S(2)}, u32[]{:S(2)}) %all-to-all-start) | async-done | bytes 1572896 | tf_op jit(solution)/shard_map/all_to_all | solution.py:138
  56.0 1.3 %reshape.603 = f32[8,4,2,24,256]{4,3,2,1,0:T(8,128)S(1)} reshape(f32[8,4,2,24,2,128]{5,4,3,2,1,0:T(2,128)S(1)} %bitcast.180) | data formatting | bytes 3145728 | tf_op jit(solution)/shard_map/reshape | solution.py:143
  58.2 0.8 %copy-done.5 = f32[192,192]{1,0:T(8,128)S(1)} copy-done((f32[192,192]{1,0:T(8,128)S(1)}, f32[192,192]{1,0:T(8,128)}, u32[]{:S(2)}) %copy-start.5) | copy-done | bytes 147480
  58.9 0.8 %fusion.51 = f32[4,256,192]{1,2,0:T(8,128)S(1)} fusion(f32[4,384,256]{2,1,0:T(8,128)S(1)} %bitcast.174, f32[192,192]{1,0:T(8,128)S(1)} %copy-done.5, f32[192,192]{1,0:T(8,128)S(1)} %fusion.66), kind=kOutput, calls=%fused_computation.75 | convolution fusion | flops 453058560 | bytes 2654208 | tf_op jit(solution)/shard_map/ay,syq->sqa/dot_general | solution.py:170
  59.8 1.0 %subtract_bitcast_fusion = (f32[1,4,256,192]{2,3,1,0:T(8,128)S(1)}, f32[1,4,256,192]{2,3,1,0:T(8,128)S(1)}) fusion(f32[4,256,192]{1,2,0:T(8,128)S(1)} %copy-done, f32[4,256,192]{1,2,0:T(8,128)S(1)} %fusion.51, f32[4,256,192]{1,2,0:T(8,128)S(1)} %copy-done.1, f32[4,384,256]{2,1,0:T(8,128)S(1)} %bitcast.175, f32[192,192]{1,0:T(8,128)S(1)} %fusion.66, ...), kind=kOutput, calls=%fused_computation.46 | convolution fusion | flops 454238208 | bytes 5799936 | tf_op jit(solution)/shard_map/ay,syq->sqa/dot_general | solution.py:171
  61.1 0.6 copy-done.2
  62.4 5.6 %collective-permute-start.1 = (f32[2,4,8,192]{3,2,1,0:T(8,128)S(1)}, f32[2,4,8,192]{3,2,1,0:T(8,128)S(1)}, u32[]{:S(2)}, u32[]{:S(2)}) collective-permute-start(f32[2,4,8,192]{3,2,1,0:T(8,128)S(1)} %copy.28), channel_id=1, source_target_pairs={{1,0},{2,1},{3,2},{4,3},{5,4},{6,5},{7,6},{8,7},{9,8},{10,9},{11,1... | collective-permute-start | bytes 147464 | tf_op jit(solution)/shard_map/ppermute | solution.py:187
  68.0 1.4 %collective-permute-done = f32[2,4,8,192]{3,2,1,0:T(8,128)S(1)} collective-permute-done((f32[2,4,8,192]{3,2,1,0:T(8,128)S(1)}, f32[2,4,8,192]{3,2,1,0:T(8,128)S(1)}, u32[]{:S(2)}, u32[]{:S(2)}) %collective-permute-start) | collective-permute-done | bytes 49184 | tf_op jit(solution)/shard_map/ppermute | solution.py:186
  70.4 1.0 %broadcast_select_fusion.1 = f32[2,4,8,192]{2,3,1,0:T(8,128)} fusion(f32[2,4,8,192]{2,3,1,0:T(8,128)S(1)} %copy.26, f32[2,4,8,192]{2,3,1,0:T(8,128)S(1)} %copy.27, pred[]{:T(512)S(6)} %eq.66), kind=kLoop, calls=%fused_computation.72 | loop fusion | flops 12288 | bytes 147457 | tf_op jit(solution)/shard_map/jit(_where)/select_n | solution.py:188
  71.8 0.7 copy-done.3
  72.6 0.3 copy-done.4
  72.9 4.2 %fusion.9 = f32[2,4,256,192]{2,3,0,1:T(8,128)S(1)} fusion(f32[4,256]{1,0:T(4,128)S(1)} %get-tuple-element.32, s32[4,256]{1,0:T(4,128)S(1)} %get-tuple-element.48, f32[4,256]{1,0:T(4,128)S(1)} %copy-done.9, s32[4,256]{1,0:T(4,128)S(1)} %get-tuple-element.44, f32[4,256]{1,0:T(4,128)S(1)} %copy-done.10, s32[4,256]{1,0:T(4,128)S(1)} %get-tuple-element.45, ...), kind=kOutput, calls=%fused_computation.13 | convolution fusion | flops 1291116544 | bytes 3309568 | tf_op jit(solution)/shard_map/sij,csja->csia/dot_general | solution.py:209
  77.1 1.2 %copy.32 = f32[2,4,256,192]{2,3,1,0:T(8,128)} copy(f32[2,4,256,192]{2,3,0,1:T(8,128)S(1)} %fusion.9) | data formatting | bytes 3145728 | tf_op jit(solution)/shard_map/sij,csja->csia/transpose | solution.py:209
  (72 shorter events, 4.7 us)
Async XLA Ops:
  11.2 7.5 %copy-start.7 = (f32[4,256]{1,0:T(4,128)S(1)}, f32[4,256]{1,0:T(4,128)}, u32[]{:S(2)}) copy-start(f32[4,256]{1,0:T(4,128)} %param.8) | copy-start | bytes 12292
  11.2 7.5 %copy-start.15 = (f32[192]{0:T(256)S(1)}, f32[192]{0:T(256)}, u32[]{:S(2)}) copy-start(f32[192]{0:T(256)} %param.9) | copy-start | bytes 2308
  11.2 44.8 %all-to-all-start = ((f32[32,2,2,24,128]{4,1,3,2,0:T(2,128)}), f32[32,2,2,24,128]{4,1,3,2,0:T(2,128)S(1)}, u32[]{:S(2)}, u32[]{:S(2)}) async-start(f32[32,2,2,24,128]{4,1,3,2,0:T(2,128)} %copy.44), calls=%async_computation | async-start | bytes 3145728 | tf_op jit(solution)/shard_map/all_to_all | solution.py:138
  18.7 4.2 %copy-start.8 = (s32[4,256]{1,0:T(4,128)S(1)}, s32[4,256]{1,0:T(4,128)}, u32[]{:S(2)}) copy-start(s32[4,256]{1,0:T(4,128)} %param.10) | copy-start | bytes 12292
  18.7 4.3 %copy-start.6 = (f32[8,4,256]{2,1,0:T(4,128)S(1)}, f32[8,4,256]{2,1,0:T(4,128)}, u32[]{:S(2)}) copy-start(f32[8,4,256]{2,1,0:T(4,128)} %param.11) | copy-start | bytes 98308
  18.7 4.9 %copy-start.16 = (s32[192]{0:T(256)S(1)}, s32[192]{0:T(256)}, u32[]{:S(2)}) copy-start(s32[192]{0:T(256)} %param.7) | copy-start | bytes 2308
  58.0 0.9 %copy-start.5 = (f32[192,192]{1,0:T(8,128)S(1)}, f32[192,192]{1,0:T(8,128)}, u32[]{:S(2)}) copy-start(f32[192,192]{1,0:T(8,128)} %get-tuple-element.51) | copy-start | bytes 442372
  58.1 1.7 %copy-start = (f32[4,256,192]{1,2,0:T(8,128)S(1)}, f32[4,256,192]{1,2,0:T(8,128)}, u32[]{:S(2)}) copy-start(f32[4,256,192]{1,2,0:T(8,128)} %get-tuple-element.8) | copy-start | bytes 2359300
  58.1 1.7 %copy-start.1 = (f32[4,256,192]{1,2,0:T(8,128)S(1)}, f32[4,256,192]{1,2,0:T(8,128)}, u32[]{:S(2)}) copy-start(f32[4,256,192]{1,2,0:T(8,128)} %get-tuple-element.7) | copy-start | bytes 2359300
  60.9 0.9 %copy-start.2 = (f32[1,4,256,192]{2,3,1,0:T(8,128)}, f32[1,4,256,192]{2,3,1,0:T(8,128)S(1)}, u32[]{:S(2)}) copy-start(f32[1,4,256,192]{2,3,1,0:T(8,128)S(1)} %get-tuple-element.12) | copy-start | bytes 2359300
  62.0 7.3 %collective-permute-start = (f32[2,4,8,192]{3,2,1,0:T(8,128)S(1)}, f32[2,4,8,192]{3,2,1,0:T(8,128)S(1)}, u32[]{:S(2)}, u32[]{:S(2)}) collective-permute-start(f32[2,4,8,192]{3,2,1,0:T(8,128)S(1)} %copy.25), channel_id=1, source_target_pairs={{0,1},{1,2},{2,3},{3,4},{4,5},{5,6},{6,7},{7,8},{8,9},{9,10},{10,1... | collective-permute-start | bytes 147464 | tf_op jit(solution)/shard_map/ppermute | solution.py:186
  62.4 7.5 %collective-permute-start.1 = (f32[2,4,8,192]{3,2,1,0:T(8,128)S(1)}, f32[2,4,8,192]{3,2,1,0:T(8,128)S(1)}, u32[]{:S(2)}, u32[]{:S(2)}) collective-permute-start(f32[2,4,8,192]{3,2,1,0:T(8,128)S(1)} %copy.28), channel_id=1, source_target_pairs={{1,0},{2,1},{3,2},{4,3},{5,4},{6,5},{7,6},{8,7},{9,8},{10,9},{11,1... | collective-permute-start | bytes 147464 | tf_op jit(solution)/shard_map/ppermute | solution.py:187
  71.4 1.1 %copy-start.3 = (f32[1,4,256,192]{2,3,1,0:T(8,128)S(1)}, f32[1,4,256,192]{2,3,1,0:T(8,128)}, u32[]{:S(2)}) copy-start(f32[1,4,256,192]{2,3,1,0:T(8,128)} %copy-done.2) | copy-start | bytes 2359300
  71.4 1.1 %copy-start.9 = (f32[4,256]{1,0:T(4,128)S(1)}, f32[4,256]{1,0:T(4,128)}, u32[]{:S(2)}) copy-start(f32[4,256]{1,0:T(4,128)} %get-tuple-element.33) | copy-start | bytes 12292
  71.4 1.1 %copy-start.10 = (f32[4,256]{1,0:T(4,128)S(1)}, f32[4,256]{1,0:T(4,128)}, u32[]{:S(2)}) copy-start(f32[4,256]{1,0:T(4,128)} %get-tuple-element.34) | copy-start | bytes 12292
  71.4 1.1 %copy-start.11 = (f32[4,256]{1,0:T(4,128)S(1)}, f32[4,256]{1,0:T(4,128)}, u32[]{:S(2)}) copy-start(f32[4,256]{1,0:T(4,128)} %get-tuple-element.35) | copy-start | bytes 12292
  71.4 1.1 %copy-start.12 = (f32[4,256]{1,0:T(4,128)S(1)}, f32[4,256]{1,0:T(4,128)}, u32[]{:S(2)}) copy-start(f32[4,256]{1,0:T(4,128)} %get-tuple-element.36) | copy-start | bytes 12292
  71.4 1.1 %copy-start.13 = (f32[4,256]{1,0:T(4,128)S(1)}, f32[4,256]{1,0:T(4,128)}, u32[]{:S(2)}) copy-start(f32[4,256]{1,0:T(4,128)} %get-tuple-element.37) | copy-start | bytes 12292
  71.4 1.1 %copy-start.14 = (f32[4,256]{1,0:T(4,128)S(1)}, f32[4,256]{1,0:T(4,128)}, u32[]{:S(2)}) copy-start(f32[4,256]{1,0:T(4,128)} %get-tuple-element.38) | copy-start | bytes 12292
  71.7 1.2 %copy-start.4 = (f32[2,4,8,192]{2,3,1,0:T(8,128)S(1)}, f32[2,4,8,192]{2,3,1,0:T(8,128)}, u32[]{:S(2)}) copy-start(f32[2,4,8,192]{2,3,1,0:T(8,128)} %broadcast_select_fusion.1) | copy-start | bytes 147460

commit v10 on v9

--- a/solution.py
+++ b/solution.py
@@ -189,7 +189,7 @@
     right_rim = jnp.where(
         position == device_count - 1, jnp.roll(right_rim, -1, axis=1), right_rim
     )
-    widened = jnp.concatenate([left_rim, focused, right_rim], axis=2)
+
 
     tap_count = stolt_coef.shape[0]
     piece_index = jnp.arange(block_len, dtype=jnp.int32)
@@ -206,7 +206,22 @@
     for t in range(tap_count):
         band = band + jnp.where(columns[None, None, :] == target + t, weights[t][:, :, None], 0.0)
 
-    return jnp.einsum("sij,csja->csia", band, widened, precision=highest)
+    image = jnp.einsum(
+        "sij,csja->csia", band[:, :, RIM:RIM + block_len], focused, precision=highest
+    )
+    band_left = band[:, :RIM, :RIM]
+    band_right = band[:, block_len - RIM:, block_len + RIM:]
+    left_part = jnp.sum(band_left[None, :, :, :, None] * left_rim[:, :, None, :, :], axis=3)
+    right_part = jnp.sum(band_right[None, :, :, :, None] * right_rim[:, :, None, :, :], axis=3)
+    rest = block_len - RIM
+    edges = jnp.concatenate(
+        [left_part, jnp.zeros_like(image[:, :, RIM:rest]), right_part], axis=2
+    ) if rest > RIM else None
+    if edges is None:
+        edges = jnp.pad(left_part, ((0, 0), (0, 0), (0, rest), (0, 0))) + jnp.pad(
+            right_part, ((0, 0), (0, 0), (rest, 0), (0, 0))
+        )
+    return image + edges
 
 
 def solution(mesh):

time: 78.6 us -> 78.8 us (level)
  waiting for transfers between devices: 31.1 us -> 26.2 us
  other arithmetic: 9.23 us -> 14 us
  local copies, waits for them, and re-layouts: 12.1 us -> 13.5 us
  matrix products: 12.4 us -> 11.5 us
    add x0 -> x1, other arithmetic: none -> 4.43 us  [on_device(): band + jnp.where(columns[None, None, :] == target + t, weights[t][:, :, N...]
    all_to_all x1, waiting for transfers between devices: 29.5 us -> 25.7 us  [on_device(): lax.all_to_all(spectrum, ('pulse', 'rng'), split_axis=0, concat_axis=0, t...]
    reduce_sum x0 -> x2, local copies, waits for them, and re-layouts: none -> 2.32 us  [the longest x1 1.16 us: on_device(): jnp.sum(band_left[None, :, :, :, None] * left_rim[:, :, None, :, :], axis=3)]
    unnamed x36 -> x20, local copies, waits for them, and re-layouts: 2.65 us -> 0.96 us
    add x0 -> x1, local copies, waits for them, and re-layouts: none -> 1.31 us  [on_device(): return image + edges]
    transpose x1 -> x0, local copies, waits for them, and re-layouts: 1.25 us -> none  [on_device(): return jnp.einsum('sij,csja->csia', band, widened, precision=highest)]
    slice x1, local copies, waits for them, and re-layouts: 0.29 us -> 1.43 us  [on_device(): left_rim = lax.ppermute(focused[:, :, block_len - RIM:], axes, up)]
    slice x1, local copies, waits for them, and re-layouts: 0.29 us -> 1.43 us  [on_device(): right_rim = lax.ppermute(focused[:, :, :RIM], axes, down)]
  transfers between devices with their start and end apart: 3 -> 3, of which waited for: 3 -> 3; matrix products, arithmetic and copies ran while one was open for 11% -> 18% of each run, Pallas kernels for 0% -> 0%
where the time goes in v10:
time: 78.8 us; the launch traced here: 78.5 us
  waiting for transfers between devices  26.2 us (33%)
  other arithmetic  14 us (18%)
  local copies, waits for them, and re-layouts  13.5 us (17%)
  starting transfers between devices  12.9 us (16%)
  matrix products  11.5 us (15%)
    all_to_all x1, waiting for transfers between devices, on_device(): lax.all_to_all(spectrum, ('pulse', 'rng'), split_axis=0, concat_axis=0, t...  25.7 us
    all_to_all x1, starting transfers between devices, on_device(): lax.all_to_all(spectrum, ('pulse', 'rng'), split_axis=0, concat_axis=0, t...  7.48 us
    ppermute x1, starting transfers between devices, on_device(): right_rim = lax.ppermute(focused[:, :, :RIM], axes, down)  5.35 us
    add x1, other arithmetic, on_device(): band + jnp.where(columns[None, None, :] == target + t, weights[t][:, :, N...  4.43 us
    sin x1, other arithmetic, on_device(): jnp.sin(phase_angle)  4.12 us
    dot_general x1, matrix products, on_device(): jnp.einsum('sij,csja->csia', band[:, :, RIM:RIM + block_len], focused, pr...  3.27 us
    dot_general x1, matrix products, range_dft_blocks(): jnp.einsum('ducb,crba->drua', stacked_table(outer_len, 1.0), signal, prec...  2.66 us
    reshape x1, local copies, waits for them, and re-layouts, range_dft_blocks(): signal = pair.reshape(2, rows, outer_len, inner_len)  2.41 us
  transfers between devices with their start and end apart: 3, of which 3 were waited for; matrix products, arithmetic and copies ran while one was open for 18% of the time, Pallas kernels for 0%

profile of v10, /device:TPU:0, one launch (start us, length us, event | category | flops | bytes accessed | tf_op | source)
XLA Modules:
  0.0 78.5 jit_solution(6332690758294670616)
XLA Ops:
  1.0 2.4 %reshape.594 = f32[2,24,128,64]{3,2,1,0:T(8,128)S(1)} reshape(f32[2,24,8192]{2,1,0:T(8,128)} %param.6) | data formatting | bytes 3145728 | tf_op jit(solution)/shard_map/reshape | solution.py:77
  3.7 2.7 %fusion.9 = f32[2,24,128,64]{2,3,1,0:T(8,128)S(1)} fusion(f32[2,24,128,64]{3,2,1,0:T(8,128)S(1)} %reshape.594, f32[1,128,2,128]{3,1,2,0:T(8,128)S(1)} %get-tuple-element.32, f32[1,128,2,128]{3,1,2,0:T(8,128)S(1)} %get-tuple-element.31), kind=kOutput, calls=%fused_computation.25 | convolution fusion | flops 604045312 | bytes 3407872 | tf_op jit(solution)/shard_map/ducb,crba->drua/dot_general | solution.py:78
  6.6 0.8 %fusion.6 = f32[64,2,24,128]{3,0,1,2:T(8,128)S(1)} fusion(f32[1,64,2,64]{3,1,2,0:T(8,128)S(1)} %get-tuple-element.42, f32[1,64,2,64]{3,1,2,0:T(8,128)S(1)} %get-tuple-element.41, f32[1,24,128,64]{2,3,1,0:T(8,128)S(1)} %get-tuple-element.16, f32[1,24,128,64]{2,3,1,0:T(8,128)S(1)} %get-tuple-element.15), kind=kOutput, calls=%fused_computation.24 | convolution fusion | flops 302399488 | bytes 3211264 | tf_op jit(solution)/shard_map/dvca,crua->vdru/dot_general | solution.py:90
  7.6 1.4 %pad_maximum_fusion.1 = f32[32,2,2,24,128]{4,1,0,3,2:T(2,128)S(1)} fusion(f32[32,2,1,24,128]{4,1,0,3,2:T(2,128)S(1)} %bitcast.182, f32[32,2,1,24,128]{4,1,0,3,2:T(2,128)S(1)} %bitcast.181), kind=kLoop, calls=%fused_computation.8 | loop fusion | flops 393216 | bytes 3145728 | tf_op jit(solution)/shard_map/stack | solution.py:99
  9.1 2.0 %copy.55 = f32[32,2,2,24,128]{4,1,3,2,0:T(2,128)} copy(f32[32,2,2,24,128]{4,1,0,3,2:T(2,128)S(1)} %pad_maximum_fusion.1) | data formatting | bytes 3145728 | tf_op jit(solution)/shard_map/stack | solution.py:99
  11.1 7.5 %all-to-all-start = ((f32[32,2,2,24,128]{4,1,3,2,0:T(2,128)}), f32[32,2,2,24,128]{4,1,3,2,0:T(2,128)S(1)}, u32[]{:S(2)}, u32[]{:S(2)}) async-start(f32[32,2,2,24,128]{4,1,3,2,0:T(2,128)} %copy.55), calls=%async_computation | async-start | bytes 3145728 | tf_op jit(solution)/shard_map/all_to_all | solution.py:138
  18.6 4.1 %fusion.16 = (f32[4,256,192]{1,2,0:T(8,128)}, f32[4,256,192]{1,2,0:T(8,128)}) fusion(f32[192]{0:T(256)S(1)} %integer_pow.9, f32[4,256]{1,0:T(4,128)S(1)} %integer_pow.8), kind=kLoop, calls=%fused_computation.36 | loop fusion | flops 393216 | bytes 1577728 | tf_op jit(solution)/shard_map/sin | solution.py:177
  22.9 1.1 %fusion.33 = f32[192,192]{1,0:T(8,128)S(1)} fusion(s32[192]{0:T(256)S(1)} %copy-done.8), kind=kOutput, calls=%fused_computation.71 | convolution fusion | flops 85340160 | bytes 148224 | tf_op jit(solution)/shard_map/ji,ja->ai/dot_general | solution.py:118
  24.0 1.8 %fusion.102 = (f32[192,192]{1,0:T(8,128)}, f32[192,192]{1,0:T(8,128)S(1)}) fusion(s32[192]{0:T(256)S(1)} %copy-done.8), kind=kOutput, calls=%fused_computation.184 | convolution fusion | flops 85377024 | bytes 295680 | tf_op jit(solution)/shard_map/ji,ja->ai/dot_general | solution.py:119
  25.8 4.4 %select_add_fusion = f32[4,256,272]{2,1,0:T(8,128)} fusion(f32[4,256]{1,0:T(4,128)S(1)} %get-tuple-element.34, s32[4,256]{1,0:T(4,128)S(1)} %get-tuple-element.50, f32[4,256]{1,0:T(4,128)S(1)} %get-tuple-element.35, s32[4,256]{1,0:T(4,128)S(1)} %get-tuple-element.46, f32[4,256]{1,0:T(4,128)S(1)} %get-tuple-element.36, s32[4,256]{1,0:T(4,128)S(1)} %get-tuple-element.47, ...), kind=kLoop, calls=%fused_computation.15 | loop fusion | flops 6406144 | bytes 1179648 | tf_op jit(solution)/shard_map/add | solution.py:207
  30.2 25.7 %all-to-all-done = f32[32,2,2,24,128]{4,1,3,2,0:T(2,128)S(1)} async-done(((f32[32,2,2,24,128]{4,1,3,2,0:T(2,128)}), f32[32,2,2,24,128]{4,1,3,2,0:T(2,128)S(1)}, u32[]{:S(2)}, u32[]{:S(2)}) %all-to-all-start) | async-done | bytes 1572896 | tf_op jit(solution)/shard_map/all_to_all | solution.py:138
  55.9 1.3 %reshape.607 = f32[8,4,2,24,256]{4,3,2,1,0:T(8,128)S(1)} reshape(f32[8,4,2,24,2,128]{5,4,3,2,1,0:T(2,128)S(1)} %bitcast.180) | data formatting | bytes 3145728 | tf_op jit(solution)/shard_map/reshape | solution.py:143
  58.1 0.8 %copy-done.3 = f32[192,192]{1,0:T(8,128)S(1)} copy-done((f32[192,192]{1,0:T(8,128)S(1)}, f32[192,192]{1,0:T(8,128)}, u32[]{:S(2)}) %copy-start.3) | copy-done | bytes 147480
  58.9 0.8 %fusion.18 = f32[4,256,192]{1,2,0:T(8,128)S(1)} fusion(f32[4,384,256]{2,1,0:T(8,128)S(1)} %bitcast.174, f32[192,192]{1,0:T(8,128)S(1)} %copy-done.3, f32[192,192]{1,0:T(8,128)S(1)} %fusion.33), kind=kOutput, calls=%fused_computation.46 | convolution fusion | flops 453058560 | bytes 2654208 | tf_op jit(solution)/shard_map/ay,syq->sqa/dot_general | solution.py:170
  59.7 1.0 %add_bitcast_fusion = (f32[1,4,256,192]{2,3,1,0:T(8,128)S(1)}, f32[1,4,256,192]{2,3,1,0:T(8,128)S(1)}) fusion(f32[4,256,192]{1,2,0:T(8,128)S(1)} %copy-done.2, f32[4,256,192]{1,2,0:T(8,128)S(1)} %fusion.18, f32[4,256,192]{1,2,0:T(8,128)S(1)} %copy-done.1, f32[4,384,256]{2,1,0:T(8,128)S(1)} %bitcast.175, f32[192,192]{1,0:T(8,128)S(1)} %fusion.33, ...), kind=kOutput, calls=%fused_computation.33 | convolution fusion | flops 454238208 | bytes 5799936 | tf_op jit(solution)/shard_map/ay,syq->sqa/dot_general | solution.py:171
  60.8 1.4 %fusion.14 = (f32[2,4,8,192]{2,3,1,0:T(8,128)}, f32[2,4,8,192]{2,3,1,0:T(8,128)}) fusion(f32[1,4,256,192]{2,3,1,0:T(8,128)S(1)} %get-tuple-element.12, f32[1,4,256,192]{2,3,1,0:T(8,128)S(1)} %get-tuple-element.11), kind=kLoop, calls=%fused_computation.27 | loop fusion | flops 24576 | bytes 1671168 | tf_op jit(solution)/shard_map/stack | solution.py:181
  62.2 1.4 %copy.40 = f32[2,4,8,192]{3,2,1,0:T(8,128)S(1)} copy(f32[2,4,8,192]{2,3,1,0:T(8,128)} %get-tuple-element.19) | data formatting | bytes 98304 | tf_op jit(solution)/shard_map/slice | solution.py:186
  63.8 1.4 %copy.41 = f32[2,4,8,192]{3,2,1,0:T(8,128)S(1)} copy(f32[2,4,8,192]{2,3,1,0:T(8,128)} %get-tuple-element.20) | data formatting | bytes 98304 | tf_op jit(solution)/shard_map/slice | solution.py:187
  65.2 5.3 %collective-permute-start.1 = (f32[2,4,8,192]{3,2,1,0:T(8,128)S(1)}, f32[2,4,8,192]{3,2,1,0:T(8,128)S(1)}, u32[]{:S(2)}, u32[]{:S(2)}) collective-permute-start(f32[2,4,8,192]{3,2,1,0:T(8,128)S(1)} %copy.41), channel_id=1, source_target_pairs={{1,0},{2,1},{3,2},{4,3},{5,4},{6,5},{7,6},{8,7},{9,8},{10,9},{11,1... | collective-permute-start | bytes 147464 | tf_op jit(solution)/shard_map/ppermute | solution.py:187
  70.6 0.4 collective-permute-done
  71.3 1.2 %copy.42 = f32[2,4,8,192]{2,3,0,1:T(8,128)} copy(f32[2,4,8,192]{3,2,1,0:T(8,128)S(1)} %multiply_reduce_fusion.1) | data formatting | bytes 98304 | tf_op jit(solution)/shard_map/reduce_sum | solution.py:214
  72.7 1.2 %copy.43 = f32[2,4,8,192]{2,3,0,1:T(8,128)} copy(f32[2,4,8,192]{3,2,1,0:T(8,128)S(1)} %multiply_reduce_fusion) | data formatting | bytes 98304 | tf_op jit(solution)/shard_map/reduce_sum | solution.py:215
  73.9 3.3 %maximum_add_fusion = f32[2,4,256,192]{2,3,0,1:T(8,128)S(1)} fusion(f32[2,4,8,192]{2,3,0,1:T(8,128)} %copy.43, f32[2,4,8,192]{2,3,0,1:T(8,128)} %copy.42, f32[4,256,272]{2,1,0:T(8,128)S(1)} %copy-done, f32[256]{0:T(256)S(1)} %pad.1.clone, f32[1,4,256,192]{2,3,1,0:T(8,128)S(1)} %get-tuple-element.11, f32[1,4,256,192]{2,3,1,0:T(8,128)S(1)} %get-tuple-element.12), kind=kOutput, calls=%fused_computation.10 | convolution fusion | flops 1209532416 | bytes 4293632 | tf_op jit(solution)/shard_map/sij,csja->csia/dot_general | solution.py:209
  77.2 1.3 %copy.44 = f32[2,4,256,192]{2,3,1,0:T(8,128)} copy(f32[2,4,256,192]{2,3,0,1:T(8,128)S(1)} %maximum_add_fusion) | data formatting | bytes 3145728 | tf_op jit(solution)/shard_map/add | solution.py:224
  (58 shorter events, 3.3 us)
Async XLA Ops:
  11.1 7.5 %copy-start.5 = (f32[4,256]{1,0:T(4,128)S(1)}, f32[4,256]{1,0:T(4,128)}, u32[]{:S(2)}) copy-start(f32[4,256]{1,0:T(4,128)} %param.8) | copy-start | bytes 12292
  11.1 7.5 %copy-start.7 = (f32[192]{0:T(256)S(1)}, f32[192]{0:T(256)}, u32[]{:S(2)}) copy-start(f32[192]{0:T(256)} %param.9) | copy-start | bytes 2308
  11.1 44.8 %all-to-all-start = ((f32[32,2,2,24,128]{4,1,3,2,0:T(2,128)}), f32[32,2,2,24,128]{4,1,3,2,0:T(2,128)S(1)}, u32[]{:S(2)}, u32[]{:S(2)}) async-start(f32[32,2,2,24,128]{4,1,3,2,0:T(2,128)} %copy.55), calls=%async_computation | async-start | bytes 3145728 | tf_op jit(solution)/shard_map/all_to_all | solution.py:138
  18.6 4.2 %copy-start.6 = (s32[4,256]{1,0:T(4,128)S(1)}, s32[4,256]{1,0:T(4,128)}, u32[]{:S(2)}) copy-start(s32[4,256]{1,0:T(4,128)} %param.10) | copy-start | bytes 12292
  18.6 4.3 %copy-start.4 = (f32[8,4,256]{2,1,0:T(4,128)S(1)}, f32[8,4,256]{2,1,0:T(4,128)}, u32[]{:S(2)}) copy-start(f32[8,4,256]{2,1,0:T(4,128)} %param.11) | copy-start | bytes 98308
  18.6 4.3 %copy-start.8 = (s32[192]{0:T(256)S(1)}, s32[192]{0:T(256)}, u32[]{:S(2)}) copy-start(s32[192]{0:T(256)} %param.7) | copy-start | bytes 2308
  57.9 0.9 %copy-start.3 = (f32[192,192]{1,0:T(8,128)S(1)}, f32[192,192]{1,0:T(8,128)}, u32[]{:S(2)}) copy-start(f32[192,192]{1,0:T(8,128)} %get-tuple-element.53) | copy-start | bytes 442372
  58.0 1.7 %copy-start.1 = (f32[4,256,192]{1,2,0:T(8,128)S(1)}, f32[4,256,192]{1,2,0:T(8,128)}, u32[]{:S(2)}) copy-start(f32[4,256,192]{1,2,0:T(8,128)} %get-tuple-element.8) | copy-start | bytes 2359300
  58.1 1.7 %copy-start.2 = (f32[4,256,192]{1,2,0:T(8,128)S(1)}, f32[4,256,192]{1,2,0:T(8,128)}, u32[]{:S(2)}) copy-start(f32[4,256,192]{1,2,0:T(8,128)} %get-tuple-element.7) | copy-start | bytes 2359300
  60.8 2.9 %copy-start = (f32[4,256,272]{2,1,0:T(8,128)S(1)}, f32[4,256,272]{2,1,0:T(8,128)}, u32[]{:S(2)}) copy-start(f32[4,256,272]{2,1,0:T(8,128)} %select_add_fusion) | copy-start | bytes 3342340
  63.6 7.4 %collective-permute-start = (f32[2,4,8,192]{3,2,1,0:T(8,128)S(1)}, f32[2,4,8,192]{3,2,1,0:T(8,128)S(1)}, u32[]{:S(2)}, u32[]{:S(2)}) collective-permute-start(f32[2,4,8,192]{3,2,1,0:T(8,128)S(1)} %copy.40), channel_id=1, source_target_pairs={{0,1},{1,2},{2,3},{3,4},{4,5},{5,6},{6,7},{7,8},{8,9},{9,10},{10,1... | collective-permute-start | bytes 147464 | tf_op jit(solution)/shard_map/ppermute | solution.py:186
  65.2 7.3 %collective-permute-start.1 = (f32[2,4,8,192]{3,2,1,0:T(8,128)S(1)}, f32[2,4,8,192]{3,2,1,0:T(8,128)S(1)}, u32[]{:S(2)}, u32[]{:S(2)}) collective-permute-start(f32[2,4,8,192]{3,2,1,0:T(8,128)S(1)} %copy.41), channel_id=1, source_target_pairs={{1,0},{2,1},{3,2},{4,3},{5,4},{6,5},{7,6},{8,7},{9,8},{10,9},{11,1... | collective-permute-start | bytes 147464 | tf_op jit(solution)/shard_map/ppermute | solution.py:187

commit v11 on v10

--- a/solution.py
+++ b/solution.py
@@ -3,6 +3,7 @@
 import jax
 import jax.numpy as jnp
 from jax import lax
+from jax.experimental.layout import Layout, with_layout_constraint
 from jax.sharding import PartitionSpec as P
 
 phase_scale = 24.0
@@ -169,6 +170,8 @@
     fold = azimuth_matrix(row_list, 1.0 / math.sqrt(range_len * total_rows))
     az_real = jnp.einsum("ay,syq->sqa", fold[:total_rows], combined, precision=fast)
     az_imag = jnp.einsum("ay,syq->sqa", fold[total_rows:], combined, precision=fast)
+    az_real = with_layout_constraint(az_real, Layout(major_to_minor=(0, 1, 2)))
+    az_imag = with_layout_constraint(az_imag, Layout(major_to_minor=(0, 1, 2)))
 
     phase_angle = phase_scale * jnp.sqrt(
         wavenumber[:, :, None] ** 2 - az_wavenumber[None, None, :] ** 2

time: 78.8 us -> 79 us (level)
  matrix products: 11.5 us -> 15 us
  local copies, waits for them, and re-layouts: 13.5 us -> 10.4 us
  waiting for transfers between devices: 26.2 us -> 25.4 us
    slice x3 -> x0, local copies, waits for them, and re-layouts: 3.05 us -> none  [the longest x1 1.43 us: on_device(): right_rim = lax.ppermute(focused[:, :, :RIM], axes, down)]
    dot_general x1, matrix products: 3.27 us -> 5.51 us  [on_device(): jnp.einsum('sij,csja->csia', band[:, :, RIM:RIM + block_len], focused, pr...]
    all_to_all x1, waiting for transfers between devices: 25.7 us -> 24 us  [on_device(): lax.all_to_all(spectrum, ('pulse', 'rng'), split_axis=0, concat_axis=0, t...]
    sin x1, other arithmetic: 4.12 us -> 5.77 us  [on_device(): jnp.sin(phase_angle)]
    another operation x1, other arithmetic: 1.38 us -> 0.01 us  [on_device(): focused = jnp.stack([focused_real, focused_imag])]
    reduce_sum x1, local copies, waits for them, and re-layouts: 1.16 us -> 0.27 us  [on_device(): jnp.sum(band_left[None, :, :, :, None] * left_rim[:, :, None, :, :], axis=3)]
  transfers between devices with their start and end apart: 3 -> 3, of which waited for: 3 -> 3; matrix products, arithmetic and copies ran while one was open for 18% -> 19% of each run, Pallas kernels for 0% -> 0%
where the time goes in v11:
time: 79 us; the launch traced here: 78.6 us
  waiting for transfers between devices  25.4 us (32%)
  matrix products  15 us (19%)
  other arithmetic  14.3 us (18%)
  starting transfers between devices  13.1 us (17%)
  local copies, waits for them, and re-layouts  10.4 us (13%)
    all_to_all x1, waiting for transfers between devices, on_device(): lax.all_to_all(spectrum, ('pulse', 'rng'), split_axis=0, concat_axis=0, t...  24 us
    all_to_all x1, starting transfers between devices, on_device(): lax.all_to_all(spectrum, ('pulse', 'rng'), split_axis=0, concat_axis=0, t...  7.48 us
    sin x1, other arithmetic, on_device(): jnp.sin(phase_angle)  5.77 us
    ppermute x1, starting transfers between devices, on_device(): right_rim = lax.ppermute(focused[:, :, :RIM], axes, down)  5.53 us
    dot_general x1, matrix products, on_device(): jnp.einsum('sij,csja->csia', band[:, :, RIM:RIM + block_len], focused, pr...  5.51 us
    add x1, other arithmetic, on_device(): band + jnp.where(columns[None, None, :] == target + t, weights[t][:, :, N...  4.46 us
    dot_general x1, matrix products, range_dft_blocks(): jnp.einsum('ducb,crba->drua', stacked_table(outer_len, 1.0), signal, prec...  2.66 us
    reshape x1, local copies, waits for them, and re-layouts, range_dft_blocks(): signal = pair.reshape(2, rows, outer_len, inner_len)  2.41 us
  transfers between devices with their start and end apart: 3, of which 3 were waited for; matrix products, arithmetic and copies ran while one was open for 19% of the time, Pallas kernels for 0%

profile of v11, /device:TPU:0, one launch (start us, length us, event | category | flops | bytes accessed | tf_op | source)
XLA Modules:
  0.0 78.6 jit_solution(9098660954747617429)
XLA Ops:
  0.0 0.3 fusion.74
  1.0 2.4 %reshape.594 = f32[2,24,128,64]{3,2,1,0:T(8,128)S(1)} reshape(f32[2,24,8192]{2,1,0:T(8,128)} %param.6) | data formatting | bytes 3145728 | tf_op jit(solution)/shard_map/reshape | solution.py:78
  3.7 2.7 %fusion.11 = f32[2,24,128,64]{2,3,1,0:T(8,128)S(1)} fusion(f32[2,24,128,64]{3,2,1,0:T(8,128)S(1)} %reshape.594, f32[1,128,2,128]{3,1,2,0:T(8,128)S(1)} %get-tuple-element.32, f32[1,128,2,128]{3,1,2,0:T(8,128)S(1)} %get-tuple-element.31), kind=kOutput, calls=%fused_computation.26 | convolution fusion | flops 604045312 | bytes 3407872 | tf_op jit(solution)/shard_map/ducb,crba->drua/dot_general | solution.py:79
  6.6 0.8 %fusion.6 = f32[64,2,24,128]{3,0,1,2:T(8,128)S(1)} fusion(f32[1,64,2,64]{3,1,2,0:T(8,128)S(1)} %get-tuple-element.42, f32[1,64,2,64]{3,1,2,0:T(8,128)S(1)} %get-tuple-element.41, f32[1,24,128,64]{2,3,1,0:T(8,128)S(1)} %get-tuple-element.18, f32[1,24,128,64]{2,3,1,0:T(8,128)S(1)} %get-tuple-element.17), kind=kOutput, calls=%fused_computation.25 | convolution fusion | flops 302399488 | bytes 3211264 | tf_op jit(solution)/shard_map/dvca,crua->vdru/dot_general | solution.py:91
  7.6 1.4 %pad_maximum_fusion.1 = f32[32,2,2,24,128]{4,1,0,3,2:T(2,128)S(1)} fusion(f32[32,2,1,24,128]{4,1,0,3,2:T(2,128)S(1)} %bitcast.180, f32[32,2,1,24,128]{4,1,0,3,2:T(2,128)S(1)} %bitcast.179), kind=kLoop, calls=%fused_computation.10 | loop fusion | flops 393216 | bytes 3145728 | tf_op jit(solution)/shard_map/stack | solution.py:100
  9.1 2.0 %copy.56 = f32[32,2,2,24,128]{4,1,3,2,0:T(2,128)} copy(f32[32,2,2,24,128]{4,1,0,3,2:T(2,128)S(1)} %pad_maximum_fusion.1) | data formatting | bytes 3145728 | tf_op jit(solution)/shard_map/stack | solution.py:100
  11.1 7.5 %all-to-all-start = ((f32[32,2,2,24,128]{4,1,3,2,0:T(2,128)}), f32[32,2,2,24,128]{4,1,3,2,0:T(2,128)S(1)}, u32[]{:S(2)}, u32[]{:S(2)}) async-start(f32[32,2,2,24,128]{4,1,3,2,0:T(2,128)} %copy.56), calls=%async_computation | async-start | bytes 3145728 | tf_op jit(solution)/shard_map/all_to_all | solution.py:139
  18.6 5.8 %fusion.14 = (f32[4,256,192]{2,1,0:T(8,128)}, f32[4,256,192]{2,1,0:T(8,128)}) fusion(f32[192]{0:T(256)S(1)} %integer_pow.9, f32[4,256]{1,0:T(4,128)S(1)} %integer_pow.8), kind=kLoop, calls=%fused_computation.31 | loop fusion | flops 393216 | bytes 1577728 | tf_op jit(solution)/shard_map/sin | solution.py:180
  24.6 1.1 %fusion.31 = f32[192,192]{1,0:T(8,128)S(1)} fusion(s32[192]{0:T(256)S(1)} %copy-done.7), kind=kOutput, calls=%fused_computation.70 | convolution fusion | flops 85340160 | bytes 148224 | tf_op jit(solution)/shard_map/ji,ja->ai/dot_general | solution.py:119
  25.7 1.8 %fusion.101 = (f32[192,192]{1,0:T(8,128)}, f32[192,192]{1,0:T(8,128)S(1)}) fusion(s32[192]{0:T(256)S(1)} %copy-done.7), kind=kOutput, calls=%fused_computation.184 | convolution fusion | flops 85377024 | bytes 295680 | tf_op jit(solution)/shard_map/ji,ja->ai/dot_general | solution.py:120
  27.4 4.5 %select_add_fusion = f32[4,256,272]{2,1,0:T(8,128)} fusion(f32[4,256]{1,0:T(4,128)S(1)} %get-tuple-element.34, s32[4,256]{1,0:T(4,128)S(1)} %get-tuple-element.50, f32[4,256]{1,0:T(4,128)S(1)} %get-tuple-element.35, s32[4,256]{1,0:T(4,128)S(1)} %get-tuple-element.46, f32[4,256]{1,0:T(4,128)S(1)} %get-tuple-element.36, s32[4,256]{1,0:T(4,128)S(1)} %get-tuple-element.47, ...), kind=kLoop, calls=%fused_computation.16 | loop fusion | flops 6406144 | bytes 1179648 | tf_op jit(solution)/shard_map/add | solution.py:210
  31.9 24.0 %all-to-all-done = f32[32,2,2,24,128]{4,1,3,2,0:T(2,128)S(1)} async-done(((f32[32,2,2,24,128]{4,1,3,2,0:T(2,128)}), f32[32,2,2,24,128]{4,1,3,2,0:T(2,128)S(1)}, u32[]{:S(2)}, u32[]{:S(2)}) %all-to-all-start) | async-done | bytes 1572896 | tf_op jit(solution)/shard_map/all_to_all | solution.py:139
  56.0 1.3 %reshape.596 = f32[8,4,2,24,256]{4,3,0,1,2:T(8,128)S(1)} reshape(f32[8,4,2,24,2,128]{5,4,3,0,1,2:T(2,128)S(1)} %bitcast.178) | data formatting | bytes 3145728 | tf_op jit(solution)/shard_map/reshape | solution.py:144
  58.0 0.8 copy-done.2
  58.8 1.5 %fusion.16 = f32[4,256,192]{2,1,0:T(8,128)S(1)} fusion(f32[4,384,256]{2,1,0:T(8,128)S(1)} %bitcast.175, f32[192,192]{1,0:T(8,128)S(1)} %copy-done.2, f32[192,192]{1,0:T(8,128)S(1)} %fusion.31), kind=kOutput, calls=%fused_computation.45 | convolution fusion | flops 453058560 | bytes 2654208 | tf_op jit(solution)/shard_map/ay,syq->sqa/dot_general | solution.py:171
  60.3 1.7 %add_bitcast_fusion = (f32[1,4,256,192]{3,2,1,0:T(8,128)S(1)}, f32[1,4,256,192]{3,2,1,0:T(8,128)S(1)}) fusion(f32[4,256,192]{2,1,0:T(8,128)S(1)} %copy-done.1, f32[4,256,192]{2,1,0:T(8,128)S(1)} %fusion.16, f32[4,256,192]{2,1,0:T(8,128)S(1)} %copy-done, f32[4,384,256]{2,1,0:T(8,128)S(1)} %bitcast.176, f32[192,192]{1,0:T(8,128)S(1)} %fusion.31, ...), kind=kOutput, calls=%fused_computation.28 | convolution fusion | flops 454238208 | bytes 5799936 | tf_op jit(solution)/shard_map/ay,syq->sqa/dot_general | solution.py:172
  62.1 0.8 %fusion.100 = (f32[4,8,8]{2,1,0:T(8,128)S(1)}, f32[4,8,8]{2,1,0:T(8,128)S(1)}) fusion(f32[4,256,272]{2,1,0:T(8,128)} %select_add_fusion), kind=kLoop, calls=%fused_computation.183 | loop fusion | bytes 4096 | tf_op jit(solution)/shard_map/slice | solution.py:215
  63.0 5.5 %collective-permute-start.1 = (f32[2,4,8,192]{3,2,1,0:T(8,128)S(1)}, f32[2,4,8,192]{3,2,1,0:T(8,128)S(1)}, u32[]{:S(2)}, u32[]{:S(2)}) collective-permute-start(f32[2,4,8,192]{3,2,1,0:T(8,128)S(1)} %get-tuple-element.14), channel_id=1, source_target_pairs={{1,0},{2,1},{3,2},{4,3},{5,4},{6,5},{7,6},{8,7},{9,8},{10,9},{11,1... | collective-permute-start | bytes 147464 | tf_op jit(solution)/shard_map/ppermute | solution.py:190
  68.5 0.8 %collective-permute-done = f32[2,4,8,192]{3,2,1,0:T(8,128)S(1)} collective-permute-done((f32[2,4,8,192]{3,2,1,0:T(8,128)S(1)}, f32[2,4,8,192]{3,2,1,0:T(8,128)S(1)}, u32[]{:S(2)}, u32[]{:S(2)}) %collective-permute-start) | collective-permute-done | bytes 49184 | tf_op jit(solution)/shard_map/ppermute | solution.py:189
  69.6 0.3 copy.40
  69.9 0.6 collective-permute-done.1
  70.7 1.2 %copy.41 = f32[2,4,8,192]{2,3,0,1:T(8,128)} copy(f32[2,4,8,192]{3,2,1,0:T(8,128)S(1)} %multiply_reduce_fusion) | data formatting | bytes 98304 | tf_op jit(solution)/shard_map/reduce_sum | solution.py:218
  71.8 5.5 %maximum_add_fusion = f32[2,4,256,192]{2,3,0,1:T(8,128)S(1)} fusion(f32[2,4,8,192]{2,3,0,1:T(8,128)} %copy.41, f32[2,4,8,192]{2,3,0,1:T(8,128)S(1)} %copy.40, f32[4,256,272]{2,1,0:T(8,128)} %select_add_fusion, f32[256]{0:T(256)S(1)} %pad.1.clone, f32[1,4,256,192]{3,2,1,0:T(8,128)S(1)} %get-tuple-element.11, f32[1,4,256,192]{3,2,1,0:T(8,128)S(1)} %get-tuple-element.12), kind=kOutput, calls=%fused_computation.12 | convolution fusion | flops 1209532416 | bytes 5030912 | tf_op jit(solution)/shard_map/sij,csja->csia/dot_general | solution.py:212
  77.3 1.3 %copy.42 = f32[2,4,256,192]{2,3,1,0:T(8,128)} copy(f32[2,4,256,192]{2,3,0,1:T(8,128)S(1)} %maximum_add_fusion) | data formatting | bytes 3145728 | tf_op jit(solution)/shard_map/add | solution.py:227
  (53 shorter events, 2.9 us)
Async XLA Ops:
  11.1 7.5 %copy-start.4 = (f32[4,256]{1,0:T(4,128)S(1)}, f32[4,256]{1,0:T(4,128)}, u32[]{:S(2)}) copy-start(f32[4,256]{1,0:T(4,128)} %param.8) | copy-start | bytes 12292
  11.1 7.5 %copy-start.6 = (f32[192]{0:T(256)S(1)}, f32[192]{0:T(256)}, u32[]{:S(2)}) copy-start(f32[192]{0:T(256)} %param.9) | copy-start | bytes 2308
  11.1 44.8 %all-to-all-start = ((f32[32,2,2,24,128]{4,1,3,2,0:T(2,128)}), f32[32,2,2,24,128]{4,1,3,2,0:T(2,128)S(1)}, u32[]{:S(2)}, u32[]{:S(2)}) async-start(f32[32,2,2,24,128]{4,1,3,2,0:T(2,128)} %copy.56), calls=%async_computation | async-start | bytes 3145728 | tf_op jit(solution)/shard_map/all_to_all | solution.py:139
  18.6 5.9 %copy-start.5 = (s32[4,256]{1,0:T(4,128)S(1)}, s32[4,256]{1,0:T(4,128)}, u32[]{:S(2)}) copy-start(s32[4,256]{1,0:T(4,128)} %param.10) | copy-start | bytes 12292
  18.6 5.9 %copy-start.3 = (f32[8,4,256]{2,1,0:T(4,128)S(1)}, f32[8,4,256]{2,1,0:T(4,128)}, u32[]{:S(2)}) copy-start(f32[8,4,256]{2,1,0:T(4,128)} %param.11) | copy-start | bytes 98308
  18.6 6.0 %copy-start.7 = (s32[192]{0:T(256)S(1)}, s32[192]{0:T(256)}, u32[]{:S(2)}) copy-start(s32[192]{0:T(256)} %param.7) | copy-start | bytes 2308
  57.8 0.9 %copy-start.2 = (f32[192,192]{1,0:T(8,128)S(1)}, f32[192,192]{1,0:T(8,128)}, u32[]{:S(2)}) copy-start(f32[192,192]{1,0:T(8,128)} %get-tuple-element.53) | copy-start | bytes 442372
  58.0 2.3 %copy-start = (f32[4,256,192]{2,1,0:T(8,128)S(1)}, f32[4,256,192]{2,1,0:T(8,128)}, u32[]{:S(2)}) copy-start(f32[4,256,192]{2,1,0:T(8,128)} %get-tuple-element.8) | copy-start | bytes 2359300
  58.0 2.3 %copy-start.1 = (f32[4,256,192]{2,1,0:T(8,128)S(1)}, f32[4,256,192]{2,1,0:T(8,128)}, u32[]{:S(2)}) copy-start(f32[4,256,192]{2,1,0:T(8,128)} %get-tuple-element.7) | copy-start | bytes 2359300
  62.0 7.3 %collective-permute-start = (f32[2,4,8,192]{3,2,1,0:T(8,128)S(1)}, f32[2,4,8,192]{3,2,1,0:T(8,128)S(1)}, u32[]{:S(2)}, u32[]{:S(2)}) collective-permute-start(f32[2,4,8,192]{3,2,1,0:T(8,128)S(1)} %get-tuple-element.13), channel_id=1, source_target_pairs={{0,1},{1,2},{2,3},{3,4},{4,5},{5,6},{6,7},{7,8},{8,9},{9,10},{10,1... | collective-permute-start | bytes 147464 | tf_op jit(solution)/shard_map/ppermute | solution.py:189
  63.0 7.4 %collective-permute-start.1 = (f32[2,4,8,192]{3,2,1,0:T(8,128)S(1)}, f32[2,4,8,192]{3,2,1,0:T(8,128)S(1)}, u32[]{:S(2)}, u32[]{:S(2)}) collective-permute-start(f32[2,4,8,192]{3,2,1,0:T(8,128)S(1)} %get-tuple-element.14), channel_id=1, source_target_pairs={{1,0},{2,1},{3,2},{4,3},{5,4},{6,5},{7,6},{8,7},{9,8},{10,9},{11,1... | collective-permute-start | bytes 147464 | tf_op jit(solution)/shard_map/ppermute | solution.py:190

commit v12 on v9

--- a/solution.py
+++ b/solution.py
@@ -181,10 +181,15 @@
     focused = jnp.stack([focused_real, focused_imag])
 
     axes = ("pulse", "rng")
-    up = [(i, (i + 1) % device_count) for i in range(device_count)]
-    down = [(j, i) for i, j in up]
-    left_rim = lax.ppermute(focused[:, :, block_len - RIM:], axes, up)
-    right_rim = lax.ppermute(focused[:, :, :RIM], axes, down)
+    even = position % 2 == 0
+    right_edge = focused[:, :, block_len - RIM:]
+    left_edge = focused[:, :, :RIM]
+    on_chip = [(i, i ^ 1) for i in range(device_count)]
+    across = [(i, (i + 1) % device_count if i % 2 else (i - 1) % device_count) for i in range(device_count)]
+    from_partner = lax.ppermute(jnp.where(even, right_edge, left_edge), axes, on_chip)
+    from_far = lax.ppermute(jnp.where(even, left_edge, right_edge), axes, across)
+    left_rim = jnp.where(even, from_far, from_partner)
+    right_rim = jnp.where(even, from_partner, from_far)
     left_rim = jnp.where(position == 0, jnp.roll(left_rim, 1, axis=1), left_rim)
     right_rim = jnp.where(
         position == device_count - 1, jnp.roll(right_rim, -1, axis=1), right_rim

time: 78.6 us -> 79 us (level)
  starting transfers between devices: 13.1 us -> 10.4 us
  waiting for transfers between devices: 31.1 us -> 33.7 us
  local copies, waits for them, and re-layouts: 12.1 us -> 13.2 us
    ppermute x2, starting transfers between devices: 5.59 us -> 3.06 us  [the longest x1 3.01 us: on_device(): lax.ppermute(jnp.where(even, left_edge, right_edge), axes, across)]
    ppermute x2, waiting for transfers between devices: 1.61 us -> 3.95 us  [the longest x1 3.94 us: on_device(): lax.ppermute(jnp.where(even, left_edge, right_edge), axes, across)]
    unnamed x36 -> x42, local copies, waits for them, and re-layouts: 2.65 us -> 3.67 us
    select_n x1, other arithmetic: 0.97 us -> 0.09 us  [on_device(): left_rim = jnp.where(position == 0, jnp.roll(left_rim, 1, axis=1), left_rim)]
  transfers between devices with their start and end apart: 3 -> 3, of which waited for: 3 -> 2; matrix products, arithmetic and copies ran while one was open for 11% -> 11% of each run, Pallas kernels for 0% -> 0%
where the time goes in v12:
time: 79 us; the launch traced here: 78.7 us
  waiting for transfers between devices  33.7 us (43%)
  local copies, waits for them, and re-layouts  13.2 us (17%)
  matrix products  12.4 us (16%)
  starting transfers between devices  10.4 us (13%)
  other arithmetic  8.49 us (11%)
    all_to_all x1, waiting for transfers between devices, on_device(): lax.all_to_all(spectrum, ('pulse', 'rng'), split_axis=0, concat_axis=0, t...  29.7 us
    all_to_all x1, starting transfers between devices, on_device(): lax.all_to_all(spectrum, ('pulse', 'rng'), split_axis=0, concat_axis=0, t...  7.3 us
    dot_general x1, matrix products, on_device(): return jnp.einsum('sij,csja->csia', band, widened, precision=highest)  4.2 us
    sin x1, other arithmetic, on_device(): jnp.sin(phase_angle)  4.12 us
    ppermute x1, waiting for transfers between devices, on_device(): lax.ppermute(jnp.where(even, left_edge, right_edge), axes, across)  3.94 us
    unnamed x42, local copies, waits for them, and re-layouts  3.67 us
    ppermute x1, starting transfers between devices, on_device(): lax.ppermute(jnp.where(even, left_edge, right_edge), axes, across)  3.01 us
    dot_general x1, matrix products, range_dft_blocks(): jnp.einsum('ducb,crba->drua', stacked_table(outer_len, 1.0), signal, prec...  2.66 us
  transfers between devices with their start and end apart: 3, of which 2 were waited for; matrix products, arithmetic and copies ran while one was open for 11% of the time, Pallas kernels for 0%

profile of v12, /device:TPU:0, one launch (start us, length us, event | category | flops | bytes accessed | tf_op | source)
XLA Modules:
  0.0 78.7 jit_solution(3957816192613634413)
XLA Ops:
  1.0 2.4 %reshape.590 = f32[2,24,128,64]{3,2,1,0:T(8,128)S(1)} reshape(f32[2,24,8192]{2,1,0:T(8,128)} %param.6) | data formatting | bytes 3145728 | tf_op jit(solution)/shard_map/reshape | solution.py:77
  3.7 2.7 %fusion.12 = f32[2,24,128,64]{2,3,1,0:T(8,128)S(1)} fusion(f32[2,24,128,64]{3,2,1,0:T(8,128)S(1)} %reshape.590, f32[1,128,2,128]{3,1,2,0:T(8,128)S(1)} %get-tuple-element.32, f32[1,128,2,128]{3,1,2,0:T(8,128)S(1)} %get-tuple-element.31), kind=kOutput, calls=%fused_computation.14 | convolution fusion | flops 604045312 | bytes 3407872 | tf_op jit(solution)/shard_map/ducb,crba->drua/dot_general | solution.py:78
  6.3 0.3 multiply_subtract_fusion.1
  6.7 0.8 %fusion.6 = f32[64,2,24,128]{3,0,1,2:T(8,128)S(1)} fusion(f32[1,64,2,64]{3,1,2,0:T(8,128)S(1)} %get-tuple-element.42, f32[1,64,2,64]{3,1,2,0:T(8,128)S(1)} %get-tuple-element.41, f32[1,24,128,64]{2,3,1,0:T(8,128)S(1)} %get-tuple-element.16, f32[1,24,128,64]{2,3,1,0:T(8,128)S(1)} %get-tuple-element.15), kind=kOutput, calls=%fused_computation.12 | convolution fusion | flops 302399488 | bytes 3211264 | tf_op jit(solution)/shard_map/dvca,crua->vdru/dot_general | solution.py:90
  7.7 1.4 %pad_maximum_fusion.1 = f32[32,2,2,24,128]{4,1,0,3,2:T(2,128)S(1)} fusion(f32[32,2,1,24,128]{4,1,0,3,2:T(2,128)S(1)} %bitcast.182, f32[32,2,1,24,128]{4,1,0,3,2:T(2,128)S(1)} %bitcast.181), kind=kLoop, calls=%fused_computation.6 | loop fusion | flops 393216 | bytes 3145728 | tf_op jit(solution)/shard_map/stack | solution.py:99
  9.1 2.0 %copy.50 = f32[32,2,2,24,128]{4,1,3,2,0:T(2,128)} copy(f32[32,2,2,24,128]{4,1,0,3,2:T(2,128)S(1)} %pad_maximum_fusion.1) | data formatting | bytes 3145728 | tf_op jit(solution)/shard_map/stack | solution.py:99
  11.2 7.3 %all-to-all-start = ((f32[32,2,2,24,128]{4,1,3,2,0:T(2,128)}), f32[32,2,2,24,128]{4,1,3,2,0:T(2,128)S(1)}, u32[]{:S(2)}, u32[]{:S(2)}) async-start(f32[32,2,2,24,128]{4,1,3,2,0:T(2,128)} %copy.50), calls=%async_computation | async-start | bytes 3145728 | tf_op jit(solution)/shard_map/all_to_all | solution.py:138
  18.6 4.1 %fusion.32 = (f32[4,256,192]{1,2,0:T(8,128)}, f32[4,256,192]{1,2,0:T(8,128)}) fusion(f32[192]{0:T(256)S(1)} %integer_pow.9, f32[4,256]{1,0:T(4,128)S(1)} %integer_pow.8), kind=kLoop, calls=%fused_computation.48 | loop fusion | flops 393216 | bytes 1577728 | tf_op jit(solution)/shard_map/sin | solution.py:177
  22.8 0.6 slice_bitcast_fusion.15
  23.4 1.1 %fusion.66 = f32[192,192]{1,0:T(8,128)S(1)} fusion(s32[192]{0:T(256)S(1)} %copy-done.17), kind=kOutput, calls=%fused_computation.104 | convolution fusion | flops 85340160 | bytes 148224 | tf_op jit(solution)/shard_map/ji,ja->ai/dot_general | solution.py:118
  24.5 1.8 %fusion.135 = (f32[192,192]{1,0:T(8,128)}, f32[192,192]{1,0:T(8,128)S(1)}) fusion(s32[192]{0:T(256)S(1)} %copy-done.17), kind=kOutput, calls=%fused_computation.217 | convolution fusion | flops 85377024 | bytes 295680 | tf_op jit(solution)/shard_map/ji,ja->ai/dot_general | solution.py:119
  26.3 29.7 %all-to-all-done = f32[32,2,2,24,128]{4,1,3,2,0:T(2,128)S(1)} async-done(((f32[32,2,2,24,128]{4,1,3,2,0:T(2,128)}), f32[32,2,2,24,128]{4,1,3,2,0:T(2,128)S(1)}, u32[]{:S(2)}, u32[]{:S(2)}) %all-to-all-start) | async-done | bytes 1572896 | tf_op jit(solution)/shard_map/all_to_all | solution.py:138
  56.0 1.3 %reshape.603 = f32[8,4,2,24,256]{4,3,2,1,0:T(8,128)S(1)} reshape(f32[8,4,2,24,2,128]{5,4,3,2,1,0:T(2,128)S(1)} %bitcast.180) | data formatting | bytes 3145728 | tf_op jit(solution)/shard_map/reshape | solution.py:143
  58.1 0.8 copy-done.6
  58.9 0.8 %fusion.51 = f32[4,256,192]{1,2,0:T(8,128)S(1)} fusion(f32[4,384,256]{2,1,0:T(8,128)S(1)} %bitcast.174, f32[192,192]{1,0:T(8,128)S(1)} %copy-done.6, f32[192,192]{1,0:T(8,128)S(1)} %fusion.66), kind=kOutput, calls=%fused_computation.79 | convolution fusion | flops 453058560 | bytes 2654208 | tf_op jit(solution)/shard_map/ay,syq->sqa/dot_general | solution.py:170
  59.8 1.0 %subtract_bitcast_fusion = (f32[1,4,256,192]{2,3,1,0:T(8,128)S(1)}, f32[1,4,256,192]{2,3,1,0:T(8,128)S(1)}) fusion(f32[4,256,192]{1,2,0:T(8,128)S(1)} %copy-done, f32[4,256,192]{1,2,0:T(8,128)S(1)} %fusion.51, f32[4,256,192]{1,2,0:T(8,128)S(1)} %copy-done.1, f32[4,384,256]{2,1,0:T(8,128)S(1)} %bitcast.175, f32[192,192]{1,0:T(8,128)S(1)} %fusion.66, ...), kind=kOutput, calls=%fused_computation.46 | convolution fusion | flops 454238208 | bytes 5799936 | tf_op jit(solution)/shard_map/ay,syq->sqa/dot_general | solution.py:171
  60.9 0.3 broadcast_select_fusion.4
  61.2 0.6 copy-done.2
  62.0 0.3 copy.25
  62.3 3.0 %collective-permute-start = (f32[2,4,8,192]{3,2,1,0:T(8,128)S(1)}, f32[2,4,8,192]{3,2,1,0:T(8,128)S(1)}, u32[]{:S(2)}, u32[]{:S(2)}) collective-permute-start(f32[2,4,8,192]{3,2,1,0:T(8,128)S(1)} %copy.25), channel_id=1, source_target_pairs={{0,31},{1,2},{2,1},{3,4},{4,3},{5,6},{6,5},{7,8},{8,7},{9,10},{10,... | collective-permute-start | bytes 147464 | tf_op jit(solution)/shard_map/ppermute | solution.py:190
  65.7 3.9 %collective-permute-done = f32[2,4,8,192]{3,2,1,0:T(8,128)S(1)} collective-permute-done((f32[2,4,8,192]{3,2,1,0:T(8,128)S(1)}, f32[2,4,8,192]{3,2,1,0:T(8,128)S(1)}, u32[]{:S(2)}, u32[]{:S(2)}) %collective-permute-start) | collective-permute-done | bytes 49184 | tf_op jit(solution)/shard_map/ppermute | solution.py:190
  72.0 1.0 %copy-done.3 = f32[1,4,256,192]{2,3,1,0:T(8,128)S(1)} copy-done((f32[1,4,256,192]{2,3,1,0:T(8,128)S(1)}, f32[1,4,256,192]{2,3,1,0:T(8,128)}, u32[]{:S(2)}) %copy-start.3) | copy-done | bytes 786456
  73.2 4.2 %fusion.9 = f32[2,4,256,192]{2,3,0,1:T(8,128)S(1)} fusion(f32[4,256]{1,0:T(4,128)S(1)} %get-tuple-element.34, s32[4,256]{1,0:T(4,128)S(1)} %get-tuple-element.50, f32[4,256]{1,0:T(4,128)S(1)} %copy-done.10, s32[4,256]{1,0:T(4,128)S(1)} %get-tuple-element.46, f32[4,256]{1,0:T(4,128)S(1)} %copy-done.11, s32[4,256]{1,0:T(4,128)S(1)} %get-tuple-element.47, ...), kind=kOutput, calls=%fused_computation.13 | convolution fusion | flops 1291116544 | bytes 3309568 | tf_op jit(solution)/shard_map/sij,csja->csia/dot_general | solution.py:214
  77.4 1.2 %copy.38 = f32[2,4,256,192]{2,3,1,0:T(8,128)} copy(f32[2,4,256,192]{2,3,0,1:T(8,128)S(1)} %fusion.9) | data formatting | bytes 3145728 | tf_op jit(solution)/shard_map/sij,csja->csia/transpose | solution.py:214
  (79 shorter events, 5.5 us)
Async XLA Ops:
  11.2 7.4 %copy-start.8 = (f32[4,256]{1,0:T(4,128)S(1)}, f32[4,256]{1,0:T(4,128)}, u32[]{:S(2)}) copy-start(f32[4,256]{1,0:T(4,128)} %param.8) | copy-start | bytes 12292
  11.2 7.4 %copy-start.16 = (f32[192]{0:T(256)S(1)}, f32[192]{0:T(256)}, u32[]{:S(2)}) copy-start(f32[192]{0:T(256)} %param.9) | copy-start | bytes 2308
  11.2 44.8 %all-to-all-start = ((f32[32,2,2,24,128]{4,1,3,2,0:T(2,128)}), f32[32,2,2,24,128]{4,1,3,2,0:T(2,128)S(1)}, u32[]{:S(2)}, u32[]{:S(2)}) async-start(f32[32,2,2,24,128]{4,1,3,2,0:T(2,128)} %copy.50), calls=%async_computation | async-start | bytes 3145728 | tf_op jit(solution)/shard_map/all_to_all | solution.py:138
  18.5 4.2 %copy-start.9 = (s32[4,256]{1,0:T(4,128)S(1)}, s32[4,256]{1,0:T(4,128)}, u32[]{:S(2)}) copy-start(s32[4,256]{1,0:T(4,128)} %param.10) | copy-start | bytes 12292
  18.5 4.3 %copy-start.7 = (f32[8,4,256]{2,1,0:T(4,128)S(1)}, f32[8,4,256]{2,1,0:T(4,128)}, u32[]{:S(2)}) copy-start(f32[8,4,256]{2,1,0:T(4,128)} %param.11) | copy-start | bytes 98308
  18.5 4.9 %copy-start.17 = (s32[192]{0:T(256)S(1)}, s32[192]{0:T(256)}, u32[]{:S(2)}) copy-start(s32[192]{0:T(256)} %param.7) | copy-start | bytes 2308
  58.0 0.9 %copy-start.6 = (f32[192,192]{1,0:T(8,128)S(1)}, f32[192,192]{1,0:T(8,128)}, u32[]{:S(2)}) copy-start(f32[192,192]{1,0:T(8,128)} %get-tuple-element.53) | copy-start | bytes 442372
  58.1 1.7 %copy-start = (f32[4,256,192]{1,2,0:T(8,128)S(1)}, f32[4,256,192]{1,2,0:T(8,128)}, u32[]{:S(2)}) copy-start(f32[4,256,192]{1,2,0:T(8,128)} %get-tuple-element.8) | copy-start | bytes 2359300
  58.1 1.7 %copy-start.1 = (f32[4,256,192]{1,2,0:T(8,128)S(1)}, f32[4,256,192]{1,2,0:T(8,128)}, u32[]{:S(2)}) copy-start(f32[4,256,192]{1,2,0:T(8,128)} %get-tuple-element.7) | copy-start | bytes 2359300
  60.9 0.9 %copy-start.2 = (f32[1,4,256,192]{2,3,1,0:T(8,128)}, f32[1,4,256,192]{2,3,1,0:T(8,128)S(1)}, u32[]{:S(2)}) copy-start(f32[1,4,256,192]{2,3,1,0:T(8,128)S(1)} %get-tuple-element.11) | copy-start | bytes 2359300
  60.9 1.1 %copy-start.4 = (f32[1,4,256,192]{2,3,1,0:T(8,128)}, f32[1,4,256,192]{2,3,1,0:T(8,128)S(1)}, u32[]{:S(2)}) copy-start(f32[1,4,256,192]{2,3,1,0:T(8,128)S(1)} %get-tuple-element.12) | copy-start | bytes 2359300
  62.3 7.3 %collective-permute-start = (f32[2,4,8,192]{3,2,1,0:T(8,128)S(1)}, f32[2,4,8,192]{3,2,1,0:T(8,128)S(1)}, u32[]{:S(2)}, u32[]{:S(2)}) collective-permute-start(f32[2,4,8,192]{3,2,1,0:T(8,128)S(1)} %copy.25), channel_id=1, source_target_pairs={{0,31},{1,2},{2,1},{3,4},{4,3},{5,6},{6,5},{7,8},{8,7},{9,10},{10,... | collective-permute-start | bytes 147464 | tf_op jit(solution)/shard_map/ppermute | solution.py:190
  65.6 4.3 %collective-permute-start.1 = (f32[2,4,8,192]{3,2,1,0:T(8,128)S(1)}, f32[2,4,8,192]{3,2,1,0:T(8,128)S(1)}, u32[]{:S(2)}, u32[]{:S(2)}) collective-permute-start(f32[2,4,8,192]{3,2,1,0:T(8,128)S(1)} %copy.26), channel_id=1, source_target_pairs={{0,1},{1,0},{2,3},{3,2},{4,5},{5,4},{6,7},{7,6},{8,9},{9,8},{10,11... | collective-permute-start | bytes 147464 | tf_op jit(solution)/shard_map/ppermute | solution.py:189
  71.8 1.1 %copy-start.3 = (f32[1,4,256,192]{2,3,1,0:T(8,128)S(1)}, f32[1,4,256,192]{2,3,1,0:T(8,128)}, u32[]{:S(2)}) copy-start(f32[1,4,256,192]{2,3,1,0:T(8,128)} %copy-done.2) | copy-start | bytes 2359300
  71.8 1.4 %copy-start.5 = (f32[1,4,256,192]{2,3,1,0:T(8,128)S(1)}, f32[1,4,256,192]{2,3,1,0:T(8,128)}, u32[]{:S(2)}) copy-start(f32[1,4,256,192]{2,3,1,0:T(8,128)} %copy-done.4) | copy-start | bytes 2359300
  71.9 1.4 %copy-start.10 = (f32[4,256]{1,0:T(4,128)S(1)}, f32[4,256]{1,0:T(4,128)}, u32[]{:S(2)}) copy-start(f32[4,256]{1,0:T(4,128)} %get-tuple-element.35) | copy-start | bytes 12292
  71.9 1.3 %copy-start.11 = (f32[4,256]{1,0:T(4,128)S(1)}, f32[4,256]{1,0:T(4,128)}, u32[]{:S(2)}) copy-start(f32[4,256]{1,0:T(4,128)} %get-tuple-element.36) | copy-start | bytes 12292
  71.9 1.3 %copy-start.12 = (f32[4,256]{1,0:T(4,128)S(1)}, f32[4,256]{1,0:T(4,128)}, u32[]{:S(2)}) copy-start(f32[4,256]{1,0:T(4,128)} %get-tuple-element.37) | copy-start | bytes 12292
  71.9 1.3 %copy-start.13 = (f32[4,256]{1,0:T(4,128)S(1)}, f32[4,256]{1,0:T(4,128)}, u32[]{:S(2)}) copy-start(f32[4,256]{1,0:T(4,128)} %get-tuple-element.38) | copy-start | bytes 12292
  71.9 1.3 %copy-start.14 = (f32[4,256]{1,0:T(4,128)S(1)}, f32[4,256]{1,0:T(4,128)}, u32[]{:S(2)}) copy-start(f32[4,256]{1,0:T(4,128)} %get-tuple-element.39) | copy-start | bytes 12292
  71.9 1.3 %copy-start.15 = (f32[4,256]{1,0:T(4,128)S(1)}, f32[4,256]{1,0:T(4,128)}, u32[]{:S(2)}) copy-start(f32[4,256]{1,0:T(4,128)} %get-tuple-element.40) | copy-start | bytes 12292

commit v13 on v9

--- a/solution.py
+++ b/solution.py
@@ -206,7 +206,7 @@
     for t in range(tap_count):
         band = band + jnp.where(columns[None, None, :] == target + t, weights[t][:, :, None], 0.0)
 
-    return jnp.einsum("sij,csja->csia", band, widened, precision=highest)
+    return jnp.einsum("sij,csja->csia", band, widened, precision=fast)
 
 
 def solution(mesh):

time: 78.6 us -> 77.1 us (0.981)
  matrix products: 12.4 us -> 11.1 us
    dot_general x1, matrix products: 4.19 us -> 2.88 us  [on_device(): return jnp.einsum('sij,csja->csia', band, widened, precision=fast)]
  transfers between devices with their start and end apart: 3 -> 3, of which waited for: 3 -> 2; matrix products, arithmetic and copies ran while one was open for 11% -> 11% of each run, Pallas kernels for 0% -> 0%
where the time goes in v13:
time: 77.1 us; the launch traced here: 76.9 us
  waiting for transfers between devices  31.1 us (40%)
  starting transfers between devices  12.8 us (17%)
  local copies, waits for them, and re-layouts  12.1 us (16%)
  matrix products  11.1 us (14%)
  other arithmetic  9.23 us (12%)
    all_to_all x1, waiting for transfers between devices, on_device(): lax.all_to_all(spectrum, ('pulse', 'rng'), split_axis=0, concat_axis=0, t...  29.5 us
    all_to_all x1, starting transfers between devices, on_device(): lax.all_to_all(spectrum, ('pulse', 'rng'), split_axis=0, concat_axis=0, t...  7.48 us
    ppermute x1, starting transfers between devices, on_device(): right_rim = lax.ppermute(focused[:, :, :RIM], axes, down)  5.34 us
    sin x1, other arithmetic, on_device(): jnp.sin(phase_angle)  4.14 us
    dot_general x1, matrix products, on_device(): return jnp.einsum('sij,csja->csia', band, widened, precision=fast)  2.88 us
    dot_general x1, matrix products, range_dft_blocks(): jnp.einsum('ducb,crba->drua', stacked_table(outer_len, 1.0), signal, prec...  2.66 us
    unnamed x36, local copies, waits for them, and re-layouts  2.65 us
    reshape x1, local copies, waits for them, and re-layouts, range_dft_blocks(): signal = pair.reshape(2, rows, outer_len, inner_len)  2.41 us
  transfers between devices with their start and end apart: 3, of which 2 were waited for; matrix products, arithmetic and copies ran while one was open for 11% of the time, Pallas kernels for 0%

profile of v13, /device:TPU:0, one launch (start us, length us, event | category | flops | bytes accessed | tf_op | source)
XLA Modules:
  0.0 76.9 jit_solution(10023735247791441388)
XLA Ops:
  1.0 2.4 %reshape.590 = f32[2,24,128,64]{3,2,1,0:T(8,128)S(1)} reshape(f32[2,24,8192]{2,1,0:T(8,128)} %param.6) | data formatting | bytes 3145728 | tf_op jit(solution)/shard_map/reshape | solution.py:77
  3.7 2.7 %fusion.12 = f32[2,24,128,64]{2,3,1,0:T(8,128)S(1)} fusion(f32[2,24,128,64]{3,2,1,0:T(8,128)S(1)} %reshape.590, f32[1,128,2,128]{3,1,2,0:T(8,128)S(1)} %get-tuple-element.30, f32[1,128,2,128]{3,1,2,0:T(8,128)S(1)} %get-tuple-element.29), kind=kOutput, calls=%fused_computation.14 | convolution fusion | flops 604045312 | bytes 3407872 | tf_op jit(solution)/shard_map/ducb,crba->drua/dot_general | solution.py:78
  6.3 0.3 multiply_subtract_fusion.1
  6.7 0.8 %fusion.6 = f32[64,2,24,128]{3,0,1,2:T(8,128)S(1)} fusion(f32[1,64,2,64]{3,1,2,0:T(8,128)S(1)} %get-tuple-element.40, f32[1,64,2,64]{3,1,2,0:T(8,128)S(1)} %get-tuple-element.39, f32[1,24,128,64]{2,3,1,0:T(8,128)S(1)} %get-tuple-element.16, f32[1,24,128,64]{2,3,1,0:T(8,128)S(1)} %get-tuple-element.15), kind=kOutput, calls=%fused_computation.12 | convolution fusion | flops 302399488 | bytes 3211264 | tf_op jit(solution)/shard_map/dvca,crua->vdru/dot_general | solution.py:90
  7.7 1.4 %pad_maximum_fusion.1 = f32[32,2,2,24,128]{4,1,0,3,2:T(2,128)S(1)} fusion(f32[32,2,1,24,128]{4,1,0,3,2:T(2,128)S(1)} %bitcast.182, f32[32,2,1,24,128]{4,1,0,3,2:T(2,128)S(1)} %bitcast.181), kind=kLoop, calls=%fused_computation.6 | loop fusion | flops 393216 | bytes 3145728 | tf_op jit(solution)/shard_map/stack | solution.py:99
  9.1 2.0 %copy.44 = f32[32,2,2,24,128]{4,1,3,2,0:T(2,128)} copy(f32[32,2,2,24,128]{4,1,0,3,2:T(2,128)S(1)} %pad_maximum_fusion.1) | data formatting | bytes 3145728 | tf_op jit(solution)/shard_map/stack | solution.py:99
  11.2 7.5 %all-to-all-start = ((f32[32,2,2,24,128]{4,1,3,2,0:T(2,128)}), f32[32,2,2,24,128]{4,1,3,2,0:T(2,128)S(1)}, u32[]{:S(2)}, u32[]{:S(2)}) async-start(f32[32,2,2,24,128]{4,1,3,2,0:T(2,128)} %copy.44), calls=%async_computation | async-start | bytes 3145728 | tf_op jit(solution)/shard_map/all_to_all | solution.py:138
  18.7 4.1 %fusion.32 = (f32[4,256,192]{1,2,0:T(8,128)}, f32[4,256,192]{1,2,0:T(8,128)}) fusion(f32[192]{0:T(256)S(1)} %integer_pow.9, f32[4,256]{1,0:T(4,128)S(1)} %integer_pow.8), kind=kLoop, calls=%fused_computation.48 | loop fusion | flops 393216 | bytes 1577728 | tf_op jit(solution)/shard_map/sin | solution.py:177
  23.0 0.6 slice_bitcast_fusion.15
  23.6 1.1 %fusion.66 = f32[192,192]{1,0:T(8,128)S(1)} fusion(s32[192]{0:T(256)S(1)} %copy-done.16), kind=kOutput, calls=%fused_computation.100 | convolution fusion | flops 85340160 | bytes 148224 | tf_op jit(solution)/shard_map/ji,ja->ai/dot_general | solution.py:118
  24.7 1.8 %fusion.135 = (f32[192,192]{1,0:T(8,128)}, f32[192,192]{1,0:T(8,128)S(1)}) fusion(s32[192]{0:T(256)S(1)} %copy-done.16), kind=kOutput, calls=%fused_computation.213 | convolution fusion | flops 85377024 | bytes 295680 | tf_op jit(solution)/shard_map/ji,ja->ai/dot_general | solution.py:119
  26.5 29.5 %all-to-all-done = f32[32,2,2,24,128]{4,1,3,2,0:T(2,128)S(1)} async-done(((f32[32,2,2,24,128]{4,1,3,2,0:T(2,128)}), f32[32,2,2,24,128]{4,1,3,2,0:T(2,128)S(1)}, u32[]{:S(2)}, u32[]{:S(2)}) %all-to-all-start) | async-done | bytes 1572896 | tf_op jit(solution)/shard_map/all_to_all | solution.py:138
  56.0 1.3 %reshape.603 = f32[8,4,2,24,256]{4,3,2,1,0:T(8,128)S(1)} reshape(f32[8,4,2,24,2,128]{5,4,3,2,1,0:T(2,128)S(1)} %bitcast.180) | data formatting | bytes 3145728 | tf_op jit(solution)/shard_map/reshape | solution.py:143
  58.2 0.8 %copy-done.5 = f32[192,192]{1,0:T(8,128)S(1)} copy-done((f32[192,192]{1,0:T(8,128)S(1)}, f32[192,192]{1,0:T(8,128)}, u32[]{:S(2)}) %copy-start.5) | copy-done | bytes 147480
  58.9 0.8 %fusion.51 = f32[4,256,192]{1,2,0:T(8,128)S(1)} fusion(f32[4,384,256]{2,1,0:T(8,128)S(1)} %bitcast.174, f32[192,192]{1,0:T(8,128)S(1)} %copy-done.5, f32[192,192]{1,0:T(8,128)S(1)} %fusion.66), kind=kOutput, calls=%fused_computation.75 | convolution fusion | flops 453058560 | bytes 2654208 | tf_op jit(solution)/shard_map/ay,syq->sqa/dot_general | solution.py:170
  59.8 1.0 %subtract_bitcast_fusion = (f32[1,4,256,192]{2,3,1,0:T(8,128)S(1)}, f32[1,4,256,192]{2,3,1,0:T(8,128)S(1)}) fusion(f32[4,256,192]{1,2,0:T(8,128)S(1)} %copy-done, f32[4,256,192]{1,2,0:T(8,128)S(1)} %fusion.51, f32[4,256,192]{1,2,0:T(8,128)S(1)} %copy-done.1, f32[4,384,256]{2,1,0:T(8,128)S(1)} %bitcast.175, f32[192,192]{1,0:T(8,128)S(1)} %fusion.66, ...), kind=kOutput, calls=%fused_computation.46 | convolution fusion | flops 454238208 | bytes 5799936 | tf_op jit(solution)/shard_map/ay,syq->sqa/dot_general | solution.py:171
  61.1 0.6 copy-done.2
  62.4 5.3 %collective-permute-start.1 = (f32[2,4,8,192]{3,2,1,0:T(8,128)S(1)}, f32[2,4,8,192]{3,2,1,0:T(8,128)S(1)}, u32[]{:S(2)}, u32[]{:S(2)}) collective-permute-start(f32[2,4,8,192]{3,2,1,0:T(8,128)S(1)} %copy.28), channel_id=1, source_target_pairs={{1,0},{2,1},{3,2},{4,3},{5,4},{6,5},{7,6},{8,7},{9,8},{10,9},{11,1... | collective-permute-start | bytes 147464 | tf_op jit(solution)/shard_map/ppermute | solution.py:187
  67.7 1.6 %collective-permute-done = f32[2,4,8,192]{3,2,1,0:T(8,128)S(1)} collective-permute-done((f32[2,4,8,192]{3,2,1,0:T(8,128)S(1)}, f32[2,4,8,192]{3,2,1,0:T(8,128)S(1)}, u32[]{:S(2)}, u32[]{:S(2)}) %collective-permute-start) | collective-permute-done | bytes 49184 | tf_op jit(solution)/shard_map/ppermute | solution.py:186
  70.2 1.0 %broadcast_select_fusion.1 = f32[2,4,8,192]{2,3,1,0:T(8,128)} fusion(f32[2,4,8,192]{2,3,1,0:T(8,128)S(1)} %copy.26, f32[2,4,8,192]{2,3,1,0:T(8,128)S(1)} %copy.27, pred[]{:T(512)S(6)} %eq.66), kind=kLoop, calls=%fused_computation.72 | loop fusion | flops 12288 | bytes 147457 | tf_op jit(solution)/shard_map/jit(_where)/select_n | solution.py:188
  71.6 0.7 copy-done.3
  72.4 0.3 copy-done.4
  72.7 2.9 %fusion.9 = f32[2,4,256,192]{2,3,0,1:T(8,128)S(1)} fusion(f32[4,256]{1,0:T(4,128)S(1)} %get-tuple-element.32, s32[4,256]{1,0:T(4,128)S(1)} %get-tuple-element.48, f32[4,256]{1,0:T(4,128)S(1)} %copy-done.9, s32[4,256]{1,0:T(4,128)S(1)} %get-tuple-element.44, f32[4,256]{1,0:T(4,128)S(1)} %copy-done.10, s32[4,256]{1,0:T(4,128)S(1)} %get-tuple-element.45, ...), kind=kOutput, calls=%fused_computation.13 | convolution fusion | flops 649388032 | bytes 3309568 | tf_op jit(solution)/shard_map/sij,csja->csia/dot_general | solution.py:209
  75.6 1.2 %copy.32 = f32[2,4,256,192]{2,3,1,0:T(8,128)} copy(f32[2,4,256,192]{2,3,0,1:T(8,128)S(1)} %fusion.9) | data formatting | bytes 3145728 | tf_op jit(solution)/shard_map/sij,csja->csia/transpose | solution.py:209
  (72 shorter events, 4.5 us)
Async XLA Ops:
  11.2 7.5 %copy-start.7 = (f32[4,256]{1,0:T(4,128)S(1)}, f32[4,256]{1,0:T(4,128)}, u32[]{:S(2)}) copy-start(f32[4,256]{1,0:T(4,128)} %param.8) | copy-start | bytes 12292
  11.2 7.5 %copy-start.15 = (f32[192]{0:T(256)S(1)}, f32[192]{0:T(256)}, u32[]{:S(2)}) copy-start(f32[192]{0:T(256)} %param.9) | copy-start | bytes 2308
  11.2 44.8 %all-to-all-start = ((f32[32,2,2,24,128]{4,1,3,2,0:T(2,128)}), f32[32,2,2,24,128]{4,1,3,2,0:T(2,128)S(1)}, u32[]{:S(2)}, u32[]{:S(2)}) async-start(f32[32,2,2,24,128]{4,1,3,2,0:T(2,128)} %copy.44), calls=%async_computation | async-start | bytes 3145728 | tf_op jit(solution)/shard_map/all_to_all | solution.py:138
  18.7 4.2 %copy-start.8 = (s32[4,256]{1,0:T(4,128)S(1)}, s32[4,256]{1,0:T(4,128)}, u32[]{:S(2)}) copy-start(s32[4,256]{1,0:T(4,128)} %param.10) | copy-start | bytes 12292
  18.7 4.3 %copy-start.6 = (f32[8,4,256]{2,1,0:T(4,128)S(1)}, f32[8,4,256]{2,1,0:T(4,128)}, u32[]{:S(2)}) copy-start(f32[8,4,256]{2,1,0:T(4,128)} %param.11) | copy-start | bytes 98308
  18.7 4.9 %copy-start.16 = (s32[192]{0:T(256)S(1)}, s32[192]{0:T(256)}, u32[]{:S(2)}) copy-start(s32[192]{0:T(256)} %param.7) | copy-start | bytes 2308
  58.0 0.9 %copy-start.5 = (f32[192,192]{1,0:T(8,128)S(1)}, f32[192,192]{1,0:T(8,128)}, u32[]{:S(2)}) copy-start(f32[192,192]{1,0:T(8,128)} %get-tuple-element.51) | copy-start | bytes 442372
  58.1 1.7 %copy-start = (f32[4,256,192]{1,2,0:T(8,128)S(1)}, f32[4,256,192]{1,2,0:T(8,128)}, u32[]{:S(2)}) copy-start(f32[4,256,192]{1,2,0:T(8,128)} %get-tuple-element.8) | copy-start | bytes 2359300
  58.1 1.7 %copy-start.1 = (f32[4,256,192]{1,2,0:T(8,128)S(1)}, f32[4,256,192]{1,2,0:T(8,128)}, u32[]{:S(2)}) copy-start(f32[4,256,192]{1,2,0:T(8,128)} %get-tuple-element.7) | copy-start | bytes 2359300
  60.9 0.9 %copy-start.2 = (f32[1,4,256,192]{2,3,1,0:T(8,128)}, f32[1,4,256,192]{2,3,1,0:T(8,128)S(1)}, u32[]{:S(2)}) copy-start(f32[1,4,256,192]{2,3,1,0:T(8,128)S(1)} %get-tuple-element.12) | copy-start | bytes 2359300
  62.0 7.3 %collective-permute-start = (f32[2,4,8,192]{3,2,1,0:T(8,128)S(1)}, f32[2,4,8,192]{3,2,1,0:T(8,128)S(1)}, u32[]{:S(2)}, u32[]{:S(2)}) collective-permute-start(f32[2,4,8,192]{3,2,1,0:T(8,128)S(1)} %copy.25), channel_id=1, source_target_pairs={{0,1},{1,2},{2,3},{3,4},{4,5},{5,6},{6,7},{7,8},{8,9},{9,10},{10,1... | collective-permute-start | bytes 147464 | tf_op jit(solution)/shard_map/ppermute | solution.py:186
  62.4 7.3 %collective-permute-start.1 = (f32[2,4,8,192]{3,2,1,0:T(8,128)S(1)}, f32[2,4,8,192]{3,2,1,0:T(8,128)S(1)}, u32[]{:S(2)}, u32[]{:S(2)}) collective-permute-start(f32[2,4,8,192]{3,2,1,0:T(8,128)S(1)} %copy.28), channel_id=1, source_target_pairs={{1,0},{2,1},{3,2},{4,3},{5,4},{6,5},{7,6},{8,7},{9,8},{10,9},{11,1... | collective-permute-start | bytes 147464 | tf_op jit(solution)/shard_map/ppermute | solution.py:187
  71.2 1.1 %copy-start.3 = (f32[1,4,256,192]{2,3,1,0:T(8,128)S(1)}, f32[1,4,256,192]{2,3,1,0:T(8,128)}, u32[]{:S(2)}) copy-start(f32[1,4,256,192]{2,3,1,0:T(8,128)} %copy-done.2) | copy-start | bytes 2359300
  71.2 1.1 %copy-start.9 = (f32[4,256]{1,0:T(4,128)S(1)}, f32[4,256]{1,0:T(4,128)}, u32[]{:S(2)}) copy-start(f32[4,256]{1,0:T(4,128)} %get-tuple-element.33) | copy-start | bytes 12292
  71.2 1.1 %copy-start.10 = (f32[4,256]{1,0:T(4,128)S(1)}, f32[4,256]{1,0:T(4,128)}, u32[]{:S(2)}) copy-start(f32[4,256]{1,0:T(4,128)} %get-tuple-element.34) | copy-start | bytes 12292
  71.2 1.1 %copy-start.11 = (f32[4,256]{1,0:T(4,128)S(1)}, f32[4,256]{1,0:T(4,128)}, u32[]{:S(2)}) copy-start(f32[4,256]{1,0:T(4,128)} %get-tuple-element.35) | copy-start | bytes 12292
  71.2 1.1 %copy-start.12 = (f32[4,256]{1,0:T(4,128)S(1)}, f32[4,256]{1,0:T(4,128)}, u32[]{:S(2)}) copy-start(f32[4,256]{1,0:T(4,128)} %get-tuple-element.36) | copy-start | bytes 12292
  71.2 1.1 %copy-start.13 = (f32[4,256]{1,0:T(4,128)S(1)}, f32[4,256]{1,0:T(4,128)}, u32[]{:S(2)}) copy-start(f32[4,256]{1,0:T(4,128)} %get-tuple-element.37) | copy-start | bytes 12292
  71.2 1.1 %copy-start.14 = (f32[4,256]{1,0:T(4,128)S(1)}, f32[4,256]{1,0:T(4,128)}, u32[]{:S(2)}) copy-start(f32[4,256]{1,0:T(4,128)} %get-tuple-element.38) | copy-start | bytes 12292
  71.5 1.2 %copy-start.4 = (f32[2,4,8,192]{2,3,1,0:T(8,128)S(1)}, f32[2,4,8,192]{2,3,1,0:T(8,128)}, u32[]{:S(2)}) copy-start(f32[2,4,8,192]{2,3,1,0:T(8,128)} %broadcast_select_fusion.1) | copy-start | bytes 147460

commit v14 on v13

--- a/solution.py
+++ b/solution.py
@@ -135,10 +135,11 @@
     lane_pos = lax.axis_index("rng")
 
     spectrum = range_dft_blocks(echoes, device_count, block_len, lane_pos, range_len)
+    pieces = spectrum.shape[1]
+    spectrum = spectrum.reshape(device_count, pieces * 2 * rows_here, block_len // pieces)
     spectrum = lax.all_to_all(
         spectrum, ("pulse", "rng"), split_axis=0, concat_axis=0, tiled=True
     )
-    pieces = spectrum.shape[1]
     spectrum = spectrum.reshape(pulse_count, lane_count, pieces, 2, rows_here, block_len // pieces)
     spectrum = jnp.transpose(spectrum, (0, 1, 3, 4, 2, 5)).reshape(
         pulse_count, lane_count, 2, rows_here, block_len

time: 77.1 us -> 75.4 us (0.978)
  other arithmetic: 9.23 us -> 6.71 us
    another operation x1, other arithmetic: 1.42 us -> 0.1 us  [range_dft_blocks(): jnp.stack([second[:, 0] * turn_real - second[:, 1] * turn_imag, second[:,...]
    sin x1, other arithmetic: 4.14 us -> 3 us  [on_device(): jnp.sin(phase_angle)]
    reshape x1, local copies, waits for them, and re-layouts: 1.26 us -> 0.14 us  [on_device(): jnp.transpose(spectrum, (0, 1, 3, 4, 2, 5))]
    unnamed x36 -> x35, local copies, waits for them, and re-layouts: 2.65 us -> 3.04 us
  transfers between devices with their start and end apart: 3 -> 3, of which waited for: 2 -> 3; matrix products, arithmetic and copies ran while one was open for 11% -> 10% of each run, Pallas kernels for 0% -> 0%
where the time goes in v14:
time: 75.4 us; the launch traced here: 75.1 us
  waiting for transfers between devices  31.5 us (42%)
  starting transfers between devices  13.1 us (17%)
  matrix products  11.8 us (16%)
  local copies, waits for them, and re-layouts  11.5 us (15%)
  other arithmetic  6.71 us (9%)
    all_to_all x1, waiting for transfers between devices, on_device(): lax.all_to_all(spectrum, ('pulse', 'rng'), split_axis=0, concat_axis=0, t...  29.9 us
    all_to_all x1, starting transfers between devices, on_device(): lax.all_to_all(spectrum, ('pulse', 'rng'), split_axis=0, concat_axis=0, t...  7.48 us
    ppermute x1, starting transfers between devices, on_device(): right_rim = lax.ppermute(focused[:, :, :RIM], axes, down)  5.56 us
    unnamed x35, local copies, waits for them, and re-layouts  3.04 us
    sin x1, other arithmetic, on_device(): jnp.sin(phase_angle)  3 us
    dot_general x1, matrix products, on_device(): return jnp.einsum('sij,csja->csia', band, widened, precision=fast)  2.9 us
    dot_general x1, matrix products, range_dft_blocks(): jnp.einsum('ducb,crba->drua', stacked_table(outer_len, 1.0), signal, prec...  2.66 us
    dot_general x1, matrix products, azimuth_matrix(): fold_imag = jnp.einsum('ji,ja->ai', select, dft_imag, precision=highest)  2.45 us
  transfers between devices with their start and end apart: 3, of which 3 were waited for; matrix products, arithmetic and copies ran while one was open for 10% of the time, Pallas kernels for 0%

profile of v14, /device:TPU:0, one launch (start us, length us, event | category | flops | bytes accessed | tf_op | source)
XLA Modules:
  0.0 75.1 jit_solution(1229044604426675946)
XLA Ops:
  0.0 0.3 fusion.107
  1.0 2.4 %reshape.587 = f32[2,24,128,64]{3,2,1,0:T(8,128)S(1)} reshape(f32[2,24,8192]{2,1,0:T(8,128)} %param.6) | data formatting | bytes 3145728 | tf_op jit(solution)/shard_map/reshape | solution.py:77
  3.7 2.7 %fusion.12 = f32[2,24,128,64]{2,3,1,0:T(8,128)S(1)} fusion(f32[2,24,128,64]{3,2,1,0:T(8,128)S(1)} %reshape.587, f32[1,128,2,128]{3,1,2,0:T(8,128)S(1)} %get-tuple-element.30, f32[1,128,2,128]{3,1,2,0:T(8,128)S(1)} %get-tuple-element.29), kind=kOutput, calls=%fused_computation.15 | convolution fusion | flops 604045312 | bytes 3407872 | tf_op jit(solution)/shard_map/ducb,crba->drua/dot_general | solution.py:78
  6.6 0.8 %fusion.6 = f32[64,2,24,128]{3,0,1,2:T(8,128)S(1)} fusion(f32[1,64,2,64]{3,1,2,0:T(8,128)S(1)} %get-tuple-element.40, f32[1,64,2,64]{3,1,2,0:T(8,128)S(1)} %get-tuple-element.39, f32[1,24,128,64]{2,3,1,0:T(8,128)S(1)} %get-tuple-element.16, f32[1,24,128,64]{2,3,1,0:T(8,128)S(1)} %get-tuple-element.15), kind=kOutput, calls=%fused_computation.13 | convolution fusion | flops 302399488 | bytes 3211264 | tf_op jit(solution)/shard_map/dvca,crua->vdru/dot_general | solution.py:90
  7.7 2.1 %copy.31 = f32[64,2,24,128]{3,2,1,0:T(8,128)} copy(f32[64,2,24,128]{3,0,1,2:T(8,128)S(1)} %pad_maximum_fusion.1) | data formatting | bytes 3145728 | tf_op jit(solution)/shard_map/stack | solution.py:99
  9.8 7.5 %all-to-all-start = ((f32[32,96,128]{2,1,0:T(8,128)}), f32[32,96,128]{2,1,0:T(8,128)S(1)}, u32[]{:S(2)}, u32[]{:S(2)}) async-start(f32[32,96,128]{2,1,0:T(8,128)} %bitcast.17), calls=%async_computation | async-start | bytes 3145728 | tf_op jit(solution)/shard_map/all_to_all | solution.py:140
  17.4 3.0 %fusion.32 = (f32[4,256,192]{1,2,0:T(8,128)S(1)}, f32[4,256,192]{1,2,0:T(8,128)S(1)}) fusion(f32[192]{0:T(256)S(1)} %integer_pow.9, f32[4,256]{1,0:T(4,128)S(1)} %integer_pow.8), kind=kLoop, calls=%fused_computation.49 | loop fusion | flops 393216 | bytes 1577728 | tf_op jit(solution)/shard_map/sin | solution.py:178
  20.5 0.6 slice_bitcast_fusion.16
  21.1 1.1 %fusion.66 = f32[192,192]{1,0:T(8,128)S(1)} fusion(s32[192]{0:T(256)S(1)} %copy-done.16), kind=kOutput, calls=%fused_computation.101 | convolution fusion | flops 85340160 | bytes 148224 | tf_op jit(solution)/shard_map/ji,ja->ai/dot_general | solution.py:118
  22.2 2.5 %fusion.134 = (f32[192,192]{1,0:T(8,128)}, f32[192,192]{1,0:T(8,128)S(1)}) fusion(s32[192]{0:T(256)} %param.7), kind=kOutput, calls=%fused_computation.213 | convolution fusion | flops 85377024 | bytes 295680 | tf_op jit(solution)/shard_map/ji,ja->ai/dot_general | solution.py:119
  24.7 29.9 %all-to-all-done = f32[32,96,128]{2,1,0:T(8,128)S(1)} async-done(((f32[32,96,128]{2,1,0:T(8,128)}), f32[32,96,128]{2,1,0:T(8,128)S(1)}, u32[]{:S(2)}, u32[]{:S(2)}) %all-to-all-start) | async-done | bytes 1572896 | tf_op jit(solution)/shard_map/all_to_all | solution.py:140
  55.7 0.8 %copy-done.5 = f32[192,192]{1,0:T(8,128)S(1)} copy-done((f32[192,192]{1,0:T(8,128)S(1)}, f32[192,192]{1,0:T(8,128)}, u32[]{:S(2)}) %copy-start.5) | copy-done | bytes 147480
  56.5 0.8 %fusion.51 = f32[4,256,192]{1,2,0:T(8,128)S(1)} fusion(f32[4,384,256]{2,1,0:T(8,128)S(1)} %bitcast.180, f32[192,192]{1,0:T(8,128)S(1)} %copy-done.5, f32[192,192]{1,0:T(8,128)S(1)} %fusion.66), kind=kOutput, calls=%fused_computation.76 | convolution fusion | flops 453058560 | bytes 2654208 | tf_op jit(solution)/shard_map/ay,syq->sqa/dot_general | solution.py:171
  57.4 1.0 %subtract_bitcast_fusion = (f32[1,4,256,192]{2,3,1,0:T(8,128)S(1)}, f32[1,4,256,192]{2,3,1,0:T(8,128)S(1)}) fusion(f32[4,256,192]{1,2,0:T(8,128)S(1)} %get-tuple-element.8, f32[4,256,192]{1,2,0:T(8,128)S(1)} %fusion.51, f32[4,256,192]{1,2,0:T(8,128)S(1)} %get-tuple-element.7, f32[4,384,256]{2,1,0:T(8,128)S(1)} %bitcast.181, f32[192,192]{1,0:T(8,128)S(1)} %fusion.66, ...), kind=kOutput, calls=%fused_computation.47 | convolution fusion | flops 454238208 | bytes 5799936 | tf_op jit(solution)/shard_map/ay,syq->sqa/dot_general | solution.py:172
  58.7 0.6 copy-done
  59.5 0.3 copy.38
  59.9 0.3 copy.41
  60.2 5.6 %collective-permute-start.1 = (f32[2,4,8,192]{3,2,1,0:T(8,128)S(1)}, f32[2,4,8,192]{3,2,1,0:T(8,128)S(1)}, u32[]{:S(2)}, u32[]{:S(2)}) collective-permute-start(f32[2,4,8,192]{3,2,1,0:T(8,128)S(1)} %copy.41), channel_id=1, source_target_pairs={{1,0},{2,1},{3,2},{4,3},{5,4},{6,5},{7,6},{8,7},{9,8},{10,9},{11,1... | collective-permute-start | bytes 147464 | tf_op jit(solution)/shard_map/ppermute | solution.py:188
  65.7 1.4 %collective-permute-done = f32[2,4,8,192]{3,2,1,0:T(8,128)S(1)} collective-permute-done((f32[2,4,8,192]{3,2,1,0:T(8,128)S(1)}, f32[2,4,8,192]{3,2,1,0:T(8,128)S(1)}, u32[]{:S(2)}, u32[]{:S(2)}) %collective-permute-start) | collective-permute-done | bytes 49184 | tf_op jit(solution)/shard_map/ppermute | solution.py:187
  68.2 1.0 %broadcast_select_fusion.1 = f32[2,4,8,192]{2,3,1,0:T(8,128)} fusion(f32[2,4,8,192]{2,3,1,0:T(8,128)S(1)} %copy.39, f32[2,4,8,192]{2,3,1,0:T(8,128)S(1)} %copy.40, pred[]{:T(512)S(6)} %eq.66), kind=kLoop, calls=%fused_computation.73 | loop fusion | flops 12288 | bytes 147457 | tf_op jit(solution)/shard_map/jit(_where)/select_n | solution.py:189
  69.6 0.7 copy-done.1
  70.6 0.3 copy-done.4
  70.9 2.9 %fusion.9 = f32[2,4,256,192]{2,3,0,1:T(8,128)S(1)} fusion(f32[4,256]{1,0:T(4,128)S(1)} %get-tuple-element.32, s32[4,256]{1,0:T(4,128)S(1)} %get-tuple-element.48, f32[4,256]{1,0:T(4,128)S(1)} %copy-done.9, s32[4,256]{1,0:T(4,128)S(1)} %get-tuple-element.44, f32[4,256]{1,0:T(4,128)S(1)} %copy-done.10, s32[4,256]{1,0:T(4,128)S(1)} %get-tuple-element.45, ...), kind=kOutput, calls=%fused_computation.14 | convolution fusion | flops 649388032 | bytes 3309568 | tf_op jit(solution)/shard_map/sij,csja->csia/dot_general | solution.py:210
  73.8 1.2 %copy.45 = f32[2,4,256,192]{2,3,1,0:T(8,128)} copy(f32[2,4,256,192]{2,3,0,1:T(8,128)S(1)} %fusion.9) | data formatting | bytes 3145728 | tf_op jit(solution)/shard_map/sij,csja->csia/transpose | solution.py:210
  (72 shorter events, 4.8 us)
Async XLA Ops:
  9.8 7.5 %copy-start.7 = (f32[4,256]{1,0:T(4,128)S(1)}, f32[4,256]{1,0:T(4,128)}, u32[]{:S(2)}) copy-start(f32[4,256]{1,0:T(4,128)} %param.8) | copy-start | bytes 12292
  9.8 7.5 %copy-start.15 = (f32[192]{0:T(256)S(1)}, f32[192]{0:T(256)}, u32[]{:S(2)}) copy-start(f32[192]{0:T(256)} %param.9) | copy-start | bytes 2308
  9.8 44.8 %all-to-all-start = ((f32[32,96,128]{2,1,0:T(8,128)}), f32[32,96,128]{2,1,0:T(8,128)S(1)}, u32[]{:S(2)}, u32[]{:S(2)}) async-start(f32[32,96,128]{2,1,0:T(8,128)} %bitcast.17), calls=%async_computation | async-start | bytes 3145728 | tf_op jit(solution)/shard_map/all_to_all | solution.py:140
  17.3 3.1 %copy-start.8 = (s32[4,256]{1,0:T(4,128)S(1)}, s32[4,256]{1,0:T(4,128)}, u32[]{:S(2)}) copy-start(s32[4,256]{1,0:T(4,128)} %param.10) | copy-start | bytes 12292
  17.3 3.2 %copy-start.6 = (f32[8,4,256]{2,1,0:T(4,128)S(1)}, f32[8,4,256]{2,1,0:T(4,128)}, u32[]{:S(2)}) copy-start(f32[8,4,256]{2,1,0:T(4,128)} %param.11) | copy-start | bytes 98308
  17.3 3.8 %copy-start.16 = (s32[192]{0:T(256)S(1)}, s32[192]{0:T(256)}, u32[]{:S(2)}) copy-start(s32[192]{0:T(256)} %param.7) | copy-start | bytes 2308
  55.6 0.9 %copy-start.5 = (f32[192,192]{1,0:T(8,128)S(1)}, f32[192,192]{1,0:T(8,128)}, u32[]{:S(2)}) copy-start(f32[192,192]{1,0:T(8,128)} %get-tuple-element.51) | copy-start | bytes 442372
  58.4 0.9 %copy-start = (f32[1,4,256,192]{2,3,1,0:T(8,128)}, f32[1,4,256,192]{2,3,1,0:T(8,128)S(1)}, u32[]{:S(2)}) copy-start(f32[1,4,256,192]{2,3,1,0:T(8,128)S(1)} %get-tuple-element.11) | copy-start | bytes 2359300
  58.4 1.1 %copy-start.2 = (f32[1,4,256,192]{2,3,1,0:T(8,128)}, f32[1,4,256,192]{2,3,1,0:T(8,128)S(1)}, u32[]{:S(2)}) copy-start(f32[1,4,256,192]{2,3,1,0:T(8,128)S(1)} %get-tuple-element.12) | copy-start | bytes 2359300
  59.8 7.3 %collective-permute-start = (f32[2,4,8,192]{3,2,1,0:T(8,128)S(1)}, f32[2,4,8,192]{3,2,1,0:T(8,128)S(1)}, u32[]{:S(2)}, u32[]{:S(2)}) collective-permute-start(f32[2,4,8,192]{3,2,1,0:T(8,128)S(1)} %copy.38), channel_id=1, source_target_pairs={{0,1},{1,2},{2,3},{3,4},{4,5},{5,6},{6,7},{7,8},{8,9},{9,10},{10,1... | collective-permute-start | bytes 147464 | tf_op jit(solution)/shard_map/ppermute | solution.py:187
  60.2 7.5 %collective-permute-start.1 = (f32[2,4,8,192]{3,2,1,0:T(8,128)S(1)}, f32[2,4,8,192]{3,2,1,0:T(8,128)S(1)}, u32[]{:S(2)}, u32[]{:S(2)}) collective-permute-start(f32[2,4,8,192]{3,2,1,0:T(8,128)S(1)} %copy.41), channel_id=1, source_target_pairs={{1,0},{2,1},{3,2},{4,3},{5,4},{6,5},{7,6},{8,7},{9,8},{10,9},{11,1... | collective-permute-start | bytes 147464 | tf_op jit(solution)/shard_map/ppermute | solution.py:188
  69.2 1.1 %copy-start.1 = (f32[1,4,256,192]{2,3,1,0:T(8,128)S(1)}, f32[1,4,256,192]{2,3,1,0:T(8,128)}, u32[]{:S(2)}) copy-start(f32[1,4,256,192]{2,3,1,0:T(8,128)} %copy-done) | copy-start | bytes 2359300
  69.2 1.4 %copy-start.3 = (f32[1,4,256,192]{2,3,1,0:T(8,128)S(1)}, f32[1,4,256,192]{2,3,1,0:T(8,128)}, u32[]{:S(2)}) copy-start(f32[1,4,256,192]{2,3,1,0:T(8,128)} %copy-done.2) | copy-start | bytes 2359300
  69.2 1.4 %copy-start.9 = (f32[4,256]{1,0:T(4,128)S(1)}, f32[4,256]{1,0:T(4,128)}, u32[]{:S(2)}) copy-start(f32[4,256]{1,0:T(4,128)} %get-tuple-element.33) | copy-start | bytes 12292
  69.2 1.4 %copy-start.10 = (f32[4,256]{1,0:T(4,128)S(1)}, f32[4,256]{1,0:T(4,128)}, u32[]{:S(2)}) copy-start(f32[4,256]{1,0:T(4,128)} %get-tuple-element.34) | copy-start | bytes 12292
  69.2 1.4 %copy-start.11 = (f32[4,256]{1,0:T(4,128)S(1)}, f32[4,256]{1,0:T(4,128)}, u32[]{:S(2)}) copy-start(f32[4,256]{1,0:T(4,128)} %get-tuple-element.35) | copy-start | bytes 12292
  69.2 1.4 %copy-start.12 = (f32[4,256]{1,0:T(4,128)S(1)}, f32[4,256]{1,0:T(4,128)}, u32[]{:S(2)}) copy-start(f32[4,256]{1,0:T(4,128)} %get-tuple-element.36) | copy-start | bytes 12292
  69.2 1.4 %copy-start.13 = (f32[4,256]{1,0:T(4,128)S(1)}, f32[4,256]{1,0:T(4,128)}, u32[]{:S(2)}) copy-start(f32[4,256]{1,0:T(4,128)} %get-tuple-element.37) | copy-start | bytes 12292
  69.2 1.4 %copy-start.14 = (f32[4,256]{1,0:T(4,128)S(1)}, f32[4,256]{1,0:T(4,128)}, u32[]{:S(2)}) copy-start(f32[4,256]{1,0:T(4,128)} %get-tuple-element.38) | copy-start | bytes 12292
  69.5 1.4 %copy-start.4 = (f32[2,4,8,192]{2,3,1,0:T(8,128)S(1)}, f32[2,4,8,192]{2,3,1,0:T(8,128)}, u32[]{:S(2)}) copy-start(f32[2,4,8,192]{2,3,1,0:T(8,128)} %broadcast_select_fusion.1) | copy-start | bytes 147460

commit v15 on v14

--- a/solution.py
+++ b/solution.py
@@ -167,29 +167,61 @@
     combined = jnp.stack([jnp.stack(combined_real), jnp.stack(combined_imag)], axis=1)
     combined = combined.reshape(lane_count, 2 * total_rows, block_len)
 
-    fold = azimuth_matrix(row_list, 1.0 / math.sqrt(range_len * total_rows))
-    az_real = jnp.einsum("ay,syq->sqa", fold[:total_rows], combined, precision=fast)
-    az_imag = jnp.einsum("ay,syq->sqa", fold[total_rows:], combined, precision=fast)
-
-    phase_angle = phase_scale * jnp.sqrt(
-        wavenumber[:, :, None] ** 2 - az_wavenumber[None, None, :] ** 2
-    )
-    phase_real, phase_imag = lax.optimization_barrier(
-        (jnp.cos(phase_angle), jnp.sin(phase_angle))
-    )
-    focused_real = az_real * phase_real - az_imag * phase_imag
-    focused_imag = az_real * phase_imag + az_imag * phase_real
-    focused = jnp.stack([focused_real, focused_imag])
-
     axes = ("pulse", "rng")
     up = [(i, (i + 1) % device_count) for i in range(device_count)]
     down = [(j, i) for i, j in up]
-    left_rim = lax.ppermute(focused[:, :, block_len - RIM:], axes, up)
-    right_rim = lax.ppermute(focused[:, :, :RIM], axes, down)
-    left_rim = jnp.where(position == 0, jnp.roll(left_rim, 1, axis=1), left_rim)
-    right_rim = jnp.where(
-        position == device_count - 1, jnp.roll(right_rim, -1, axis=1), right_rim
-    )
+
+    def beside(left_piece, right_piece, axis):
+        left = lax.ppermute(left_piece, axes, up)
+        right = lax.ppermute(right_piece, axes, down)
+        left = jnp.where(position == 0, jnp.roll(left, 1, axis=axis), left)
+        right = jnp.where(position == device_count - 1, jnp.roll(right, -1, axis=axis), right)
+        return left, right
+
+    wave_left, wave_right = beside(wavenumber[:, block_len - RIM:], wavenumber[:, :RIM], 0)
+    rim_left, rim_right = beside(
+        jnp.swapaxes(combined[:, :, block_len - RIM:], 1, 2),
+        jnp.swapaxes(combined[:, :, :RIM], 1, 2),
+        0,
+    )
+
+    fold = azimuth_matrix(row_list, 1.0 / math.sqrt(range_len * total_rows))
+
+    def focus(az_real, az_imag, wave):
+        phase_angle = phase_scale * jnp.sqrt(
+            wave[:, :, None] ** 2 - az_wavenumber[None, None, :] ** 2
+        )
+        phase_real = jnp.cos(phase_angle)
+        phase_imag = jnp.sin(phase_angle)
+        return jnp.stack(
+            [
+                az_real * phase_real - az_imag * phase_imag,
+                az_real * phase_imag + az_imag * phase_real,
+            ]
+        )
+
+    az_real = jnp.einsum("ay,syq->sqa", fold[:total_rows], combined, precision=fast)
+    az_imag = jnp.einsum("ay,syq->sqa", fold[total_rows:], combined, precision=fast)
+    phase_angle = phase_scale * jnp.sqrt(
+        wavenumber[:, :, None] ** 2 - az_wavenumber[None, None, :] ** 2
+    )
+    phase_real, phase_imag = lax.optimization_barrier(
+        (jnp.cos(phase_angle), jnp.sin(phase_angle))
+    )
+    focused = jnp.stack(
+        [
+            az_real * phase_real - az_imag * phase_imag,
+            az_real * phase_imag + az_imag * phase_real,
+        ]
+    )
+
+    def rim_focus(rim, wave):
+        rim_real = jnp.einsum("ay,sjy->sja", fold[:total_rows], rim, precision=fast)
+        rim_imag = jnp.einsum("ay,sjy->sja", fold[total_rows:], rim, precision=fast)
+        return focus(rim_real, rim_imag, wave)
+
+    left_rim = rim_focus(rim_left, wave_left)
+    right_rim = rim_focus(rim_right, wave_right)
     widened = jnp.concatenate([left_rim, focused, right_rim], axis=2)
 
     tap_count = stolt_coef.shape[0]

time: 75.4 us -> 74.8 us (level)
  waiting for transfers between devices: 31.5 us -> 23.7 us
  matrix products: 11.8 us -> 16 us
  starting transfers between devices: 13.1 us -> 15.5 us
  other arithmetic: 6.71 us -> 7.64 us
    all_to_all x1, waiting for transfers between devices: 29.9 us -> 6.03 us  [on_device(): lax.all_to_all(spectrum, ('pulse', 'rng'), split_axis=0, concat_axis=0, t...]
    ppermute x2 -> x4, waiting for transfers between devices: 1.61 us -> 17.7 us  [the longest x2 12 us: beside(): right = lax.ppermute(right_piece, axes, down)]
    dot_general x0 -> x4, matrix products: none -> 3.16 us  [the longest x2 1.64 us: rim_focus(): rim_imag = jnp.einsum('ay,sjy->sja', fold[total_rows:], rim, precision=fast)]
    unnamed x35 -> x17, local copies, waits for them, and re-layouts: 3.04 us -> 0.1 us
    ppermute x2 -> x4, starting transfers between devices: 5.59 us -> 8.2 us  [the longest x2 8.19 us: beside(): right = lax.ppermute(right_piece, axes, down)]
    transpose x0 -> x3, local copies, waits for them, and re-layouts: none -> 1.98 us  [the longest x2 1.13 us: on_device(): jnp.swapaxes(combined[:, :, block_len - RIM:], 1, 2)]
    add x2, other arithmetic: 0.08 us -> 1.28 us  [on_device(): target + t]
    sin x1, other arithmetic: 3 us -> 4.09 us  [on_device(): jnp.sin(phase_angle)]
  transfers between devices with their start and end apart: 3 -> 5, of which waited for: 3 -> 4; matrix products, arithmetic and copies ran while one was open for 10% -> 22% of each run, Pallas kernels for 0% -> 0%
where the time goes in v15:
time: 74.8 us; the launch traced here: 74.3 us
  waiting for transfers between devices  23.7 us (32%)
  matrix products  16 us (21%)
  starting transfers between devices  15.5 us (21%)
  local copies, waits for them, and re-layouts  11 us (15%)
  other arithmetic  7.64 us (10%)
    ppermute x2, waiting for transfers between devices, beside(): right = lax.ppermute(right_piece, axes, down)  12 us
    ppermute x2, starting transfers between devices, beside(): right = lax.ppermute(right_piece, axes, down)  8.19 us
    all_to_all x1, starting transfers between devices, on_device(): lax.all_to_all(spectrum, ('pulse', 'rng'), split_axis=0, concat_axis=0, t...  7.3 us
    all_to_all x1, waiting for transfers between devices, on_device(): lax.all_to_all(spectrum, ('pulse', 'rng'), split_axis=0, concat_axis=0, t...  6.03 us
    ppermute x2, waiting for transfers between devices, beside(): left = lax.ppermute(left_piece, axes, up)  5.72 us
    sin x1, other arithmetic, on_device(): jnp.sin(phase_angle)  4.09 us
    dot_general x1, matrix products, on_device(): return jnp.einsum('sij,csja->csia', band, widened, precision=fast)  3.62 us
    dot_general x1, matrix products, range_dft_blocks(): jnp.einsum('ducb,crba->drua', stacked_table(outer_len, 1.0), signal, prec...  2.66 us
  transfers between devices with their start and end apart: 5, of which 4 were waited for; matrix products, arithmetic and copies ran while one was open for 22% of the time, Pallas kernels for 0%

profile of v15, /device:TPU:0, one launch (start us, length us, event | category | flops | bytes accessed | tf_op | source)
XLA Modules:
  0.0 74.3 jit_solution(15835373822183118361)
XLA Ops:
  1.0 2.4 %reshape.591 = f32[2,24,128,64]{3,2,1,0:T(8,128)S(1)} reshape(f32[2,24,8192]{2,1,0:T(8,128)} %param.6) | data formatting | bytes 3145728 | tf_op jit(solution)/shard_map/reshape | solution.py:77
  3.7 2.7 %fusion.12 = f32[2,24,128,64]{2,3,1,0:T(8,128)S(1)} fusion(f32[2,24,128,64]{3,2,1,0:T(8,128)S(1)} %reshape.591, f32[1,128,2,128]{3,1,2,0:T(8,128)S(1)} %get-tuple-element.34, f32[1,128,2,128]{3,1,2,0:T(8,128)S(1)} %get-tuple-element.33), kind=kOutput, calls=%fused_computation.13 | convolution fusion | flops 604045312 | bytes 3407872 | tf_op jit(solution)/shard_map/ducb,crba->drua/dot_general | solution.py:78
  6.6 0.8 %fusion.6 = f32[64,2,24,128]{3,0,1,2:T(8,128)S(1)} fusion(f32[1,64,2,64]{3,1,2,0:T(8,128)S(1)} %get-tuple-element.44, f32[1,64,2,64]{3,1,2,0:T(8,128)S(1)} %get-tuple-element.43, f32[1,24,128,64]{2,3,1,0:T(8,128)S(1)} %get-tuple-element.16, f32[1,24,128,64]{2,3,1,0:T(8,128)S(1)} %get-tuple-element.15), kind=kOutput, calls=%fused_computation.11 | convolution fusion | flops 302399488 | bytes 3211264 | tf_op jit(solution)/shard_map/dvca,crua->vdru/dot_general | solution.py:90
  7.8 2.1 %copy.49 = f32[64,2,24,128]{3,2,1,0:T(8,128)} copy(f32[64,2,24,128]{3,0,1,2:T(8,128)S(1)} %pad_maximum_fusion.1) | data formatting | bytes 3145728 | tf_op jit(solution)/shard_map/stack | solution.py:99
  9.8 7.3 %all-to-all-start = ((f32[32,96,128]{2,1,0:T(8,128)}), f32[32,96,128]{2,1,0:T(8,128)S(1)}, u32[]{:S(2)}, u32[]{:S(2)}) async-start(f32[32,96,128]{2,1,0:T(8,128)} %bitcast.17), calls=%async_computation | async-start | bytes 3145728 | tf_op jit(solution)/shard_map/all_to_all | solution.py:140
  17.2 5.2 %collective-permute-start.3 = (f32[4,8]{1,0:T(4,128)S(1)}, f32[4,8]{1,0:T(4,128)S(1)}, u32[]{:S(2)}, u32[]{:S(2)}) collective-permute-start(f32[4,8]{1,0:T(4,128)S(1)} %get-tuple-element.54), channel_id=1, source_target_pairs={{1,0},{2,1},{3,2},{4,3},{5,4},{6,5},{7,6},{8,7},{9,8},{10,9},{11,1... | collective-permute-start | bytes 392 | tf_op jit(solution)/shard_map/ppermute | solution.py:176
  22.5 0.7 broadcast_add_fusion.6
  24.4 1.1 %fusion.59 = f32[192,192]{1,0:T(8,128)S(1)} fusion(s32[192]{0:T(256)S(1)} %copy-done.7), kind=kOutput, calls=%fused_computation.91 | convolution fusion | flops 85340160 | bytes 148224 | tf_op jit(solution)/shard_map/ji,ja->ai/dot_general | solution.py:118
  25.5 1.8 %fusion.144 = (f32[192,192]{1,0:T(8,128)S(1)}, f32[192,192]{1,0:T(8,128)}) fusion(s32[192]{0:T(256)S(1)} %copy-done.7), kind=kOutput, calls=%fused_computation.230 | convolution fusion | flops 85377024 | bytes 295680 | tf_op jit(solution)/shard_map/ji,ja->ai/dot_general | solution.py:119
  27.3 4.1 %fusion.31 = (f32[4,256,192]{1,2,0:T(8,128)}, f32[4,256,192]{1,2,0:T(8,128)}) fusion(f32[192]{0:T(256)S(1)} %integer_pow.19, f32[4,256]{1,0:T(4,128)S(1)} %integer_pow.20), kind=kLoop, calls=%fused_computation.47 | loop fusion | flops 393216 | bytes 1577728 | tf_op jit(solution)/shard_map/sin | solution.py:209
  31.4 12.0 %collective-permute-done.3 = f32[4,8]{1,0:T(4,128)S(1)} collective-permute-done((f32[4,8]{1,0:T(4,128)S(1)}, f32[4,8]{1,0:T(4,128)S(1)}, u32[]{:S(2)}, u32[]{:S(2)}) %collective-permute-start.3) | collective-permute-done | bytes 160 | tf_op jit(solution)/shard_map/ppermute | solution.py:176
  43.4 5.2 %collective-permute-done.1 = f32[4,8]{1,0:T(4,128)S(1)} collective-permute-done((f32[4,8]{1,0:T(4,128)S(1)}, f32[4,8]{1,0:T(4,128)S(1)}, u32[]{:S(2)}, u32[]{:S(2)}) %collective-permute-start.1) | collective-permute-done | bytes 160 | tf_op jit(solution)/shard_map/ppermute | solution.py:175
  48.6 6.0 %all-to-all-done = f32[32,96,128]{2,1,0:T(8,128)S(1)} async-done(((f32[32,96,128]{2,1,0:T(8,128)}), f32[32,96,128]{2,1,0:T(8,128)S(1)}, u32[]{:S(2)}, u32[]{:S(2)}) %all-to-all-start) | async-done | bytes 1572896 | tf_op jit(solution)/shard_map/all_to_all | solution.py:140
  56.0 0.9 %copy.57 = f32[4,8,384]{2,1,0:T(8,128)} copy(f32[4,8,384]{1,2,0:T(8,128)S(1)} %get-tuple-element.18) | data formatting | bytes 98304 | tf_op jit(solution)/shard_map/transpose | solution.py:184
  56.8 3.0 %collective-permute-start.2 = (f32[4,8,384]{2,1,0:T(8,128)}, f32[4,8,384]{2,1,0:T(8,128)}, u32[]{:S(2)}, u32[]{:S(2)}) collective-permute-start(f32[4,8,384]{2,1,0:T(8,128)} %copy.57), channel_id=1, source_target_pairs={{1,0},{2,1},{3,2},{4,3},{5,4},{6,5},{7,6},{8,7},{9,8},{10,9},{11,1... | collective-permute-start | bytes 147464 | tf_op jit(solution)/shard_map/ppermute | solution.py:176
  59.8 0.9 %copy.56 = f32[4,8,384]{2,1,0:T(8,128)} copy(f32[4,8,384]{1,2,0:T(8,128)S(1)} %get-tuple-element.17) | data formatting | bytes 98304 | tf_op jit(solution)/shard_map/transpose | solution.py:183
  60.7 1.9 %fusion.80 = f32[4,256,192]{1,2,0:T(8,128)S(1)} fusion(f32[4,384,256]{2,1,0:T(8,128)S(1)} %bitcast.200, f32[192,192]{1,0:T(8,128)S(1)} %fusion.59, f32[192,192]{1,0:T(8,128)} %get-tuple-element.60), kind=kOutput, calls=%fused_computation.123 | convolution fusion | flops 453058560 | bytes 2654208 | tf_op jit(solution)/shard_map/ay,syq->sqa/dot_general | solution.py:204
  62.6 1.0 %subtract_bitcast_fusion = (f32[1,4,256,192]{2,3,1,0:T(8,128)S(1)}, f32[1,4,256,192]{2,3,1,0:T(8,128)S(1)}) fusion(f32[4,256,192]{1,2,0:T(8,128)S(1)} %fusion.80, f32[4,256,192]{1,2,0:T(8,128)S(1)} %copy-done, f32[4,256,192]{1,2,0:T(8,128)S(1)} %copy-done.1, f32[4,384,256]{2,1,0:T(8,128)S(1)} %bitcast.201, f32[192,192]{1,0:T(8,128)S(1)} %get-tuple-element.59, ...), kind=kOutput, calls=%fused_computation.45 | convolution fusion | flops 454238208 | bytes 5799936 | tf_op jit(solution)/shard_map/ay,syq->sqa/dot_general | solution.py:203
  63.6 0.8 %slice.190 = f32[3,8,384]{2,1,0:T(8,128)S(1)} slice(f32[4,8,384]{2,1,0:T(8,128)} %collective-permute-done.2), slice={[1:4], [0:8], [0:384]} | slice | bytes 73728 | tf_op jit(solution)/shard_map/jit(_roll_static)/slice | solution.py:178
  64.4 0.7 slice.191
  65.1 1.2 %fusion.82 = f32[4,8,192]{2,1,0:T(8,128)S(1)} fusion(f32[192,192]{1,0:T(8,128)S(1)} %get-tuple-element.59, f32[192,192]{1,0:T(8,128)S(1)} %fusion.59, f32[4,8,384]{2,1,0:T(8,128)} %collective-permute-done.2, f32[1,8,384]{2,1,0:T(8,128)S(1)} %slice.191, f32[3,8,384]{2,1,0:T(8,128)S(1)} %slice.190, pred[]{:T(512)S(6)} %eq.69), kind=kOutput, calls=%fused_computation.125 | convolution fusion | flops 14254080 | bytes 417793 | tf_op jit(solution)/shard_map/ay,sjy->sja/dot_general | solution.py:219
  66.3 1.2 %fusion.79 = f32[4,8,192]{2,1,0:T(8,128)S(1)} fusion(f32[192,192]{1,0:T(8,128)S(1)} %fusion.59, f32[192,192]{1,0:T(8,128)S(1)} %copy-done.2, f32[4,8,384]{2,1,0:T(8,128)} %collective-permute-done.2, f32[1,8,384]{2,1,0:T(8,128)S(1)} %slice.191, f32[3,8,384]{2,1,0:T(8,128)S(1)} %slice.190, pred[]{:T(512)S(6)} %eq.69), kind=kOutput, calls=%fused_computation.122 | convolution fusion | flops 14254080 | bytes 417793 | tf_op jit(solution)/shard_map/ay,sjy->sja/dot_general | solution.py:220
  69.4 3.6 %fusion.9 = f32[2,4,256,192]{2,3,0,1:T(8,128)S(1)} fusion(f32[4,256]{1,0:T(4,128)} %get-tuple-element.36, s32[4,256]{1,0:T(4,128)} %get-tuple-element.52, f32[4,256]{1,0:T(4,128)} %get-tuple-element.37, s32[4,256]{1,0:T(4,128)} %get-tuple-element.48, f32[4,256]{1,0:T(4,128)} %get-tuple-element.38, s32[4,256]{1,0:T(4,128)} %get-tuple-element.49, ...), kind=kOutput, calls=%fused_computation.12 | convolution fusion | flops 649388032 | bytes 3309568 | tf_op jit(solution)/shard_map/sij,csja->csia/dot_general | solution.py:242
  73.0 1.2 %copy.61 = f32[2,4,256,192]{2,3,1,0:T(8,128)} copy(f32[2,4,256,192]{2,3,0,1:T(8,128)S(1)} %fusion.9) | data formatting | bytes 3145728 | tf_op jit(solution)/shard_map/sij,csja->csia/transpose | solution.py:242
  (64 shorter events, 6.3 us)
Async XLA Ops:
  9.8 7.3 %copy-start.3 = (f32[4,256]{1,0:T(4,128)S(1)}, f32[4,256]{1,0:T(4,128)}, u32[]{:S(2)}) copy-start(f32[4,256]{1,0:T(4,128)} %param.8) | copy-start | bytes 12292
  9.8 12.6 %copy-start.6 = (f32[192]{0:T(256)S(1)}, f32[192]{0:T(256)}, u32[]{:S(2)}) copy-start(f32[192]{0:T(256)} %param.9) | copy-start | bytes 2308
  9.8 12.7 %copy-start.5 = (s32[4,256]{1,0:T(4,128)S(1)}, s32[4,256]{1,0:T(4,128)}, u32[]{:S(2)}) copy-start(s32[4,256]{1,0:T(4,128)} %param.10) | copy-start | bytes 12292
  9.8 14.0 %copy-start.4 = (f32[8,4,256]{2,1,0:T(4,128)S(1)}, f32[8,4,256]{2,1,0:T(4,128)}, u32[]{:S(2)}) copy-start(f32[8,4,256]{2,1,0:T(4,128)} %param.11) | copy-start | bytes 98308
  9.8 14.6 %copy-start.7 = (s32[192]{0:T(256)S(1)}, s32[192]{0:T(256)}, u32[]{:S(2)}) copy-start(s32[192]{0:T(256)} %param.7) | copy-start | bytes 2308
  9.8 44.8 %all-to-all-start = ((f32[32,96,128]{2,1,0:T(8,128)}), f32[32,96,128]{2,1,0:T(8,128)S(1)}, u32[]{:S(2)}, u32[]{:S(2)}) async-start(f32[32,96,128]{2,1,0:T(8,128)} %bitcast.17), calls=%async_computation | async-start | bytes 3145728 | tf_op jit(solution)/shard_map/all_to_all | solution.py:140
  17.2 26.2 %collective-permute-start.3 = (f32[4,8]{1,0:T(4,128)S(1)}, f32[4,8]{1,0:T(4,128)S(1)}, u32[]{:S(2)}, u32[]{:S(2)}) collective-permute-start(f32[4,8]{1,0:T(4,128)S(1)} %get-tuple-element.54), channel_id=1, source_target_pairs={{1,0},{2,1},{3,2},{4,3},{5,4},{6,5},{7,6},{8,7},{9,8},{10,9},{11,1... | collective-permute-start | bytes 392 | tf_op jit(solution)/shard_map/ppermute | solution.py:176
  22.5 26.2 %collective-permute-start.1 = (f32[4,8]{1,0:T(4,128)S(1)}, f32[4,8]{1,0:T(4,128)S(1)}, u32[]{:S(2)}, u32[]{:S(2)}) collective-permute-start(f32[4,8]{1,0:T(4,128)S(1)} %get-tuple-element.53), channel_id=1, source_target_pairs={{0,1},{1,2},{2,3},{3,4},{4,5},{5,6},{6,7},{7,8},{8,9},{9,10},{10,1... | collective-permute-start | bytes 392 | tf_op jit(solution)/shard_map/ppermute | solution.py:175
  56.8 6.8 %collective-permute-start.2 = (f32[4,8,384]{2,1,0:T(8,128)}, f32[4,8,384]{2,1,0:T(8,128)}, u32[]{:S(2)}, u32[]{:S(2)}) collective-permute-start(f32[4,8,384]{2,1,0:T(8,128)} %copy.57), channel_id=1, source_target_pairs={{1,0},{2,1},{3,2},{4,3},{5,4},{6,5},{7,6},{8,7},{9,8},{10,9},{11,1... | collective-permute-start | bytes 147464 | tf_op jit(solution)/shard_map/ppermute | solution.py:176
  60.7 1.9 %copy-start = (f32[4,256,192]{1,2,0:T(8,128)S(1)}, f32[4,256,192]{1,2,0:T(8,128)}, u32[]{:S(2)}) copy-start(f32[4,256,192]{1,2,0:T(8,128)} %get-tuple-element.8) | copy-start | bytes 2359300
  60.7 1.9 %copy-start.1 = (f32[4,256,192]{1,2,0:T(8,128)S(1)}, f32[4,256,192]{1,2,0:T(8,128)}, u32[]{:S(2)}) copy-start(f32[4,256,192]{1,2,0:T(8,128)} %get-tuple-element.7) | copy-start | bytes 2359300
  60.7 7.3 %collective-permute-start = (f32[4,8,384]{2,1,0:T(8,128)}, f32[4,8,384]{2,1,0:T(8,128)S(1)}, u32[]{:S(2)}, u32[]{:S(2)}) collective-permute-start(f32[4,8,384]{2,1,0:T(8,128)} %copy.56), channel_id=1, source_target_pairs={{0,1},{1,2},{2,3},{3,4},{4,5},{5,6},{6,7},{7,8},{8,9},{9,10},{10,1... | collective-permute-start | bytes 147464 | tf_op jit(solution)/shard_map/ppermute | solution.py:175
  62.6 3.7 %copy-start.2 = (f32[192,192]{1,0:T(8,128)S(1)}, f32[192,192]{1,0:T(8,128)}, u32[]{:S(2)}) copy-start(f32[192,192]{1,0:T(8,128)} %get-tuple-element.60) | copy-start | bytes 442372

commit v16 on v15

--- a/solution.py
+++ b/solution.py
@@ -119,7 +119,7 @@
     fold_imag = jnp.einsum("ji,ja->ai", select, dft_imag, precision=highest)
     top = jnp.concatenate([fold_real, -fold_imag], axis=1)
     bottom = jnp.concatenate([fold_imag, fold_real], axis=1)
-    return jnp.concatenate([top, bottom], axis=0)
+    return top, bottom
 
 
 def on_device(echoes, row_list, wavenumber, az_wavenumber, stolt_offset, stolt_coef):
@@ -185,7 +185,7 @@
         0,
     )
 
-    fold = azimuth_matrix(row_list, 1.0 / math.sqrt(range_len * total_rows))
+    fold_top, fold_bottom = azimuth_matrix(row_list, 1.0 / math.sqrt(range_len * total_rows))
 
     def focus(az_real, az_imag, wave):
         phase_angle = phase_scale * jnp.sqrt(
@@ -200,8 +200,8 @@
             ]
         )
 
-    az_real = jnp.einsum("ay,syq->sqa", fold[:total_rows], combined, precision=fast)
-    az_imag = jnp.einsum("ay,syq->sqa", fold[total_rows:], combined, precision=fast)
+    az_real = jnp.einsum("ay,syq->sqa", fold_top, combined, precision=fast)
+    az_imag = jnp.einsum("ay,syq->sqa", fold_bottom, combined, precision=fast)
     phase_angle = phase_scale * jnp.sqrt(
         wavenumber[:, :, None] ** 2 - az_wavenumber[None, None, :] ** 2
     )
@@ -215,13 +215,12 @@
         ]
     )
 
-    def rim_focus(rim, wave):
-        rim_real = jnp.einsum("ay,sjy->sja", fold[:total_rows], rim, precision=fast)
-        rim_imag = jnp.einsum("ay,sjy->sja", fold[total_rows:], rim, precision=fast)
-        return focus(rim_real, rim_imag, wave)
-
-    left_rim = rim_focus(rim_left, wave_left)
-    right_rim = rim_focus(rim_right, wave_right)
+    rims = jnp.concatenate([rim_left, rim_right], axis=1)
+    rim_real = jnp.einsum("ay,sjy->sja", fold_top, rims, precision=fast)
+    rim_imag = jnp.einsum("ay,sjy->sja", fold_bottom, rims, precision=fast)
+    rims = focus(rim_real, rim_imag, jnp.concatenate([wave_left, wave_right], axis=1))
+    left_rim = rims[:, :, :RIM]
+    right_rim = rims[:, :, RIM:]
     widened = jnp.concatenate([left_rim, focused, right_rim], axis=2)
 
     tap_count = stolt_coef.shape[0]

time: 74.8 us -> 74.2 us (level)
  starting transfers between devices: 15.5 us -> 17.9 us
  matrix products: 16 us -> 13.7 us
    ppermute x2, starting transfers between devices: 8.19 us -> 10.6 us  [beside(): right = lax.ppermute(right_piece, axes, down)]
    dot_general x6 -> x4, matrix products: 6.05 us -> 3.71 us  [the longest x1 1.76 us: on_device(): az_imag = jnp.einsum('ay,syq->sqa', fold_bottom, combined, precision=fast)]
    transpose x3 -> x0, local copies, waits for them, and re-layouts: 1.98 us -> none  [the longest x2 1.13 us: on_device(): jnp.swapaxes(combined[:, :, block_len - RIM:], 1, 2)]
    unnamed x17 -> x19, local copies, waits for them, and re-layouts: 0.1 us -> 1.82 us
    slice x3, local copies, waits for them, and re-layouts: 0.01 us -> 1.48 us  [beside(): left = jnp.where(position == 0, jnp.roll(left, 1, axis=axis), left)]
    slice x4, local copies, waits for them, and re-layouts: 1.49 us -> 0.01 us  [beside(): jnp.roll(right, -1, axis=axis)]
    slice x0 -> x3, local copies, waits for them, and re-layouts: none -> 0.81 us  [the longest x1 0.27 us: on_device(): combined[:, :, block_len - RIM:]]
  transfers between devices with their start and end apart: 5 -> 5, of which waited for: 4 -> 3; matrix products, arithmetic and copies ran while one was open for 22% -> 18% of each run, Pallas kernels for 0% -> 0%
where the time goes in v16:
time: 74.2 us; the launch traced here: 73.8 us
  waiting for transfers between devices  23.7 us (32%)
  starting transfers between devices  17.9 us (24%)
  matrix products  13.7 us (18%)
  local copies, waits for them, and re-layouts  11 us (15%)
  other arithmetic  7.21 us (10%)
    ppermute x2, waiting for transfers between devices, beside(): right = lax.ppermute(right_piece, axes, down)  12.6 us
    ppermute x2, starting transfers between devices, beside(): right = lax.ppermute(right_piece, axes, down)  10.6 us
    all_to_all x1, starting transfers between devices, on_device(): lax.all_to_all(spectrum, ('pulse', 'rng'), split_axis=0, concat_axis=0, t...  7.3 us
    all_to_all x1, waiting for transfers between devices, on_device(): lax.all_to_all(spectrum, ('pulse', 'rng'), split_axis=0, concat_axis=0, t...  5.95 us
    ppermute x2, waiting for transfers between devices, beside(): left = lax.ppermute(left_piece, axes, up)  5.18 us
    sin x1, other arithmetic, on_device(): jnp.sin(phase_angle)  4.1 us
    dot_general x1, matrix products, on_device(): return jnp.einsum('sij,csja->csia', band, widened, precision=fast)  3.61 us
    dot_general x1, matrix products, range_dft_blocks(): jnp.einsum('ducb,crba->drua', stacked_table(outer_len, 1.0), signal, prec...  2.67 us
  transfers between devices with their start and end apart: 5, of which 3 were waited for; matrix products, arithmetic and copies ran while one was open for 18% of the time, Pallas kernels for 0%

profile of v16, /device:TPU:0, one launch (start us, length us, event | category | flops | bytes accessed | tf_op | source)
XLA Modules:
  0.0 73.8 jit_solution(1921236605630370635)
XLA Ops:
  1.0 2.4 %reshape.603 = f32[2,24,128,64]{3,2,1,0:T(8,128)S(1)} reshape(f32[2,24,8192]{2,1,0:T(8,128)} %param.6) | data formatting | bytes 3145728 | tf_op jit(solution)/shard_map/reshape | solution.py:77
  3.7 2.7 %fusion.12 = f32[2,24,128,64]{2,3,1,0:T(8,128)S(1)} fusion(f32[2,24,128,64]{3,2,1,0:T(8,128)S(1)} %reshape.603, f32[1,128,2,128]{3,1,2,0:T(8,128)S(1)} %get-tuple-element.34, f32[1,128,2,128]{3,1,2,0:T(8,128)S(1)} %get-tuple-element.33), kind=kOutput, calls=%fused_computation.13 | convolution fusion | flops 604045312 | bytes 3407872 | tf_op jit(solution)/shard_map/ducb,crba->drua/dot_general | solution.py:78
  6.6 0.8 %fusion.6 = f32[64,2,24,128]{3,0,1,2:T(8,128)S(1)} fusion(f32[1,64,2,64]{3,1,2,0:T(8,128)S(1)} %get-tuple-element.44, f32[1,64,2,64]{3,1,2,0:T(8,128)S(1)} %get-tuple-element.43, f32[1,24,128,64]{2,3,1,0:T(8,128)S(1)} %get-tuple-element.16, f32[1,24,128,64]{2,3,1,0:T(8,128)S(1)} %get-tuple-element.15), kind=kOutput, calls=%fused_computation.11 | convolution fusion | flops 302399488 | bytes 3211264 | tf_op jit(solution)/shard_map/dvca,crua->vdru/dot_general | solution.py:90
  7.8 2.1 %copy.28 = f32[64,2,24,128]{3,2,1,0:T(8,128)} copy(f32[64,2,24,128]{3,0,1,2:T(8,128)S(1)} %pad_maximum_fusion.1) | data formatting | bytes 3145728 | tf_op jit(solution)/shard_map/stack | solution.py:99
  9.8 7.3 %all-to-all-start = ((f32[32,96,128]{2,1,0:T(8,128)}), f32[32,96,128]{2,1,0:T(8,128)S(1)}, u32[]{:S(2)}, u32[]{:S(2)}) async-start(f32[32,96,128]{2,1,0:T(8,128)} %bitcast.17), calls=%async_computation | async-start | bytes 3145728 | tf_op jit(solution)/shard_map/all_to_all | solution.py:140
  17.3 5.2 %collective-permute-start.3 = (f32[4,8]{1,0:T(4,128)S(1)}, f32[4,8]{1,0:T(4,128)S(1)}, u32[]{:S(2)}, u32[]{:S(2)}) collective-permute-start(f32[4,8]{1,0:T(4,128)S(1)} %get-tuple-element.54), channel_id=1, source_target_pairs={{1,0},{2,1},{3,2},{4,3},{5,4},{6,5},{7,6},{8,7},{9,8},{10,9},{11,1... | collective-permute-start | bytes 392 | tf_op jit(solution)/shard_map/ppermute | solution.py:176
  22.5 4.1 %fusion.31 = (f32[4,256,192]{1,2,0:T(8,128)}, f32[4,256,192]{1,2,0:T(8,128)}) fusion(f32[192]{0:T(256)S(1)} %integer_pow.18, f32[4,256]{1,0:T(4,128)S(1)} %integer_pow.19), kind=kLoop, calls=%fused_computation.45 | loop fusion | flops 393216 | bytes 1577728 | tf_op jit(solution)/shard_map/sin | solution.py:209
  26.7 0.6 broadcast_add_fusion.5
  27.3 0.6 slice_bitcast_fusion.16
  28.0 1.1 %fusion.59 = f32[192,192]{1,0:T(8,128)S(1)} fusion(s32[192]{0:T(256)S(1)} %copy-done.7), kind=kOutput, calls=%fused_computation.89 | convolution fusion | flops 85340160 | bytes 148224 | tf_op jit(solution)/shard_map/ji,ja->ai/dot_general | solution.py:118
  29.1 1.8 %fusion.138 = (f32[192,192]{1,0:T(8,128)S(1)}, f32[192,192]{1,0:T(8,128)}) fusion(s32[192]{0:T(256)S(1)} %copy-done.7), kind=kOutput, calls=%fused_computation.222 | convolution fusion | flops 85377024 | bytes 295680 | tf_op jit(solution)/shard_map/ji,ja->ai/dot_general | solution.py:119
  30.8 12.6 %collective-permute-done.3 = f32[4,8]{1,0:T(4,128)S(1)} collective-permute-done((f32[4,8]{1,0:T(4,128)S(1)}, f32[4,8]{1,0:T(4,128)S(1)}, u32[]{:S(2)}, u32[]{:S(2)}) %collective-permute-start.3) | collective-permute-done | bytes 160 | tf_op jit(solution)/shard_map/ppermute | solution.py:176
  43.4 5.2 %collective-permute-done.2 = f32[4,8]{1,0:T(4,128)S(1)} collective-permute-done((f32[4,8]{1,0:T(4,128)S(1)}, f32[4,8]{1,0:T(4,128)S(1)}, u32[]{:S(2)}, u32[]{:S(2)}) %collective-permute-start.2) | collective-permute-done | bytes 160 | tf_op jit(solution)/shard_map/ppermute | solution.py:175
  48.7 6.0 %all-to-all-done = f32[32,96,128]{2,1,0:T(8,128)S(1)} async-done(((f32[32,96,128]{2,1,0:T(8,128)}), f32[32,96,128]{2,1,0:T(8,128)S(1)}, u32[]{:S(2)}, u32[]{:S(2)}) %all-to-all-start) | async-done | bytes 1572896 | tf_op jit(solution)/shard_map/all_to_all | solution.py:140
  56.0 0.9 %copy.57 = f32[4,384,8]{1,2,0:T(8,128)} copy(f32[4,384,8]{2,1,0:T(8,128)S(1)} %get-tuple-element.17) | data formatting | bytes 98304
  56.9 0.9 %copy.58 = f32[4,384,8]{1,2,0:T(8,128)} copy(f32[4,384,8]{2,1,0:T(8,128)S(1)} %get-tuple-element.18) | data formatting | bytes 98304
  57.7 5.3 %collective-permute-start.1 = (f32[4,8,384]{2,1,0:T(8,128)}, f32[4,8,384]{2,1,0:T(8,128)S(1)}, u32[]{:S(2)}, u32[]{:S(2)}) collective-permute-start(f32[4,8,384]{2,1,0:T(8,128)} %bitcast.34), channel_id=1, source_target_pairs={{1,0},{2,1},{3,2},{4,3},{5,4},{6,5},{7,6},{8,7},{9,8},{10,9},{11,1... | collective-permute-start | bytes 147464 | tf_op jit(solution)/shard_map/ppermute | solution.py:176
  63.1 1.8 %fusion.67 = f32[4,256,192]{1,2,0:T(8,128)S(1)} fusion(f32[4,384,256]{2,1,0:T(8,128)S(1)} %bitcast.192, f32[192,192]{1,0:T(8,128)S(1)} %fusion.59, f32[192,192]{1,0:T(8,128)} %get-tuple-element.58), kind=kOutput, calls=%fused_computation.104 | convolution fusion | flops 453058560 | bytes 2654208 | tf_op jit(solution)/shard_map/ay,syq->sqa/dot_general | solution.py:204
  64.9 1.0 %subtract_bitcast_fusion = (f32[1,4,256,192]{2,3,1,0:T(8,128)S(1)}, f32[1,4,256,192]{2,3,1,0:T(8,128)S(1)}) fusion(f32[4,256,192]{1,2,0:T(8,128)S(1)} %fusion.67, f32[4,256,192]{1,2,0:T(8,128)S(1)} %copy-done, f32[4,256,192]{1,2,0:T(8,128)S(1)} %copy-done.1, f32[4,384,256]{2,1,0:T(8,128)S(1)} %bitcast.193, f32[192,192]{1,0:T(8,128)S(1)} %get-tuple-element.57, ...), kind=kOutput, calls=%fused_computation.43 | convolution fusion | flops 454238208 | bytes 5799936 | tf_op jit(solution)/shard_map/ay,syq->sqa/dot_general | solution.py:203
  65.9 0.8 %slice.196 = f32[3,8,384]{2,1,0:T(8,128)S(1)} slice(f32[4,8,384]{2,1,0:T(8,128)} %collective-permute-done), slice={[0:3], [0:8], [0:384]} | slice | bytes 73728 | tf_op jit(solution)/shard_map/jit(_roll_static)/slice | solution.py:177
  66.7 0.7 slice.195
  67.9 0.5 subtract_bitcast_fusion.1
  69.0 3.6 %fusion.9 = f32[2,4,256,192]{2,3,0,1:T(8,128)S(1)} fusion(f32[4,256]{1,0:T(4,128)} %get-tuple-element.36, s32[4,256]{1,0:T(4,128)} %get-tuple-element.52, f32[4,256]{1,0:T(4,128)} %get-tuple-element.37, s32[4,256]{1,0:T(4,128)} %get-tuple-element.48, f32[4,256]{1,0:T(4,128)} %get-tuple-element.38, s32[4,256]{1,0:T(4,128)} %get-tuple-element.49, ...), kind=kOutput, calls=%fused_computation.12 | convolution fusion | flops 649388032 | bytes 3309568 | tf_op jit(solution)/shard_map/sij,csja->csia/dot_general | solution.py:241
  72.6 1.2 %copy.40 = f32[2,4,256,192]{2,3,1,0:T(8,128)} copy(f32[2,4,256,192]{2,3,0,1:T(8,128)S(1)} %fusion.9) | data formatting | bytes 3145728 | tf_op jit(solution)/shard_map/sij,csja->csia/transpose | solution.py:241
  (64 shorter events, 4.4 us)
Async XLA Ops:
  9.8 7.3 %copy-start.3 = (f32[4,256]{1,0:T(4,128)S(1)}, f32[4,256]{1,0:T(4,128)}, u32[]{:S(2)}) copy-start(f32[4,256]{1,0:T(4,128)} %param.8) | copy-start | bytes 12292
  9.8 12.7 %copy-start.6 = (f32[192]{0:T(256)S(1)}, f32[192]{0:T(256)}, u32[]{:S(2)}) copy-start(f32[192]{0:T(256)} %param.9) | copy-start | bytes 2308
  9.8 44.8 %all-to-all-start = ((f32[32,96,128]{2,1,0:T(8,128)}), f32[32,96,128]{2,1,0:T(8,128)S(1)}, u32[]{:S(2)}, u32[]{:S(2)}) async-start(f32[32,96,128]{2,1,0:T(8,128)} %bitcast.17), calls=%async_computation | async-start | bytes 3145728 | tf_op jit(solution)/shard_map/all_to_all | solution.py:140
  17.1 9.5 %copy-start.5 = (s32[4,256]{1,0:T(4,128)S(1)}, s32[4,256]{1,0:T(4,128)}, u32[]{:S(2)}) copy-start(s32[4,256]{1,0:T(4,128)} %param.10) | copy-start | bytes 12292
  17.2 10.2 %copy-start.4 = (f32[8,4,256]{2,1,0:T(4,128)S(1)}, f32[8,4,256]{2,1,0:T(4,128)}, u32[]{:S(2)}) copy-start(f32[8,4,256]{2,1,0:T(4,128)} %param.11) | copy-start | bytes 98308
  17.2 10.8 %copy-start.7 = (s32[192]{0:T(256)S(1)}, s32[192]{0:T(256)}, u32[]{:S(2)}) copy-start(s32[192]{0:T(256)} %param.7) | copy-start | bytes 2308
  17.3 26.2 %collective-permute-start.3 = (f32[4,8]{1,0:T(4,128)S(1)}, f32[4,8]{1,0:T(4,128)S(1)}, u32[]{:S(2)}, u32[]{:S(2)}) collective-permute-start(f32[4,8]{1,0:T(4,128)S(1)} %get-tuple-element.54), channel_id=1, source_target_pairs={{1,0},{2,1},{3,2},{4,3},{5,4},{6,5},{7,6},{8,7},{9,8},{10,9},{11,1... | collective-permute-start | bytes 392 | tf_op jit(solution)/shard_map/ppermute | solution.py:176
  22.5 26.1 %collective-permute-start.2 = (f32[4,8]{1,0:T(4,128)S(1)}, f32[4,8]{1,0:T(4,128)S(1)}, u32[]{:S(2)}, u32[]{:S(2)}) collective-permute-start(f32[4,8]{1,0:T(4,128)S(1)} %get-tuple-element.53), channel_id=1, source_target_pairs={{0,1},{1,2},{2,3},{3,4},{4,5},{5,6},{6,7},{7,8},{8,9},{9,10},{10,1... | collective-permute-start | bytes 392 | tf_op jit(solution)/shard_map/ppermute | solution.py:175
  56.9 9.0 %collective-permute-start = (f32[4,8,384]{2,1,0:T(8,128)}, f32[4,8,384]{2,1,0:T(8,128)}, u32[]{:S(2)}, u32[]{:S(2)}) collective-permute-start(f32[4,8,384]{2,1,0:T(8,128)} %bitcast.198), channel_id=1, source_target_pairs={{0,1},{1,2},{2,3},{3,4},{4,5},{5,6},{6,7},{7,8},{8,9},{9,10},{10,1... | collective-permute-start | bytes 147464 | tf_op jit(solution)/shard_map/ppermute | solution.py:175
  57.7 7.1 %copy-start = (f32[4,256,192]{1,2,0:T(8,128)S(1)}, f32[4,256,192]{1,2,0:T(8,128)}, u32[]{:S(2)}) copy-start(f32[4,256,192]{1,2,0:T(8,128)} %get-tuple-element.8) | copy-start | bytes 2359300
  57.7 7.1 %copy-start.1 = (f32[4,256,192]{1,2,0:T(8,128)S(1)}, f32[4,256,192]{1,2,0:T(8,128)}, u32[]{:S(2)}) copy-start(f32[4,256,192]{1,2,0:T(8,128)} %get-tuple-element.7) | copy-start | bytes 2359300
  57.7 9.7 %collective-permute-start.1 = (f32[4,8,384]{2,1,0:T(8,128)}, f32[4,8,384]{2,1,0:T(8,128)S(1)}, u32[]{:S(2)}, u32[]{:S(2)}) collective-permute-start(f32[4,8,384]{2,1,0:T(8,128)} %bitcast.34), channel_id=1, source_target_pairs={{1,0},{2,1},{3,2},{4,3},{5,4},{6,5},{7,6},{8,7},{9,8},{10,9},{11,1... | collective-permute-start | bytes 147464 | tf_op jit(solution)/shard_map/ppermute | solution.py:176
  64.9 3.0 %copy-start.2 = (f32[192,192]{1,0:T(8,128)S(1)}, f32[192,192]{1,0:T(8,128)}, u32[]{:S(2)}) copy-start(f32[192,192]{1,0:T(8,128)} %get-tuple-element.58) | copy-start | bytes 442372

commit v17 on v16

--- a/solution.py
+++ b/solution.py
@@ -219,9 +219,7 @@
     rim_real = jnp.einsum("ay,sjy->sja", fold_top, rims, precision=fast)
     rim_imag = jnp.einsum("ay,sjy->sja", fold_bottom, rims, precision=fast)
     rims = focus(rim_real, rim_imag, jnp.concatenate([wave_left, wave_right], axis=1))
-    left_rim = rims[:, :, :RIM]
-    right_rim = rims[:, :, RIM:]
-    widened = jnp.concatenate([left_rim, focused, right_rim], axis=2)
+    widened = jnp.concatenate([focused, rims], axis=2)
 
     tap_count = stolt_coef.shape[0]
     piece_index = jnp.arange(block_len, dtype=jnp.int32)
@@ -238,6 +236,9 @@
     for t in range(tap_count):
         band = band + jnp.where(columns[None, None, :] == target + t, weights[t][:, :, None], 0.0)
 
+    band = jnp.concatenate(
+        [band[:, :, RIM:RIM + block_len], band[:, :, :RIM], band[:, :, RIM + block_len:]], axis=2
+    )
     return jnp.einsum("sij,csja->csia", band, widened, precision=fast)
 
 

time: 74.2 us -> 72.8 us (0.981)
  matrix products: 13.7 us -> 12.2 us
  local copies, waits for them, and re-layouts: 11 us -> 9.59 us
    transpose x0 -> x3, local copies, waits for them, and re-layouts: none -> 2.74 us  [the longest x2 2.51 us: on_device(): jnp.swapaxes(combined[:, :, block_len - RIM:], 1, 2)]
    unnamed x19, local copies, waits for them, and re-layouts: 1.82 us -> 0.23 us
    slice x3, local copies, waits for them, and re-layouts: 1.48 us -> 0.01 us  [beside(): left = jnp.where(position == 0, jnp.roll(left, 1, axis=axis), left)]
    add x0 -> x1, other arithmetic: none -> 1.17 us  [on_device(): band + jnp.where(columns[None, None, :] == target + t, weights[t][:, :, N...]
    dot_general x1, matrix products: 1.03 us -> 2.14 us  [on_device(): az_real = jnp.einsum('ay,syq->sqa', fold_top, combined, precision=fast)]
    dot_general x1, matrix products: 3.61 us -> 2.61 us  [on_device(): return jnp.einsum('sij,csja->csia', band, widened, precision=fast)]
    dot_general x1, matrix products: 1.76 us -> 0.83 us  [on_device(): az_imag = jnp.einsum('ay,syq->sqa', fold_bottom, combined, precision=fast)]
    slice x3, local copies, waits for them, and re-layouts: 0.81 us -> 0.01 us  [the longest x1 0.01 us: on_device(): band[:, :, :RIM]]
  transfers between devices with their start and end apart: 5 -> 5, of which waited for: 3 -> 3; matrix products, arithmetic and copies ran while one was open for 18% -> 15% of each run, Pallas kernels for 0% -> 0%
where the time goes in v17:
time: 72.8 us; the launch traced here: 72.4 us
  waiting for transfers between devices  24.4 us (34%)
  starting transfers between devices  17.9 us (25%)
  matrix products  12.2 us (17%)
  local copies, waits for them, and re-layouts  9.59 us (13%)
  other arithmetic  7.93 us (11%)
    ppermute x2, waiting for transfers between devices, beside(): right = lax.ppermute(right_piece, axes, down)  13.2 us
    ppermute x2, starting transfers between devices, beside(): right = lax.ppermute(right_piece, axes, down)  10.6 us
    all_to_all x1, starting transfers between devices, on_device(): lax.all_to_all(spectrum, ('pulse', 'rng'), split_axis=0, concat_axis=0, t...  7.3 us
    all_to_all x1, waiting for transfers between devices, on_device(): lax.all_to_all(spectrum, ('pulse', 'rng'), split_axis=0, concat_axis=0, t...  5.95 us
    ppermute x2, waiting for transfers between devices, beside(): left = lax.ppermute(left_piece, axes, up)  5.18 us
    sin x1, other arithmetic, on_device(): jnp.sin(phase_angle)  4.12 us
    dot_general x1, matrix products, range_dft_blocks(): jnp.einsum('ducb,crba->drua', stacked_table(outer_len, 1.0), signal, prec...  2.66 us
    dot_general x1, matrix products, on_device(): return jnp.einsum('sij,csja->csia', band, widened, precision=fast)  2.61 us
  transfers between devices with their start and end apart: 5, of which 3 were waited for; matrix products, arithmetic and copies ran while one was open for 15% of the time, Pallas kernels for 0%

profile of v17, /device:TPU:0, one launch (start us, length us, event | category | flops | bytes accessed | tf_op | source)
XLA Modules:
  0.0 72.4 jit_solution(5500517493391822628)
XLA Ops:
  1.0 2.4 %reshape.603 = f32[2,24,128,64]{3,2,1,0:T(8,128)S(1)} reshape(f32[2,24,8192]{2,1,0:T(8,128)} %param.6) | data formatting | bytes 3145728 | tf_op jit(solution)/shard_map/reshape | solution.py:77
  3.7 2.7 %fusion.12 = f32[2,24,128,64]{2,3,1,0:T(8,128)S(1)} fusion(f32[2,24,128,64]{3,2,1,0:T(8,128)S(1)} %reshape.603, f32[1,128,2,128]{3,1,2,0:T(8,128)S(1)} %get-tuple-element.34, f32[1,128,2,128]{3,1,2,0:T(8,128)S(1)} %get-tuple-element.33), kind=kOutput, calls=%fused_computation.13 | convolution fusion | flops 604045312 | bytes 3407872 | tf_op jit(solution)/shard_map/ducb,crba->drua/dot_general | solution.py:78
  6.3 0.3 multiply_subtract_fusion.1
  6.7 0.8 %fusion.6 = f32[64,2,24,128]{3,0,1,2:T(8,128)S(1)} fusion(f32[1,64,2,64]{3,1,2,0:T(8,128)S(1)} %get-tuple-element.44, f32[1,64,2,64]{3,1,2,0:T(8,128)S(1)} %get-tuple-element.43, f32[1,24,128,64]{2,3,1,0:T(8,128)S(1)} %get-tuple-element.16, f32[1,24,128,64]{2,3,1,0:T(8,128)S(1)} %get-tuple-element.15), kind=kOutput, calls=%fused_computation.11 | convolution fusion | flops 302399488 | bytes 3211264 | tf_op jit(solution)/shard_map/dvca,crua->vdru/dot_general | solution.py:90
  7.5 0.3 multiply_subtract_fusion
  7.9 2.1 %copy.49 = f32[64,2,24,128]{3,2,1,0:T(8,128)} copy(f32[64,2,24,128]{3,0,1,2:T(8,128)S(1)} %pad_maximum_fusion.1) | data formatting | bytes 3145728 | tf_op jit(solution)/shard_map/stack | solution.py:99
  10.0 7.3 %all-to-all-start = ((f32[32,96,128]{2,1,0:T(8,128)}), f32[32,96,128]{2,1,0:T(8,128)S(1)}, u32[]{:S(2)}, u32[]{:S(2)}) async-start(f32[32,96,128]{2,1,0:T(8,128)} %bitcast.17), calls=%async_computation | async-start | bytes 3145728 | tf_op jit(solution)/shard_map/all_to_all | solution.py:140
  17.4 5.2 %collective-permute-start.3 = (f32[4,8]{1,0:T(4,128)S(1)}, f32[4,8]{1,0:T(4,128)S(1)}, u32[]{:S(2)}, u32[]{:S(2)}) collective-permute-start(f32[4,8]{1,0:T(4,128)S(1)} %get-tuple-element.54), channel_id=1, source_target_pairs={{1,0},{2,1},{3,2},{4,3},{5,4},{6,5},{7,6},{8,7},{9,8},{10,9},{11,1... | collective-permute-start | bytes 392 | tf_op jit(solution)/shard_map/ppermute | solution.py:176
  22.6 4.1 %fusion.19 = (f32[4,256,192]{1,2,0:T(8,128)}, f32[4,256,192]{1,2,0:T(8,128)}) fusion(f32[192]{0:T(256)S(1)} %integer_pow.18, f32[4,256]{1,0:T(4,128)S(1)} %integer_pow.17), kind=kLoop, calls=%fused_computation.37 | loop fusion | flops 393216 | bytes 1577728 | tf_op jit(solution)/shard_map/sin | solution.py:209
  26.9 1.2 %select_add_fusion = f32[4,256,272]{1,2,0:T(8,128)S(1)} fusion(f32[4,256]{1,0:T(4,128)S(1)} %get-tuple-element.36, s32[4,256]{1,0:T(4,128)S(1)} %get-tuple-element.52, f32[4,256]{1,0:T(4,128)S(1)} %get-tuple-element.37, s32[4,256]{1,0:T(4,128)S(1)} %get-tuple-element.48, f32[4,256]{1,0:T(4,128)S(1)} %get-tuple-element.38, ...), kind=kLoop, calls=%fused_computation.19 | loop fusion | flops 6406144 | bytes 1179648 | tf_op jit(solution)/shard_map/add | solution.py:237
  28.1 1.1 %fusion.30 = f32[192,192]{1,0:T(8,128)S(1)} fusion(s32[192]{0:T(256)S(1)} %copy-done.8), kind=kOutput, calls=%fused_computation.64 | convolution fusion | flops 85340160 | bytes 148224 | tf_op jit(solution)/shard_map/ji,ja->ai/dot_general | solution.py:118
  29.2 1.1 %fusion.108 = (f32[192,192]{1,0:T(8,128)S(1)}, f32[192,192]{1,0:T(8,128)S(1)}) fusion(s32[192]{0:T(256)S(1)} %copy-done.8), kind=kOutput, calls=%fused_computation.194 | convolution fusion | flops 85377024 | bytes 295680 | tf_op jit(solution)/shard_map/ji,ja->ai/dot_general | solution.py:119
  30.3 13.2 %collective-permute-done.3 = f32[4,8]{1,0:T(4,128)S(1)} collective-permute-done((f32[4,8]{1,0:T(4,128)S(1)}, f32[4,8]{1,0:T(4,128)S(1)}, u32[]{:S(2)}, u32[]{:S(2)}) %collective-permute-start.3) | collective-permute-done | bytes 160 | tf_op jit(solution)/shard_map/ppermute | solution.py:176
  43.6 5.2 %collective-permute-done.2 = f32[4,8]{1,0:T(4,128)S(1)} collective-permute-done((f32[4,8]{1,0:T(4,128)S(1)}, f32[4,8]{1,0:T(4,128)S(1)}, u32[]{:S(2)}, u32[]{:S(2)}) %collective-permute-start.2) | collective-permute-done | bytes 160 | tf_op jit(solution)/shard_map/ppermute | solution.py:175
  48.8 6.0 %all-to-all-done = f32[32,96,128]{2,1,0:T(8,128)S(1)} async-done(((f32[32,96,128]{2,1,0:T(8,128)}), f32[32,96,128]{2,1,0:T(8,128)S(1)}, u32[]{:S(2)}, u32[]{:S(2)}) %all-to-all-start) | async-done | bytes 1572896 | tf_op jit(solution)/shard_map/all_to_all | solution.py:140
  55.9 1.2 %slice_bitcast_fusion.1 = (f32[4,8,384]{1,2,0:T(8,128)}, f32[4,8,384]{1,2,0:T(8,128)S(1)}) fusion(f32[4,384,256]{2,1,0:T(8,128)S(1)} %bitcast.193), kind=kLoop, calls=%fused_computation.29 | loop fusion | bytes 196608 | tf_op jit(solution)/shard_map/transpose | solution.py:183
  57.0 1.4 %copy.56 = f32[4,8,384]{2,1,0:T(8,128)S(1)} copy(f32[4,8,384]{1,2,0:T(8,128)} %get-tuple-element.17) | data formatting | bytes 98304 | tf_op jit(solution)/shard_map/transpose | solution.py:183
  58.7 5.4 %collective-permute-start.1 = (f32[4,8,384]{2,1,0:T(8,128)S(1)}, f32[4,8,384]{2,1,0:T(8,128)S(1)}, u32[]{:S(2)}, u32[]{:S(2)}) collective-permute-start(f32[4,8,384]{2,1,0:T(8,128)S(1)} %copy.57), channel_id=1, source_target_pairs={{1,0},{2,1},{3,2},{4,3},{5,4},{6,5},{7,6},{8,7},{9,8},{10,9},{11,1... | collective-permute-start | bytes 147464 | tf_op jit(solution)/shard_map/ppermute | solution.py:176
  64.0 0.8 %fusion.39 = f32[4,256,192]{1,2,0:T(8,128)S(1)} fusion(f32[4,384,256]{2,1,0:T(8,128)S(1)} %bitcast.194, f32[192,192]{1,0:T(8,128)S(1)} %fusion.30, f32[192,192]{1,0:T(8,128)S(1)} %get-tuple-element.58), kind=kOutput, calls=%fused_computation.80 | convolution fusion | flops 453058560 | bytes 2654208 | tf_op jit(solution)/shard_map/ay,syq->sqa/dot_general | solution.py:204
  64.9 2.1 %subtract_bitcast_fusion = (f32[1,4,256,192]{2,3,1,0:T(8,128)}, f32[1,4,256,192]{2,3,1,0:T(8,128)}) fusion(f32[4,256,192]{1,2,0:T(8,128)S(1)} %fusion.39, f32[4,256,192]{1,2,0:T(8,128)S(1)} %copy-done.1, f32[4,256,192]{1,2,0:T(8,128)S(1)} %copy-done.2, f32[4,384,256]{2,1,0:T(8,128)S(1)} %bitcast.195, f32[192,192]{1,0:T(8,128)S(1)} %get-tuple-element.57, ...), kind=kOutput, calls=%fused_computation.35 | convolution fusion | flops 454238208 | bytes 5799936 | tf_op jit(solution)/shard_map/ay,syq->sqa/dot_general | solution.py:203
  67.1 0.4 fusion.40
  67.5 0.5 subtract_bitcast_fusion.1
  68.5 2.6 %fusion.9 = f32[2,4,256,192]{2,3,0,1:T(8,128)S(1)} fusion(f32[4,256,8]{1,2,0:T(8,128)S(1)} %get-tuple-element.26, f32[4,256,8]{1,2,0:T(8,128)S(1)} %get-tuple-element.25, f32[4,256,256]{1,2,0:T(8,128)S(1)} %slice-done, f32[2,4,16,192]{2,3,1,0:T(8,128)S(1)} %copy.58, f32[1,4,256,192]{2,3,1,0:T(8,128)} %get-tuple-element.12, f32[1,4,256,192]{2,3,1,0:T(8,128)S(1)} %copy-done.3), kind=kOutput, calls=%fused_computation.12 | convolution fusion | flops 643121152 | bytes 4358144 | tf_op jit(solution)/shard_map/sij,csja->csia/dot_general | solution.py:242
  71.1 1.3 %copy.60 = f32[2,4,256,192]{2,3,1,0:T(8,128)} copy(f32[2,4,256,192]{2,3,0,1:T(8,128)S(1)} %fusion.9) | data formatting | bytes 3145728 | tf_op jit(solution)/shard_map/sij,csja->csia/transpose | solution.py:242
  (69 shorter events, 3.4 us)
Async XLA Ops:
  10.0 7.3 %copy-start.4 = (f32[4,256]{1,0:T(4,128)S(1)}, f32[4,256]{1,0:T(4,128)}, u32[]{:S(2)}) copy-start(f32[4,256]{1,0:T(4,128)} %param.8) | copy-start | bytes 12292
  10.0 12.6 %copy-start.7 = (f32[192]{0:T(256)S(1)}, f32[192]{0:T(256)}, u32[]{:S(2)}) copy-start(f32[192]{0:T(256)} %param.9) | copy-start | bytes 2308
  10.0 44.8 %all-to-all-start = ((f32[32,96,128]{2,1,0:T(8,128)}), f32[32,96,128]{2,1,0:T(8,128)S(1)}, u32[]{:S(2)}, u32[]{:S(2)}) async-start(f32[32,96,128]{2,1,0:T(8,128)} %bitcast.17), calls=%async_computation | async-start | bytes 3145728 | tf_op jit(solution)/shard_map/all_to_all | solution.py:140
  17.3 9.5 %copy-start.6 = (s32[4,256]{1,0:T(4,128)S(1)}, s32[4,256]{1,0:T(4,128)}, u32[]{:S(2)}) copy-start(s32[4,256]{1,0:T(4,128)} %param.10) | copy-start | bytes 12292
  17.3 9.6 %copy-start.5 = (f32[8,4,256]{2,1,0:T(4,128)S(1)}, f32[8,4,256]{2,1,0:T(4,128)}, u32[]{:S(2)}) copy-start(f32[8,4,256]{2,1,0:T(4,128)} %param.11) | copy-start | bytes 98308
  17.4 26.2 %collective-permute-start.3 = (f32[4,8]{1,0:T(4,128)S(1)}, f32[4,8]{1,0:T(4,128)S(1)}, u32[]{:S(2)}, u32[]{:S(2)}) collective-permute-start(f32[4,8]{1,0:T(4,128)S(1)} %get-tuple-element.54), channel_id=1, source_target_pairs={{1,0},{2,1},{3,2},{4,3},{5,4},{6,5},{7,6},{8,7},{9,8},{10,9},{11,1... | collective-permute-start | bytes 392 | tf_op jit(solution)/shard_map/ppermute | solution.py:176
  22.6 26.1 %collective-permute-start.2 = (f32[4,8]{1,0:T(4,128)S(1)}, f32[4,8]{1,0:T(4,128)S(1)}, u32[]{:S(2)}, u32[]{:S(2)}) collective-permute-start(f32[4,8]{1,0:T(4,128)S(1)} %get-tuple-element.53), channel_id=1, source_target_pairs={{0,1},{1,2},{2,3},{3,4},{4,5},{5,6},{6,7},{7,8},{8,9},{9,10},{10,1... | collective-permute-start | bytes 392 | tf_op jit(solution)/shard_map/ppermute | solution.py:175
  26.9 1.2 %copy-start.8 = (s32[192]{0:T(256)S(1)}, s32[192]{0:T(256)}, u32[]{:S(2)}) copy-start(s32[192]{0:T(256)} %param.7) | copy-start | bytes 2308
  28.1 2.2 %copy-start = (f32[4,256,272]{1,2,0:T(8,128)}, f32[4,256,272]{1,2,0:T(8,128)S(1)}, u32[]{:S(2)}) copy-start(f32[4,256,272]{1,2,0:T(8,128)S(1)} %select_add_fusion) | copy-start | bytes 3342340
  58.4 8.7 %collective-permute-start = (f32[4,8,384]{2,1,0:T(8,128)S(1)}, f32[4,8,384]{2,1,0:T(8,128)S(1)}, u32[]{:S(2)}, u32[]{:S(2)}) collective-permute-start(f32[4,8,384]{2,1,0:T(8,128)S(1)} %copy.56), channel_id=1, source_target_pairs={{0,1},{1,2},{2,3},{3,4},{4,5},{5,6},{6,7},{7,8},{8,9},{9,10},{10,1... | collective-permute-start | bytes 147464 | tf_op jit(solution)/shard_map/ppermute | solution.py:175
  58.7 6.2 %copy-start.1 = (f32[4,256,192]{1,2,0:T(8,128)S(1)}, f32[4,256,192]{1,2,0:T(8,128)}, u32[]{:S(2)}) copy-start(f32[4,256,192]{1,2,0:T(8,128)} %get-tuple-element.8) | copy-start | bytes 2359300
  58.7 6.2 %copy-start.2 = (f32[4,256,192]{1,2,0:T(8,128)S(1)}, f32[4,256,192]{1,2,0:T(8,128)}, u32[]{:S(2)}) copy-start(f32[4,256,192]{1,2,0:T(8,128)} %get-tuple-element.7) | copy-start | bytes 2359300
  58.7 8.4 %collective-permute-start.1 = (f32[4,8,384]{2,1,0:T(8,128)S(1)}, f32[4,8,384]{2,1,0:T(8,128)S(1)}, u32[]{:S(2)}, u32[]{:S(2)}) collective-permute-start(f32[4,8,384]{2,1,0:T(8,128)S(1)} %copy.57), channel_id=1, source_target_pairs={{1,0},{2,1},{3,2},{4,3},{5,4},{6,5},{7,6},{8,7},{9,8},{10,9},{11,1... | collective-permute-start | bytes 147464 | tf_op jit(solution)/shard_map/ppermute | solution.py:176
  67.0 1.3 %slice-start = ((f32[4,256,272]{1,2,0:T(8,128)}), f32[4,256,256]{1,2,0:T(8,128)S(1)}, s32[]{:S(2)}) async-start(f32[4,256,272]{1,2,0:T(8,128)} %copy-done), calls=%async_computation.1 | async-start | bytes 2097152 | tf_op jit(solution)/shard_map/slice | solution.py:240
  67.0 1.4 %copy-start.3 = (f32[1,4,256,192]{2,3,1,0:T(8,128)S(1)}, f32[1,4,256,192]{2,3,1,0:T(8,128)}, u32[]{:S(2)}) copy-start(f32[1,4,256,192]{2,3,1,0:T(8,128)} %get-tuple-element.11) | copy-start | bytes 2359300

commit v18 on v17

--- a/solution.py
+++ b/solution.py
@@ -88,21 +88,6 @@
         ]
     )
     second = jnp.einsum("dvca,crua->vdru", stacked_table(inner_len, 1.0), first, precision=fast)
-    q_index = jnp.arange(inner_len, dtype=jnp.int32)[:, None] * outer_len + jnp.arange(
-        outer_len, dtype=jnp.int32
-    )[None, :]
-    turn_angle = ((lane_pos * q_index) % range_len).astype(jnp.float32) * (
-        -2.0 * math.pi / range_len
-    )
-    turn_real = jnp.cos(turn_angle)[:, None, :]
-    turn_imag = jnp.sin(turn_angle)[:, None, :]
-    second = jnp.stack(
-        [
-            second[:, 0] * turn_real - second[:, 1] * turn_imag,
-            second[:, 0] * turn_imag + second[:, 1] * turn_real,
-        ],
-        axis=1,
-    )
     if block_len % outer_len == 0:
         per_block = block_len // outer_len
         return second.reshape(device_count, per_block, 2, rows, outer_len)
@@ -145,8 +130,15 @@
         pulse_count, lane_count, 2, rows_here, block_len
     )
 
-    lane_real = spectrum[:, :, 0]
-    lane_imag = spectrum[:, :, 1]
+    q_global = position * block_len + jnp.arange(block_len, dtype=jnp.int32)
+    lane_index = jnp.arange(lane_count, dtype=jnp.int32)[:, None]
+    turn_angle = ((lane_index * q_global[None, :]) % range_len).astype(jnp.float32) * (
+        -2.0 * math.pi / range_len
+    )
+    turn_real = jnp.cos(turn_angle)[None, :, None, :]
+    turn_imag = jnp.sin(turn_angle)[None, :, None, :]
+    lane_real = spectrum[:, :, 0] * turn_real - spectrum[:, :, 1] * turn_imag
+    lane_imag = spectrum[:, :, 0] * turn_imag + spectrum[:, :, 1] * turn_real
     combined_real = []
     combined_imag = []
     for s in range(lane_count):

time: 72.8 us -> 73 us (level)
  local copies, waits for them, and re-layouts: 9.59 us -> 11.2 us
  waiting for transfers between devices: 24.4 us -> 23.4 us
    another operation x1 -> x0, local copies, waits for them, and re-layouts: 2.06 us -> none  [range_dft_blocks(): jnp.stack([second[:, 0] * turn_real - second[:, 1] * turn_imag, second[:,...]
    transpose x0 -> x1, local copies, waits for them, and re-layouts: none -> 2.06 us  [range_dft_blocks(): jnp.einsum('dvca,crua->vdru', stacked_table(inner_len, 1.0), first, preci...]
    unnamed x19 -> x18, local copies, waits for them, and re-layouts: 0.23 us -> 1.85 us
    ppermute x2, waiting for transfers between devices: 13.2 us -> 12.3 us  [beside(): right = lax.ppermute(right_piece, axes, down)]
where the time goes in v18:
time: 73 us; the launch traced here: 72.6 us
  waiting for transfers between devices  23.4 us (32%)
  starting transfers between devices  17.9 us (25%)
  matrix products  12.2 us (17%)
  local copies, waits for them, and re-layouts  11.2 us (15%)
  other arithmetic  7.57 us (10%)
    ppermute x2, waiting for transfers between devices, beside(): right = lax.ppermute(right_piece, axes, down)  12.3 us
    ppermute x2, starting transfers between devices, beside(): right = lax.ppermute(right_piece, axes, down)  10.6 us
    all_to_all x1, starting transfers between devices, on_device(): lax.all_to_all(spectrum, ('pulse', 'rng'), split_axis=0, concat_axis=0, t...  7.3 us
    all_to_all x1, waiting for transfers between devices, on_device(): lax.all_to_all(spectrum, ('pulse', 'rng'), split_axis=0, concat_axis=0, t...  5.95 us
    ppermute x2, waiting for transfers between devices, beside(): left = lax.ppermute(left_piece, axes, up)  5.18 us
    sin x1, other arithmetic, on_device(): jnp.sin(phase_angle)  4.12 us
    dot_general x1, matrix products, range_dft_blocks(): jnp.einsum('ducb,crba->drua', stacked_table(outer_len, 1.0), signal, prec...  2.65 us
    dot_general x1, matrix products, on_device(): return jnp.einsum('sij,csja->csia', band, widened, precision=fast)  2.6 us
  transfers between devices with their start and end apart: 5, of which 3 were waited for; matrix products, arithmetic and copies ran while one was open for 15% of the time, Pallas kernels for 0%

profile of v18, /device:TPU:0, one launch (start us, length us, event | category | flops | bytes accessed | tf_op | source)
XLA Modules:
  0.0 72.6 jit_solution(17650591122421209051)
XLA Ops:
  1.0 2.4 %reshape.603 = f32[2,24,128,64]{3,2,1,0:T(8,128)S(1)} reshape(f32[2,24,8192]{2,1,0:T(8,128)} %param.6) | data formatting | bytes 3145728 | tf_op jit(solution)/shard_map/reshape | solution.py:77
  3.4 2.7 %fusion.12 = f32[2,24,128,64]{2,3,1,0:T(8,128)S(1)} fusion(f32[2,24,128,64]{3,2,1,0:T(8,128)S(1)} %reshape.603, f32[1,128,2,128]{3,1,2,0:T(8,128)S(1)} %get-tuple-element.34, f32[1,128,2,128]{3,1,2,0:T(8,128)S(1)} %get-tuple-element.33), kind=kOutput, calls=%fused_computation.12 | convolution fusion | flops 604045312 | bytes 3407872 | tf_op jit(solution)/shard_map/ducb,crba->drua/dot_general | solution.py:78
  6.3 0.8 %fusion.6 = f32[64,2,24,128]{3,0,1,2:T(8,128)S(1)} fusion(f32[1,64,2,64]{3,1,2,0:T(8,128)S(1)} %get-tuple-element.44, f32[1,64,2,64]{3,1,2,0:T(8,128)S(1)} %get-tuple-element.43, f32[1,24,128,64]{2,3,1,0:T(8,128)S(1)} %get-tuple-element.14, f32[1,24,128,64]{2,3,1,0:T(8,128)S(1)} %get-tuple-element.13), kind=kOutput, calls=%fused_computation.10 | convolution fusion | flops 302399488 | bytes 3211264 | tf_op jit(solution)/shard_map/dvca,crua->vdru/dot_general | solution.py:90
  7.2 2.1 %copy.52 = f32[64,2,24,128]{3,2,1,0:T(8,128)} copy(f32[64,2,24,128]{3,0,1,2:T(8,128)S(1)} %fusion.6) | data formatting | bytes 3145728 | tf_op jit(solution)/shard_map/dvca,crua->vdru/transpose | solution.py:90
  9.2 7.3 %all-to-all-start = ((f32[32,96,128]{2,1,0:T(8,128)}), f32[32,96,128]{2,1,0:T(8,128)S(1)}, u32[]{:S(2)}, u32[]{:S(2)}) async-start(f32[32,96,128]{2,1,0:T(8,128)} %bitcast.16), calls=%async_computation | async-start | bytes 3145728 | tf_op jit(solution)/shard_map/all_to_all | solution.py:125
  16.6 5.2 %collective-permute-start.3 = (f32[4,8]{1,0:T(4,128)S(1)}, f32[4,8]{1,0:T(4,128)S(1)}, u32[]{:S(2)}, u32[]{:S(2)}) collective-permute-start(f32[4,8]{1,0:T(4,128)S(1)} %get-tuple-element.54), channel_id=1, source_target_pairs={{1,0},{2,1},{3,2},{4,3},{5,4},{6,5},{7,6},{8,7},{9,8},{10,9},{11,1... | collective-permute-start | bytes 392 | tf_op jit(solution)/shard_map/ppermute | solution.py:168
  21.9 4.1 %fusion.20 = (f32[4,256,192]{1,2,0:T(8,128)}, f32[4,256,192]{1,2,0:T(8,128)}) fusion(f32[192]{0:T(256)S(1)} %integer_pow.18, f32[4,256]{1,0:T(4,128)S(1)} %integer_pow.17), kind=kLoop, calls=%fused_computation.39 | loop fusion | flops 393216 | bytes 1577728 | tf_op jit(solution)/shard_map/sin | solution.py:201
  26.2 1.2 %select_add_fusion = f32[4,256,272]{1,2,0:T(8,128)S(1)} fusion(f32[4,256]{1,0:T(4,128)S(1)} %get-tuple-element.36, s32[4,256]{1,0:T(4,128)S(1)} %get-tuple-element.52, f32[4,256]{1,0:T(4,128)S(1)} %get-tuple-element.37, s32[4,256]{1,0:T(4,128)S(1)} %get-tuple-element.48, f32[4,256]{1,0:T(4,128)S(1)} %get-tuple-element.38, ...), kind=kLoop, calls=%fused_computation.18 | loop fusion | flops 6406144 | bytes 1179648 | tf_op jit(solution)/shard_map/add | solution.py:229
  27.4 0.9 %copy-done = f32[4,256,272]{1,2,0:T(8,128)} copy-done((f32[4,256,272]{1,2,0:T(8,128)}, f32[4,256,272]{1,2,0:T(8,128)S(1)}, u32[]{:S(2)}) %copy-start) | copy-done | bytes 1114136
  28.3 1.1 %fusion.32 = f32[192,192]{1,0:T(8,128)S(1)} fusion(s32[192]{0:T(256)S(1)} %copy-done.8), kind=kOutput, calls=%fused_computation.65 | convolution fusion | flops 85340160 | bytes 148224 | tf_op jit(solution)/shard_map/ji,ja->ai/dot_general | solution.py:103
  29.4 1.1 %fusion.111 = (f32[192,192]{1,0:T(8,128)S(1)}, f32[192,192]{1,0:T(8,128)S(1)}) fusion(s32[192]{0:T(256)S(1)} %copy-done.8), kind=kOutput, calls=%fused_computation.195 | convolution fusion | flops 85377024 | bytes 295680 | tf_op jit(solution)/shard_map/ji,ja->ai/dot_general | solution.py:104
  30.6 12.3 %collective-permute-done.3 = f32[4,8]{1,0:T(4,128)S(1)} collective-permute-done((f32[4,8]{1,0:T(4,128)S(1)}, f32[4,8]{1,0:T(4,128)S(1)}, u32[]{:S(2)}, u32[]{:S(2)}) %collective-permute-start.3) | collective-permute-done | bytes 160 | tf_op jit(solution)/shard_map/ppermute | solution.py:168
  42.8 5.2 %collective-permute-done.2 = f32[4,8]{1,0:T(4,128)S(1)} collective-permute-done((f32[4,8]{1,0:T(4,128)S(1)}, f32[4,8]{1,0:T(4,128)S(1)}, u32[]{:S(2)}, u32[]{:S(2)}) %collective-permute-start.2) | collective-permute-done | bytes 160 | tf_op jit(solution)/shard_map/ppermute | solution.py:167
  48.1 6.0 %all-to-all-done = f32[32,96,128]{2,1,0:T(8,128)S(1)} async-done(((f32[32,96,128]{2,1,0:T(8,128)}), f32[32,96,128]{2,1,0:T(8,128)S(1)}, u32[]{:S(2)}, u32[]{:S(2)}) %all-to-all-start) | async-done | bytes 1572896 | tf_op jit(solution)/shard_map/all_to_all | solution.py:125
  55.3 1.2 %slice_bitcast_fusion.1 = (f32[4,8,384]{1,2,0:T(8,128)}, f32[4,8,384]{1,2,0:T(8,128)S(1)}) fusion(f32[4,384,256]{2,1,0:T(8,128)S(1)} %bitcast.198), kind=kLoop, calls=%fused_computation.28 | loop fusion | bytes 196608 | tf_op jit(solution)/shard_map/transpose | solution.py:175
  56.5 1.4 %copy.62 = f32[4,8,384]{2,1,0:T(8,128)S(1)} copy(f32[4,8,384]{1,2,0:T(8,128)} %get-tuple-element.15) | data formatting | bytes 98304 | tf_op jit(solution)/shard_map/transpose | solution.py:175
  58.1 5.4 %collective-permute-start.1 = (f32[4,8,384]{2,1,0:T(8,128)S(1)}, f32[4,8,384]{2,1,0:T(8,128)S(1)}, u32[]{:S(2)}, u32[]{:S(2)}) collective-permute-start(f32[4,8,384]{2,1,0:T(8,128)S(1)} %copy.63), channel_id=1, source_target_pairs={{1,0},{2,1},{3,2},{4,3},{5,4},{6,5},{7,6},{8,7},{9,8},{10,9},{11,1... | collective-permute-start | bytes 147464 | tf_op jit(solution)/shard_map/ppermute | solution.py:168
  63.5 0.8 %fusion.41 = f32[4,256,192]{1,2,0:T(8,128)S(1)} fusion(f32[4,384,256]{2,1,0:T(8,128)S(1)} %bitcast.199, f32[192,192]{1,0:T(8,128)S(1)} %fusion.32, f32[192,192]{1,0:T(8,128)S(1)} %get-tuple-element.58), kind=kOutput, calls=%fused_computation.81 | convolution fusion | flops 453058560 | bytes 2654208 | tf_op jit(solution)/shard_map/ay,syq->sqa/dot_general | solution.py:196
  64.9 2.1 %subtract_bitcast_fusion = (f32[1,4,256,192]{2,3,1,0:T(8,128)}, f32[1,4,256,192]{2,3,1,0:T(8,128)}) fusion(f32[4,256,192]{1,2,0:T(8,128)S(1)} %fusion.41, f32[4,256,192]{1,2,0:T(8,128)S(1)} %copy-done.1, f32[4,256,192]{1,2,0:T(8,128)S(1)} %copy-done.2, f32[4,384,256]{2,1,0:T(8,128)S(1)} %bitcast.200, f32[192,192]{1,0:T(8,128)S(1)} %get-tuple-element.57, ...), kind=kOutput, calls=%fused_computation.37 | convolution fusion | flops 454238208 | bytes 5799936 | tf_op jit(solution)/shard_map/ay,syq->sqa/dot_general | solution.py:195
  67.1 0.4 fusion.42
  67.5 0.5 subtract_bitcast_fusion.1
  68.3 0.4 copy-done.3
  68.7 2.6 %fusion.9 = f32[2,4,256,192]{2,3,0,1:T(8,128)S(1)} fusion(f32[4,256,8]{1,2,0:T(8,128)S(1)} %get-tuple-element.24, f32[4,256,8]{1,2,0:T(8,128)S(1)} %get-tuple-element.23, f32[4,256,256]{1,2,0:T(8,128)S(1)} %slice-done, f32[2,4,16,192]{2,3,1,0:T(8,128)S(1)} %copy.64, f32[1,4,256,192]{2,3,1,0:T(8,128)} %get-tuple-element.12, f32[1,4,256,192]{2,3,1,0:T(8,128)S(1)} %copy-done.3), kind=kOutput, calls=%fused_computation.11 | convolution fusion | flops 643121152 | bytes 4358144 | tf_op jit(solution)/shard_map/sij,csja->csia/dot_general | solution.py:234
  71.3 1.3 %copy.66 = f32[2,4,256,192]{2,3,1,0:T(8,128)} copy(f32[2,4,256,192]{2,3,0,1:T(8,128)S(1)} %fusion.9) | data formatting | bytes 3145728 | tf_op jit(solution)/shard_map/sij,csja->csia/transpose | solution.py:234
  (67 shorter events, 3.9 us)
Async XLA Ops:
  9.2 7.3 %copy-start.4 = (f32[4,256]{1,0:T(4,128)S(1)}, f32[4,256]{1,0:T(4,128)}, u32[]{:S(2)}) copy-start(f32[4,256]{1,0:T(4,128)} %param.8) | copy-start | bytes 12292
  9.2 12.6 %copy-start.7 = (f32[192]{0:T(256)S(1)}, f32[192]{0:T(256)}, u32[]{:S(2)}) copy-start(f32[192]{0:T(256)} %param.9) | copy-start | bytes 2308
  9.2 44.8 %all-to-all-start = ((f32[32,96,128]{2,1,0:T(8,128)}), f32[32,96,128]{2,1,0:T(8,128)S(1)}, u32[]{:S(2)}, u32[]{:S(2)}) async-start(f32[32,96,128]{2,1,0:T(8,128)} %bitcast.16), calls=%async_computation | async-start | bytes 3145728 | tf_op jit(solution)/shard_map/all_to_all | solution.py:125
  16.6 9.5 %copy-start.6 = (s32[4,256]{1,0:T(4,128)S(1)}, s32[4,256]{1,0:T(4,128)}, u32[]{:S(2)}) copy-start(s32[4,256]{1,0:T(4,128)} %param.10) | copy-start | bytes 12292
  16.6 9.6 %copy-start.5 = (f32[8,4,256]{2,1,0:T(4,128)S(1)}, f32[8,4,256]{2,1,0:T(4,128)}, u32[]{:S(2)}) copy-start(f32[8,4,256]{2,1,0:T(4,128)} %param.11) | copy-start | bytes 98308
  16.6 26.2 %collective-permute-start.3 = (f32[4,8]{1,0:T(4,128)S(1)}, f32[4,8]{1,0:T(4,128)S(1)}, u32[]{:S(2)}, u32[]{:S(2)}) collective-permute-start(f32[4,8]{1,0:T(4,128)S(1)} %get-tuple-element.54), channel_id=1, source_target_pairs={{1,0},{2,1},{3,2},{4,3},{5,4},{6,5},{7,6},{8,7},{9,8},{10,9},{11,1... | collective-permute-start | bytes 392 | tf_op jit(solution)/shard_map/ppermute | solution.py:168
  21.9 26.1 %collective-permute-start.2 = (f32[4,8]{1,0:T(4,128)S(1)}, f32[4,8]{1,0:T(4,128)S(1)}, u32[]{:S(2)}, u32[]{:S(2)}) collective-permute-start(f32[4,8]{1,0:T(4,128)S(1)} %get-tuple-element.53), channel_id=1, source_target_pairs={{0,1},{1,2},{2,3},{3,4},{4,5},{5,6},{6,7},{7,8},{8,9},{9,10},{10,1... | collective-permute-start | bytes 392 | tf_op jit(solution)/shard_map/ppermute | solution.py:167
  27.3 1.0 %copy-start = (f32[4,256,272]{1,2,0:T(8,128)}, f32[4,256,272]{1,2,0:T(8,128)S(1)}, u32[]{:S(2)}) copy-start(f32[4,256,272]{1,2,0:T(8,128)S(1)} %select_add_fusion) | copy-start | bytes 3342340
  27.3 1.0 %copy-start.8 = (s32[192]{0:T(256)S(1)}, s32[192]{0:T(256)}, u32[]{:S(2)}) copy-start(s32[192]{0:T(256)} %param.7) | copy-start | bytes 2308
  57.9 9.1 %collective-permute-start = (f32[4,8,384]{2,1,0:T(8,128)S(1)}, f32[4,8,384]{2,1,0:T(8,128)S(1)}, u32[]{:S(2)}, u32[]{:S(2)}) collective-permute-start(f32[4,8,384]{2,1,0:T(8,128)S(1)} %copy.62), channel_id=1, source_target_pairs={{0,1},{1,2},{2,3},{3,4},{4,5},{5,6},{6,7},{7,8},{8,9},{9,10},{10,1... | collective-permute-start | bytes 147464 | tf_op jit(solution)/shard_map/ppermute | solution.py:167
  58.1 8.9 %collective-permute-start.1 = (f32[4,8,384]{2,1,0:T(8,128)S(1)}, f32[4,8,384]{2,1,0:T(8,128)S(1)}, u32[]{:S(2)}, u32[]{:S(2)}) collective-permute-start(f32[4,8,384]{2,1,0:T(8,128)S(1)} %copy.63), channel_id=1, source_target_pairs={{1,0},{2,1},{3,2},{4,3},{5,4},{6,5},{7,6},{8,7},{9,8},{10,9},{11,1... | collective-permute-start | bytes 147464 | tf_op jit(solution)/shard_map/ppermute | solution.py:168
  63.5 1.1 %copy-start.1 = (f32[4,256,192]{1,2,0:T(8,128)S(1)}, f32[4,256,192]{1,2,0:T(8,128)}, u32[]{:S(2)}) copy-start(f32[4,256,192]{1,2,0:T(8,128)} %get-tuple-element.8) | copy-start | bytes 2359300
  63.5 1.4 %copy-start.2 = (f32[4,256,192]{1,2,0:T(8,128)S(1)}, f32[4,256,192]{1,2,0:T(8,128)}, u32[]{:S(2)}) copy-start(f32[4,256,192]{1,2,0:T(8,128)} %get-tuple-element.7) | copy-start | bytes 2359300
  67.1 1.2 %slice-start = ((f32[4,256,272]{1,2,0:T(8,128)}), f32[4,256,256]{1,2,0:T(8,128)S(1)}, s32[]{:S(2)}) async-start(f32[4,256,272]{1,2,0:T(8,128)} %copy-done), calls=%async_computation.1 | async-start | bytes 2097152 | tf_op jit(solution)/shard_map/slice | solution.py:232
  67.5 1.2 %copy-start.3 = (f32[1,4,256,192]{2,3,1,0:T(8,128)S(1)}, f32[1,4,256,192]{2,3,1,0:T(8,128)}, u32[]{:S(2)}) copy-start(f32[1,4,256,192]{2,3,1,0:T(8,128)} %get-tuple-element.11) | copy-start | bytes 2359300

commit v19 on v17

--- a/solution.py
+++ b/solution.py
@@ -200,8 +200,10 @@
             ]
         )
 
-    az_real = jnp.einsum("ay,syq->sqa", fold_top, combined, precision=fast)
-    az_imag = jnp.einsum("ay,syq->sqa", fold_bottom, combined, precision=fast)
+    fold_both = jnp.concatenate([fold_top, fold_bottom], axis=0)
+    az_both = jnp.einsum("xy,syq->sqx", fold_both, combined, precision=fast)
+    az_real = az_both[..., :total_rows]
+    az_imag = az_both[..., total_rows:]
     phase_angle = phase_scale * jnp.sqrt(
         wavenumber[:, :, None] ** 2 - az_wavenumber[None, None, :] ** 2
     )

time: 72.8 us -> 72.6 us (level)
  starting transfers between devices: 17.9 us -> 15.7 us
  other arithmetic: 7.93 us -> 10.1 us
  matrix products: 12.2 us -> 13.7 us
  local copies, waits for them, and re-layouts: 9.59 us -> 8.47 us
    ppermute x2, waiting for transfers between devices: 13.2 us -> 10.3 us  [beside(): right = lax.ppermute(right_piece, axes, down)]
    transpose x3 -> x0, local copies, waits for them, and re-layouts: 2.74 us -> none  [the longest x2 2.51 us: on_device(): jnp.swapaxes(combined[:, :, block_len - RIM:], 1, 2)]
    ppermute x2, waiting for transfers between devices: 5.18 us -> 7.66 us  [beside(): left = lax.ppermute(left_piece, axes, up)]
    ppermute x2, starting transfers between devices: 10.6 us -> 8.19 us  [beside(): right = lax.ppermute(right_piece, axes, down)]
    sin x1, other arithmetic: 4.12 us -> 5.72 us  [on_device(): jnp.sin(phase_angle)]
    unnamed x19 -> x25, local copies, waits for them, and re-layouts: 0.23 us -> 1.2 us
    dot_general x2 -> x1, matrix products: 2.97 us -> 3.88 us  [on_device(): az_both = jnp.einsum('xy,syq->sqx', fold_both, combined, precision=fast)]
  transfers between devices with their start and end apart: 5 -> 5, of which waited for: 3 -> 4; matrix products, arithmetic and copies ran while one was open for 15% -> 21% of each run, Pallas kernels for 0% -> 0%
where the time goes in v19:
time: 72.6 us; the launch traced here: 72.3 us
  waiting for transfers between devices  23.9 us (33%)
  starting transfers between devices  15.7 us (22%)
  matrix products  13.7 us (19%)
  other arithmetic  10.1 us (14%)
  local copies, waits for them, and re-layouts  8.47 us (12%)
    ppermute x2, waiting for transfers between devices, beside(): right = lax.ppermute(right_piece, axes, down)  10.3 us
    ppermute x2, starting transfers between devices, beside(): right = lax.ppermute(right_piece, axes, down)  8.19 us
    ppermute x2, waiting for transfers between devices, beside(): left = lax.ppermute(left_piece, axes, up)  7.66 us
    all_to_all x1, starting transfers between devices, on_device(): lax.all_to_all(spectrum, ('pulse', 'rng'), split_axis=0, concat_axis=0, t...  7.3 us
    all_to_all x1, waiting for transfers between devices, on_device(): lax.all_to_all(spectrum, ('pulse', 'rng'), split_axis=0, concat_axis=0, t...  5.95 us
    sin x1, other arithmetic, on_device(): jnp.sin(phase_angle)  5.72 us
    dot_general x1, matrix products, on_device(): az_both = jnp.einsum('xy,syq->sqx', fold_both, combined, precision=fast)  3.88 us
    dot_general x1, matrix products, range_dft_blocks(): jnp.einsum('ducb,crba->drua', stacked_table(outer_len, 1.0), signal, prec...  2.66 us
  transfers between devices with their start and end apart: 5, of which 4 were waited for; matrix products, arithmetic and copies ran while one was open for 21% of the time, Pallas kernels for 0%

profile of v19, /device:TPU:0, one launch (start us, length us, event | category | flops | bytes accessed | tf_op | source)
XLA Modules:
  0.0 72.3 jit_solution(1459158533945017057)
XLA Ops:
  1.0 2.4 %reshape.603 = f32[2,24,128,64]{3,2,1,0:T(8,128)S(1)} reshape(f32[2,24,8192]{2,1,0:T(8,128)} %param.6) | data formatting | bytes 3145728 | tf_op jit(solution)/shard_map/reshape | solution.py:77
  3.7 2.7 %fusion.12 = f32[2,24,128,64]{2,3,1,0:T(8,128)S(1)} fusion(f32[2,24,128,64]{3,2,1,0:T(8,128)S(1)} %reshape.603, f32[1,128,2,128]{3,1,2,0:T(8,128)S(1)} %get-tuple-element.34, f32[1,128,2,128]{3,1,2,0:T(8,128)S(1)} %get-tuple-element.33), kind=kOutput, calls=%fused_computation.13 | convolution fusion | flops 604045312 | bytes 3407872 | tf_op jit(solution)/shard_map/ducb,crba->drua/dot_general | solution.py:78
  6.4 0.3 multiply_subtract_fusion.1
  6.7 0.8 %fusion.6 = f32[64,2,24,128]{3,0,1,2:T(8,128)S(1)} fusion(f32[1,64,2,64]{3,1,2,0:T(8,128)S(1)} %get-tuple-element.44, f32[1,64,2,64]{3,1,2,0:T(8,128)S(1)} %get-tuple-element.43, f32[1,24,128,64]{2,3,1,0:T(8,128)S(1)} %get-tuple-element.16, f32[1,24,128,64]{2,3,1,0:T(8,128)S(1)} %get-tuple-element.15), kind=kOutput, calls=%fused_computation.11 | convolution fusion | flops 302399488 | bytes 3211264 | tf_op jit(solution)/shard_map/dvca,crua->vdru/dot_general | solution.py:90
  7.9 2.1 %copy.23 = f32[64,2,24,128]{3,2,1,0:T(8,128)} copy(f32[64,2,24,128]{3,0,1,2:T(8,128)S(1)} %pad_maximum_fusion) | data formatting | bytes 3145728 | tf_op jit(solution)/shard_map/stack | solution.py:99
  10.0 7.3 %all-to-all-start = ((f32[32,96,128]{2,1,0:T(8,128)}), f32[32,96,128]{2,1,0:T(8,128)S(1)}, u32[]{:S(2)}, u32[]{:S(2)}) async-start(f32[32,96,128]{2,1,0:T(8,128)} %bitcast.17), calls=%async_computation | async-start | bytes 3145728 | tf_op jit(solution)/shard_map/all_to_all | solution.py:140
  17.4 5.2 %collective-permute-start.3 = (f32[4,8]{1,0:T(4,128)S(1)}, f32[4,8]{1,0:T(4,128)S(1)}, u32[]{:S(2)}, u32[]{:S(2)}) collective-permute-start(f32[4,8]{1,0:T(4,128)S(1)} %get-tuple-element.54), channel_id=1, source_target_pairs={{1,0},{2,1},{3,2},{4,3},{5,4},{6,5},{7,6},{8,7},{9,8},{10,9},{11,1... | collective-permute-start | bytes 392 | tf_op jit(solution)/shard_map/ppermute | solution.py:176
  22.8 1.2 %select_add_fusion = f32[4,256,272]{1,2,0:T(8,128)S(1)} fusion(f32[4,256]{1,0:T(4,128)S(1)} %get-tuple-element.36, s32[4,256]{1,0:T(4,128)S(1)} %get-tuple-element.52, f32[4,256]{1,0:T(4,128)S(1)} %get-tuple-element.37, s32[4,256]{1,0:T(4,128)S(1)} %get-tuple-element.48, f32[4,256]{1,0:T(4,128)S(1)} %get-tuple-element.38, ...), kind=kLoop, calls=%fused_computation.19 | loop fusion | flops 6406144 | bytes 1179648 | tf_op jit(solution)/shard_map/add | solution.py:239
  24.0 0.7 fusion.115
  24.7 1.1 %fusion.43 = f32[192,192]{1,0:T(8,128)S(1)} fusion(s32[192]{0:T(256)S(1)} %copy-done.10), kind=kOutput, calls=%fused_computation.76 | convolution fusion | flops 85340160 | bytes 148224 | tf_op jit(solution)/shard_map/ji,ja->ai/dot_general | solution.py:118
  25.8 1.8 %fusion.117 = (f32[192,192]{1,0:T(8,128)S(1)}, f32[192,192]{1,0:T(8,128)}) fusion(s32[192]{0:T(256)S(1)} %copy-done.10), kind=kOutput, calls=%fused_computation.201 | convolution fusion | flops 85377024 | bytes 295680 | tf_op jit(solution)/shard_map/ji,ja->ai/dot_general | solution.py:119
  27.6 5.7 %fusion.19 = (f32[4,256,192]{2,1,0:T(8,128)}, f32[4,256,192]{2,1,0:T(8,128)}) fusion(f32[192]{0:T(256)S(1)} %integer_pow.18, f32[4,256]{1,0:T(4,128)S(1)} %integer_pow.17), kind=kLoop, calls=%fused_computation.31 | loop fusion | flops 393216 | bytes 1577728 | tf_op jit(solution)/shard_map/sin | solution.py:211
  33.3 10.3 %collective-permute-done.3 = f32[4,8]{1,0:T(4,128)S(1)} collective-permute-done((f32[4,8]{1,0:T(4,128)S(1)}, f32[4,8]{1,0:T(4,128)S(1)}, u32[]{:S(2)}, u32[]{:S(2)}) %collective-permute-start.3) | collective-permute-done | bytes 160 | tf_op jit(solution)/shard_map/ppermute | solution.py:176
  43.6 5.2 %collective-permute-done.2 = f32[4,8]{1,0:T(4,128)S(1)} collective-permute-done((f32[4,8]{1,0:T(4,128)S(1)}, f32[4,8]{1,0:T(4,128)S(1)}, u32[]{:S(2)}, u32[]{:S(2)}) %collective-permute-start.2) | collective-permute-done | bytes 160 | tf_op jit(solution)/shard_map/ppermute | solution.py:175
  48.9 6.0 %all-to-all-done = f32[32,96,128]{2,1,0:T(8,128)S(1)} async-done(((f32[32,96,128]{2,1,0:T(8,128)}), f32[32,96,128]{2,1,0:T(8,128)S(1)}, u32[]{:S(2)}, u32[]{:S(2)}) %all-to-all-start) | async-done | bytes 1572896 | tf_op jit(solution)/shard_map/all_to_all | solution.py:140
  56.1 0.9 %copy.51 = f32[4,384,8]{1,2,0:T(8,128)} copy(f32[4,384,8]{2,1,0:T(8,128)S(1)} %get-tuple-element.18) | data formatting | bytes 98304
  57.0 3.0 %collective-permute-start.1 = (f32[4,8,384]{2,1,0:T(8,128)}, f32[4,8,384]{2,1,0:T(8,128)S(1)}, u32[]{:S(2)}, u32[]{:S(2)}) collective-permute-start(f32[4,8,384]{2,1,0:T(8,128)} %bitcast.195), channel_id=1, source_target_pairs={{1,0},{2,1},{3,2},{4,3},{5,4},{6,5},{7,6},{8,7},{9,8},{10,9},{11,1... | collective-permute-start | bytes 147464 | tf_op jit(solution)/shard_map/ppermute | solution.py:176
  60.5 3.9 %fusion.21 = f32[4,256,384]{2,1,0:T(8,128)S(1)} fusion(f32[4,384,256]{2,1,0:T(8,128)S(1)} %bitcast.190, f32[192,192]{1,0:T(8,128)S(1)} %fusion.43, f32[192,192]{1,0:T(8,128)} %get-tuple-element.58, f32[192,192]{1,0:T(8,128)S(1)} %get-tuple-element.57), kind=kOutput, calls=%fused_computation.42 | convolution fusion | flops 906412032 | bytes 3588096 | tf_op jit(solution)/shard_map/xy,syq->sqx/dot_general | solution.py:204
  64.4 0.6 subtract_bitcast_fusion
  65.1 2.5 %collective-permute-done = f32[4,8,384]{2,1,0:T(8,128)S(1)} collective-permute-done((f32[4,8,384]{2,1,0:T(8,128)S(1)}, f32[4,8,384]{2,1,0:T(8,128)S(1)}, u32[]{:S(2)}, u32[]{:S(2)}) %collective-permute-start) | collective-permute-done | bytes 49184 | tf_op jit(solution)/shard_map/ppermute | solution.py:175
  67.6 0.4 fusion.28
  68.0 0.5 subtract_bitcast_fusion.1
  68.6 2.5 %fusion.9 = f32[2,4,256,192]{2,3,0,1:T(8,128)S(1)} fusion(f32[4,256,8]{1,2,0:T(8,128)S(1)} %copy-done.7, f32[4,256,8]{1,2,0:T(8,128)S(1)} %copy-done.6, f32[4,256,256]{1,2,0:T(8,128)S(1)} %slice-done, f32[1,4,16,192]{3,2,1,0:T(8,128)S(1)} %get-tuple-element.32, f32[1,4,16,192]{3,2,1,0:T(8,128)S(1)} %get-tuple-element.31, ...), kind=kOutput, calls=%fused_computation.12 | convolution fusion | flops 643538944 | bytes 4358144 | tf_op jit(solution)/shard_map/sij,csja->csia/dot_general | solution.py:244
  71.1 1.2 %copy.34 = f32[2,4,256,192]{2,3,1,0:T(8,128)} copy(f32[2,4,256,192]{2,3,0,1:T(8,128)S(1)} %fusion.9) | data formatting | bytes 3145728 | tf_op jit(solution)/shard_map/sij,csja->csia/transpose | solution.py:244
  (71 shorter events, 3.8 us)
Async XLA Ops:
  10.0 7.3 %copy-start.4 = (f32[4,256]{1,0:T(4,128)S(1)}, f32[4,256]{1,0:T(4,128)}, u32[]{:S(2)}) copy-start(f32[4,256]{1,0:T(4,128)} %param.8) | copy-start | bytes 12292
  10.0 12.6 %copy-start.8 = (s32[4,256]{1,0:T(4,128)S(1)}, s32[4,256]{1,0:T(4,128)}, u32[]{:S(2)}) copy-start(s32[4,256]{1,0:T(4,128)} %param.10) | copy-start | bytes 12292
  10.0 12.7 %copy-start.5 = (f32[8,4,256]{2,1,0:T(4,128)S(1)}, f32[8,4,256]{2,1,0:T(4,128)}, u32[]{:S(2)}) copy-start(f32[8,4,256]{2,1,0:T(4,128)} %param.11) | copy-start | bytes 98308
  10.0 44.8 %all-to-all-start = ((f32[32,96,128]{2,1,0:T(8,128)}), f32[32,96,128]{2,1,0:T(8,128)S(1)}, u32[]{:S(2)}, u32[]{:S(2)}) async-start(f32[32,96,128]{2,1,0:T(8,128)} %bitcast.17), calls=%async_computation | async-start | bytes 3145728 | tf_op jit(solution)/shard_map/all_to_all | solution.py:140
  17.4 26.2 %collective-permute-start.3 = (f32[4,8]{1,0:T(4,128)S(1)}, f32[4,8]{1,0:T(4,128)S(1)}, u32[]{:S(2)}, u32[]{:S(2)}) collective-permute-start(f32[4,8]{1,0:T(4,128)S(1)} %get-tuple-element.54), channel_id=1, source_target_pairs={{1,0},{2,1},{3,2},{4,3},{5,4},{6,5},{7,6},{8,7},{9,8},{10,9},{11,1... | collective-permute-start | bytes 392 | tf_op jit(solution)/shard_map/ppermute | solution.py:176
  22.6 26.2 %collective-permute-start.2 = (f32[4,8]{1,0:T(4,128)S(1)}, f32[4,8]{1,0:T(4,128)S(1)}, u32[]{:S(2)}, u32[]{:S(2)}) collective-permute-start(f32[4,8]{1,0:T(4,128)S(1)} %get-tuple-element.53), channel_id=1, source_target_pairs={{0,1},{1,2},{2,3},{3,4},{4,5},{5,6},{6,7},{7,8},{8,9},{9,10},{10,1... | collective-permute-start | bytes 392 | tf_op jit(solution)/shard_map/ppermute | solution.py:175
  22.8 1.2 %copy-start.9 = (f32[192]{0:T(256)S(1)}, f32[192]{0:T(256)}, u32[]{:S(2)}) copy-start(f32[192]{0:T(256)} %param.9) | copy-start | bytes 2308
  22.8 1.9 %copy-start.10 = (s32[192]{0:T(256)S(1)}, s32[192]{0:T(256)}, u32[]{:S(2)}) copy-start(s32[192]{0:T(256)} %param.7) | copy-start | bytes 2308
  23.9 3.6 %copy-start = (f32[4,256,272]{1,2,0:T(8,128)}, f32[4,256,272]{1,2,0:T(8,128)S(1)}, u32[]{:S(2)}) copy-start(f32[4,256,272]{1,2,0:T(8,128)S(1)} %select_add_fusion) | copy-start | bytes 3342340
  57.0 8.0 %collective-permute-start.1 = (f32[4,8,384]{2,1,0:T(8,128)}, f32[4,8,384]{2,1,0:T(8,128)S(1)}, u32[]{:S(2)}, u32[]{:S(2)}) collective-permute-start(f32[4,8,384]{2,1,0:T(8,128)} %bitcast.195), channel_id=1, source_target_pairs={{1,0},{2,1},{3,2},{4,3},{5,4},{6,5},{7,6},{8,7},{9,8},{10,9},{11,1... | collective-permute-start | bytes 147464 | tf_op jit(solution)/shard_map/ppermute | solution.py:176
  60.2 7.4 %collective-permute-start = (f32[4,8,384]{2,1,0:T(8,128)S(1)}, f32[4,8,384]{2,1,0:T(8,128)S(1)}, u32[]{:S(2)}, u32[]{:S(2)}) collective-permute-start(f32[4,8,384]{2,1,0:T(8,128)S(1)} %bitcast.196), channel_id=1, source_target_pairs={{0,1},{1,2},{2,3},{3,4},{4,5},{5,6},{6,7},{7,8},{8,9},{9,10},{10,1... | collective-permute-start | bytes 147464 | tf_op jit(solution)/shard_map/ppermute | solution.py:175
  60.5 3.9 %copy-start.1 = (f32[4,256,192]{2,1,0:T(8,128)S(1)}, f32[4,256,192]{2,1,0:T(8,128)}, u32[]{:S(2)}) copy-start(f32[4,256,192]{2,1,0:T(8,128)} %get-tuple-element.8) | copy-start | bytes 2359300
  60.5 3.9 %copy-start.2 = (f32[4,256,192]{2,1,0:T(8,128)S(1)}, f32[4,256,192]{2,1,0:T(8,128)}, u32[]{:S(2)}) copy-start(f32[4,256,192]{2,1,0:T(8,128)} %get-tuple-element.7) | copy-start | bytes 2359300
  64.4 3.6 %copy-start.3 = (f32[192,192]{1,0:T(8,128)S(1)}, f32[192,192]{1,0:T(8,128)}, u32[]{:S(2)}) copy-start(f32[192,192]{1,0:T(8,128)} %get-tuple-element.58) | copy-start | bytes 442372
  65.0 3.5 %slice-start = ((f32[4,256,272]{1,2,0:T(8,128)}), f32[4,256,256]{1,2,0:T(8,128)S(1)}, s32[]{:S(2)}) async-start(f32[4,256,272]{1,2,0:T(8,128)} %copy-done), calls=%async_computation.1 | async-start | bytes 2097152 | tf_op jit(solution)/shard_map/slice | solution.py:242
  65.0 3.5 %copy-start.6 = (f32[4,256,8]{1,2,0:T(8,128)S(1)}, f32[4,256,8]{1,2,0:T(8,128)}, u32[]{:S(2)}) copy-start(f32[4,256,8]{1,2,0:T(8,128)} %get-tuple-element.25) | copy-start | bytes 98308
  65.0 3.5 %copy-start.7 = (f32[4,256,8]{1,2,0:T(8,128)S(1)}, f32[4,256,8]{1,2,0:T(8,128)}, u32[]{:S(2)}) copy-start(f32[4,256,8]{1,2,0:T(8,128)} %get-tuple-element.26) | copy-start | bytes 98308

commit v20 on v19

--- a/solution.py
+++ b/solution.py
@@ -218,8 +218,9 @@
     )
 
     rims = jnp.concatenate([rim_left, rim_right], axis=1)
-    rim_real = jnp.einsum("ay,sjy->sja", fold_top, rims, precision=fast)
-    rim_imag = jnp.einsum("ay,sjy->sja", fold_bottom, rims, precision=fast)
+    rim_both = jnp.einsum("xy,sjy->sjx", fold_both, rims, precision=fast)
+    rim_real = rim_both[..., :total_rows]
+    rim_imag = rim_both[..., total_rows:]
     rims = focus(rim_real, rim_imag, jnp.concatenate([wave_left, wave_right], axis=1))
     widened = jnp.concatenate([focused, rims], axis=2)
 

time: 72.6 us -> 72.6 us (level)
  no operation moved by 1% of the time
where the time goes in v20:
time: 72.6 us; the launch traced here: 72.3 us
  waiting for transfers between devices  23.9 us (33%)
  starting transfers between devices  15.7 us (22%)
  matrix products  13.3 us (18%)
  other arithmetic  10.5 us (14%)
  local copies, waits for them, and re-layouts  8.47 us (12%)
    ppermute x2, waiting for transfers between devices, beside(): right = lax.ppermute(right_piece, axes, down)  10.3 us
    ppermute x2, starting transfers between devices, beside(): right = lax.ppermute(right_piece, axes, down)  8.19 us
    ppermute x2, waiting for transfers between devices, beside(): left = lax.ppermute(left_piece, axes, up)  7.66 us
    all_to_all x1, starting transfers between devices, on_device(): lax.all_to_all(spectrum, ('pulse', 'rng'), split_axis=0, concat_axis=0, t...  7.3 us
    all_to_all x1, waiting for transfers between devices, on_device(): lax.all_to_all(spectrum, ('pulse', 'rng'), split_axis=0, concat_axis=0, t...  5.95 us
    sin x1, other arithmetic, on_device(): jnp.sin(phase_angle)  5.72 us
    dot_general x1, matrix products, on_device(): az_both = jnp.einsum('xy,syq->sqx', fold_both, combined, precision=fast)  3.88 us
    dot_general x1, matrix products, range_dft_blocks(): jnp.einsum('ducb,crba->drua', stacked_table(outer_len, 1.0), signal, prec...  2.66 us
  transfers between devices with their start and end apart: 5, of which 4 were waited for; matrix products, arithmetic and copies ran while one was open for 21% of the time, Pallas kernels for 0%

profile of v20, /device:TPU:0, one launch (start us, length us, event | category | flops | bytes accessed | tf_op | source)
XLA Modules:
  0.0 72.3 jit_solution(15846013160231182652)
XLA Ops:
  1.0 2.4 %reshape.603 = f32[2,24,128,64]{3,2,1,0:T(8,128)S(1)} reshape(f32[2,24,8192]{2,1,0:T(8,128)} %param.6) | data formatting | bytes 3145728 | tf_op jit(solution)/shard_map/reshape | solution.py:77
  3.7 2.7 %fusion.12 = f32[2,24,128,64]{2,3,1,0:T(8,128)S(1)} fusion(f32[2,24,128,64]{3,2,1,0:T(8,128)S(1)} %reshape.603, f32[1,128,2,128]{3,1,2,0:T(8,128)S(1)} %get-tuple-element.34, f32[1,128,2,128]{3,1,2,0:T(8,128)S(1)} %get-tuple-element.33), kind=kOutput, calls=%fused_computation.13 | convolution fusion | flops 604045312 | bytes 3407872 | tf_op jit(solution)/shard_map/ducb,crba->drua/dot_general | solution.py:78
  6.4 0.3 multiply_subtract_fusion.1
  6.7 0.8 %fusion.6 = f32[64,2,24,128]{3,0,1,2:T(8,128)S(1)} fusion(f32[1,64,2,64]{3,1,2,0:T(8,128)S(1)} %get-tuple-element.44, f32[1,64,2,64]{3,1,2,0:T(8,128)S(1)} %get-tuple-element.43, f32[1,24,128,64]{2,3,1,0:T(8,128)S(1)} %get-tuple-element.16, f32[1,24,128,64]{2,3,1,0:T(8,128)S(1)} %get-tuple-element.15), kind=kOutput, calls=%fused_computation.11 | convolution fusion | flops 302399488 | bytes 3211264 | tf_op jit(solution)/shard_map/dvca,crua->vdru/dot_general | solution.py:90
  7.9 2.1 %copy.23 = f32[64,2,24,128]{3,2,1,0:T(8,128)} copy(f32[64,2,24,128]{3,0,1,2:T(8,128)S(1)} %pad_maximum_fusion) | data formatting | bytes 3145728 | tf_op jit(solution)/shard_map/stack | solution.py:99
  10.0 7.3 %all-to-all-start = ((f32[32,96,128]{2,1,0:T(8,128)}), f32[32,96,128]{2,1,0:T(8,128)S(1)}, u32[]{:S(2)}, u32[]{:S(2)}) async-start(f32[32,96,128]{2,1,0:T(8,128)} %bitcast.17), calls=%async_computation | async-start | bytes 3145728 | tf_op jit(solution)/shard_map/all_to_all | solution.py:140
  17.4 5.2 %collective-permute-start.3 = (f32[4,8]{1,0:T(4,128)S(1)}, f32[4,8]{1,0:T(4,128)S(1)}, u32[]{:S(2)}, u32[]{:S(2)}) collective-permute-start(f32[4,8]{1,0:T(4,128)S(1)} %get-tuple-element.54), channel_id=1, source_target_pairs={{1,0},{2,1},{3,2},{4,3},{5,4},{6,5},{7,6},{8,7},{9,8},{10,9},{11,1... | collective-permute-start | bytes 392 | tf_op jit(solution)/shard_map/ppermute | solution.py:176
  22.8 1.2 %select_add_fusion = f32[4,256,272]{1,2,0:T(8,128)S(1)} fusion(f32[4,256]{1,0:T(4,128)S(1)} %get-tuple-element.36, s32[4,256]{1,0:T(4,128)S(1)} %get-tuple-element.52, f32[4,256]{1,0:T(4,128)S(1)} %get-tuple-element.37, s32[4,256]{1,0:T(4,128)S(1)} %get-tuple-element.48, f32[4,256]{1,0:T(4,128)S(1)} %get-tuple-element.38, ...), kind=kLoop, calls=%fused_computation.19 | loop fusion | flops 6406144 | bytes 1179648 | tf_op jit(solution)/shard_map/add | solution.py:240
  24.0 0.7 fusion.106
  24.7 1.1 %fusion.32 = f32[192,192]{1,0:T(8,128)S(1)} fusion(s32[192]{0:T(256)S(1)} %copy-done.10), kind=kOutput, calls=%fused_computation.63 | convolution fusion | flops 85340160 | bytes 148224 | tf_op jit(solution)/shard_map/ji,ja->ai/dot_general | solution.py:118
  25.8 1.8 %fusion.108 = (f32[192,192]{1,0:T(8,128)S(1)}, f32[192,192]{1,0:T(8,128)}) fusion(s32[192]{0:T(256)S(1)} %copy-done.10), kind=kOutput, calls=%fused_computation.189 | convolution fusion | flops 85377024 | bytes 295680 | tf_op jit(solution)/shard_map/ji,ja->ai/dot_general | solution.py:119
  27.6 5.7 %fusion.19 = (f32[4,256,192]{2,1,0:T(8,128)}, f32[4,256,192]{2,1,0:T(8,128)}) fusion(f32[192]{0:T(256)S(1)} %integer_pow.18, f32[4,256]{1,0:T(4,128)S(1)} %integer_pow.17), kind=kLoop, calls=%fused_computation.31 | loop fusion | flops 393216 | bytes 1577728 | tf_op jit(solution)/shard_map/sin | solution.py:211
  33.3 10.3 %collective-permute-done.3 = f32[4,8]{1,0:T(4,128)S(1)} collective-permute-done((f32[4,8]{1,0:T(4,128)S(1)}, f32[4,8]{1,0:T(4,128)S(1)}, u32[]{:S(2)}, u32[]{:S(2)}) %collective-permute-start.3) | collective-permute-done | bytes 160 | tf_op jit(solution)/shard_map/ppermute | solution.py:176
  43.6 5.2 %collective-permute-done.2 = f32[4,8]{1,0:T(4,128)S(1)} collective-permute-done((f32[4,8]{1,0:T(4,128)S(1)}, f32[4,8]{1,0:T(4,128)S(1)}, u32[]{:S(2)}, u32[]{:S(2)}) %collective-permute-start.2) | collective-permute-done | bytes 160 | tf_op jit(solution)/shard_map/ppermute | solution.py:175
  48.9 6.0 %all-to-all-done = f32[32,96,128]{2,1,0:T(8,128)S(1)} async-done(((f32[32,96,128]{2,1,0:T(8,128)}), f32[32,96,128]{2,1,0:T(8,128)S(1)}, u32[]{:S(2)}, u32[]{:S(2)}) %all-to-all-start) | async-done | bytes 1572896 | tf_op jit(solution)/shard_map/all_to_all | solution.py:140
  56.1 0.9 %copy.51 = f32[4,384,8]{1,2,0:T(8,128)} copy(f32[4,384,8]{2,1,0:T(8,128)S(1)} %get-tuple-element.18) | data formatting | bytes 98304
  57.0 3.0 %collective-permute-start.1 = (f32[4,8,384]{2,1,0:T(8,128)}, f32[4,8,384]{2,1,0:T(8,128)S(1)}, u32[]{:S(2)}, u32[]{:S(2)}) collective-permute-start(f32[4,8,384]{2,1,0:T(8,128)} %bitcast.188), channel_id=1, source_target_pairs={{1,0},{2,1},{3,2},{4,3},{5,4},{6,5},{7,6},{8,7},{9,8},{10,9},{11,1... | collective-permute-start | bytes 147464 | tf_op jit(solution)/shard_map/ppermute | solution.py:176
  60.5 3.9 %fusion.22 = f32[4,256,384]{2,1,0:T(8,128)S(1)} fusion(f32[4,384,256]{2,1,0:T(8,128)S(1)} %bitcast.183, f32[192,192]{1,0:T(8,128)S(1)} %fusion.32, f32[192,192]{1,0:T(8,128)} %get-tuple-element.58, f32[192,192]{1,0:T(8,128)S(1)} %get-tuple-element.57), kind=kOutput, calls=%fused_computation.43 | convolution fusion | flops 906412032 | bytes 3588096 | tf_op jit(solution)/shard_map/xy,syq->sqx/dot_general | solution.py:204
  64.4 0.6 subtract_bitcast_fusion
  65.1 2.5 %collective-permute-done = f32[4,8,384]{2,1,0:T(8,128)S(1)} collective-permute-done((f32[4,8,384]{2,1,0:T(8,128)S(1)}, f32[4,8,384]{2,1,0:T(8,128)S(1)}, u32[]{:S(2)}, u32[]{:S(2)}) %collective-permute-start) | collective-permute-done | bytes 49184 | tf_op jit(solution)/shard_map/ppermute | solution.py:175
  67.6 0.5 fusion.21
  68.1 0.3 subtract_bitcast_fusion.1
  68.5 2.5 %fusion.9 = f32[2,4,256,192]{2,3,0,1:T(8,128)S(1)} fusion(f32[4,256,8]{1,2,0:T(8,128)S(1)} %copy-done.7, f32[4,256,8]{1,2,0:T(8,128)S(1)} %copy-done.6, f32[4,256,256]{1,2,0:T(8,128)S(1)} %slice-done, f32[1,4,16,192]{3,2,1,0:T(8,128)S(1)} %get-tuple-element.32, f32[1,4,16,192]{3,2,1,0:T(8,128)S(1)} %get-tuple-element.31, ...), kind=kOutput, calls=%fused_computation.12 | convolution fusion | flops 643538944 | bytes 4358144 | tf_op jit(solution)/shard_map/sij,csja->csia/dot_general | solution.py:245
  71.0 1.2 %copy.34 = f32[2,4,256,192]{2,3,1,0:T(8,128)} copy(f32[2,4,256,192]{2,3,0,1:T(8,128)S(1)} %fusion.9) | data formatting | bytes 3145728 | tf_op jit(solution)/shard_map/sij,csja->csia/transpose | solution.py:245
  (71 shorter events, 3.8 us)
Async XLA Ops:
  10.0 7.3 %copy-start.4 = (f32[4,256]{1,0:T(4,128)S(1)}, f32[4,256]{1,0:T(4,128)}, u32[]{:S(2)}) copy-start(f32[4,256]{1,0:T(4,128)} %param.8) | copy-start | bytes 12292
  10.0 12.6 %copy-start.8 = (s32[4,256]{1,0:T(4,128)S(1)}, s32[4,256]{1,0:T(4,128)}, u32[]{:S(2)}) copy-start(s32[4,256]{1,0:T(4,128)} %param.10) | copy-start | bytes 12292
  10.0 12.7 %copy-start.5 = (f32[8,4,256]{2,1,0:T(4,128)S(1)}, f32[8,4,256]{2,1,0:T(4,128)}, u32[]{:S(2)}) copy-start(f32[8,4,256]{2,1,0:T(4,128)} %param.11) | copy-start | bytes 98308
  10.0 44.8 %all-to-all-start = ((f32[32,96,128]{2,1,0:T(8,128)}), f32[32,96,128]{2,1,0:T(8,128)S(1)}, u32[]{:S(2)}, u32[]{:S(2)}) async-start(f32[32,96,128]{2,1,0:T(8,128)} %bitcast.17), calls=%async_computation | async-start | bytes 3145728 | tf_op jit(solution)/shard_map/all_to_all | solution.py:140
  17.4 26.2 %collective-permute-start.3 = (f32[4,8]{1,0:T(4,128)S(1)}, f32[4,8]{1,0:T(4,128)S(1)}, u32[]{:S(2)}, u32[]{:S(2)}) collective-permute-start(f32[4,8]{1,0:T(4,128)S(1)} %get-tuple-element.54), channel_id=1, source_target_pairs={{1,0},{2,1},{3,2},{4,3},{5,4},{6,5},{7,6},{8,7},{9,8},{10,9},{11,1... | collective-permute-start | bytes 392 | tf_op jit(solution)/shard_map/ppermute | solution.py:176
  22.6 26.2 %collective-permute-start.2 = (f32[4,8]{1,0:T(4,128)S(1)}, f32[4,8]{1,0:T(4,128)S(1)}, u32[]{:S(2)}, u32[]{:S(2)}) collective-permute-start(f32[4,8]{1,0:T(4,128)S(1)} %get-tuple-element.53), channel_id=1, source_target_pairs={{0,1},{1,2},{2,3},{3,4},{4,5},{5,6},{6,7},{7,8},{8,9},{9,10},{10,1... | collective-permute-start | bytes 392 | tf_op jit(solution)/shard_map/ppermute | solution.py:175
  22.8 1.2 %copy-start.9 = (f32[192]{0:T(256)S(1)}, f32[192]{0:T(256)}, u32[]{:S(2)}) copy-start(f32[192]{0:T(256)} %param.9) | copy-start | bytes 2308
  22.8 1.9 %copy-start.10 = (s32[192]{0:T(256)S(1)}, s32[192]{0:T(256)}, u32[]{:S(2)}) copy-start(s32[192]{0:T(256)} %param.7) | copy-start | bytes 2308
  23.9 3.6 %copy-start = (f32[4,256,272]{1,2,0:T(8,128)}, f32[4,256,272]{1,2,0:T(8,128)S(1)}, u32[]{:S(2)}) copy-start(f32[4,256,272]{1,2,0:T(8,128)S(1)} %select_add_fusion) | copy-start | bytes 3342340
  57.0 8.0 %collective-permute-start.1 = (f32[4,8,384]{2,1,0:T(8,128)}, f32[4,8,384]{2,1,0:T(8,128)S(1)}, u32[]{:S(2)}, u32[]{:S(2)}) collective-permute-start(f32[4,8,384]{2,1,0:T(8,128)} %bitcast.188), channel_id=1, source_target_pairs={{1,0},{2,1},{3,2},{4,3},{5,4},{6,5},{7,6},{8,7},{9,8},{10,9},{11,1... | collective-permute-start | bytes 147464 | tf_op jit(solution)/shard_map/ppermute | solution.py:176
  60.2 7.4 %collective-permute-start = (f32[4,8,384]{2,1,0:T(8,128)S(1)}, f32[4,8,384]{2,1,0:T(8,128)S(1)}, u32[]{:S(2)}, u32[]{:S(2)}) collective-permute-start(f32[4,8,384]{2,1,0:T(8,128)S(1)} %bitcast.189), channel_id=1, source_target_pairs={{0,1},{1,2},{2,3},{3,4},{4,5},{5,6},{6,7},{7,8},{8,9},{9,10},{10,1... | collective-permute-start | bytes 147464 | tf_op jit(solution)/shard_map/ppermute | solution.py:175
  60.5 3.9 %copy-start.1 = (f32[4,256,192]{2,1,0:T(8,128)S(1)}, f32[4,256,192]{2,1,0:T(8,128)}, u32[]{:S(2)}) copy-start(f32[4,256,192]{2,1,0:T(8,128)} %get-tuple-element.8) | copy-start | bytes 2359300
  60.5 3.9 %copy-start.2 = (f32[4,256,192]{2,1,0:T(8,128)S(1)}, f32[4,256,192]{2,1,0:T(8,128)}, u32[]{:S(2)}) copy-start(f32[4,256,192]{2,1,0:T(8,128)} %get-tuple-element.7) | copy-start | bytes 2359300
  64.4 3.2 %copy-start.3 = (f32[192,192]{1,0:T(8,128)S(1)}, f32[192,192]{1,0:T(8,128)}, u32[]{:S(2)}) copy-start(f32[192,192]{1,0:T(8,128)} %get-tuple-element.58) | copy-start | bytes 442372
  65.0 3.5 %slice-start = ((f32[4,256,272]{1,2,0:T(8,128)}), f32[4,256,256]{1,2,0:T(8,128)S(1)}, s32[]{:S(2)}) async-start(f32[4,256,272]{1,2,0:T(8,128)} %copy-done), calls=%async_computation.1 | async-start | bytes 2097152 | tf_op jit(solution)/shard_map/slice | solution.py:243
  65.0 3.5 %copy-start.6 = (f32[4,256,8]{1,2,0:T(8,128)S(1)}, f32[4,256,8]{1,2,0:T(8,128)}, u32[]{:S(2)}) copy-start(f32[4,256,8]{1,2,0:T(8,128)} %get-tuple-element.25) | copy-start | bytes 98308
  65.0 3.5 %copy-start.7 = (f32[4,256,8]{1,2,0:T(8,128)S(1)}, f32[4,256,8]{1,2,0:T(8,128)}, u32[]{:S(2)}) copy-start(f32[4,256,8]{1,2,0:T(8,128)} %get-tuple-element.26) | copy-start | bytes 98308
